TPU v7x, 32 devices: a whole 2x2x4 slice. The times are simulated.
32 devices in a mesh: gx: 8 (over z, core), gy: 4 (over y, x).
Axes of the slice: x: 2, y: 2, z: 4, core: 2. Of those that a mesh axis runs over, the one named last changes fastest.
Arguments:
- pressure: float32 [256, 128, 512], P('gx', 'gy'), may hold values from -6 to 6
- vel_x: float32 [256, 128, 512], P('gx', 'gy'), may hold values from -3 to 3
- vel_y: float32 [256, 128, 512], P('gx', 'gy'), may hold values from -3 to 3
- vel_z: float32 [256, 128, 512], P('gx', 'gy'), may hold values from -3 to 3
- void_frac: float32 [256, 128, 512], P('gx', 'gy'), may hold values from 1e-05 to 0.001
- waves: bfloat16 [24576, 2, 512], P(('gx', 'gy')), may hold values from -6 to 6
- bubble_dest: int32 [24576, 1], P(('gx', 'gy')), may hold values from 0 to 31; in each aligned block of 768 rows (0 to 767, 768 to 1535, ...) at most 48 rows name the same one
- bubble_column: int32 [24576], P(('gx', 'gy')), may hold values from 0 to 1023
- history: bfloat16 [128, 128, 512], P('gx', 'gy'), may hold values from -3 to 3
- delays: int32 [8, 8], replicated, may hold values from 0 to 15
Outputs:
- pressure_out: float32 [256, 128, 512], P('gx', 'gy')
- vel_x_out: float32 [256, 128, 512], P('gx', 'gy')
- vel_y_out: float32 [256, 128, 512], P('gx', 'gy')
- vel_z_out: float32 [256, 128, 512], P('gx', 'gy')
Inputs may be any that keep to these rules, and one draw needn't show every extreme that they name: `bubble_dest`: among the 768 bubbles listed on one device (an aligned block of rows), no tile is named more than 48 times.
All inputs are finite; a program needn't handle non-finite values.
Results may differ from a plain program's by a relative error of at most 0.00045.
Values may be sent and summed in bfloat16 or wider, within the bound.
No kernel may reach another device: no remote copies, remote signals or barrier semaphores. Data moves between devices by JAX's collectives and lax.ppermute only.
A program may use at most 128 MiB of HBM per device.

v0:
```python
import jax
import jax.numpy as jnp
from jax import lax
from jax.sharding import PartitionSpec as P

step_ratio = 0.4
gas_density = 0.001
gas_stiffness = 5.29e-05


def shortened(array):

    def short(part):
        return part.astype(jnp.bfloat16) if part.dtype == jnp.float32 else part

    return jax.tree.map(short, array)


def from_behind(block, axis, distance):
    devices = range(lax.axis_size(axis))
    route = [(i - distance, i) for i in devices if i - distance in devices]
    return lax.ppermute(block, axis, route)


def material(void_frac):
    liquid = 1.0 - void_frac
    buoyancy = 1.0 / (liquid + void_frac * gas_density)
    stiffness = 1.0 / (liquid + void_frac / gas_stiffness)
    return (buoyancy, stiffness)


def body(
    pressure, vel_x, vel_y, vel_z, void_frac, waves, bubble_dest, bubble_column, history, delays
):
    size_x, size_y, depth = pressure.shape
    tiles_x = lax.axis_size("gx")
    tiles_y = lax.axis_size("gy")
    devices = tiles_x * tiles_y
    bubbles = waves.shape[0]
    steps = waves.shape[1]
    capacity = 2 * bubbles // devices
    slots = devices * capacity
    buoyancy, stiffness = material(void_frac)
    dest = bubble_dest[:, 0]
    owners = (dest[:, None] == jnp.arange(devices, dtype=jnp.int32)[None, :]).astype(jnp.int32)
    rank = jnp.sum(jnp.cumsum(owners, axis=0) * owners, axis=1) - 1
    slot_ids = dest * capacity + rank
    placed = slot_ids[None, :] == jnp.arange(slots, dtype=jnp.int32)[:, None]
    outgoing = jnp.dot(
        placed.astype(jnp.bfloat16),
        waves.reshape(bubbles, steps * depth),
        preferred_element_type=jnp.float32,
    ).astype(jnp.bfloat16)
    out_cols = jnp.max(jnp.where(placed, bubble_column[None, :] + 1, 0), axis=1) - 1
    incoming, in_cols = (
        lax.all_to_all(
            outgoing.reshape(devices, capacity, steps * depth),
            ("gx", "gy"),
            split_axis=0,
            concat_axis=0,
            tiled=True,
        ),
        lax.all_to_all(
            out_cols.reshape(devices, capacity),
            ("gx", "gy"),
            split_axis=0,
            concat_axis=0,
            tiled=True,
        ),
    )
    hits = (
        jnp.arange(size_x * size_y, dtype=jnp.int32)[:, None] == in_cols.reshape(slots)[None, :]
    ).astype(jnp.bfloat16)
    source = jnp.dot(
        hits, incoming.reshape(slots, steps * depth), preferred_element_type=jnp.float32
    )
    source = source.reshape(size_x, size_y, steps, depth)
    my_tile = lax.axis_index("gx")
    cycle = jnp.arange(tiles_x, dtype=jnp.int32)
    dist = jnp.abs(cycle - my_tile)
    dist = jnp.minimum(dist, tiles_x - dist)
    weight = 1.0 / (1.0 + 2.0 * dist.astype(jnp.float32) / tiles_x)
    levels = history.shape[0]
    my_delays = lax.dynamic_index_in_dim(delays, my_tile, 0, keepdims=False)
    piece = lax.all_gather(history, "gx", axis=0, tiled=True)
    count = piece.shape[0]
    row_ids = jnp.arange(count, dtype=jnp.int32)
    source_tile = row_ids // levels
    picked = row_ids % levels == jnp.take(my_delays, source_tile)
    coeff = jnp.where(picked, jnp.take(weight, source_tile), 0.0)
    summed = jnp.dot(
        coeff,
        piece.reshape(count, size_y * depth),
        precision=lax.Precision.HIGHEST,
        preferred_element_type=jnp.float32,
    )
    incident = summed.reshape(size_y, depth)
    forcing = jnp.zeros_like(pressure).at[0].set(incident)
    z_edge = jnp.zeros((size_x, size_y, 1), jnp.float32)
    for step in range(steps):
        upper_x = from_behind(shortened(pressure[0:1]), "gx", -1)
        upper_y = from_behind(shortened(pressure[:, 0:1]), "gy", -1)
        next_x = jnp.concatenate([pressure[1:], upper_x], 0)
        next_y = jnp.concatenate([pressure[:, 1:], upper_y], 1)
        next_z = jnp.concatenate([pressure[:, :, 1:], z_edge], 2)
        vel_x = vel_x - step_ratio * buoyancy * (next_x - pressure)
        vel_y = vel_y - step_ratio * buoyancy * (next_y - pressure)
        vel_z = vel_z - step_ratio * buoyancy * (next_z - pressure)
        lower_x = from_behind(shortened(vel_x[-1:]), "gx", 1)
        lower_y = from_behind(shortened(vel_y[:, -1:]), "gy", 1)
        prev_x = jnp.concatenate([lower_x, vel_x[:-1]], 0)
        prev_y = jnp.concatenate([lower_y, vel_y[:, :-1]], 1)
        prev_z = jnp.concatenate([z_edge, vel_z[:, :, :-1]], 2)
        divergence = vel_x - prev_x + (vel_y - prev_y) + (vel_z - prev_z)
        pressure = pressure + step_ratio * stiffness * (
            source[:, :, step, :] + forcing - divergence
        )
    return (pressure, vel_x, vel_y, vel_z)


def solution(mesh):
    in_specs = (
        P("gx", "gy", None),
        P("gx", "gy", None),
        P("gx", "gy", None),
        P("gx", "gy", None),
        P("gx", "gy", None),
        P(("gx", "gy"), None, None),
        P(("gx", "gy"), None),
        P(("gx", "gy")),
        P("gx", "gy", None),
        P(),
    )
    out_specs = (P("gx", "gy", None), P("gx", "gy", None), P("gx", "gy", None), P("gx", "gy", None))
    return jax.shard_map(body, mesh=mesh, in_specs=in_specs, out_specs=out_specs, check_vma=False)
```

profile of v0, /device:TPU:18, one launch (start us, length us, event | category | flops | bytes accessed | tf_op | source)
XLA Modules:
  0.0 207.5 jit_solution(8199547124684229068)
XLA Ops:
  7.9 0.7 reduce.2
  8.6 1.7 reduce-window.6
  10.8 0.7 add_add_fusion
  11.5 0.7 select_reduce_fusion
  12.2 0.7 sub.97
  12.9 5.9 %all-to-all-start = ((s32[32,1,48]{2,1,0:T(1,128)}), s32[32,1,48]{2,1,0:T(1,128)S(1)}, u32[]{:S(2)}, u32[]{:S(2)}) async-start(s32[32,1,48]{2,1,0:T(1,128)} %sub.97), calls=%async_computation | async-start | bytes 32768 | tf_op jit(solution)/shard_map/all_to_all | solution.py:63
  18.8 2.1 %copy.31 = bf16[96,8,2,512]{3,1,2,0:T(8,128)(2,1)S(1)} copy(bf16[96,8,2,512]{3,2,1,0:T(2,128)(2,1)} %bitcast.142) | data formatting | bytes 3145728
  21.0 4.0 %fusion.7 = bf16[1536,1024]{1,0:T(8,128)(2,1)} fusion(bf16[768,1024]{1,0:T(8,128)(2,1)S(1)} %bitcast.143, s32[768]{0:T(1024)S(1)} %get-tuple-element.44), kind=kOutput, calls=%fused_computation.9 | convolution fusion | flops 2418671616 | bytes 4721664 | tf_op jit(solution)/shard_map/dot_general | solution.py:49
  24.9 5.9 %all-to-all-start.1 = ((bf16[32,48,1024]{2,1,0:T(8,128)(2,1)}), bf16[32,48,1024]{2,1,0:T(8,128)(2,1)}, u32[]{:S(2)}, u32[]{:S(2)}) async-start(bf16[32,48,1024]{2,1,0:T(8,128)(2,1)} %bitcast.140), calls=%async_computation.1 | async-start | bytes 6291456 | tf_op jit(solution)/shard_map/all_to_all | solution.py:56
  31.0 2.2 %collective-permute-start = (bf16[1,32,512]{2,1,0:T(8,128)(2,1)S(1)}, bf16[1,32,512]{2,1,0:T(8,128)(2,1)S(1)}, u32[]{:S(2)}, u32[]{:S(2)}) collective-permute-start(bf16[1,32,512]{2,1,0:T(8,128)(2,1)S(1)} %slice.156), channel_id=1, source_target_pairs={{4,0},{8,4},{12,8},{16,12},{20,16},{24,20},{28,24},{5,1},{9,5},{13... | collective-permute-start | bytes 98312 | tf_op jit(solution)/shard_map/ppermute | solution.py:22
  33.3 2.5 %collective-permute-start.2 = (bf16[32,1,512]{2,1,0:T(2,128)(2,1)S(1)}, bf16[32,1,512]{2,1,0:T(2,128)(2,1)S(1)}, u32[]{:S(2)}, u32[]{:S(2)}) collective-permute-start(bf16[32,1,512]{2,1,0:T(2,128)(2,1)S(1)} %slice.159), channel_id=1, source_target_pairs={{1,0},{2,1},{3,2},{5,4},{6,5},{7,6},{9,8},{10,9},{11,10},{13,12},{... | collective-permute-start | bytes 98312 | tf_op jit(solution)/shard_map/ppermute | solution.py:22
  37.5 83.9 %collective-permute-done = bf16[1,32,512]{2,1,0:T(8,128)(2,1)S(1)} collective-permute-done((bf16[1,32,512]{2,1,0:T(8,128)(2,1)S(1)}, bf16[1,32,512]{2,1,0:T(8,128)(2,1)S(1)}, u32[]{:S(2)}, u32[]{:S(2)}) %collective-permute-start) | collective-permute-done | bytes 32800 | tf_op jit(solution)/shard_map/ppermute | solution.py:22
  121.5 3.4 %fusion.12 = (f32[32,32,512]{2,1,0:T(8,128)S(1)}, f32[32,32,512]{2,1,0:T(8,128)S(1)}, f32[32,32,512]{2,1,0:T(8,128)}) fusion(f32[32,32,512]{2,1,0:T(8,128)S(1)} %copy-done.15, f32[32,32,512]{2,1,0:T(8,128)S(1)} %copy-done.2, f32[1,32,512]{2,1,0:T(8,128)S(1)} %convert_element_type.48, f32[31,32,512]{2,1,0:T(8,128)S(1)} %slice-done, ...), kind=kLoop, calls=%fused_computation.17 | loop fusion | flops 8388608 | bytes 23064576 | tf_op jit(solution)/shard_map/sub | solution.py:106
  125.0 1.9 collective-permute-start.1
  127.0 3.6 %collective-permute-start.3 = (bf16[32,1,512]{2,1,0:T(2,128)(2,1)S(1)}, bf16[32,1,512]{2,1,0:T(2,128)(2,1)S(1)}, u32[]{:S(2)}, u32[]{:S(2)}) collective-permute-start(bf16[32,1,512]{2,1,0:T(2,128)(2,1)S(1)} %slice.183), channel_id=1, source_target_pairs={{0,1},{1,2},{2,3},{4,5},{5,6},{6,7},{8,9},{9,10},{10,11},{12,13},{... | collective-permute-start | bytes 98312 | tf_op jit(solution)/shard_map/ppermute | solution.py:22
  131.7 0.7 reduce.9
  132.5 3.1 %slice.158 = f32[31,32,512]{2,1,0:T(8,128)} slice(f32[32,32,512]{2,1,0:T(8,128)} %copy-done.8), slice={[0:31], [0:32], [0:512]} | slice | bytes 4063232 | tf_op jit(solution)/shard_map/slice | solution.py:111
  135.8 4.7 %copy.23 = bf16[1536,1024]{0,1:T(8,128)(2,1)} copy(bf16[1536,1024]{1,0:T(8,128)(2,1)} %bitcast.4) | data formatting | bytes 6291456 | tf_op jit(solution)/shard_map/reshape | solution.py:75
  140.5 5.3 %fusion = f32[32,32,2,512]{3,1,2,0:T(8,128)S(1)} fusion(bf16[2,512,1536,1]{2,1,0,3:T(8,128)(2,1)} %bitcast.141, s32[1536]{0:T(1024)S(1)} %eq.81, s32[32,32]{1,0:T(8,128)S(1)} %multiply_add_fusion), kind=kOutput, calls=%fused_computation | convolution fusion | flops 3222798336 | bytes 7350272 | tf_op jit(solution)/shard_map/dot_general | solution.py:74
  145.8 2.0 copy-done.14
  147.8 2.5 %slice_bitcast_fusion = (f32[32,32,512]{2,1,0:T(8,128)}, f32[32,32,512]{2,1,0:T(8,128)}) fusion(f32[32,32,2,512]{3,1,2,0:T(8,128)S(1)} %fusion), kind=kLoop, calls=%fused_computation.13 | loop fusion | bytes 8388608 | tf_op jit(solution)/shard_map/squeeze | solution.py:116
  150.3 18.8 %fusion.4 = f32[1,32,512]{2,0,1:T(1,128)S(1)} fusion(f32[]{:T(128)} %bitcast.21, s32[]{:T(128)} %bitcast.12, f32[]{:T(128)} %bitcast.22, s32[]{:T(128)} %bitcast.13, f32[]{:T(128)} %bitcast.23, s32[]{:T(128)} %bitcast.14, f32[]{:T(128)} %bitcast.24, s32[]{:T(128)} %bitcast.15, f32[]{:T(128)} %bitcast.25, s32[]{:T(128)} %bitcast.16, f32[]{:T(128)} %bitcast.27, ...), kind=kOutput, calls=%fused_computation.6 | convolution fusion | flops 25172736 | bytes 4259904 | tf_op jit(solution)/shard_map/dot_general | solution.py:91
  169.1 1.5 fusion.34
  170.6 4.4 %fusion.102 = (bf16[32,32,512]{2,1,0:T(8,128)(2,1)S(1)}, f32[32,32,512]{2,1,0:T(8,128)S(1)}) fusion(f32[32,32,512]{2,1,0:T(8,128)S(1)} %copy-done.2, f32[32,32,512]{2,1,0:T(8,128)} %get-tuple-element.19, f32[32,32,512]{2,1,0:T(8,128)S(1)} %copy-done.7, f32[32,32,511]{2,1,0:T(8,128)S(1)} %bitcast.137, f32[32,32,512]{2,1,0:T(8,128)S(1)} %copy-done.4, ...), kind=kLoop, calls=%fused_computation.160 | loop fusion | flops 8388608 | bytes 22016000 | tf_op jit(solution)/shard_map/convert.3
  175.1 3.5 %collective-permute-start.4 = (bf16[1,32,512]{2,1,0:T(8,128)(2,1)S(1)}, bf16[1,32,512]{2,1,0:T(8,128)(2,1)S(1)}, u32[]{:S(2)}, u32[]{:S(2)}) collective-permute-start(bf16[1,32,512]{2,1,0:T(8,128)(2,1)S(1)} %slice.165), channel_id=1, source_target_pairs={{4,0},{8,4},{12,8},{16,12},{20,16},{24,20},{28,24},{5,1},{9,5},{13... | collective-permute-start | bytes 98312 | tf_op jit(solution)/shard_map/ppermute | solution.py:22
  178.6 2.7 %collective-permute-start.6 = (bf16[32,1,512]{2,1,0:T(2,128)(2,1)S(1)}, bf16[32,1,512]{2,1,0:T(2,128)(2,1)S(1)}, u32[]{:S(2)}, u32[]{:S(2)}) collective-permute-start(bf16[32,1,512]{2,1,0:T(2,128)(2,1)S(1)} %slice.169), channel_id=1, source_target_pairs={{1,0},{2,1},{3,2},{5,4},{6,5},{7,6},{9,8},{10,9},{11,10},{13,12},{... | collective-permute-start | bytes 98312 | tf_op jit(solution)/shard_map/ppermute | solution.py:22
  182.6 3.1 %collective-permute-done.6 = bf16[32,1,512]{2,1,0:T(2,128)(2,1)S(1)} collective-permute-done((bf16[32,1,512]{2,1,0:T(2,128)(2,1)S(1)}, bf16[32,1,512]{2,1,0:T(2,128)(2,1)S(1)}, u32[]{:S(2)}, u32[]{:S(2)}) %collective-permute-start.6) | collective-permute-done | bytes 32800 | tf_op jit(solution)/shard_map/ppermute | solution.py:22
  185.8 2.8 %multiply_subtract_fusion = (f32[32,32,512]{2,1,0:T(8,128)S(1)}, f32[32,32,512]{2,1,0:T(8,128)S(1)}, f32[32,32,512]{2,1,0:T(8,128)S(1)}) fusion(f32[32,32,512]{2,1,0:T(8,128)S(1)} %copy-done.7, f32[32,32,512]{2,1,0:T(8,128)S(1)} %get-tuple-element.17, f32[32,32,511]{2,1,0:T(8,128)S(1)} %slice.172, f32[32,32,512]{2,1,0:T(8,128)S(1)} %copy-done.6, ...), kind=kLoop, calls=%fused_computation.41 | loop fusion | flops 8388608 | bytes 23064576 | tf_op jit(solution)/shard_map/sub | solution.py:108
  188.7 1.9 collective-permute-start.5
  190.7 2.8 %collective-permute-start.7 = (bf16[32,1,512]{2,1,0:T(2,128)(2,1)S(1)}, bf16[32,1,512]{2,1,0:T(2,128)(2,1)S(1)}, u32[]{:S(2)}, u32[]{:S(2)}) collective-permute-start(bf16[32,1,512]{2,1,0:T(2,128)(2,1)S(1)} %slice.181), channel_id=1, source_target_pairs={{0,1},{1,2},{2,3},{4,5},{5,6},{6,7},{8,9},{9,10},{10,11},{12,13},{... | collective-permute-start | bytes 98312 | tf_op jit(solution)/shard_map/ppermute | solution.py:22
  193.9 3.1 %collective-permute-done.7 = bf16[32,1,512]{2,1,0:T(2,128)(2,1)S(1)} collective-permute-done((bf16[32,1,512]{2,1,0:T(2,128)(2,1)S(1)}, bf16[32,1,512]{2,1,0:T(2,128)(2,1)S(1)}, u32[]{:S(2)}, u32[]{:S(2)}) %collective-permute-start.7) | collective-permute-done | bytes 32800 | tf_op jit(solution)/shard_map/ppermute | solution.py:22
  197.1 3.6 %fusion.26 = f32[32,32,512]{2,1,0:T(8,128)} fusion(f32[32,32,512]{2,1,0:T(8,128)S(1)} %get-tuple-element.17, f32[32,32,512]{2,1,0:T(8,128)S(1)} %copy-done.13, f32[32,32,512]{2,1,0:T(8,128)S(1)} %get-tuple-element.22, f32[31,32,512]{2,1,0:T(8,128)S(1)} %slice.167, f32[1,32,512]{2,1,0:T(8,128)S(1)} %convert_element_type.53, ...), kind=kLoop, calls=%fused_computation.36 | loop fusion | flops 7864320 | bytes 20967424 | tf_op jit(solution)/shard_map/add | solution.py:115
  (82 shorter events, 6.5 us)
Async XLA Ops:
  7.2 28.6 %copy-start = (s32[8,8]{1,0:T(8,128)S(1)}, s32[8,8]{1,0:T(8,128)}, u32[]{:S(2)}) copy-start(s32[8,8]{1,0:T(8,128)} %param.21) | copy-start | bytes 772
  7.2 143.1 %all-gather.2.cloned.1.call-start = ((), (), s32[]{:S(2)}) async-start(), calls=%async_computation.2 | async-start | bytes 4718592 | tf_op jit(solution)/shard_map/all_gather | solution.py:85
  12.9 12.0 %all-to-all-start = ((s32[32,1,48]{2,1,0:T(1,128)}), s32[32,1,48]{2,1,0:T(1,128)S(1)}, u32[]{:S(2)}, u32[]{:S(2)}) async-start(s32[32,1,48]{2,1,0:T(1,128)} %sub.97), calls=%async_computation | async-start | bytes 32768 | tf_op jit(solution)/shard_map/all_to_all | solution.py:63
  24.9 5.9 %copy-start.2 = (f32[32,32,512]{2,1,0:T(8,128)S(1)}, f32[32,32,512]{2,1,0:T(8,128)}, u32[]{:S(2)}) copy-start(f32[32,32,512]{2,1,0:T(8,128)} %param.12) | copy-start | bytes 6291460
  24.9 110.8 %all-to-all-start.1 = ((bf16[32,48,1024]{2,1,0:T(8,128)(2,1)}), bf16[32,48,1024]{2,1,0:T(8,128)(2,1)}, u32[]{:S(2)}, u32[]{:S(2)}) async-start(bf16[32,48,1024]{2,1,0:T(8,128)(2,1)} %bitcast.140), calls=%async_computation.1 | async-start | bytes 6291456 | tf_op jit(solution)/shard_map/all_to_all | solution.py:56
  31.0 90.4 %collective-permute-start = (bf16[1,32,512]{2,1,0:T(8,128)(2,1)S(1)}, bf16[1,32,512]{2,1,0:T(8,128)(2,1)S(1)}, u32[]{:S(2)}, u32[]{:S(2)}) collective-permute-start(bf16[1,32,512]{2,1,0:T(8,128)(2,1)S(1)} %slice.156), channel_id=1, source_target_pairs={{4,0},{8,4},{12,8},{16,12},{20,16},{24,20},{28,24},{5,1},{9,5},{13... | collective-permute-start | bytes 98312 | tf_op jit(solution)/shard_map/ppermute | solution.py:22
  33.3 88.1 %collective-permute-start.2 = (bf16[32,1,512]{2,1,0:T(2,128)(2,1)S(1)}, bf16[32,1,512]{2,1,0:T(2,128)(2,1)S(1)}, u32[]{:S(2)}, u32[]{:S(2)}) collective-permute-start(bf16[32,1,512]{2,1,0:T(2,128)(2,1)S(1)} %slice.159), channel_id=1, source_target_pairs={{1,0},{2,1},{3,2},{5,4},{6,5},{7,6},{9,8},{10,9},{11,10},{13,12},{... | collective-permute-start | bytes 98312 | tf_op jit(solution)/shard_map/ppermute | solution.py:22
  36.5 85.0 %copy-start.17 = (f32[32,32,512]{2,1,0:T(8,128)S(1)}, f32[32,32,512]{2,1,0:T(8,128)}, u32[]{:S(2)}) copy-start(f32[32,32,512]{2,1,0:T(8,128)} %param.15) | copy-start | bytes 6291460
  36.5 85.0 %copy-start.15 = (f32[32,32,512]{2,1,0:T(8,128)S(1)}, f32[32,32,512]{2,1,0:T(8,128)}, u32[]{:S(2)}) copy-start(f32[32,32,512]{2,1,0:T(8,128)} %param.13) | copy-start | bytes 6291460
  36.5 85.0 %copy-start.16 = (f32[32,32,512]{2,1,0:T(8,128)S(1)}, f32[32,32,512]{2,1,0:T(8,128)}, u32[]{:S(2)}) copy-start(f32[32,32,512]{2,1,0:T(8,128)} %param.14) | copy-start | bytes 6291460
  36.9 84.6 %slice-start = ((f32[32,32,512]{2,1,0:T(8,128)}), f32[31,32,512]{2,1,0:T(8,128)S(1)}, s32[]{:S(2)}) async-start(f32[32,32,512]{2,1,0:T(8,128)} %param.12), calls=%async_computation.3 | async-start | bytes 4063232 | tf_op jit(solution)/shard_map/slice | solution.py:103
  36.9 84.6 %copy-start.5 = (f32[32,32,512]{2,1,0:T(8,128)S(1)}, f32[32,32,512]{2,1,0:T(8,128)}, u32[]{:S(2)}) copy-start(f32[32,32,512]{2,1,0:T(8,128)} %param.16) | copy-start | bytes 6291460
  124.9 1.9 copy-start.3
  124.9 2.0 copy-start.8
  125.0 10.7 %collective-permute-start.1 = (bf16[1,32,512]{2,1,0:T(8,128)(2,1)S(1)}, bf16[1,32,512]{2,1,0:T(8,128)(2,1)S(1)}, u32[]{:S(2)}, u32[]{:S(2)}) collective-permute-start(bf16[1,32,512]{2,1,0:T(8,128)(2,1)S(1)} %slice.184), channel_id=1, source_target_pairs={{0,4},{4,8},{8,12},{12,16},{16,20},{20,24},{24,28},{1,5},{5,9},{9,... | collective-permute-start | bytes 98312 | tf_op jit(solution)/shard_map/ppermute | solution.py:22
  127.0 8.7 %collective-permute-start.3 = (bf16[32,1,512]{2,1,0:T(2,128)(2,1)S(1)}, bf16[32,1,512]{2,1,0:T(2,128)(2,1)S(1)}, u32[]{:S(2)}, u32[]{:S(2)}) collective-permute-start(bf16[32,1,512]{2,1,0:T(2,128)(2,1)S(1)} %slice.183), channel_id=1, source_target_pairs={{0,1},{1,2},{2,3},{4,5},{5,6},{6,7},{8,9},{9,10},{10,11},{12,13},{... | collective-permute-start | bytes 98312 | tf_op jit(solution)/shard_map/ppermute | solution.py:22
  145.8 2.0 copy-start.14
  150.3 20.3 %copy-start.4 = (f32[32,32,512]{2,1,0:T(8,128)S(1)}, f32[32,32,512]{2,1,0:T(8,128)}, u32[]{:S(2)}) copy-start(f32[32,32,512]{2,1,0:T(8,128)} %copy-done.3) | copy-start | bytes 6291460
  150.3 20.3 %copy-start.6 = (f32[32,32,512]{2,1,0:T(8,128)S(1)}, f32[32,32,512]{2,1,0:T(8,128)}, u32[]{:S(2)}) copy-start(f32[32,32,512]{2,1,0:T(8,128)} %param.16) | copy-start | bytes 6291460
  150.3 20.3 %copy-start.7 = (f32[32,32,512]{2,1,0:T(8,128)S(1)}, f32[32,32,512]{2,1,0:T(8,128)}, u32[]{:S(2)}) copy-start(f32[32,32,512]{2,1,0:T(8,128)} %get-tuple-element.27) | copy-start | bytes 6291460
  175.1 7.5 %collective-permute-start.4 = (bf16[1,32,512]{2,1,0:T(8,128)(2,1)S(1)}, bf16[1,32,512]{2,1,0:T(8,128)(2,1)S(1)}, u32[]{:S(2)}, u32[]{:S(2)}) collective-permute-start(bf16[1,32,512]{2,1,0:T(8,128)(2,1)S(1)} %slice.165), channel_id=1, source_target_pairs={{4,0},{8,4},{12,8},{16,12},{20,16},{24,20},{28,24},{5,1},{9,5},{13... | collective-permute-start | bytes 98312 | tf_op jit(solution)/shard_map/ppermute | solution.py:22
  178.6 7.1 %collective-permute-start.6 = (bf16[32,1,512]{2,1,0:T(2,128)(2,1)S(1)}, bf16[32,1,512]{2,1,0:T(2,128)(2,1)S(1)}, u32[]{:S(2)}, u32[]{:S(2)}) collective-permute-start(bf16[32,1,512]{2,1,0:T(2,128)(2,1)S(1)} %slice.169), channel_id=1, source_target_pairs={{1,0},{2,1},{3,2},{5,4},{6,5},{7,6},{9,8},{10,9},{11,10},{13,12},{... | collective-permute-start | bytes 98312 | tf_op jit(solution)/shard_map/ppermute | solution.py:22
  182.0 3.8 %copy-start.9 = (f32[32,32,512]{2,1,0:T(8,128)S(1)}, f32[32,32,512]{2,1,0:T(8,128)}, u32[]{:S(2)}) copy-start(f32[32,32,512]{2,1,0:T(8,128)} %copy-done.8) | copy-start | bytes 6291460
  188.6 8.4 %copy-start.10 = (f32[32,32,512]{2,1,0:T(8,128)}, f32[32,32,512]{2,1,0:T(8,128)S(1)}, u32[]{:S(2)}) copy-start(f32[32,32,512]{2,1,0:T(8,128)S(1)} %get-tuple-element.21) | copy-start | bytes 6291460
  188.6 8.4 %copy-start.11 = (f32[32,32,512]{2,1,0:T(8,128)}, f32[32,32,512]{2,1,0:T(8,128)S(1)}, u32[]{:S(2)}) copy-start(f32[32,32,512]{2,1,0:T(8,128)S(1)} %get-tuple-element.20) | copy-start | bytes 6291460
  188.7 12.0 %copy-start.12 = (f32[32,32,512]{2,1,0:T(8,128)}, f32[32,32,512]{2,1,0:T(8,128)S(1)}, u32[]{:S(2)}) copy-start(f32[32,32,512]{2,1,0:T(8,128)S(1)} %get-tuple-element.22) | copy-start | bytes 6291460
  188.7 5.2 %collective-permute-start.5 = (bf16[1,32,512]{2,1,0:T(8,128)(2,1)S(1)}, bf16[1,32,512]{2,1,0:T(8,128)(2,1)S(1)}, u32[]{:S(2)}, u32[]{:S(2)}) collective-permute-start(bf16[1,32,512]{2,1,0:T(8,128)(2,1)S(1)} %slice.182), channel_id=1, source_target_pairs={{0,4},{4,8},{8,12},{12,16},{16,20},{20,24},{24,28},{1,5},{5,9},{9,... | collective-permute-start | bytes 98312 | tf_op jit(solution)/shard_map/ppermute | solution.py:22
  190.7 6.4 %copy-start.13 = (f32[32,32,512]{2,1,0:T(8,128)S(1)}, f32[32,32,512]{2,1,0:T(8,128)}, u32[]{:S(2)}) copy-start(f32[32,32,512]{2,1,0:T(8,128)} %get-tuple-element.18) | copy-start | bytes 6291460
  190.7 6.3 %collective-permute-start.7 = (bf16[32,1,512]{2,1,0:T(2,128)(2,1)S(1)}, bf16[32,1,512]{2,1,0:T(2,128)(2,1)S(1)}, u32[]{:S(2)}, u32[]{:S(2)}) collective-permute-start(bf16[32,1,512]{2,1,0:T(2,128)(2,1)S(1)} %slice.181), channel_id=1, source_target_pairs={{0,1},{1,2},{2,3},{4,5},{5,6},{6,7},{8,9},{9,10},{10,11},{12,13},{... | collective-permute-start | bytes 98312 | tf_op jit(solution)/shard_map/ppermute | solution.py:22
  197.1 3.6 %copy-start.1 = (s32[8,8]{1,0:T(8,128)S(1)}, s32[8,8]{1,0:T(8,128)}, u32[]{:S(2)}) copy-start(s32[8,8]{1,0:T(8,128)} %param.21) | copy-start | bytes 772
Sparse Core Ops, SparseCore 0:
  9.6 70.9 all-gather.1
where the time goes:
time: 210 us; the launch traced here: 208 us
  waiting for transfers between devices  90.9 us (43%)
  starting transfers between devices  32.9 us (16%)
  matrix products  28.1 us (13%)
  other arithmetic  20.9 us (10%)
  local copies, waits for them, and re-layouts  20.2 us (10%)
  between operations  14.6 us (7%)
    ppermute x8, waiting for transfers between devices, from_behind(): return lax.ppermute(block, axis, route)  90.2 us
    ppermute x8, starting transfers between devices, from_behind(): return lax.ppermute(block, axis, route)  21.1 us
    dot_general x1, matrix products, body(): jnp.dot(coeff, piece.reshape(count, size_y * depth), precision=lax.Precis...  18.8 us
    another operation x4, other arithmetic  6.31 us
    all_to_all x1, starting transfers between devices, body(): lax.all_to_all(out_cols.reshape(devices, capacity), ('gx', 'gy'), split_a...  5.91 us
    all_to_all x1, starting transfers between devices, body(): lax.all_to_all(outgoing.reshape(devices, capacity, steps * depth), ('gx',...  5.87 us
    dot_general x1, matrix products, body(): jnp.dot(hits, incoming.reshape(slots, steps * depth), preferred_element_t...  5.34 us
    reshape x1, local copies, waits for them, and re-layouts, body(): incoming.reshape(slots, steps * depth)  4.71 us
  transfers between devices with their start and end apart: 11, of which 4 were waited for; matrix products, arithmetic and copies ran while one was open for 17% of the time, Pallas kernels for 0%

commit v1 on v0

v1 whole, which is shorter than its diff:
```python
import jax
import jax.numpy as jnp
from jax import lax
from jax.sharding import PartitionSpec as P

step_ratio = 0.4
gas_density = 0.001
gas_stiffness = 5.29e-05


def from_behind(block, axis, distance):
    devices = range(lax.axis_size(axis))
    route = [(i - distance, i) for i in devices if i - distance in devices]
    return lax.ppermute(block, axis, route)


def material(void_frac):
    liquid = 1.0 - void_frac
    buoyancy = 1.0 / (liquid + void_frac * gas_density)
    stiffness = 1.0 / (liquid + void_frac / gas_stiffness)
    return (buoyancy, stiffness)


def bubble_source(waves, bubble_dest, bubble_column, cells):
    tiles_x = lax.axis_size("gx")
    tiles_y = lax.axis_size("gy")
    devices = tiles_x * tiles_y
    bubbles = waves.shape[0]
    steps = waves.shape[1]
    depth = waves.shape[2]
    capacity = 2 * bubbles // devices
    slots = devices * capacity
    me = lax.axis_index("gx") * tiles_y + lax.axis_index("gy")
    dest = bubble_dest[:, 0]
    owners = (dest[:, None] == jnp.arange(devices, dtype=jnp.int32)[None, :]).astype(jnp.int32)
    rank = jnp.sum(jnp.cumsum(owners, axis=0) * owners, axis=1) - 1
    slot_ids = dest * capacity + rank
    placed = slot_ids[None, :] == jnp.arange(slots, dtype=jnp.int32)[:, None]
    outgoing = jnp.dot(
        placed.astype(jnp.bfloat16),
        waves.reshape(bubbles, steps * depth),
        preferred_element_type=jnp.float32,
    ).astype(jnp.bfloat16)
    code = dest * cells + bubble_column
    all_code = lax.all_gather(code, ("gx", "gy"), axis=0, tiled=True).reshape(devices, bubbles)
    all_dest = all_code // cells
    all_col = all_code % cells
    mine = (all_dest == me).astype(jnp.int32)
    in_rank = jnp.cumsum(mine, axis=1) - 1
    in_rank = jnp.where(mine > 0, in_rank, -1)
    slot_of = jnp.arange(capacity, dtype=jnp.int32)
    match = in_rank[:, None, :] == slot_of[None, :, None]
    in_cols = jnp.max(jnp.where(match, all_col[:, None, :] + 1, 0), axis=2) - 1
    incoming = lax.all_to_all(
        outgoing.reshape(devices, capacity, steps * depth),
        ("gx", "gy"),
        split_axis=0,
        concat_axis=0,
        tiled=True,
    )
    hits = (
        jnp.arange(cells, dtype=jnp.int32)[:, None] == in_cols.reshape(slots)[None, :]
    ).astype(jnp.bfloat16)
    source = jnp.dot(
        hits, incoming.reshape(slots, steps * depth), preferred_element_type=jnp.float32
    )
    return source


def incident_plane(history, delays, size_y, depth):
    tiles_x = lax.axis_size("gx")
    my_tile = lax.axis_index("gx")
    cycle = jnp.arange(tiles_x, dtype=jnp.int32)
    dist = jnp.abs(cycle - my_tile)
    dist = jnp.minimum(dist, tiles_x - dist)
    weight = 1.0 / (1.0 + 2.0 * dist.astype(jnp.float32) / tiles_x)
    wanted = lax.dynamic_index_in_dim(delays, my_tile, 1, keepdims=False)
    chosen = jnp.take(history, wanted, axis=0)
    rows = lax.all_to_all(chosen, "gx", split_axis=0, concat_axis=0, tiled=True)
    return jnp.sum(weight[:, None, None] * rows.astype(jnp.float32), axis=0)


def body(
    pressure, vel_x, vel_y, vel_z, void_frac, waves, bubble_dest, bubble_column, history, delays
):
    size_x, size_y, depth = pressure.shape
    steps = waves.shape[1]
    ix = lax.axis_index("gx")
    iy = lax.axis_index("gy")
    has_below_x = ix > 0
    has_below_y = iy > 0
    buoyancy, stiffness = material(void_frac)

    above_x = from_behind(pressure[0:1], "gx", -1)
    above_y = from_behind(pressure[:, 0:1], "gy", -1)
    below_x = from_behind(
        jnp.concatenate([pressure[-1:], vel_x[-1:], void_frac[-1:]], 0), "gx", 1
    )
    below_y = from_behind(
        jnp.concatenate([pressure[:, -1:], vel_y[:, -1:], void_frac[:, -1:]], 1), "gy", 1
    )
    p_bx, vx_bx, void_bx = below_x[0:1], below_x[1:2], below_x[2:3]
    p_by, vy_by, void_by = below_y[:, 0:1], below_y[:, 1:2], below_y[:, 2:3]
    b_bx, _ = material(void_bx)
    b_by, _ = material(void_by)

    source = bubble_source(waves, bubble_dest, bubble_column, size_x * size_y)
    source = source.reshape(size_x, size_y, steps, depth)
    incident = incident_plane(history, delays, size_y, depth)
    forcing = jnp.zeros_like(pressure).at[0].set(incident)
    z_edge = jnp.zeros((size_x, size_y, 1), jnp.float32)

    for step in range(steps):
        next_x = jnp.concatenate([pressure[1:], above_x], 0)
        next_y = jnp.concatenate([pressure[:, 1:], above_y], 1)
        next_z = jnp.concatenate([pressure[:, :, 1:], z_edge], 2)
        vel_x = vel_x - step_ratio * buoyancy * (next_x - pressure)
        vel_y = vel_y - step_ratio * buoyancy * (next_y - pressure)
        vel_z = vel_z - step_ratio * buoyancy * (next_z - pressure)
        vx_bx = vx_bx - step_ratio * b_bx * (pressure[0:1] - p_bx)
        vy_by = vy_by - step_ratio * b_by * (pressure[:, 0:1] - p_by)
        lower_x = jnp.where(has_below_x, vx_bx, 0.0)
        lower_y = jnp.where(has_below_y, vy_by, 0.0)
        prev_x = jnp.concatenate([lower_x, vel_x[:-1]], 0)
        prev_y = jnp.concatenate([lower_y, vel_y[:, :-1]], 1)
        prev_z = jnp.concatenate([z_edge, vel_z[:, :, :-1]], 2)
        divergence = vel_x - prev_x + (vel_y - prev_y) + (vel_z - prev_z)
        pressure = pressure + step_ratio * stiffness * (
            source[:, :, step, :] + forcing - divergence
        )
        if step + 1 < steps:
            above_x = from_behind(pressure[0:1], "gx", -1)
            above_y = from_behind(pressure[:, 0:1], "gy", -1)
            p_bx = from_behind(pressure[-1:], "gx", 1)
            p_by = from_behind(pressure[:, -1:], "gy", 1)
    return (pressure, vel_x, vel_y, vel_z)


def solution(mesh):
    in_specs = (
        P("gx", "gy", None),
        P("gx", "gy", None),
        P("gx", "gy", None),
        P("gx", "gy", None),
        P("gx", "gy", None),
        P(("gx", "gy"), None, None),
        P(("gx", "gy"), None),
        P(("gx", "gy")),
        P("gx", "gy", None),
        P(),
    )
    out_specs = (P("gx", "gy", None), P("gx", "gy", None), P("gx", "gy", None), P("gx", "gy", None))
    return jax.shard_map(body, mesh=mesh, in_specs=in_specs, out_specs=out_specs, check_vma=False)
```

time: 210 us -> 211 us (level)
  blocking collectives: 0 us -> 111 us
  waiting for transfers between devices: 90.9 us -> 10 us
  matrix products: 28.1 us -> 9.47 us
  between operations: 14.6 us -> 1.32 us
  other arithmetic: 20.9 us -> 26.9 us
  starting transfers between devices: 32.9 us -> 29.6 us
    all_gather x0 -> x1, blocking collectives: none -> 111 us  [bubble_source(): lax.all_gather(code, ('gx', 'gy'), axis=0, tiled=True)]
    ppermute x8, waiting for transfers between devices: 90.2 us -> 10 us  [from_behind(): return lax.ppermute(block, axis, route)]
    dot_general x3 -> x2, matrix products: 28.1 us -> 9.47 us  [the longest x1 5.48 us: bubble_source(): jnp.dot(hits, incoming.reshape(slots, steps * depth), preferred_element_t...]
    sub x1 -> x2, other arithmetic: 2.84 us -> 10.5 us  [body(): vel_z = vel_z - step_ratio * buoyancy * (next_z - pressure)]
    slice x13 -> x15, local copies, waits for them, and re-layouts: 1.18 us -> 6.21 us  [the longest x2 2.07 us: body(): next_y = jnp.concatenate([pressure[:, 1:], above_y], 1)]
    sub x2 -> x1, other arithmetic: 3.42 us -> 0.01 us  [bubble_source(): in_cols = jnp.max(jnp.where(match, all_col[:, None, :] + 1, 0), axis=2) - 1]
    select_n x0 -> x7, other arithmetic: none -> 3.41 us  [the longest x2 1.67 us: incident_plane(): chosen = jnp.take(history, wanted, axis=0)]
    another operation x4, other arithmetic: 6.31 us -> 3.53 us
  transfers between devices with their start and end apart: 11 -> 10, of which waited for: 4 -> 4; matrix products, arithmetic and copies ran while one was open for 17% -> 14% of each run, Pallas kernels for 0% -> 0%
where the time goes in v1:
time: 211 us; the launch traced here: 210 us
  blocking collectives  111 us (53%)
  starting transfers between devices  29.6 us (14%)
  other arithmetic  26.9 us (13%)
  local copies, waits for them, and re-layouts  21.4 us (10%)
  waiting for transfers between devices  10 us (5%)
  matrix products  9.47 us (4%)
    all_gather x1, blocking collectives, bubble_source(): lax.all_gather(code, ('gx', 'gy'), axis=0, tiled=True)  111 us
    ppermute x8, starting transfers between devices, from_behind(): return lax.ppermute(block, axis, route)  18.4 us
    sub x2, other arithmetic, body(): vel_z = vel_z - step_ratio * buoyancy * (next_z - pressure)  10.5 us
    ppermute x8, waiting for transfers between devices, from_behind(): return lax.ppermute(block, axis, route)  10 us
    add x2, other arithmetic, body(): pressure + step_ratio * stiffness * (source[:, :, step, :] + forcing - di...  6.19 us
    all_to_all x1, starting transfers between devices, bubble_source(): lax.all_to_all(outgoing.reshape(devices, capacity, steps * depth), ('gx',...  5.85 us
    dot_general x1, matrix products, bubble_source(): jnp.dot(hits, incoming.reshape(slots, steps * depth), preferred_element_t...  5.48 us
    all_to_all x1, starting transfers between devices, incident_plane(): rows = lax.all_to_all(chosen, 'gx', split_axis=0, concat_axis=0, tiled=True)  5.34 us
  transfers between devices with their start and end apart: 10, of which 4 were waited for; matrix products, arithmetic and copies ran while one was open for 14% of the time, Pallas kernels for 0%

profile of v1, /device:TPU:18, one launch (start us, length us, event | category | flops | bytes accessed | tf_op | source)
XLA Modules:
  0.0 210.2 jit_solution(8483388829325773895)
XLA Ops:
  3.9 5.3 %all-to-all-start.1 = ((bf16[8,32,512]{2,1,0:T(8,128)(2,1)}), bf16[8,32,512]{2,1,0:T(8,128)(2,1)S(1)}, u32[]{:S(2)}, u32[]{:S(2)}) async-start(bf16[8,32,512]{2,1,0:T(8,128)(2,1)} %broadcast_select_fusion), calls=%async_computation.1 | async-start | bytes 524288 | tf_op jit(solution)/shard_map/all_to_all | solution.py:79
  10.0 1.7 reduce-window.16
  12.6 4.0 %fusion.4 = bf16[1536,1024]{1,0:T(8,128)(2,1)} fusion(bf16[768,1024]{1,0:T(8,128)(2,1)S(1)} %bitcast.120, s32[768]{0:T(1024)S(1)} %get-tuple-element.40), kind=kOutput, calls=%fused_computation.8 | convolution fusion | flops 2418671616 | bytes 4721664 | tf_op jit(solution)/shard_map/dot_general | solution.py:39
  16.6 5.8 %all-to-all-start = ((bf16[32,48,1024]{2,1,0:T(8,128)(2,1)}), bf16[32,48,1024]{2,1,0:T(8,128)(2,1)}, u32[]{:S(2)}, u32[]{:S(2)}) async-start(bf16[32,48,1024]{2,1,0:T(8,128)(2,1)} %bitcast.117), calls=%async_computation | async-start | bytes 6291456 | tf_op jit(solution)/shard_map/all_to_all | solution.py:54
  22.5 2.1 collective-permute-start.1
  24.6 1.1 slice.153
  25.8 1.1 slice.152
  27.1 3.4 %collective-permute-start.3 = (f32[32,3,512]{2,1,0:T(4,128)S(1)}, f32[32,3,512]{2,1,0:T(4,128)}, u32[]{:S(2)}, u32[]{:S(2)}) collective-permute-start(f32[32,3,512]{2,1,0:T(4,128)S(1)} %pad_maximum_fusion), channel_id=1, source_target_pairs={{0,1},{1,2},{2,3},{4,5},{5,6},{6,7},{8,9},{9,10},{10,11},{12,13},{... | collective-permute-start | bytes 589832 | tf_op jit(solution)/shard_map/ppermute | solution.py:14
  30.5 111.4 %all-gather = s32[32,1,768]{2,1,0:T(1,128)S(1)} all-gather(s32[1,1,768]{2,1,0:T(1,128)S(1)} %reshape.246), channel_id=1, replica_groups=mesh['gx'=8,'gy'=4] {'gx','gy'}, dimensions={0}, use_global_device_ids=true | all-gather | bytes 101376 | tf_op jit(solution)/shard_map/all_gather | solution.py:45
  142.2 1.7 reduce-window.14
  145.2 1.5 slice.140
  146.7 1.9 slice.158
  148.6 1.7 slice.149
  150.5 1.9 collective-permute-start
  152.4 1.4 broadcast_select_fusion.2
  153.8 2.1 collective-permute-start.2
  156.0 5.2 %collective-permute-done.2 = f32[32,1,512]{2,1,0:T(1,128)S(1)} collective-permute-done((f32[32,1,512]{2,1,0:T(1,128)S(1)}, f32[32,1,512]{2,1,0:T(1,128)S(1)}, u32[]{:S(2)}, u32[]{:S(2)}) %collective-permute-start.2) | collective-permute-done | bytes 65568 | tf_op jit(solution)/shard_map/ppermute | solution.py:14
  161.1 7.7 %multiply_subtract_fusion.1 = (f32[32,32,512]{2,1,0:T(8,128)}, f32[32,32,512]{2,1,0:T(8,128)}, f32[32,32,512]{2,1,0:T(8,128)S(1)}) fusion(f32[32,32,512]{2,1,0:T(8,128)} %param.15, f32[32,32,512]{2,1,0:T(8,128)S(1)} %copy-done.2, f32[32,32,511]{2,1,0:T(8,128)} %slice.158, f32[32,32,512]{2,1,0:T(8,128)} %param.16, f32[32,32,512]{2,1,0:T(8,128)} %param.14, ...), kind=kLoop, calls=%fused_computation.41 | loop fusion | flops 8388608 | bytes 23064576 | tf_op jit(solution)/shard_map/sub | solution.py:119
  168.8 1.3 copy-done.6
  170.1 1.5 slice.179
  171.7 4.6 %copy.38 = bf16[1536,1024]{0,1:T(8,128)(2,1)} copy(bf16[1536,1024]{1,0:T(8,128)(2,1)} %bitcast.4) | data formatting | bytes 6291456 | tf_op jit(solution)/shard_map/reshape | solution.py:65
  176.4 5.5 %fusion = f32[32,32,2,512]{3,1,2,0:T(8,128)S(1)} fusion(bf16[2,512,1536,1]{2,1,0,3:T(8,128)(2,1)} %bitcast.118, s32[1536]{0:T(1024)S(1)} %sub.140, s32[32,32]{1,0:T(8,128)S(1)} %multiply_add_fusion), kind=kOutput, calls=%fused_computation.1 | convolution fusion | flops 3222798336 | bytes 7350272 | tf_op jit(solution)/shard_map/dot_general | solution.py:64
  182.4 1.1 copy-done.3
  185.3 2.5 %fusion.14 = f32[32,32,512]{2,1,0:T(8,128)S(1)} fusion(f32[32,32,512]{2,1,0:T(8,128)S(1)} %copy-done.2, f32[32,32,512]{2,1,0:T(8,128)S(1)} %get-tuple-element.22, f32[32,32,512]{2,1,0:T(8,128)S(1)} %copy-done.7, f32[31,32,512]{2,1,0:T(8,128)S(1)} %copy-done.11, f32[1,32,512]{2,1,0:T(8,128)S(1)} %get-tuple-element.19, f32[32,32,512]{2,1,0:T(8,128)S(1)} %copy-done.5, ...), kind=kLoop, calls=%fused_computation.22 | loop fusion | flops 7864320 | bytes 20967424 | tf_op jit(solution)/shard_map/add | solution.py:128
  187.9 1.9 collective-permute-start.5
  189.9 1.9 collective-permute-start.7
  191.8 1.7 collective-permute-done.5
  193.5 2.0 collective-permute-start.4
  196.2 3.1 %collective-permute-start.6 = (f32[32,1,512]{2,1,0:T(1,128)S(1)}, f32[32,1,512]{2,1,0:T(1,128)S(1)}, u32[]{:S(2)}, u32[]{:S(2)}) collective-permute-start(f32[32,1,512]{2,1,0:T(1,128)S(1)} %get-tuple-element.32), channel_id=1, source_target_pairs={{1,0},{2,1},{3,2},{5,4},{6,5},{7,6},{9,8},{10,9},{11,10},{13,12},{... | collective-permute-start | bytes 196616 | tf_op jit(solution)/shard_map/ppermute | solution.py:14
  200.6 2.7 %collective-permute-done.6 = f32[32,1,512]{2,1,0:T(1,128)S(1)} collective-permute-done((f32[32,1,512]{2,1,0:T(1,128)S(1)}, f32[32,1,512]{2,1,0:T(1,128)S(1)}, u32[]{:S(2)}, u32[]{:S(2)}) %collective-permute-start.6) | collective-permute-done | bytes 65568 | tf_op jit(solution)/shard_map/ppermute | solution.py:14
  203.3 2.8 %multiply_subtract_fusion = (f32[32,32,512]{2,1,0:T(8,128)S(1)}, f32[32,32,512]{2,1,0:T(8,128)S(1)}, f32[32,32,512]{2,1,0:T(8,128)S(1)}) fusion(f32[32,32,512]{2,1,0:T(8,128)S(1)} %copy-done.4, f32[32,32,512]{2,1,0:T(8,128)S(1)} %fusion.14, f32[32,32,511]{2,1,0:T(8,128)S(1)} %slice.194, f32[32,32,512]{2,1,0:T(8,128)S(1)} %copy-done.3, ...), kind=kLoop, calls=%fused_computation.40 | loop fusion | flops 8388608 | bytes 23064576 | tf_op jit(solution)/shard_map/sub | solution.py:119
  206.4 3.7 %fusion.23 = f32[32,32,512]{2,1,0:T(8,128)} fusion(f32[32,32,512]{2,1,0:T(8,128)S(1)} %fusion.14, f32[32,32,512]{2,1,0:T(8,128)S(1)} %get-tuple-element.21, f32[32,32,512]{2,1,0:T(8,128)S(1)} %get-tuple-element.25, f32[31,32,512]{2,1,0:T(8,128)S(1)} %slice.189, f32[1,32,512]{2,1,0:T(8,128)S(1)} %get-tuple-element.33, ...), kind=kLoop, calls=%fused_computation.35 | loop fusion | flops 7864320 | bytes 20967424 | tf_op jit(solution)/shard_map/add | solution.py:128
  (77 shorter events, 11.5 us)
Async XLA Ops:
  0.6 1.9 copy-start
  0.6 11.5 %copy-start.12 = (bf16[768,2,512]{2,1,0:T(2,128)(2,1)S(1)}, bf16[768,2,512]{2,1,0:T(2,128)(2,1)}, u32[]{:S(2)}) copy-start(bf16[768,2,512]{2,1,0:T(2,128)(2,1)} %param.17) | copy-start | bytes 4718596
  3.9 8.6 %copy-start.13 = (s32[768]{0:T(1024)S(1)}, s32[768]{0:T(1024)}, u32[]{:S(2)}) copy-start(s32[768]{0:T(1024)} %param.19) | copy-start | bytes 9220
  3.9 12.7 %all-to-all-start.1 = ((bf16[8,32,512]{2,1,0:T(8,128)(2,1)}), bf16[8,32,512]{2,1,0:T(8,128)(2,1)S(1)}, u32[]{:S(2)}, u32[]{:S(2)}) async-start(bf16[8,32,512]{2,1,0:T(8,128)(2,1)} %broadcast_select_fusion), calls=%async_computation.1 | async-start | bytes 524288 | tf_op jit(solution)/shard_map/all_to_all | solution.py:79
  16.6 5.9 %slice-start = ((f32[32,32,512]{2,1,0:T(8,128)}), f32[1,32,512]{2,1,0:T(8,128)S(1)}, s32[]{:S(2)}) async-start(f32[32,32,512]{2,1,0:T(8,128)} %param.12), calls=%async_computation.2 | async-start | bytes 131072 | tf_op jit(solution)/shard_map/slice | solution.py:97
  16.6 5.9 %slice-start.1 = ((f32[32,32,512]{2,1,0:T(8,128)}), f32[1,32,512]{2,1,0:T(8,128)S(1)}, s32[]{:S(2)}) async-start(f32[32,32,512]{2,1,0:T(8,128)} %param.16), calls=%async_computation.3 | async-start | bytes 131072 | tf_op jit(solution)/shard_map/slice | solution.py:97
  16.6 5.9 %slice-start.2 = ((f32[32,32,512]{2,1,0:T(8,128)}), f32[1,32,512]{2,1,0:T(8,128)S(1)}, s32[]{:S(2)}) async-start(f32[32,32,512]{2,1,0:T(8,128)} %param.13), calls=%async_computation.4 | async-start | bytes 131072 | tf_op jit(solution)/shard_map/slice | solution.py:97
  16.6 9.1 %copy-start.2 = (f32[32,32,512]{2,1,0:T(8,128)S(1)}, f32[32,32,512]{2,1,0:T(8,128)}, u32[]{:S(2)}) copy-start(f32[32,32,512]{2,1,0:T(8,128)} %param.12) | copy-start | bytes 6291460
  16.6 155.1 %all-to-all-start = ((bf16[32,48,1024]{2,1,0:T(8,128)(2,1)}), bf16[32,48,1024]{2,1,0:T(8,128)(2,1)}, u32[]{:S(2)}, u32[]{:S(2)}) async-start(bf16[32,48,1024]{2,1,0:T(8,128)(2,1)} %bitcast.117), calls=%async_computation | async-start | bytes 6291456 | tf_op jit(solution)/shard_map/all_to_all | solution.py:54
  22.5 127.9 %collective-permute-start.1 = (f32[3,32,512]{2,1,0:T(8,128)S(1)}, f32[3,32,512]{2,1,0:T(8,128)S(1)}, u32[]{:S(2)}, u32[]{:S(2)}) collective-permute-start(f32[3,32,512]{2,1,0:T(8,128)S(1)} %pad_maximum_fusion.1), channel_id=1, source_target_pairs={{0,4},{4,8},{8,12},{12,16},{16,20},{20,24},{24,28},{1,5},{5,9},{9,... | collective-permute-start | bytes 589832 | tf_op jit(solution)/shard_map/ppermute | solution.py:14
  27.1 125.3 %collective-permute-start.3 = (f32[32,3,512]{2,1,0:T(4,128)S(1)}, f32[32,3,512]{2,1,0:T(4,128)}, u32[]{:S(2)}, u32[]{:S(2)}) collective-permute-start(f32[32,3,512]{2,1,0:T(4,128)S(1)} %pad_maximum_fusion), channel_id=1, source_target_pairs={{0,1},{1,2},{2,3},{4,5},{5,6},{6,7},{8,9},{9,10},{10,11},{12,13},{... | collective-permute-start | bytes 589832 | tf_op jit(solution)/shard_map/ppermute | solution.py:14
  150.5 5.5 %collective-permute-start = (f32[1,32,512]{2,1,0:T(8,128)S(1)}, f32[1,32,512]{2,1,0:T(8,128)S(1)}, u32[]{:S(2)}, u32[]{:S(2)}) collective-permute-start(f32[1,32,512]{2,1,0:T(8,128)S(1)} %get-tuple-element.36), channel_id=1, source_target_pairs={{4,0},{8,4},{12,8},{16,12},{20,16},{24,20},{28,24},{5,1},{9,5},{13... | collective-permute-start | bytes 196616 | tf_op jit(solution)/shard_map/ppermute | solution.py:14
  153.8 7.3 %collective-permute-start.2 = (f32[32,1,512]{2,1,0:T(1,128)S(1)}, f32[32,1,512]{2,1,0:T(1,128)S(1)}, u32[]{:S(2)}, u32[]{:S(2)}) collective-permute-start(f32[32,1,512]{2,1,0:T(1,128)S(1)} %get-tuple-element.35), channel_id=1, source_target_pairs={{1,0},{2,1},{3,2},{5,4},{6,5},{7,6},{9,8},{10,9},{11,10},{13,12},{... | collective-permute-start | bytes 196616 | tf_op jit(solution)/shard_map/ppermute | solution.py:14
  168.8 1.3 copy-start.6
  176.4 6.0 %copy-start.11 = (f32[31,32,512]{2,1,0:T(8,128)S(1)}, f32[31,32,512]{2,1,0:T(8,128)}, u32[]{:S(2)}) copy-start(f32[31,32,512]{2,1,0:T(8,128)} %slice.179) | copy-start | bytes 6094852
  181.8 1.6 copy-start.3
  181.9 2.2 %copy-start.4 = (f32[32,32,512]{2,1,0:T(8,128)S(1)}, f32[32,32,512]{2,1,0:T(8,128)}, u32[]{:S(2)}) copy-start(f32[32,32,512]{2,1,0:T(8,128)} %get-tuple-element.28) | copy-start | bytes 6291460
  181.9 2.8 %copy-start.5 = (f32[32,32,512]{2,1,0:T(8,128)S(1)}, f32[32,32,512]{2,1,0:T(8,128)}, u32[]{:S(2)}) copy-start(f32[32,32,512]{2,1,0:T(8,128)} %get-tuple-element.29) | copy-start | bytes 6291460
  181.9 3.4 %copy-start.7 = (f32[32,32,512]{2,1,0:T(8,128)S(1)}, f32[32,32,512]{2,1,0:T(8,128)}, u32[]{:S(2)}) copy-start(f32[32,32,512]{2,1,0:T(8,128)} %copy-done.6) | copy-start | bytes 6291460
  187.9 5.6 %collective-permute-start.5 = (f32[1,32,512]{2,1,0:T(8,128)S(1)}, f32[1,32,512]{2,1,0:T(8,128)S(1)}, u32[]{:S(2)}, u32[]{:S(2)}) collective-permute-start(f32[1,32,512]{2,1,0:T(8,128)S(1)} %slice.188), channel_id=1, source_target_pairs={{0,4},{4,8},{8,12},{12,16},{16,20},{20,24},{24,28},{1,5},{5,9},{9,... | collective-permute-start | bytes 196616 | tf_op jit(solution)/shard_map/ppermute | solution.py:14
  189.9 6.2 %collective-permute-start.7 = (f32[32,1,512]{2,1,0:T(1,128)S(1)}, f32[32,1,512]{2,1,0:T(1,128)S(1)}, u32[]{:S(2)}, u32[]{:S(2)}) collective-permute-start(f32[32,1,512]{2,1,0:T(1,128)S(1)} %slice.192), channel_id=1, source_target_pairs={{0,1},{1,2},{2,3},{4,5},{5,6},{6,7},{8,9},{9,10},{10,11},{12,13},{... | collective-permute-start | bytes 196616 | tf_op jit(solution)/shard_map/ppermute | solution.py:14
  193.5 7.1 %collective-permute-start.4 = (f32[1,32,512]{2,1,0:T(8,128)S(1)}, f32[1,32,512]{2,1,0:T(8,128)S(1)}, u32[]{:S(2)}, u32[]{:S(2)}) collective-permute-start(f32[1,32,512]{2,1,0:T(8,128)S(1)} %get-tuple-element.34), channel_id=1, source_target_pairs={{4,0},{8,4},{12,8},{16,12},{20,16},{24,20},{28,24},{5,1},{9,5},{13... | collective-permute-start | bytes 196616 | tf_op jit(solution)/shard_map/ppermute | solution.py:14
  196.2 7.1 %collective-permute-start.6 = (f32[32,1,512]{2,1,0:T(1,128)S(1)}, f32[32,1,512]{2,1,0:T(1,128)S(1)}, u32[]{:S(2)}, u32[]{:S(2)}) collective-permute-start(f32[32,1,512]{2,1,0:T(1,128)S(1)} %get-tuple-element.32), channel_id=1, source_target_pairs={{1,0},{2,1},{3,2},{5,4},{6,5},{7,6},{9,8},{10,9},{11,10},{13,12},{... | collective-permute-start | bytes 196616 | tf_op jit(solution)/shard_map/ppermute | solution.py:14
  206.1 4.0 %copy-start.8 = (f32[32,32,512]{2,1,0:T(8,128)}, f32[32,32,512]{2,1,0:T(8,128)S(1)}, u32[]{:S(2)}) copy-start(f32[32,32,512]{2,1,0:T(8,128)S(1)} %get-tuple-element.23) | copy-start | bytes 6291460
  206.1 4.0 %copy-start.9 = (f32[32,32,512]{2,1,0:T(8,128)}, f32[32,32,512]{2,1,0:T(8,128)S(1)}, u32[]{:S(2)}) copy-start(f32[32,32,512]{2,1,0:T(8,128)S(1)} %get-tuple-element.24) | copy-start | bytes 6291460
  206.1 4.0 %copy-start.10 = (f32[32,32,512]{2,1,0:T(8,128)}, f32[32,32,512]{2,1,0:T(8,128)S(1)}, u32[]{:S(2)}) copy-start(f32[32,32,512]{2,1,0:T(8,128)S(1)} %get-tuple-element.25) | copy-start | bytes 6291460
  206.4 3.7 %copy-start.1 = (bf16[16,32,512]{2,1,0:T(8,128)(2,1)S(1)}, bf16[16,32,512]{2,1,0:T(8,128)(2,1)}, u32[]{:S(2)}) copy-start(bf16[16,32,512]{2,1,0:T(8,128)(2,1)} %param.20) | copy-start | bytes 1572868

commit v2 on v1

--- a/solution.py
+++ b/solution.py
@@ -21,7 +21,7 @@
     return (buoyancy, stiffness)
 
 
-def bubble_source(waves, bubble_dest, bubble_column, cells):
+def bubble_source(waves, bubble_dest, bubble_column, cells, ready):
     tiles_x = lax.axis_size("gx")
     tiles_y = lax.axis_size("gy")
     devices = tiles_x * tiles_y
@@ -51,6 +51,7 @@
     slot_of = jnp.arange(capacity, dtype=jnp.int32)
     match = in_rank[:, None, :] == slot_of[None, :, None]
     in_cols = jnp.max(jnp.where(match, all_col[:, None, :] + 1, 0), axis=2) - 1
+    in_cols, outgoing, ready = lax.optimization_barrier((in_cols, outgoing, ready))
     incoming = lax.all_to_all(
         outgoing.reshape(devices, capacity, steps * depth),
         ("gx", "gy"),
@@ -64,7 +65,7 @@
     source = jnp.dot(
         hits, incoming.reshape(slots, steps * depth), preferred_element_type=jnp.float32
     )
-    return source
+    return source, ready
 
 
 def incident_plane(history, delays, size_y, depth):
@@ -99,14 +100,16 @@
     below_y = from_behind(
         jnp.concatenate([pressure[:, -1:], vel_y[:, -1:], void_frac[:, -1:]], 1), "gy", 1
     )
+
+    incident = incident_plane(history, delays, size_y, depth)
+    ready = (above_x, above_y, below_x, below_y, incident)
+    source, ready = bubble_source(waves, bubble_dest, bubble_column, size_x * size_y, ready)
+    above_x, above_y, below_x, below_y, incident = ready
+    source = source.reshape(size_x, size_y, steps, depth)
     p_bx, vx_bx, void_bx = below_x[0:1], below_x[1:2], below_x[2:3]
     p_by, vy_by, void_by = below_y[:, 0:1], below_y[:, 1:2], below_y[:, 2:3]
     b_bx, _ = material(void_bx)
     b_by, _ = material(void_by)
-
-    source = bubble_source(waves, bubble_dest, bubble_column, size_x * size_y)
-    source = source.reshape(size_x, size_y, steps, depth)
-    incident = incident_plane(history, delays, size_y, depth)
     forcing = jnp.zeros_like(pressure).at[0].set(incident)
     z_edge = jnp.zeros((size_x, size_y, 1), jnp.float32)
 

time: 211 us -> 217 us (1.028)
  blocking collectives: 111 us -> 50.5 us
  waiting for transfers between devices: 10 us -> 56.8 us
  starting transfers between devices: 29.6 us -> 46.6 us
  local copies, waits for them, and re-layouts: 21.4 us -> 24.5 us
    all_gather x1, blocking collectives: 111 us -> 50.5 us  [bubble_source(): lax.all_gather(code, ('gx', 'gy'), axis=0, tiled=True)]
    all_to_all x1, waiting for transfers between devices: 0.01 us -> 53 us  [bubble_source(): lax.all_to_all(outgoing.reshape(devices, capacity, steps * depth), ('gx',...]
    all_to_all x1, starting transfers between devices: 5.85 us -> 19.1 us  [bubble_source(): lax.all_to_all(outgoing.reshape(devices, capacity, steps * depth), ('gx',...]
    ppermute x8, waiting for transfers between devices: 10 us -> 3.75 us  [from_behind(): return lax.ppermute(block, axis, route)]
    ppermute x8, starting transfers between devices: 18.4 us -> 22.3 us  [from_behind(): return lax.ppermute(block, axis, route)]
    unnamed x30 -> x32, local copies, waits for them, and re-layouts: 4.75 us -> 3.83 us
  transfers between devices with their start and end apart: 10 -> 10, of which waited for: 4 -> 2; matrix products, arithmetic and copies ran while one was open for 14% -> 16% of each run, Pallas kernels for 0% -> 0%
where the time goes in v2:
time: 217 us; the launch traced here: 214 us
  waiting for transfers between devices  56.8 us (26%)
  blocking collectives  50.5 us (23%)
  starting transfers between devices  46.6 us (21%)
  other arithmetic  24.9 us (11%)
  local copies, waits for them, and re-layouts  24.5 us (11%)
  matrix products  9.48 us (4%)
    all_to_all x1, waiting for transfers between devices, bubble_source(): lax.all_to_all(outgoing.reshape(devices, capacity, steps * depth), ('gx',...  53 us
    all_gather x1, blocking collectives, bubble_source(): lax.all_gather(code, ('gx', 'gy'), axis=0, tiled=True)  50.5 us
    ppermute x8, starting transfers between devices, from_behind(): return lax.ppermute(block, axis, route)  22.3 us
    all_to_all x1, starting transfers between devices, bubble_source(): lax.all_to_all(outgoing.reshape(devices, capacity, steps * depth), ('gx',...  19.1 us
    sub x2, other arithmetic, body(): vel_z = vel_z - step_ratio * buoyancy * (next_z - pressure)  10.5 us
    add x2, other arithmetic, body(): pressure + step_ratio * stiffness * (source[:, :, step, :] + forcing - di...  6.18 us
    dot_general x1, matrix products, bubble_source(): jnp.dot(hits, incoming.reshape(slots, steps * depth), preferred_element_t...  5.48 us
    all_to_all x1, starting transfers between devices, incident_plane(): rows = lax.all_to_all(chosen, 'gx', split_axis=0, concat_axis=0, tiled=True)  5.21 us
  transfers between devices with their start and end apart: 10, of which 2 were waited for; matrix products, arithmetic and copies ran while one was open for 16% of the time, Pallas kernels for 0%

profile of v2, /device:TPU:18, one launch (start us, length us, event | category | flops | bytes accessed | tf_op | source)
XLA Modules:
  0.0 214.1 jit_solution(4152463765882377466)
XLA Ops:
  0.7 1.4 fusion.50
  2.0 2.4 %collective-permute-start.1 = (f32[32,1,512]{2,1,0:T(1,128)S(1)}, f32[32,1,512]{2,1,0:T(1,128)S(1)}, u32[]{:S(2)}, u32[]{:S(2)}) collective-permute-start(f32[32,1,512]{2,1,0:T(1,128)S(1)} %get-tuple-element.50), channel_id=1, source_target_pairs={{1,0},{2,1},{3,2},{5,4},{6,5},{7,6},{9,8},{10,9},{11,10},{13,12},{... | collective-permute-start | bytes 196616 | tf_op jit(solution)/shard_map/ppermute | solution.py:14
  4.5 0.9 fusion.51
  5.4 1.9 collective-permute-start
  9.0 2.5 %collective-permute-start.2 = (f32[3,32,512]{2,1,0:T(8,128)S(1)}, f32[3,32,512]{2,1,0:T(8,128)S(1)}, u32[]{:S(2)}, u32[]{:S(2)}) collective-permute-start(f32[3,32,512]{2,1,0:T(8,128)S(1)} %pad_maximum_fusion.1), channel_id=1, source_target_pairs={{0,4},{4,8},{8,12},{12,16},{16,20},{20,24},{24,28},{1,5},{5,9},{9,... | collective-permute-start | bytes 589832 | tf_op jit(solution)/shard_map/ppermute | solution.py:14
  11.6 0.9 and_reduce_fusion
  14.7 5.2 %all-to-all-start = ((bf16[8,32,512]{2,1,0:T(8,128)(2,1)}), bf16[8,32,512]{2,1,0:T(8,128)(2,1)S(1)}, u32[]{:S(2)}, u32[]{:S(2)}) async-start(bf16[8,32,512]{2,1,0:T(8,128)(2,1)} %broadcast_select_fusion), calls=%async_computation | async-start | bytes 524288 | tf_op jit(solution)/shard_map/all_to_all | solution.py:80
  19.9 1.1 slice.146
  21.0 1.1 slice.145
  22.3 4.3 %collective-permute-start.3 = (f32[32,3,512]{2,1,0:T(4,128)S(1)}, f32[32,3,512]{2,1,0:T(4,128)S(1)}, u32[]{:S(2)}, u32[]{:S(2)}) collective-permute-start(f32[32,3,512]{2,1,0:T(4,128)S(1)} %pad_maximum_fusion), channel_id=1, source_target_pairs={{0,1},{1,2},{2,3},{4,5},{5,6},{6,7},{8,9},{9,10},{10,11},{12,13},{... | collective-permute-start | bytes 589832 | tf_op jit(solution)/shard_map/ppermute | solution.py:14
  26.7 1.7 reduce-window.16
  28.9 50.5 %all-gather = s32[32,1,768]{2,1,0:T(1,128)S(1)} all-gather(s32[1,1,768]{2,1,0:T(1,128)S(1)} %reshape.220), channel_id=1, replica_groups=mesh['gx'=8,'gy'=4] {'gx','gy'}, dimensions={0}, use_global_device_ids=true | all-gather | bytes 101376 | tf_op jit(solution)/shard_map/all_gather | solution.py:45
  79.7 1.7 reduce-window.14
  82.3 4.0 %fusion.4 = bf16[1536,1024]{1,0:T(8,128)(2,1)} fusion(bf16[768,1024]{1,0:T(8,128)(2,1)S(1)} %bitcast.129, s32[768]{0:T(1024)S(1)} %get-tuple-element.55), kind=kOutput, calls=%fused_computation.8 | convolution fusion | flops 2418671616 | bytes 4721664 | tf_op jit(solution)/shard_map/dot_general | solution.py:39
  87.3 19.1 %all-to-all-start.1 = ((bf16[32,48,1024]{2,1,0:T(8,128)(2,1)}), bf16[32,48,1024]{2,1,0:T(8,128)(2,1)}, u32[]{:S(2)}, u32[]{:S(2)}) async-start(bf16[32,48,1024]{2,1,0:T(8,128)(2,1)} %bitcast.126), calls=%async_computation.1 | async-start | bytes 6291456 | tf_op jit(solution)/shard_map/all_to_all | solution.py:55
  106.4 1.5 slice.148
  107.9 1.7 slice.153
  109.6 1.9 slice.158
  111.6 7.7 %multiply_subtract_fusion.1 = (f32[32,32,512]{2,1,0:T(8,128)}, f32[32,32,512]{2,1,0:T(8,128)}, f32[32,32,512]{2,1,0:T(8,128)S(1)}) fusion(f32[32,32,512]{2,1,0:T(8,128)} %param.15, f32[32,32,512]{2,1,0:T(8,128)S(1)} %copy-done.2, f32[32,32,511]{2,1,0:T(8,128)} %slice.158, f32[32,32,512]{2,1,0:T(8,128)} %param.16, f32[32,32,512]{2,1,0:T(8,128)} %param.14, ...), kind=kLoop, calls=%fused_computation.41 | loop fusion | flops 8388608 | bytes 23064576 | tf_op jit(solution)/shard_map/sub | solution.py:122
  119.3 1.6 slice.176
  121.6 53.0 %all-to-all-done.1 = bf16[32,48,1024]{2,1,0:T(8,128)(2,1)} async-done(((bf16[32,48,1024]{2,1,0:T(8,128)(2,1)}), bf16[32,48,1024]{2,1,0:T(8,128)(2,1)}, u32[]{:S(2)}, u32[]{:S(2)}) %all-to-all-start.1) | async-done | bytes 3145760 | tf_op jit(solution)/shard_map/all_to_all | solution.py:55
  174.6 4.7 %copy.38 = bf16[1536,1024]{0,1:T(8,128)(2,1)} copy(bf16[1536,1024]{1,0:T(8,128)(2,1)} %bitcast.4) | data formatting | bytes 6291456 | tf_op jit(solution)/shard_map/reshape | solution.py:66
  179.3 5.5 %fusion = f32[32,32,2,512]{3,1,2,0:T(8,128)S(1)} fusion(bf16[2,512,1536,1]{2,1,0,3:T(8,128)(2,1)} %bitcast.127, s32[1536]{0:T(1024)S(1)} %eq.113, s32[32,32]{1,0:T(8,128)S(1)} %multiply_add_fusion), kind=kOutput, calls=%fused_computation.1 | convolution fusion | flops 3222798336 | bytes 7350272 | tf_op jit(solution)/shard_map/dot_general | solution.py:65
  185.3 1.1 copy-done.3
  188.2 2.5 %fusion.14 = f32[32,32,512]{2,1,0:T(8,128)S(1)} fusion(f32[32,32,512]{2,1,0:T(8,128)S(1)} %copy-done.2, f32[32,32,512]{2,1,0:T(8,128)S(1)} %get-tuple-element.36, f32[32,32,512]{2,1,0:T(8,128)S(1)} %copy-done.7, f32[31,32,512]{2,1,0:T(8,128)S(1)} %copy-done.11, f32[1,32,512]{2,1,0:T(8,128)S(1)} %get-tuple-element.33, f32[32,32,512]{2,1,0:T(8,128)S(1)} %copy-done.5, ...), kind=kLoop, calls=%fused_computation.22 | loop fusion | flops 7864320 | bytes 20967424 | tf_op jit(solution)/shard_map/add | solution.py:131
  190.8 1.9 collective-permute-start.5
  192.8 3.5 %collective-permute-start.7 = (f32[32,1,512]{2,1,0:T(1,128)S(1)}, f32[32,1,512]{2,1,0:T(1,128)S(1)}, u32[]{:S(2)}, u32[]{:S(2)}) collective-permute-start(f32[32,1,512]{2,1,0:T(1,128)S(1)} %slice.186), channel_id=1, source_target_pairs={{0,1},{1,2},{2,3},{4,5},{5,6},{6,7},{8,9},{9,10},{10,11},{12,13},{... | collective-permute-start | bytes 196616 | tf_op jit(solution)/shard_map/ppermute | solution.py:14
  196.4 3.3 %collective-permute-start.4 = (f32[1,32,512]{2,1,0:T(8,128)S(1)}, f32[1,32,512]{2,1,0:T(8,128)S(1)}, u32[]{:S(2)}, u32[]{:S(2)}) collective-permute-start(f32[1,32,512]{2,1,0:T(8,128)S(1)} %get-tuple-element.48), channel_id=1, source_target_pairs={{4,0},{8,4},{12,8},{16,12},{20,16},{24,20},{28,24},{5,1},{9,5},{13... | collective-permute-start | bytes 196616 | tf_op jit(solution)/shard_map/ppermute | solution.py:14
  199.9 2.3 %collective-permute-start.6 = (f32[32,1,512]{2,1,0:T(1,128)S(1)}, f32[32,1,512]{2,1,0:T(1,128)S(1)}, u32[]{:S(2)}, u32[]{:S(2)}) collective-permute-start(f32[32,1,512]{2,1,0:T(1,128)S(1)} %get-tuple-element.46), channel_id=1, source_target_pairs={{1,0},{2,1},{3,2},{5,4},{6,5},{7,6},{9,8},{10,9},{11,10},{13,12},{... | collective-permute-start | bytes 196616 | tf_op jit(solution)/shard_map/ppermute | solution.py:14
  203.5 3.7 %collective-permute-done.6 = f32[32,1,512]{2,1,0:T(1,128)S(1)} collective-permute-done((f32[32,1,512]{2,1,0:T(1,128)S(1)}, f32[32,1,512]{2,1,0:T(1,128)S(1)}, u32[]{:S(2)}, u32[]{:S(2)}) %collective-permute-start.6) | collective-permute-done | bytes 65568 | tf_op jit(solution)/shard_map/ppermute | solution.py:14
  207.2 2.8 %multiply_subtract_fusion = (f32[32,32,512]{2,1,0:T(8,128)S(1)}, f32[32,32,512]{2,1,0:T(8,128)S(1)}, f32[32,32,512]{2,1,0:T(8,128)S(1)}) fusion(f32[32,32,512]{2,1,0:T(8,128)S(1)} %copy-done.4, f32[32,32,512]{2,1,0:T(8,128)S(1)} %fusion.14, f32[32,32,511]{2,1,0:T(8,128)S(1)} %slice.188, f32[32,32,512]{2,1,0:T(8,128)S(1)} %copy-done.3, ...), kind=kLoop, calls=%fused_computation.40 | loop fusion | flops 8388608 | bytes 23064576 | tf_op jit(solution)/shard_map/sub | solution.py:122
  210.3 3.6 %fusion.23 = f32[32,32,512]{2,1,0:T(8,128)} fusion(f32[32,32,512]{2,1,0:T(8,128)S(1)} %fusion.14, f32[32,32,512]{2,1,0:T(8,128)S(1)} %get-tuple-element.35, f32[32,32,512]{2,1,0:T(8,128)S(1)} %get-tuple-element.39, f32[31,32,512]{2,1,0:T(8,128)S(1)} %slice.183, f32[1,32,512]{2,1,0:T(8,128)S(1)} %get-tuple-element.47, ...), kind=kLoop, calls=%fused_computation.35 | loop fusion | flops 7864320 | bytes 20967424 | tf_op jit(solution)/shard_map/add | solution.py:131
  (76 shorter events, 11.5 us)
Async XLA Ops:
  0.6 12.7 %copy-start = (bf16[16,32,512]{2,1,0:T(8,128)(2,1)S(1)}, bf16[16,32,512]{2,1,0:T(8,128)(2,1)}, u32[]{:S(2)}) copy-start(bf16[16,32,512]{2,1,0:T(8,128)(2,1)} %param.20) | copy-start | bytes 1572868
  0.6 26.0 %copy-start.14 = (s32[768,1]{0,1:T(1,128)S(1)}, s32[768,1]{0,1:T(1,128)}, u32[]{:S(2)}) copy-start(s32[768,1]{0,1:T(1,128)} %param.18) | copy-start | bytes 9220
  0.7 28.2 %copy-start.13 = (s32[768]{0:T(1024)S(1)}, s32[768]{0:T(1024)}, u32[]{:S(2)}) copy-start(s32[768]{0:T(1024)} %param.19) | copy-start | bytes 9220
  2.0 85.2 %collective-permute-start.1 = (f32[32,1,512]{2,1,0:T(1,128)S(1)}, f32[32,1,512]{2,1,0:T(1,128)S(1)}, u32[]{:S(2)}, u32[]{:S(2)}) collective-permute-start(f32[32,1,512]{2,1,0:T(1,128)S(1)} %get-tuple-element.50), channel_id=1, source_target_pairs={{1,0},{2,1},{3,2},{5,4},{6,5},{7,6},{9,8},{10,9},{11,10},{13,12},{... | collective-permute-start | bytes 196616 | tf_op jit(solution)/shard_map/ppermute | solution.py:14
  5.4 81.9 %collective-permute-start = (f32[1,32,512]{2,1,0:T(8,128)S(1)}, f32[1,32,512]{2,1,0:T(8,128)S(1)}, u32[]{:S(2)}, u32[]{:S(2)}) collective-permute-start(f32[1,32,512]{2,1,0:T(8,128)S(1)} %get-tuple-element.52), channel_id=1, source_target_pairs={{4,0},{8,4},{12,8},{16,12},{20,16},{24,20},{28,24},{5,1},{9,5},{13... | collective-permute-start | bytes 196616 | tf_op jit(solution)/shard_map/ppermute | solution.py:14
  9.0 72.8 %copy-start.12 = (bf16[768,2,512]{2,1,0:T(2,128)(2,1)S(1)}, bf16[768,2,512]{2,1,0:T(2,128)(2,1)}, u32[]{:S(2)}) copy-start(bf16[768,2,512]{2,1,0:T(2,128)(2,1)} %param.17) | copy-start | bytes 4718596
  9.0 78.2 %collective-permute-start.2 = (f32[3,32,512]{2,1,0:T(8,128)S(1)}, f32[3,32,512]{2,1,0:T(8,128)S(1)}, u32[]{:S(2)}, u32[]{:S(2)}) collective-permute-start(f32[3,32,512]{2,1,0:T(8,128)S(1)} %pad_maximum_fusion.1), channel_id=1, source_target_pairs={{0,4},{4,8},{8,12},{12,16},{16,20},{20,24},{24,28},{1,5},{5,9},{9,... | collective-permute-start | bytes 589832 | tf_op jit(solution)/shard_map/ppermute | solution.py:14
  14.7 72.4 %all-to-all-start = ((bf16[8,32,512]{2,1,0:T(8,128)(2,1)}), bf16[8,32,512]{2,1,0:T(8,128)(2,1)S(1)}, u32[]{:S(2)}, u32[]{:S(2)}) async-start(bf16[8,32,512]{2,1,0:T(8,128)(2,1)} %broadcast_select_fusion), calls=%async_computation | async-start | bytes 524288 | tf_op jit(solution)/shard_map/all_to_all | solution.py:80
  22.3 64.9 %collective-permute-start.3 = (f32[32,3,512]{2,1,0:T(4,128)S(1)}, f32[32,3,512]{2,1,0:T(4,128)S(1)}, u32[]{:S(2)}, u32[]{:S(2)}) collective-permute-start(f32[32,3,512]{2,1,0:T(4,128)S(1)} %pad_maximum_fusion), channel_id=1, source_target_pairs={{0,1},{1,2},{2,3},{4,5},{5,6},{6,7},{8,9},{9,10},{10,11},{12,13},{... | collective-permute-start | bytes 589832 | tf_op jit(solution)/shard_map/ppermute | solution.py:14
  87.3 19.1 %copy-start.2 = (f32[32,32,512]{2,1,0:T(8,128)S(1)}, f32[32,32,512]{2,1,0:T(8,128)}, u32[]{:S(2)}) copy-start(f32[32,32,512]{2,1,0:T(8,128)} %param.12) | copy-start | bytes 6291460
  87.3 87.3 %all-to-all-start.1 = ((bf16[32,48,1024]{2,1,0:T(8,128)(2,1)}), bf16[32,48,1024]{2,1,0:T(8,128)(2,1)}, u32[]{:S(2)}, u32[]{:S(2)}) async-start(bf16[32,48,1024]{2,1,0:T(8,128)(2,1)} %bitcast.126), calls=%async_computation.1 | async-start | bytes 6291456 | tf_op jit(solution)/shard_map/all_to_all | solution.py:55
  119.3 2.0 copy-start.6
  179.3 6.0 %copy-start.11 = (f32[31,32,512]{2,1,0:T(8,128)S(1)}, f32[31,32,512]{2,1,0:T(8,128)}, u32[]{:S(2)}) copy-start(f32[31,32,512]{2,1,0:T(8,128)} %slice.176) | copy-start | bytes 6094852
  184.8 1.6 copy-start.3
  184.8 2.2 %copy-start.4 = (f32[32,32,512]{2,1,0:T(8,128)S(1)}, f32[32,32,512]{2,1,0:T(8,128)}, u32[]{:S(2)}) copy-start(f32[32,32,512]{2,1,0:T(8,128)} %get-tuple-element.42) | copy-start | bytes 6291460
  184.8 2.8 %copy-start.5 = (f32[32,32,512]{2,1,0:T(8,128)S(1)}, f32[32,32,512]{2,1,0:T(8,128)}, u32[]{:S(2)}) copy-start(f32[32,32,512]{2,1,0:T(8,128)} %get-tuple-element.43) | copy-start | bytes 6291460
  184.8 3.4 %copy-start.7 = (f32[32,32,512]{2,1,0:T(8,128)S(1)}, f32[32,32,512]{2,1,0:T(8,128)}, u32[]{:S(2)}) copy-start(f32[32,32,512]{2,1,0:T(8,128)} %copy-done.6) | copy-start | bytes 6291460
  190.8 5.6 %collective-permute-start.5 = (f32[1,32,512]{2,1,0:T(8,128)S(1)}, f32[1,32,512]{2,1,0:T(8,128)S(1)}, u32[]{:S(2)}, u32[]{:S(2)}) collective-permute-start(f32[1,32,512]{2,1,0:T(8,128)S(1)} %slice.182), channel_id=1, source_target_pairs={{0,4},{4,8},{8,12},{12,16},{16,20},{20,24},{24,28},{1,5},{5,9},{9,... | collective-permute-start | bytes 196616 | tf_op jit(solution)/shard_map/ppermute | solution.py:14
  192.8 7.0 %collective-permute-start.7 = (f32[32,1,512]{2,1,0:T(1,128)S(1)}, f32[32,1,512]{2,1,0:T(1,128)S(1)}, u32[]{:S(2)}, u32[]{:S(2)}) collective-permute-start(f32[32,1,512]{2,1,0:T(1,128)S(1)} %slice.186), channel_id=1, source_target_pairs={{0,1},{1,2},{2,3},{4,5},{5,6},{6,7},{8,9},{9,10},{10,11},{12,13},{... | collective-permute-start | bytes 196616 | tf_op jit(solution)/shard_map/ppermute | solution.py:14
  196.4 7.1 %collective-permute-start.4 = (f32[1,32,512]{2,1,0:T(8,128)S(1)}, f32[1,32,512]{2,1,0:T(8,128)S(1)}, u32[]{:S(2)}, u32[]{:S(2)}) collective-permute-start(f32[1,32,512]{2,1,0:T(8,128)S(1)} %get-tuple-element.48), channel_id=1, source_target_pairs={{4,0},{8,4},{12,8},{16,12},{20,16},{24,20},{28,24},{5,1},{9,5},{13... | collective-permute-start | bytes 196616 | tf_op jit(solution)/shard_map/ppermute | solution.py:14
  199.9 7.3 %collective-permute-start.6 = (f32[32,1,512]{2,1,0:T(1,128)S(1)}, f32[32,1,512]{2,1,0:T(1,128)S(1)}, u32[]{:S(2)}, u32[]{:S(2)}) collective-permute-start(f32[32,1,512]{2,1,0:T(1,128)S(1)} %get-tuple-element.46), channel_id=1, source_target_pairs={{1,0},{2,1},{3,2},{5,4},{6,5},{7,6},{9,8},{10,9},{11,10},{13,12},{... | collective-permute-start | bytes 196616 | tf_op jit(solution)/shard_map/ppermute | solution.py:14
  210.0 4.0 %copy-start.8 = (f32[32,32,512]{2,1,0:T(8,128)}, f32[32,32,512]{2,1,0:T(8,128)S(1)}, u32[]{:S(2)}) copy-start(f32[32,32,512]{2,1,0:T(8,128)S(1)} %get-tuple-element.37) | copy-start | bytes 6291460
  210.0 4.0 %copy-start.9 = (f32[32,32,512]{2,1,0:T(8,128)}, f32[32,32,512]{2,1,0:T(8,128)S(1)}, u32[]{:S(2)}) copy-start(f32[32,32,512]{2,1,0:T(8,128)S(1)} %get-tuple-element.38) | copy-start | bytes 6291460
  210.0 3.9 %copy-start.10 = (f32[32,32,512]{2,1,0:T(8,128)}, f32[32,32,512]{2,1,0:T(8,128)S(1)}, u32[]{:S(2)}) copy-start(f32[32,32,512]{2,1,0:T(8,128)S(1)} %get-tuple-element.39) | copy-start | bytes 6291460
  210.3 3.7 %copy-start.1 = (bf16[16,32,512]{2,1,0:T(8,128)(2,1)S(1)}, bf16[16,32,512]{2,1,0:T(8,128)(2,1)}, u32[]{:S(2)}) copy-start(bf16[16,32,512]{2,1,0:T(8,128)(2,1)} %param.20) | copy-start | bytes 1572868

commit v3 on v2

--- a/solution.py
+++ b/solution.py
@@ -30,7 +30,6 @@
     depth = waves.shape[2]
     capacity = 2 * bubbles // devices
     slots = devices * capacity
-    me = lax.axis_index("gx") * tiles_y + lax.axis_index("gy")
     dest = bubble_dest[:, 0]
     owners = (dest[:, None] == jnp.arange(devices, dtype=jnp.int32)[None, :]).astype(jnp.int32)
     rank = jnp.sum(jnp.cumsum(owners, axis=0) * owners, axis=1) - 1
@@ -41,16 +40,14 @@
         waves.reshape(bubbles, steps * depth),
         preferred_element_type=jnp.float32,
     ).astype(jnp.bfloat16)
-    code = dest * cells + bubble_column
-    all_code = lax.all_gather(code, ("gx", "gy"), axis=0, tiled=True).reshape(devices, bubbles)
-    all_dest = all_code // cells
-    all_col = all_code % cells
-    mine = (all_dest == me).astype(jnp.int32)
-    in_rank = jnp.cumsum(mine, axis=1) - 1
-    in_rank = jnp.where(mine > 0, in_rank, -1)
-    slot_of = jnp.arange(capacity, dtype=jnp.int32)
-    match = in_rank[:, None, :] == slot_of[None, :, None]
-    in_cols = jnp.max(jnp.where(match, all_col[:, None, :] + 1, 0), axis=2) - 1
+    out_cols = jnp.max(jnp.where(placed, bubble_column[None, :] + 1, 0), axis=1) - 1
+    in_cols = lax.all_to_all(
+        out_cols.reshape(devices, capacity),
+        ("gx", "gy"),
+        split_axis=0,
+        concat_axis=0,
+        tiled=True,
+    )
     in_cols, outgoing, ready = lax.optimization_barrier((in_cols, outgoing, ready))
     incoming = lax.all_to_all(
         outgoing.reshape(devices, capacity, steps * depth),
@@ -101,10 +98,10 @@
         jnp.concatenate([pressure[:, -1:], vel_y[:, -1:], void_frac[:, -1:]], 1), "gy", 1
     )
 
+    ready = (above_x, above_y, below_x, below_y)
+    source, ready = bubble_source(waves, bubble_dest, bubble_column, size_x * size_y, ready)
+    above_x, above_y, below_x, below_y = ready
     incident = incident_plane(history, delays, size_y, depth)
-    ready = (above_x, above_y, below_x, below_y, incident)
-    source, ready = bubble_source(waves, bubble_dest, bubble_column, size_x * size_y, ready)
-    above_x, above_y, below_x, below_y, incident = ready
     source = source.reshape(size_x, size_y, steps, depth)
     p_bx, vx_bx, void_bx = below_x[0:1], below_x[1:2], below_x[2:3]
     p_by, vy_by, void_by = below_y[:, 0:1], below_y[:, 1:2], below_y[:, 2:3]

time: 217 us -> 162 us (0.75)
  blocking collectives: 50.5 us -> 0 us
  starting transfers between devices: 46.6 us -> 38.9 us
    all_gather x1 -> x0, blocking collectives: 50.5 us -> none  [bubble_source(): lax.all_gather(code, ('gx', 'gy'), axis=0, tiled=True)]
    all_to_all x1, starting transfers between devices: 19.1 us -> 5.68 us  [bubble_source(): lax.all_to_all(outgoing.reshape(devices, capacity, steps * depth), ('gx',...]
    all_to_all x0 -> x1, starting transfers between devices: none -> 5.91 us  [bubble_source(): lax.all_to_all(out_cols.reshape(devices, capacity), ('gx', 'gy'), split_a...]
    unnamed x32 -> x33, local copies, waits for them, and re-layouts: 3.83 us -> 4.98 us
  transfers between devices with their start and end apart: 10 -> 11, of which waited for: 2 -> 3; matrix products, arithmetic and copies ran while one was open for 16% -> 21% of each run, Pallas kernels for 0% -> 0%
where the time goes in v3:
time: 162 us; the launch traced here: 160 us
  waiting for transfers between devices  58.2 us (36%)
  starting transfers between devices  38.9 us (24%)
  local copies, waits for them, and re-layouts  26.2 us (16%)
  other arithmetic  24.5 us (15%)
  matrix products  10.9 us (7%)
    all_to_all x1, waiting for transfers between devices, bubble_source(): lax.all_to_all(outgoing.reshape(devices, capacity, steps * depth), ('gx',...  52.9 us
    ppermute x8, starting transfers between devices, from_behind(): return lax.ppermute(block, axis, route)  22.2 us
    sub x2, other arithmetic, body(): vel_z = vel_z - step_ratio * buoyancy * (next_z - pressure)  10.5 us
    add x2, other arithmetic, body(): pressure + step_ratio * stiffness * (source[:, :, step, :] + forcing - di...  6.18 us
    all_to_all x1, starting transfers between devices, bubble_source(): lax.all_to_all(out_cols.reshape(devices, capacity), ('gx', 'gy'), split_a...  5.91 us
    all_to_all x1, starting transfers between devices, bubble_source(): lax.all_to_all(outgoing.reshape(devices, capacity, steps * depth), ('gx',...  5.68 us
    dot_general x1, matrix products, bubble_source(): jnp.dot(hits, incoming.reshape(slots, steps * depth), preferred_element_t...  5.48 us
    dot_general x1, matrix products, bubble_source(): jnp.dot(placed.astype(jnp.bfloat16), waves.reshape(bubbles, steps * depth...  5.37 us
  transfers between devices with their start and end apart: 11, of which 3 were waited for; matrix products, arithmetic and copies ran while one was open for 21% of the time, Pallas kernels for 0%

profile of v3, /device:TPU:18, one launch (start us, length us, event | category | flops | bytes accessed | tf_op | source)
XLA Modules:
  0.0 159.9 jit_solution(11649384603792977460)
XLA Ops:
  2.2 1.7 %reduce-window.6 = s32[32,6,128]{2,0,1:T(8,128)S(1)} reduce-window(s32[32,6,128]{2,0,1:T(8,128)S(1)} %fusion.28, s32[]{:T(128)} %constant.87.clone.1), window={size=1x1x128 pad=0_0x0_0x127_0}, to_apply=%region_0.0 | reduce-window | flops 3121152 | bytes 196612 | tf_op jit(solution)/shard_map/reduce-window
  5.8 5.9 %all-to-all-start = ((s32[32,1,48]{2,1,0:T(1,128)}), s32[32,1,48]{2,1,0:T(1,128)S(1)}, u32[]{:S(2)}, u32[]{:S(2)}) async-start(s32[32,1,48]{2,1,0:T(1,128)} %sub.123), calls=%async_computation | async-start | bytes 32768 | tf_op jit(solution)/shard_map/all_to_all | solution.py:44
  11.7 1.3 fusion.38
  13.0 2.5 %collective-permute-start.1 = (f32[32,1,512]{2,1,0:T(1,128)S(1)}, f32[32,1,512]{2,1,0:T(1,128)S(1)}, u32[]{:S(2)}, u32[]{:S(2)}) collective-permute-start(f32[32,1,512]{2,1,0:T(1,128)S(1)} %get-tuple-element.48), channel_id=1, source_target_pairs={{1,0},{2,1},{3,2},{5,4},{6,5},{7,6},{9,8},{10,9},{11,10},{13,12},{... | collective-permute-start | bytes 196616 | tf_op jit(solution)/shard_map/ppermute | solution.py:14
  16.4 1.9 %collective-permute-start = (f32[1,32,512]{2,1,0:T(8,128)S(1)}, f32[1,32,512]{2,1,0:T(8,128)S(1)}, u32[]{:S(2)}, u32[]{:S(2)}) collective-permute-start(f32[1,32,512]{2,1,0:T(8,128)S(1)} %get-tuple-element.50), channel_id=1, source_target_pairs={{4,0},{8,4},{12,8},{16,12},{20,16},{24,20},{28,24},{5,1},{9,5},{13... | collective-permute-start | bytes 196616 | tf_op jit(solution)/shard_map/ppermute | solution.py:14
  20.1 2.4 %collective-permute-start.2 = (f32[3,32,512]{2,1,0:T(8,128)S(1)}, f32[3,32,512]{2,1,0:T(8,128)S(1)}, u32[]{:S(2)}, u32[]{:S(2)}) collective-permute-start(f32[3,32,512]{2,1,0:T(8,128)S(1)} %pad_maximum_fusion.1), channel_id=1, source_target_pairs={{0,4},{4,8},{8,12},{12,16},{16,20},{20,24},{24,28},{1,5},{5,9},{9,... | collective-permute-start | bytes 589832 | tf_op jit(solution)/shard_map/ppermute | solution.py:14
  22.5 1.1 slice.138
  23.6 1.1 slice.137
  24.9 4.3 %collective-permute-start.3 = (f32[32,3,512]{2,1,0:T(4,128)S(1)}, f32[32,3,512]{2,1,0:T(4,128)S(1)}, u32[]{:S(2)}, u32[]{:S(2)}) collective-permute-start(f32[32,3,512]{2,1,0:T(4,128)S(1)} %pad_maximum_fusion), channel_id=1, source_target_pairs={{0,1},{1,2},{2,3},{4,5},{5,6},{6,7},{8,9},{9,10},{10,11},{12,13},{... | collective-permute-start | bytes 589832 | tf_op jit(solution)/shard_map/ppermute | solution.py:14
  31.4 1.4 broadcast_select_fusion
  32.8 1.6 copy.25
  34.4 5.2 %all-to-all-start.2 = ((bf16[8,32,512]{2,1,0:T(8,128)(2,1)}), bf16[8,32,512]{2,1,0:T(8,128)(2,1)S(1)}, u32[]{:S(2)}, u32[]{:S(2)}) async-start(bf16[8,32,512]{2,1,0:T(8,128)(2,1)} %broadcast_select_fusion), calls=%async_computation.2 | async-start | bytes 524288 | tf_op jit(solution)/shard_map/all_to_all | solution.py:77
  39.5 5.4 %fusion.4 = bf16[1536,1024]{1,0:T(8,128)(2,1)} fusion(bf16[768,1024]{1,0:T(8,128)(2,1)} %bitcast.66, s32[768]{0:T(1024)S(1)} %copy-done.15), kind=kOutput, calls=%fused_computation.7 | convolution fusion | flops 2418671616 | bytes 4721664 | tf_op jit(solution)/shard_map/dot_general | solution.py:38
  44.9 1.1 all-to-all-done.2
  46.0 5.7 %all-to-all-start.1 = ((bf16[32,48,1024]{2,1,0:T(8,128)(2,1)}), bf16[32,48,1024]{2,1,0:T(8,128)(2,1)}, u32[]{:S(2)}, u32[]{:S(2)}) async-start(bf16[32,48,1024]{2,1,0:T(8,128)(2,1)} %bitcast.63), calls=%async_computation.1 | async-start | bytes 6291456 | tf_op jit(solution)/shard_map/all_to_all | solution.py:52
  51.7 1.5 slice.140
  53.3 1.7 %slice.145 = f32[32,31,512]{2,1,0:T(8,128)} slice(f32[32,32,512]{2,1,0:T(8,128)S(1)} %copy-done.2), slice={[0:32], [1:32], [0:512]} | slice | bytes 4063232 | tf_op jit(solution)/shard_map/slice | solution.py:115
  55.0 1.9 %slice.150 = f32[32,32,511]{2,1,0:T(8,128)} slice(f32[32,32,512]{2,1,0:T(8,128)S(1)} %copy-done.2), slice={[0:32], [0:32], [1:512]} | slice | bytes 4186112 | tf_op jit(solution)/shard_map/slice | solution.py:116
  57.0 7.7 %multiply_subtract_fusion.1 = (f32[32,32,512]{2,1,0:T(8,128)}, f32[32,32,512]{2,1,0:T(8,128)}, f32[32,32,512]{2,1,0:T(8,128)S(1)}) fusion(f32[32,32,512]{2,1,0:T(8,128)} %param.15, f32[32,32,512]{2,1,0:T(8,128)S(1)} %copy-done.2, f32[32,32,511]{2,1,0:T(8,128)} %slice.150, f32[32,32,512]{2,1,0:T(8,128)} %param.16, f32[32,32,512]{2,1,0:T(8,128)} %param.14, ...), kind=kLoop, calls=%fused_computation.40 | loop fusion | flops 8388608 | bytes 23064576 | tf_op jit(solution)/shard_map/sub | solution.py:119
  64.7 1.6 slice.167
  67.0 52.9 %all-to-all-done.1 = bf16[32,48,1024]{2,1,0:T(8,128)(2,1)} async-done(((bf16[32,48,1024]{2,1,0:T(8,128)(2,1)}), bf16[32,48,1024]{2,1,0:T(8,128)(2,1)}, u32[]{:S(2)}, u32[]{:S(2)}) %all-to-all-start.1) | async-done | bytes 3145760 | tf_op jit(solution)/shard_map/all_to_all | solution.py:52
  119.9 4.7 %copy.20 = bf16[1536,1024]{0,1:T(8,128)(2,1)} copy(bf16[1536,1024]{1,0:T(8,128)(2,1)} %bitcast.5) | data formatting | bytes 6291456 | tf_op jit(solution)/shard_map/reshape | solution.py:63
  124.6 5.5 %fusion = f32[32,32,2,512]{3,1,2,0:T(8,128)S(1)} fusion(bf16[2,512,1536,1]{2,1,0,3:T(8,128)(2,1)} %bitcast.64, s32[1536]{0:T(1024)S(1)} %eq.76, s32[32,32]{1,0:T(8,128)S(1)} %multiply_add_fusion), kind=kOutput, calls=%fused_computation.1 | convolution fusion | flops 3222798336 | bytes 7350272 | tf_op jit(solution)/shard_map/dot_general | solution.py:62
  130.6 1.1 copy-done.3
  133.5 2.5 %fusion.14 = f32[32,32,512]{2,1,0:T(8,128)S(1)} fusion(f32[32,32,512]{2,1,0:T(8,128)S(1)} %copy-done.2, f32[32,32,512]{2,1,0:T(8,128)S(1)} %get-tuple-element.34, f32[32,32,512]{2,1,0:T(8,128)S(1)} %copy-done.7, f32[31,32,512]{2,1,0:T(8,128)S(1)} %copy-done.11, f32[1,32,512]{2,1,0:T(8,128)S(1)} %get-tuple-element.31, f32[32,32,512]{2,1,0:T(8,128)S(1)} %copy-done.5, ...), kind=kLoop, calls=%fused_computation.21 | loop fusion | flops 7864320 | bytes 20967424 | tf_op jit(solution)/shard_map/add | solution.py:128
  136.1 1.9 %collective-permute-start.5 = (f32[1,32,512]{2,1,0:T(8,128)S(1)}, f32[1,32,512]{2,1,0:T(8,128)S(1)}, u32[]{:S(2)}, u32[]{:S(2)}) collective-permute-start(f32[1,32,512]{2,1,0:T(8,128)S(1)} %slice.173), channel_id=1, source_target_pairs={{0,4},{4,8},{8,12},{12,16},{16,20},{20,24},{24,28},{1,5},{5,9},{9,... | collective-permute-start | bytes 196616 | tf_op jit(solution)/shard_map/ppermute | solution.py:14
  138.1 3.5 %collective-permute-start.7 = (f32[32,1,512]{2,1,0:T(1,128)S(1)}, f32[32,1,512]{2,1,0:T(1,128)S(1)}, u32[]{:S(2)}, u32[]{:S(2)}) collective-permute-start(f32[32,1,512]{2,1,0:T(1,128)S(1)} %slice.177), channel_id=1, source_target_pairs={{0,1},{1,2},{2,3},{4,5},{5,6},{6,7},{8,9},{9,10},{10,11},{12,13},{... | collective-permute-start | bytes 196616 | tf_op jit(solution)/shard_map/ppermute | solution.py:14
  141.7 3.3 %collective-permute-start.4 = (f32[1,32,512]{2,1,0:T(8,128)S(1)}, f32[1,32,512]{2,1,0:T(8,128)S(1)}, u32[]{:S(2)}, u32[]{:S(2)}) collective-permute-start(f32[1,32,512]{2,1,0:T(8,128)S(1)} %get-tuple-element.46), channel_id=1, source_target_pairs={{4,0},{8,4},{12,8},{16,12},{20,16},{24,20},{28,24},{5,1},{9,5},{13... | collective-permute-start | bytes 196616 | tf_op jit(solution)/shard_map/ppermute | solution.py:14
  145.2 2.3 %collective-permute-start.6 = (f32[32,1,512]{2,1,0:T(1,128)S(1)}, f32[32,1,512]{2,1,0:T(1,128)S(1)}, u32[]{:S(2)}, u32[]{:S(2)}) collective-permute-start(f32[32,1,512]{2,1,0:T(1,128)S(1)} %get-tuple-element.44), channel_id=1, source_target_pairs={{1,0},{2,1},{3,2},{5,4},{6,5},{7,6},{9,8},{10,9},{11,10},{13,12},{... | collective-permute-start | bytes 196616 | tf_op jit(solution)/shard_map/ppermute | solution.py:14
  148.8 4.2 %collective-permute-done.6 = f32[32,1,512]{2,1,0:T(1,128)S(1)} collective-permute-done((f32[32,1,512]{2,1,0:T(1,128)S(1)}, f32[32,1,512]{2,1,0:T(1,128)S(1)}, u32[]{:S(2)}, u32[]{:S(2)}) %collective-permute-start.6) | collective-permute-done | bytes 65568 | tf_op jit(solution)/shard_map/ppermute | solution.py:14
  153.0 2.8 %multiply_subtract_fusion = (f32[32,32,512]{2,1,0:T(8,128)S(1)}, f32[32,32,512]{2,1,0:T(8,128)S(1)}, f32[32,32,512]{2,1,0:T(8,128)S(1)}) fusion(f32[32,32,512]{2,1,0:T(8,128)S(1)} %copy-done.4, f32[32,32,512]{2,1,0:T(8,128)S(1)} %fusion.14, f32[32,32,511]{2,1,0:T(8,128)S(1)} %slice.179, f32[32,32,512]{2,1,0:T(8,128)S(1)} %copy-done.3, ...), kind=kLoop, calls=%fused_computation.39 | loop fusion | flops 8388608 | bytes 23064576 | tf_op jit(solution)/shard_map/sub | solution.py:119
  156.1 3.6 %fusion.23 = f32[32,32,512]{2,1,0:T(8,128)} fusion(f32[32,32,512]{2,1,0:T(8,128)S(1)} %fusion.14, f32[32,32,512]{2,1,0:T(8,128)S(1)} %get-tuple-element.33, f32[32,32,512]{2,1,0:T(8,128)S(1)} %get-tuple-element.37, f32[31,32,512]{2,1,0:T(8,128)S(1)} %slice.174, f32[1,32,512]{2,1,0:T(8,128)S(1)} %get-tuple-element.45, ...), kind=kLoop, calls=%fused_computation.34 | loop fusion | flops 7864320 | bytes 20967424 | tf_op jit(solution)/shard_map/add | solution.py:128
  (74 shorter events, 13.4 us)
Async XLA Ops:
  0.6 30.0 %copy-start = (bf16[16,32,512]{2,1,0:T(8,128)(2,1)S(1)}, bf16[16,32,512]{2,1,0:T(8,128)(2,1)}, u32[]{:S(2)}) copy-start(bf16[16,32,512]{2,1,0:T(8,128)(2,1)} %param.20) | copy-start | bytes 1572868
  0.6 28.5 %copy-start.13 = (s32[8,8]{1,0:T(8,128)S(1)}, s32[8,8]{1,0:T(8,128)}, u32[]{:S(2)}) copy-start(s32[8,8]{1,0:T(8,128)} %param.21) | copy-start | bytes 772
  0.7 32.1 %copy-start.12 = (bf16[768,2,512]{2,1,0:T(2,128)(2,1)S(1)}, bf16[768,2,512]{2,1,0:T(2,128)(2,1)}, u32[]{:S(2)}) copy-start(bf16[768,2,512]{2,1,0:T(2,128)(2,1)} %param.17) | copy-start | bytes 4718596
  4.4 14.0 %copy-start.14 = (s32[768]{0:T(1024)}, s32[768]{0:T(1024)S(1)}, u32[]{:S(2)}) copy-start(s32[768]{0:T(1024)S(1)} %add_add_fusion) | copy-start | bytes 9220
  5.8 28.5 %all-to-all-start = ((s32[32,1,48]{2,1,0:T(1,128)}), s32[32,1,48]{2,1,0:T(1,128)S(1)}, u32[]{:S(2)}, u32[]{:S(2)}) async-start(s32[32,1,48]{2,1,0:T(1,128)} %sub.123), calls=%async_computation | async-start | bytes 32768 | tf_op jit(solution)/shard_map/all_to_all | solution.py:44
  13.0 31.8 %collective-permute-start.1 = (f32[32,1,512]{2,1,0:T(1,128)S(1)}, f32[32,1,512]{2,1,0:T(1,128)S(1)}, u32[]{:S(2)}, u32[]{:S(2)}) collective-permute-start(f32[32,1,512]{2,1,0:T(1,128)S(1)} %get-tuple-element.48), channel_id=1, source_target_pairs={{1,0},{2,1},{3,2},{5,4},{6,5},{7,6},{9,8},{10,9},{11,10},{13,12},{... | collective-permute-start | bytes 196616 | tf_op jit(solution)/shard_map/ppermute | solution.py:14
  16.4 28.5 %collective-permute-start = (f32[1,32,512]{2,1,0:T(8,128)S(1)}, f32[1,32,512]{2,1,0:T(8,128)S(1)}, u32[]{:S(2)}, u32[]{:S(2)}) collective-permute-start(f32[1,32,512]{2,1,0:T(8,128)S(1)} %get-tuple-element.50), channel_id=1, source_target_pairs={{4,0},{8,4},{12,8},{16,12},{20,16},{24,20},{28,24},{5,1},{9,5},{13... | collective-permute-start | bytes 196616 | tf_op jit(solution)/shard_map/ppermute | solution.py:14
  20.1 24.8 %collective-permute-start.2 = (f32[3,32,512]{2,1,0:T(8,128)S(1)}, f32[3,32,512]{2,1,0:T(8,128)S(1)}, u32[]{:S(2)}, u32[]{:S(2)}) collective-permute-start(f32[3,32,512]{2,1,0:T(8,128)S(1)} %pad_maximum_fusion.1), channel_id=1, source_target_pairs={{0,4},{4,8},{8,12},{12,16},{16,20},{20,24},{24,28},{1,5},{5,9},{9,... | collective-permute-start | bytes 589832 | tf_op jit(solution)/shard_map/ppermute | solution.py:14
  24.9 20.0 %collective-permute-start.3 = (f32[32,3,512]{2,1,0:T(4,128)S(1)}, f32[32,3,512]{2,1,0:T(4,128)S(1)}, u32[]{:S(2)}, u32[]{:S(2)}) collective-permute-start(f32[32,3,512]{2,1,0:T(4,128)S(1)} %pad_maximum_fusion), channel_id=1, source_target_pairs={{0,1},{1,2},{2,3},{4,5},{5,6},{6,7},{8,9},{9,10},{10,11},{12,13},{... | collective-permute-start | bytes 589832 | tf_op jit(solution)/shard_map/ppermute | solution.py:14
  31.4 8.2 %copy-start.15 = (s32[768]{0:T(1024)S(1)}, s32[768]{0:T(1024)}, u32[]{:S(2)}) copy-start(s32[768]{0:T(1024)} %copy-done.14) | copy-start | bytes 9220
  34.4 11.7 %all-to-all-start.2 = ((bf16[8,32,512]{2,1,0:T(8,128)(2,1)}), bf16[8,32,512]{2,1,0:T(8,128)(2,1)S(1)}, u32[]{:S(2)}, u32[]{:S(2)}) async-start(bf16[8,32,512]{2,1,0:T(8,128)(2,1)} %broadcast_select_fusion), calls=%async_computation.2 | async-start | bytes 524288 | tf_op jit(solution)/shard_map/all_to_all | solution.py:77
  46.0 5.7 %copy-start.2 = (f32[32,32,512]{2,1,0:T(8,128)S(1)}, f32[32,32,512]{2,1,0:T(8,128)}, u32[]{:S(2)}) copy-start(f32[32,32,512]{2,1,0:T(8,128)} %param.12) | copy-start | bytes 6291460
  46.0 73.9 %all-to-all-start.1 = ((bf16[32,48,1024]{2,1,0:T(8,128)(2,1)}), bf16[32,48,1024]{2,1,0:T(8,128)(2,1)}, u32[]{:S(2)}, u32[]{:S(2)}) async-start(bf16[32,48,1024]{2,1,0:T(8,128)(2,1)} %bitcast.63), calls=%async_computation.1 | async-start | bytes 6291456 | tf_op jit(solution)/shard_map/all_to_all | solution.py:52
  64.7 2.0 %copy-start.6 = (f32[32,32,512]{2,1,0:T(8,128)}, f32[32,32,512]{2,1,0:T(8,128)S(1)}, u32[]{:S(2)}) copy-start(f32[32,32,512]{2,1,0:T(8,128)S(1)} %get-tuple-element.42) | copy-start | bytes 6291460
  124.6 6.0 %copy-start.11 = (f32[31,32,512]{2,1,0:T(8,128)S(1)}, f32[31,32,512]{2,1,0:T(8,128)}, u32[]{:S(2)}) copy-start(f32[31,32,512]{2,1,0:T(8,128)} %slice.167) | copy-start | bytes 6094852
  130.1 1.6 copy-start.3
  130.1 2.2 %copy-start.4 = (f32[32,32,512]{2,1,0:T(8,128)S(1)}, f32[32,32,512]{2,1,0:T(8,128)}, u32[]{:S(2)}) copy-start(f32[32,32,512]{2,1,0:T(8,128)} %get-tuple-element.40) | copy-start | bytes 6291460
  130.1 2.8 %copy-start.5 = (f32[32,32,512]{2,1,0:T(8,128)S(1)}, f32[32,32,512]{2,1,0:T(8,128)}, u32[]{:S(2)}) copy-start(f32[32,32,512]{2,1,0:T(8,128)} %get-tuple-element.41) | copy-start | bytes 6291460
  130.1 3.4 %copy-start.7 = (f32[32,32,512]{2,1,0:T(8,128)S(1)}, f32[32,32,512]{2,1,0:T(8,128)}, u32[]{:S(2)}) copy-start(f32[32,32,512]{2,1,0:T(8,128)} %copy-done.6) | copy-start | bytes 6291460
  136.1 5.6 %collective-permute-start.5 = (f32[1,32,512]{2,1,0:T(8,128)S(1)}, f32[1,32,512]{2,1,0:T(8,128)S(1)}, u32[]{:S(2)}, u32[]{:S(2)}) collective-permute-start(f32[1,32,512]{2,1,0:T(8,128)S(1)} %slice.173), channel_id=1, source_target_pairs={{0,4},{4,8},{8,12},{12,16},{16,20},{20,24},{24,28},{1,5},{5,9},{9,... | collective-permute-start | bytes 196616 | tf_op jit(solution)/shard_map/ppermute | solution.py:14
  138.1 7.0 %collective-permute-start.7 = (f32[32,1,512]{2,1,0:T(1,128)S(1)}, f32[32,1,512]{2,1,0:T(1,128)S(1)}, u32[]{:S(2)}, u32[]{:S(2)}) collective-permute-start(f32[32,1,512]{2,1,0:T(1,128)S(1)} %slice.177), channel_id=1, source_target_pairs={{0,1},{1,2},{2,3},{4,5},{5,6},{6,7},{8,9},{9,10},{10,11},{12,13},{... | collective-permute-start | bytes 196616 | tf_op jit(solution)/shard_map/ppermute | solution.py:14
  141.7 7.1 %collective-permute-start.4 = (f32[1,32,512]{2,1,0:T(8,128)S(1)}, f32[1,32,512]{2,1,0:T(8,128)S(1)}, u32[]{:S(2)}, u32[]{:S(2)}) collective-permute-start(f32[1,32,512]{2,1,0:T(8,128)S(1)} %get-tuple-element.46), channel_id=1, source_target_pairs={{4,0},{8,4},{12,8},{16,12},{20,16},{24,20},{28,24},{5,1},{9,5},{13... | collective-permute-start | bytes 196616 | tf_op jit(solution)/shard_map/ppermute | solution.py:14
  145.2 7.7 %collective-permute-start.6 = (f32[32,1,512]{2,1,0:T(1,128)S(1)}, f32[32,1,512]{2,1,0:T(1,128)S(1)}, u32[]{:S(2)}, u32[]{:S(2)}) collective-permute-start(f32[32,1,512]{2,1,0:T(1,128)S(1)} %get-tuple-element.44), channel_id=1, source_target_pairs={{1,0},{2,1},{3,2},{5,4},{6,5},{7,6},{9,8},{10,9},{11,10},{13,12},{... | collective-permute-start | bytes 196616 | tf_op jit(solution)/shard_map/ppermute | solution.py:14
  155.8 4.0 %copy-start.8 = (f32[32,32,512]{2,1,0:T(8,128)}, f32[32,32,512]{2,1,0:T(8,128)S(1)}, u32[]{:S(2)}) copy-start(f32[32,32,512]{2,1,0:T(8,128)S(1)} %get-tuple-element.35) | copy-start | bytes 6291460
  155.8 4.0 %copy-start.9 = (f32[32,32,512]{2,1,0:T(8,128)}, f32[32,32,512]{2,1,0:T(8,128)S(1)}, u32[]{:S(2)}) copy-start(f32[32,32,512]{2,1,0:T(8,128)S(1)} %get-tuple-element.36) | copy-start | bytes 6291460
  155.8 3.9 %copy-start.10 = (f32[32,32,512]{2,1,0:T(8,128)}, f32[32,32,512]{2,1,0:T(8,128)S(1)}, u32[]{:S(2)}) copy-start(f32[32,32,512]{2,1,0:T(8,128)S(1)} %get-tuple-element.37) | copy-start | bytes 6291460
  156.1 3.7 %copy-start.1 = (bf16[16,32,512]{2,1,0:T(8,128)(2,1)S(1)}, bf16[16,32,512]{2,1,0:T(8,128)(2,1)}, u32[]{:S(2)}) copy-start(bf16[16,32,512]{2,1,0:T(8,128)(2,1)} %param.20) | copy-start | bytes 1572868

commit v4 on v3

--- a/solution.py
+++ b/solution.py
@@ -21,7 +21,7 @@
     return (buoyancy, stiffness)
 
 
-def bubble_source(waves, bubble_dest, bubble_column, cells, ready):
+def bubble_source(waves, bubble_dest, bubble_column, cells):
     tiles_x = lax.axis_size("gx")
     tiles_y = lax.axis_size("gy")
     devices = tiles_x * tiles_y
@@ -48,21 +48,15 @@
         concat_axis=0,
         tiled=True,
     )
-    in_cols, outgoing, ready = lax.optimization_barrier((in_cols, outgoing, ready))
-    incoming = lax.all_to_all(
-        outgoing.reshape(devices, capacity, steps * depth),
-        ("gx", "gy"),
-        split_axis=0,
-        concat_axis=0,
-        tiled=True,
-    )
     hits = (
         jnp.arange(cells, dtype=jnp.int32)[:, None] == in_cols.reshape(slots)[None, :]
     ).astype(jnp.bfloat16)
-    source = jnp.dot(
-        hits, incoming.reshape(slots, steps * depth), preferred_element_type=jnp.float32
-    )
-    return source, ready
+    outgoing = outgoing.reshape(devices, capacity, steps, depth)
+    return hits, outgoing
+
+
+def exchange(sending):
+    return lax.all_to_all(sending, ("gx", "gy"), split_axis=0, concat_axis=0, tiled=True)
 
 
 def incident_plane(history, delays, size_y, depth):
@@ -98,11 +92,9 @@
         jnp.concatenate([pressure[:, -1:], vel_y[:, -1:], void_frac[:, -1:]], 1), "gy", 1
     )
 
-    ready = (above_x, above_y, below_x, below_y)
-    source, ready = bubble_source(waves, bubble_dest, bubble_column, size_x * size_y, ready)
-    above_x, above_y, below_x, below_y = ready
+    hits, outgoing = bubble_source(waves, bubble_dest, bubble_column, size_x * size_y)
+    slots = hits.shape[1]
     incident = incident_plane(history, delays, size_y, depth)
-    source = source.reshape(size_x, size_y, steps, depth)
     p_bx, vx_bx, void_bx = below_x[0:1], below_x[1:2], below_x[2:3]
     p_by, vy_by, void_by = below_y[:, 0:1], below_y[:, 1:2], below_y[:, 2:3]
     b_bx, _ = material(void_bx)
@@ -110,7 +102,9 @@
     forcing = jnp.zeros_like(pressure).at[0].set(incident)
     z_edge = jnp.zeros((size_x, size_y, 1), jnp.float32)
 
+    sending = outgoing[:, :, 0, :]
     for step in range(steps):
+        incoming = exchange(sending)
         next_x = jnp.concatenate([pressure[1:], above_x], 0)
         next_y = jnp.concatenate([pressure[:, 1:], above_y], 1)
         next_z = jnp.concatenate([pressure[:, :, 1:], z_edge], 2)
@@ -125,10 +119,15 @@
         prev_y = jnp.concatenate([lower_y, vel_y[:, :-1]], 1)
         prev_z = jnp.concatenate([z_edge, vel_z[:, :, :-1]], 2)
         divergence = vel_x - prev_x + (vel_y - prev_y) + (vel_z - prev_z)
-        pressure = pressure + step_ratio * stiffness * (
-            source[:, :, step, :] + forcing - divergence
+        rest = forcing - divergence
+        incoming, vel_x, vel_y, vel_z, vx_bx, vy_by, rest = lax.optimization_barrier(
+            (incoming, vel_x, vel_y, vel_z, vx_bx, vy_by, rest)
         )
+        source = jnp.dot(hits, incoming.reshape(slots, depth), preferred_element_type=jnp.float32)
+        source = source.reshape(size_x, size_y, depth)
+        pressure = pressure + step_ratio * stiffness * (source + rest)
         if step + 1 < steps:
+            sending, pressure = lax.optimization_barrier((outgoing[:, :, step + 1, :], pressure))
             above_x = from_behind(pressure[0:1], "gx", -1)
             above_y = from_behind(pressure[:, 0:1], "gy", -1)
             p_bx = from_behind(pressure[-1:], "gx", 1)

time: 162 us -> 170 us (1.049)
  local copies, waits for them, and re-layouts: 26.2 us -> 35.3 us
  waiting for transfers between devices: 58.2 us -> 53.2 us
  other arithmetic: 24.5 us -> 27.5 us
    all_to_all x1 -> x2, waiting for transfers between devices: 52.9 us -> 0.01 us  [exchange(): lax.all_to_all(sending, ('gx', 'gy'), split_axis=0, concat_axis=0, tiled=...]
    ppermute x8, waiting for transfers between devices: 4.22 us -> 53.2 us  [from_behind(): return lax.ppermute(block, axis, route)]
    unnamed x33 -> x39, local copies, waits for them, and re-layouts: 4.98 us -> 14 us
    sub x0 -> x2, other arithmetic: none -> 6.32 us  [body(): rest = forcing - divergence]
    slice x0 -> x1, local copies, waits for them, and re-layouts: none -> 5.33 us  [body(): sending = outgoing[:, :, 0, :]]
    all_to_all x1 -> x2, starting transfers between devices: 5.68 us -> 9.93 us  [exchange(): lax.all_to_all(sending, ('gx', 'gy'), split_axis=0, concat_axis=0, tiled=...]
    ppermute x8, starting transfers between devices: 22.2 us -> 19.4 us  [from_behind(): return lax.ppermute(block, axis, route)]
    add x3 -> x2, other arithmetic: 6.19 us -> 3.42 us  [body(): pressure = pressure + step_ratio * stiffness * (source + rest)]
  transfers between devices with their start and end apart: 11 -> 12, of which waited for: 3 -> 5; matrix products, arithmetic and copies ran while one was open for 21% -> 31% of each run, Pallas kernels for 0% -> 0%
where the time goes in v4:
time: 170 us; the launch traced here: 168 us
  waiting for transfers between devices  53.2 us (31%)
  starting transfers between devices  40.4 us (24%)
  local copies, waits for them, and re-layouts  35.3 us (21%)
  other arithmetic  27.5 us (16%)
  matrix products  10.7 us (6%)
    ppermute x8, waiting for transfers between devices, from_behind(): return lax.ppermute(block, axis, route)  53.2 us
    ppermute x8, starting transfers between devices, from_behind(): return lax.ppermute(block, axis, route)  19.4 us
    unnamed x39, local copies, waits for them, and re-layouts  14 us
    all_to_all x2, starting transfers between devices, exchange(): lax.all_to_all(sending, ('gx', 'gy'), split_axis=0, concat_axis=0, tiled=...  9.93 us
    sub x2, other arithmetic, body(): vel_z = vel_z - step_ratio * buoyancy * (next_z - pressure)  8.41 us
    dot_general x2, matrix products, body(): jnp.dot(hits, incoming.reshape(slots, depth), preferred_element_type=jnp....  6.77 us
    sub x2, other arithmetic, body(): rest = forcing - divergence  6.32 us
    all_to_all x1, starting transfers between devices, bubble_source(): lax.all_to_all(out_cols.reshape(devices, capacity), ('gx', 'gy'), split_a...  5.91 us
  transfers between devices with their start and end apart: 12, of which 5 were waited for; matrix products, arithmetic and copies ran while one was open for 31% of the time, Pallas kernels for 0%

profile of v4, /device:TPU:18, one launch (start us, length us, event | category | flops | bytes accessed | tf_op | source)
XLA Modules:
  0.0 168.2 jit_solution(4328693427080933875)
XLA Ops:
  2.1 1.7 %reduce-window.6 = s32[32,6,128]{2,0,1:T(8,128)S(1)} reduce-window(s32[32,6,128]{2,0,1:T(8,128)S(1)} %fusion.25, s32[]{:T(128)} %constant.82.clone.1), window={size=1x1x128 pad=0_0x0_0x127_0}, to_apply=%region_0.0 | reduce-window | flops 3121152 | bytes 196612 | tf_op jit(solution)/shard_map/reduce-window
  5.7 5.9 %all-to-all-start = ((s32[32,1,48]{2,1,0:T(1,128)}), s32[32,1,48]{2,1,0:T(1,128)S(1)}, u32[]{:S(2)}, u32[]{:S(2)}) async-start(s32[32,1,48]{2,1,0:T(1,128)} %sub.123), calls=%async_computation | async-start | bytes 32768 | tf_op jit(solution)/shard_map/all_to_all | solution.py:44
  13.4 1.8 %copy.23 = bf16[96,8,2,512]{3,1,2,0:T(8,128)(2,1)S(1)} copy(bf16[96,8,2,512]{3,2,1,0:T(2,128)(2,1)} %bitcast.45) | data formatting | bytes 3145728
  15.2 4.0 %fusion.5 = bf16[1536,1024]{1,0:T(8,128)(2,1)} fusion(bf16[768,1024]{1,0:T(8,128)(2,1)S(1)} %bitcast.46, s32[768]{0:T(1024)S(1)} %add_add_fusion), kind=kOutput, calls=%fused_computation.8 | convolution fusion | flops 2418671616 | bytes 4721664 | tf_op jit(solution)/shard_map/dot_general | solution.py:38
  20.5 4.8 %reshape.147 = bf16[32,48,2,512]{3,2,1,0:T(2,128)(2,1)S(1)} reshape(bf16[1536,1024]{1,0:T(8,128)(2,1)} %fusion.5) | data formatting | bytes 6291456 | tf_op jit(solution)/shard_map/reshape | solution.py:54
  25.3 5.2 %all-to-all-start.2 = ((bf16[8,32,512]{2,1,0:T(8,128)(2,1)}), bf16[8,32,512]{2,1,0:T(8,128)(2,1)S(1)}, u32[]{:S(2)}, u32[]{:S(2)}) async-start(bf16[8,32,512]{2,1,0:T(8,128)(2,1)} %broadcast_select_fusion), calls=%async_computation.2 | async-start | bytes 524288 | tf_op jit(solution)/shard_map/all_to_all | solution.py:71
  30.5 5.3 %fusion.37 = (bf16[32,48,1,512]{3,2,1,0:T(2,128)(2,1)S(1)}, bf16[32,48,1,512]{3,2,1,0:T(2,128)(2,1)}) fusion(bf16[32,48,2,512]{3,2,1,0:T(2,128)(2,1)S(1)} %reshape.147), kind=kLoop, calls=%fused_computation.83 | loop fusion | bytes 6291456 | tf_op jit(solution)/shard_map/slice | solution.py:105
  35.8 1.7 %copy.27 = bf16[32,48,1,512]{3,1,0,2:T(8,128)(2,1)} copy(bf16[32,48,1,512]{3,2,1,0:T(2,128)(2,1)S(1)} %get-tuple-element.59) | data formatting | bytes 3145728
  37.6 5.9 %all-to-all-start.1 = ((bf16[32,48,512]{2,1,0:T(8,128)(2,1)}), bf16[32,48,512]{2,1,0:T(8,128)(2,1)}, u32[]{:S(2)}, u32[]{:S(2)}) async-start(bf16[32,48,512]{2,1,0:T(8,128)(2,1)} %bitcast.44), calls=%async_computation.1 | async-start | bytes 3145728 | tf_op jit(solution)/shard_map/all_to_all | solution.py:59
  43.6 2.1 %collective-permute-start.2 = (f32[3,32,512]{2,1,0:T(8,128)S(1)}, f32[3,32,512]{2,1,0:T(8,128)S(1)}, u32[]{:S(2)}, u32[]{:S(2)}) collective-permute-start(f32[3,32,512]{2,1,0:T(8,128)S(1)} %pad_maximum_fusion.1), channel_id=1, source_target_pairs={{0,4},{4,8},{8,12},{12,16},{16,20},{20,24},{24,28},{1,5},{5,9},{9,... | collective-permute-start | bytes 589832 | tf_op jit(solution)/shard_map/ppermute | solution.py:14
  48.1 3.4 %collective-permute-start.3 = (f32[32,3,512]{2,1,0:T(4,128)S(1)}, f32[32,3,512]{2,1,0:T(4,128)}, u32[]{:S(2)}, u32[]{:S(2)}) collective-permute-start(f32[32,3,512]{2,1,0:T(4,128)S(1)} %pad_maximum_fusion), channel_id=1, source_target_pairs={{0,1},{1,2},{2,3},{4,5},{5,6},{6,7},{8,9},{9,10},{10,11},{12,13},{... | collective-permute-start | bytes 589832 | tf_op jit(solution)/shard_map/ppermute | solution.py:14
  53.0 1.9 %slice.133 = f32[32,32,511]{2,1,0:T(8,128)} slice(f32[32,32,512]{2,1,0:T(8,128)S(1)} %copy-done.2), slice={[0:32], [0:32], [1:512]} | slice | bytes 4186112 | tf_op jit(solution)/shard_map/slice | solution.py:110
  54.9 1.7 %slice.131 = f32[32,31,512]{2,1,0:T(8,128)} slice(f32[32,32,512]{2,1,0:T(8,128)S(1)} %copy-done.2), slice={[0:32], [1:32], [0:512]} | slice | bytes 4063232 | tf_op jit(solution)/shard_map/slice | solution.py:109
  56.6 3.5 %copy.28 = bf16[32,48,1,512]{3,1,0,2:T(8,128)(2,1)} copy(bf16[32,48,1,512]{3,2,1,0:T(2,128)(2,1)} %get-tuple-element.60) | data formatting | bytes 3145728
  60.2 20.8 %collective-permute-done.2 = f32[3,32,512]{2,1,0:T(8,128)S(1)} collective-permute-done((f32[3,32,512]{2,1,0:T(8,128)S(1)}, f32[3,32,512]{2,1,0:T(8,128)S(1)}, u32[]{:S(2)}, u32[]{:S(2)}) %collective-permute-start.2) | collective-permute-done | bytes 196640 | tf_op jit(solution)/shard_map/ppermute | solution.py:14
  81.0 1.9 %collective-permute-start = (f32[1,32,512]{2,1,0:T(8,128)S(1)}, f32[1,32,512]{2,1,0:T(8,128)S(1)}, u32[]{:S(2)}, u32[]{:S(2)}) collective-permute-start(f32[1,32,512]{2,1,0:T(8,128)S(1)} %get-tuple-element.64), channel_id=1, source_target_pairs={{4,0},{8,4},{12,8},{16,12},{20,16},{24,20},{28,24},{5,1},{9,5},{13... | collective-permute-start | bytes 196616 | tf_op jit(solution)/shard_map/ppermute | solution.py:14
  84.5 2.6 %collective-permute-start.1 = (f32[32,1,512]{2,1,0:T(1,128)S(1)}, f32[32,1,512]{2,1,0:T(1,128)S(1)}, u32[]{:S(2)}, u32[]{:S(2)}) collective-permute-start(f32[32,1,512]{2,1,0:T(1,128)S(1)} %get-tuple-element.63), channel_id=1, source_target_pairs={{1,0},{2,1},{3,2},{5,4},{6,5},{7,6},{9,8},{10,9},{11,10},{13,12},{... | collective-permute-start | bytes 196616 | tf_op jit(solution)/shard_map/ppermute | solution.py:14
  88.4 3.3 %collective-permute-done.1 = f32[32,1,512]{2,1,0:T(1,128)S(1)} collective-permute-done((f32[32,1,512]{2,1,0:T(1,128)S(1)}, f32[32,1,512]{2,1,0:T(1,128)S(1)}, u32[]{:S(2)}, u32[]{:S(2)}) %collective-permute-start.1) | collective-permute-done | bytes 65568 | tf_op jit(solution)/shard_map/ppermute | solution.py:14
  91.8 6.2 %multiply_subtract_fusion.1 = (f32[32,32,512]{2,1,0:T(8,128)S(1)}, f32[32,32,512]{2,1,0:T(8,128)S(1)}, f32[32,32,512]{2,1,0:T(8,128)S(1)}) fusion(f32[32,32,512]{2,1,0:T(8,128)} %param.15, f32[32,32,512]{2,1,0:T(8,128)S(1)} %copy-done.2, f32[32,32,511]{2,1,0:T(8,128)} %slice.133, f32[32,32,512]{2,1,0:T(8,128)} %param.16, f32[32,32,512]{2,1,0:T(8,128)} %param.14, ...), kind=kLoop, calls=%fused_computation.39 | loop fusion | flops 8388608 | bytes 23064576 | tf_op jit(solution)/shard_map/sub | solution.py:113
  100.7 3.2 %pad_subtract_fusion.1 = f32[32,32,512]{2,1,0:T(8,128)} fusion(f32[1,32,512]{2,1,0:T(8,128)S(1)} %bitcast.47, f32[32,32,512]{2,1,0:T(8,128)S(1)} %get-tuple-element.34, f32[31,32,512]{2,1,0:T(8,128)S(1)} %slice.170, f32[1,32,512]{2,1,0:T(8,128)S(1)} %get-tuple-element.51, f32[32,32,512]{2,1,0:T(8,128)S(1)} %get-tuple-element.35, ...), kind=kLoop, calls=%fused_computation.14 | loop fusion | flops 4194304 | bytes 14741504 | tf_op jit(solution)/shard_map/sub | solution.py:122
  103.9 3.4 %fusion.2 = f32[32,32,512]{2,1,0:T(8,128)S(1)} fusion(bf16[1536,512,1]{1,0,2:T(8,128)(2,1)} %bitcast.5, s32[1536]{0:T(1024)S(1)} %eq.78, s32[32,32]{1,0:T(8,128)S(1)} %multiply_add_fusion.2), kind=kOutput, calls=%fused_computation.3 | convolution fusion | flops 1612185600 | bytes 3680256 | tf_op jit(solution)/shard_map/dot_general | solution.py:126
  108.3 4.0 %all-to-all-start.3 = ((bf16[32,48,512]{2,1,0:T(8,128)(2,1)}), bf16[32,48,512]{2,1,0:T(8,128)(2,1)}, u32[]{:S(2)}, u32[]{:S(2)}) async-start(bf16[32,48,512]{2,1,0:T(8,128)(2,1)} %bitcast.43), calls=%async_computation.3 | async-start | bytes 3145728 | tf_op jit(solution)/shard_map/all_to_all | solution.py:59
  112.4 3.4 %collective-permute-start.7 = (f32[32,1,512]{2,1,0:T(1,128)S(1)}, f32[32,1,512]{2,1,0:T(1,128)S(1)}, u32[]{:S(2)}, u32[]{:S(2)}) collective-permute-start(f32[32,1,512]{2,1,0:T(1,128)S(1)} %slice.155), channel_id=1, source_target_pairs={{0,1},{1,2},{2,3},{4,5},{5,6},{6,7},{8,9},{9,10},{10,11},{12,13},{... | collective-permute-start | bytes 196616 | tf_op jit(solution)/shard_map/ppermute | solution.py:14
  115.8 1.9 %collective-permute-start.6 = (f32[1,32,512]{2,1,0:T(8,128)S(1)}, f32[1,32,512]{2,1,0:T(8,128)S(1)}, u32[]{:S(2)}, u32[]{:S(2)}) collective-permute-start(f32[1,32,512]{2,1,0:T(8,128)S(1)} %slice.154), channel_id=1, source_target_pairs={{0,4},{4,8},{8,12},{12,16},{16,20},{20,24},{24,28},{1,5},{5,9},{9,... | collective-permute-start | bytes 196616 | tf_op jit(solution)/shard_map/ppermute | solution.py:14
  117.8 6.9 %collective-permute-done.7 = f32[32,1,512]{2,1,0:T(1,128)S(1)} collective-permute-done((f32[32,1,512]{2,1,0:T(1,128)S(1)}, f32[32,1,512]{2,1,0:T(1,128)S(1)}, u32[]{:S(2)}, u32[]{:S(2)}) %collective-permute-start.7) | collective-permute-done | bytes 65568 | tf_op jit(solution)/shard_map/ppermute | solution.py:14
  124.8 1.9 %collective-permute-start.5 = (f32[32,1,512]{2,1,0:T(1,128)S(1)}, f32[32,1,512]{2,1,0:T(1,128)S(1)}, u32[]{:S(2)}, u32[]{:S(2)}) collective-permute-start(f32[32,1,512]{2,1,0:T(1,128)S(1)} %get-tuple-element.61), channel_id=1, source_target_pairs={{1,0},{2,1},{3,2},{5,4},{6,5},{7,6},{9,8},{10,9},{11,10},{13,12},{... | collective-permute-start | bytes 196616 | tf_op jit(solution)/shard_map/ppermute | solution.py:14
  126.7 21.7 %collective-permute-done.6 = f32[1,32,512]{2,1,0:T(8,128)S(1)} collective-permute-done((f32[1,32,512]{2,1,0:T(8,128)S(1)}, f32[1,32,512]{2,1,0:T(8,128)S(1)}, u32[]{:S(2)}, u32[]{:S(2)}) %collective-permute-start.6) | collective-permute-done | bytes 65568 | tf_op jit(solution)/shard_map/ppermute | solution.py:14
  148.4 2.1 %collective-permute-start.4 = (f32[1,32,512]{2,1,0:T(8,128)S(1)}, f32[1,32,512]{2,1,0:T(8,128)S(1)}, u32[]{:S(2)}, u32[]{:S(2)}) collective-permute-start(f32[1,32,512]{2,1,0:T(8,128)S(1)} %get-tuple-element.62), channel_id=1, source_target_pairs={{4,0},{8,4},{12,8},{16,12},{20,16},{24,20},{28,24},{5,1},{9,5},{13... | collective-permute-start | bytes 196616 | tf_op jit(solution)/shard_map/ppermute | solution.py:14
  154.4 2.2 %multiply_subtract_fusion = (f32[32,32,512]{2,1,0:T(8,128)S(1)}, f32[32,32,512]{2,1,0:T(8,128)S(1)}, f32[32,32,512]{2,1,0:T(8,128)S(1)}) fusion(f32[32,32,512]{2,1,0:T(8,128)S(1)} %copy-done.8, f32[32,32,512]{2,1,0:T(8,128)S(1)} %multiply_add_fusion.1, f32[32,32,511]{2,1,0:T(8,128)S(1)} %slice.153, f32[32,32,512]{2,1,0:T(8,128)S(1)} %copy-done.5, ...), kind=kLoop, calls=%fused_computation.37 | loop fusion | flops 8388608 | bytes 23064576 | tf_op jit(solution)/shard_map/sub | solution.py:113
  159.3 3.2 %pad_subtract_fusion = f32[32,32,512]{2,1,0:T(8,128)} fusion(f32[1,32,512]{2,1,0:T(8,128)S(1)} %bitcast.48, f32[32,32,512]{2,1,0:T(8,128)S(1)} %get-tuple-element.27, f32[31,32,512]{2,1,0:T(8,128)S(1)} %slice.173, f32[1,32,512]{2,1,0:T(8,128)S(1)} %get-tuple-element.46, f32[32,32,512]{2,1,0:T(8,128)S(1)} %get-tuple-element.28, ...), kind=kLoop, calls=%fused_computation.13 | loop fusion | flops 4194304 | bytes 14741504 | tf_op jit(solution)/shard_map/sub | solution.py:122
  162.4 3.4 %fusion = f32[32,32,512]{2,1,0:T(8,128)S(1)} fusion(bf16[1536,512,1]{1,0,2:T(8,128)(2,1)} %bitcast.7, s32[1536]{0:T(1024)S(1)} %eq.78, s32[32,32]{1,0:T(8,128)S(1)} %multiply_add_fusion.2), kind=kOutput, calls=%fused_computation.1 | convolution fusion | flops 1612185600 | bytes 3680256 | tf_op jit(solution)/shard_map/dot_general | solution.py:126
  165.9 2.4 %multiply_add_fusion = f32[32,32,512]{2,1,0:T(8,128)} fusion(f32[32,32,512]{2,1,0:T(8,128)S(1)} %multiply_add_fusion.1, f32[32,32,512]{2,1,0:T(8,128)S(1)} %fusion, f32[32,32,512]{2,1,0:T(8,128)S(1)} %copy-done.16, f32[32,32,512]{2,1,0:T(8,128)S(1)} %copy-done.6), kind=kLoop, calls=%fused_computation.36 | loop fusion | flops 4194304 | bytes 10485760 | tf_op jit(solution)/shard_map/add | solution.py:128
  (89 shorter events, 23.6 us)
Async XLA Ops:
  0.6 18.5 %copy-start = (bf16[16,32,512]{2,1,0:T(8,128)(2,1)S(1)}, bf16[16,32,512]{2,1,0:T(8,128)(2,1)}, u32[]{:S(2)}) copy-start(bf16[16,32,512]{2,1,0:T(8,128)(2,1)} %param.20) | copy-start | bytes 1572868
  5.7 19.6 %all-to-all-start = ((s32[32,1,48]{2,1,0:T(1,128)}), s32[32,1,48]{2,1,0:T(1,128)S(1)}, u32[]{:S(2)}, u32[]{:S(2)}) async-start(s32[32,1,48]{2,1,0:T(1,128)} %sub.123), calls=%async_computation | async-start | bytes 32768 | tf_op jit(solution)/shard_map/all_to_all | solution.py:44
  25.3 12.2 %all-to-all-start.2 = ((bf16[8,32,512]{2,1,0:T(8,128)(2,1)}), bf16[8,32,512]{2,1,0:T(8,128)(2,1)S(1)}, u32[]{:S(2)}, u32[]{:S(2)}) async-start(bf16[8,32,512]{2,1,0:T(8,128)(2,1)} %broadcast_select_fusion), calls=%async_computation.2 | async-start | bytes 524288 | tf_op jit(solution)/shard_map/all_to_all | solution.py:71
  37.5 6.0 %slice-start = ((f32[32,32,512]{2,1,0:T(8,128)}), f32[1,32,512]{2,1,0:T(8,128)S(1)}, s32[]{:S(2)}) async-start(f32[32,32,512]{2,1,0:T(8,128)} %param.12), calls=%async_computation.4 | async-start | bytes 131072 | tf_op jit(solution)/shard_map/slice | solution.py:89
  37.5 6.0 %slice-start.1 = ((f32[32,32,512]{2,1,0:T(8,128)}), f32[1,32,512]{2,1,0:T(8,128)S(1)}, s32[]{:S(2)}) async-start(f32[32,32,512]{2,1,0:T(8,128)} %param.16), calls=%async_computation.5 | async-start | bytes 131072 | tf_op jit(solution)/shard_map/slice | solution.py:89
  37.6 6.0 %slice-start.2 = ((f32[32,32,512]{2,1,0:T(8,128)}), f32[1,32,512]{2,1,0:T(8,128)S(1)}, s32[]{:S(2)}) async-start(f32[32,32,512]{2,1,0:T(8,128)} %param.13), calls=%async_computation.6 | async-start | bytes 131072 | tf_op jit(solution)/shard_map/slice | solution.py:89
  37.6 9.2 %copy-start.2 = (f32[32,32,512]{2,1,0:T(8,128)S(1)}, f32[32,32,512]{2,1,0:T(8,128)}, u32[]{:S(2)}) copy-start(f32[32,32,512]{2,1,0:T(8,128)} %param.12) | copy-start | bytes 6291460
  37.6 66.3 %all-to-all-start.1 = ((bf16[32,48,512]{2,1,0:T(8,128)(2,1)}), bf16[32,48,512]{2,1,0:T(8,128)(2,1)}, u32[]{:S(2)}, u32[]{:S(2)}) async-start(bf16[32,48,512]{2,1,0:T(8,128)(2,1)} %bitcast.44), calls=%async_computation.1 | async-start | bytes 3145728 | tf_op jit(solution)/shard_map/all_to_all | solution.py:59
  43.6 37.4 %collective-permute-start.2 = (f32[3,32,512]{2,1,0:T(8,128)S(1)}, f32[3,32,512]{2,1,0:T(8,128)S(1)}, u32[]{:S(2)}, u32[]{:S(2)}) collective-permute-start(f32[3,32,512]{2,1,0:T(8,128)S(1)} %pad_maximum_fusion.1), channel_id=1, source_target_pairs={{0,4},{4,8},{8,12},{12,16},{16,20},{20,24},{24,28},{1,5},{5,9},{9,... | collective-permute-start | bytes 589832 | tf_op jit(solution)/shard_map/ppermute | solution.py:14
  48.1 34.8 %collective-permute-start.3 = (f32[32,3,512]{2,1,0:T(4,128)S(1)}, f32[32,3,512]{2,1,0:T(4,128)}, u32[]{:S(2)}, u32[]{:S(2)}) collective-permute-start(f32[32,3,512]{2,1,0:T(4,128)S(1)} %pad_maximum_fusion), channel_id=1, source_target_pairs={{0,1},{1,2},{2,3},{4,5},{5,6},{6,7},{8,9},{9,10},{10,11},{12,13},{... | collective-permute-start | bytes 589832 | tf_op jit(solution)/shard_map/ppermute | solution.py:14
  81.0 7.4 %collective-permute-start = (f32[1,32,512]{2,1,0:T(8,128)S(1)}, f32[1,32,512]{2,1,0:T(8,128)S(1)}, u32[]{:S(2)}, u32[]{:S(2)}) collective-permute-start(f32[1,32,512]{2,1,0:T(8,128)S(1)} %get-tuple-element.64), channel_id=1, source_target_pairs={{4,0},{8,4},{12,8},{16,12},{20,16},{24,20},{28,24},{5,1},{9,5},{13... | collective-permute-start | bytes 196616 | tf_op jit(solution)/shard_map/ppermute | solution.py:14
  84.5 7.3 %collective-permute-start.1 = (f32[32,1,512]{2,1,0:T(1,128)S(1)}, f32[32,1,512]{2,1,0:T(1,128)S(1)}, u32[]{:S(2)}, u32[]{:S(2)}) collective-permute-start(f32[32,1,512]{2,1,0:T(1,128)S(1)} %get-tuple-element.63), channel_id=1, source_target_pairs={{1,0},{2,1},{3,2},{5,4},{6,5},{7,6},{9,8},{10,9},{11,10},{13,12},{... | collective-permute-start | bytes 196616 | tf_op jit(solution)/shard_map/ppermute | solution.py:14
  98.0 1.3 copy-start.7
  98.0 2.0 %copy-start.9 = (f32[32,32,512]{2,1,0:T(8,128)}, f32[32,32,512]{2,1,0:T(8,128)S(1)}, u32[]{:S(2)}) copy-start(f32[32,32,512]{2,1,0:T(8,128)S(1)} %get-tuple-element.35) | copy-start | bytes 6291460
  98.0 2.7 %copy-start.11 = (f32[32,32,512]{2,1,0:T(8,128)}, f32[32,32,512]{2,1,0:T(8,128)S(1)}, u32[]{:S(2)}) copy-start(f32[32,32,512]{2,1,0:T(8,128)S(1)} %get-tuple-element.34) | copy-start | bytes 6291460
  103.9 3.4 %copy-start.3 = (f32[32,32,512]{2,1,0:T(8,128)S(1)}, f32[32,32,512]{2,1,0:T(8,128)}, u32[]{:S(2)}) copy-start(f32[32,32,512]{2,1,0:T(8,128)} %param.12) | copy-start | bytes 6291460
  103.9 3.4 %copy-start.4 = (f32[32,32,512]{2,1,0:T(8,128)S(1)}, f32[32,32,512]{2,1,0:T(8,128)}, u32[]{:S(2)}) copy-start(f32[32,32,512]{2,1,0:T(8,128)} %param.16) | copy-start | bytes 6291460
  103.9 3.4 %copy-start.17 = (f32[32,32,512]{2,1,0:T(8,128)S(1)}, f32[32,32,512]{2,1,0:T(8,128)}, u32[]{:S(2)}) copy-start(f32[32,32,512]{2,1,0:T(8,128)} %pad_subtract_fusion.1) | copy-start | bytes 6291460
  108.3 54.1 %all-to-all-start.3 = ((bf16[32,48,512]{2,1,0:T(8,128)(2,1)}), bf16[32,48,512]{2,1,0:T(8,128)(2,1)}, u32[]{:S(2)}, u32[]{:S(2)}) async-start(bf16[32,48,512]{2,1,0:T(8,128)(2,1)} %bitcast.43), calls=%async_computation.3 | async-start | bytes 3145728 | tf_op jit(solution)/shard_map/all_to_all | solution.py:59
  112.4 12.2 %collective-permute-start.7 = (f32[32,1,512]{2,1,0:T(1,128)S(1)}, f32[32,1,512]{2,1,0:T(1,128)S(1)}, u32[]{:S(2)}, u32[]{:S(2)}) collective-permute-start(f32[32,1,512]{2,1,0:T(1,128)S(1)} %slice.155), channel_id=1, source_target_pairs={{0,1},{1,2},{2,3},{4,5},{5,6},{6,7},{8,9},{9,10},{10,11},{12,13},{... | collective-permute-start | bytes 196616 | tf_op jit(solution)/shard_map/ppermute | solution.py:14
  115.8 32.6 %collective-permute-start.6 = (f32[1,32,512]{2,1,0:T(8,128)S(1)}, f32[1,32,512]{2,1,0:T(8,128)S(1)}, u32[]{:S(2)}, u32[]{:S(2)}) collective-permute-start(f32[1,32,512]{2,1,0:T(8,128)S(1)} %slice.154), channel_id=1, source_target_pairs={{0,4},{4,8},{8,12},{12,16},{16,20},{20,24},{24,28},{1,5},{5,9},{9,... | collective-permute-start | bytes 196616 | tf_op jit(solution)/shard_map/ppermute | solution.py:14
  124.8 27.0 %collective-permute-start.5 = (f32[32,1,512]{2,1,0:T(1,128)S(1)}, f32[32,1,512]{2,1,0:T(1,128)S(1)}, u32[]{:S(2)}, u32[]{:S(2)}) collective-permute-start(f32[32,1,512]{2,1,0:T(1,128)S(1)} %get-tuple-element.61), channel_id=1, source_target_pairs={{1,0},{2,1},{3,2},{5,4},{6,5},{7,6},{9,8},{10,9},{11,10},{13,12},{... | collective-permute-start | bytes 196616 | tf_op jit(solution)/shard_map/ppermute | solution.py:14
  148.4 3.8 %collective-permute-start.4 = (f32[1,32,512]{2,1,0:T(8,128)S(1)}, f32[1,32,512]{2,1,0:T(8,128)S(1)}, u32[]{:S(2)}, u32[]{:S(2)}) collective-permute-start(f32[1,32,512]{2,1,0:T(8,128)S(1)} %get-tuple-element.62), channel_id=1, source_target_pairs={{4,0},{8,4},{12,8},{16,12},{20,16},{24,20},{28,24},{5,1},{9,5},{13... | collective-permute-start | bytes 196616 | tf_op jit(solution)/shard_map/ppermute | solution.py:14
  150.7 1.6 copy-start.10
  150.8 2.2 %copy-start.12 = (f32[32,32,512]{2,1,0:T(8,128)S(1)}, f32[32,32,512]{2,1,0:T(8,128)}, u32[]{:S(2)}) copy-start(f32[32,32,512]{2,1,0:T(8,128)} %copy-done.11) | copy-start | bytes 6291460
  151.4 2.4 %copy-start.5 = (f32[32,32,512]{2,1,0:T(8,128)S(1)}, f32[32,32,512]{2,1,0:T(8,128)}, u32[]{:S(2)}) copy-start(f32[32,32,512]{2,1,0:T(8,128)} %param.16) | copy-start | bytes 6291460
  151.4 3.0 %copy-start.8 = (f32[32,32,512]{2,1,0:T(8,128)S(1)}, f32[32,32,512]{2,1,0:T(8,128)}, u32[]{:S(2)}) copy-start(f32[32,32,512]{2,1,0:T(8,128)} %copy-done.7) | copy-start | bytes 6291460
  156.6 2.0 %copy-start.14 = (f32[32,32,512]{2,1,0:T(8,128)}, f32[32,32,512]{2,1,0:T(8,128)S(1)}, u32[]{:S(2)}) copy-start(f32[32,32,512]{2,1,0:T(8,128)S(1)} %get-tuple-element.28) | copy-start | bytes 6291460
  156.6 2.7 %copy-start.15 = (f32[32,32,512]{2,1,0:T(8,128)}, f32[32,32,512]{2,1,0:T(8,128)S(1)}, u32[]{:S(2)}) copy-start(f32[32,32,512]{2,1,0:T(8,128)S(1)} %get-tuple-element.27) | copy-start | bytes 6291460
  162.4 3.4 %copy-start.6 = (f32[32,32,512]{2,1,0:T(8,128)S(1)}, f32[32,32,512]{2,1,0:T(8,128)}, u32[]{:S(2)}) copy-start(f32[32,32,512]{2,1,0:T(8,128)} %param.16) | copy-start | bytes 6291460
  162.4 3.4 %copy-start.16 = (f32[32,32,512]{2,1,0:T(8,128)S(1)}, f32[32,32,512]{2,1,0:T(8,128)}, u32[]{:S(2)}) copy-start(f32[32,32,512]{2,1,0:T(8,128)} %pad_subtract_fusion) | copy-start | bytes 6291460
  165.9 2.4 %copy-start.1 = (bf16[16,32,512]{2,1,0:T(8,128)(2,1)S(1)}, bf16[16,32,512]{2,1,0:T(8,128)(2,1)}, u32[]{:S(2)}) copy-start(bf16[16,32,512]{2,1,0:T(8,128)(2,1)} %param.20) | copy-start | bytes 1572868
  (1 other events, 1.3 us)

commit v5 on v3

--- a/solution.py
+++ b/solution.py
@@ -48,7 +48,6 @@
         concat_axis=0,
         tiled=True,
     )
-    in_cols, outgoing, ready = lax.optimization_barrier((in_cols, outgoing, ready))
     incoming = lax.all_to_all(
         outgoing.reshape(devices, capacity, steps * depth),
         ("gx", "gy"),
@@ -65,17 +64,21 @@
     return source, ready
 
 
-def incident_plane(history, delays, size_y, depth):
+def incident_plane(history, delays):
     tiles_x = lax.axis_size("gx")
     my_tile = lax.axis_index("gx")
-    cycle = jnp.arange(tiles_x, dtype=jnp.int32)
-    dist = jnp.abs(cycle - my_tile)
-    dist = jnp.minimum(dist, tiles_x - dist)
+    shifts = jnp.arange(tiles_x, dtype=jnp.int32)
+    dist = jnp.minimum(shifts, tiles_x - shifts)
     weight = 1.0 / (1.0 + 2.0 * dist.astype(jnp.float32) / tiles_x)
-    wanted = lax.dynamic_index_in_dim(delays, my_tile, 1, keepdims=False)
+    readers = (my_tile + shifts) % tiles_x
+    wanted = jnp.take(lax.dynamic_index_in_dim(delays, my_tile, 1, keepdims=False), readers)
     chosen = jnp.take(history, wanted, axis=0)
-    rows = lax.all_to_all(chosen, "gx", split_axis=0, concat_axis=0, tiled=True)
-    return jnp.sum(weight[:, None, None] * rows.astype(jnp.float32), axis=0)
+    total = weight[0] * chosen[0].astype(jnp.float32)
+    for shift in range(1, tiles_x):
+        route = [(j, (j + shift) % tiles_x) for j in range(tiles_x)]
+        got = lax.ppermute(chosen[shift], "gx", route)
+        total = total + weight[shift] * got.astype(jnp.float32)
+    return total
 
 
 def body(
@@ -101,7 +104,7 @@
     ready = (above_x, above_y, below_x, below_y)
     source, ready = bubble_source(waves, bubble_dest, bubble_column, size_x * size_y, ready)
     above_x, above_y, below_x, below_y = ready
-    incident = incident_plane(history, delays, size_y, depth)
+    incident = incident_plane(history, delays)
     source = source.reshape(size_x, size_y, steps, depth)
     p_bx, vx_bx, void_bx = below_x[0:1], below_x[1:2], below_x[2:3]
     p_by, vy_by, void_by = below_y[:, 0:1], below_y[:, 1:2], below_y[:, 2:3]

time: 162 us -> 168 us (1.037)
  waiting for transfers between devices: 58.2 us -> 64.3 us
  other arithmetic: 24.5 us -> 29.2 us
  local copies, waits for them, and re-layouts: 26.2 us -> 23 us
    ppermute x8, waiting for transfers between devices: 4.22 us -> 63.2 us  [from_behind(): return lax.ppermute(block, axis, route)]
    all_to_all x1, waiting for transfers between devices: 52.9 us -> 0.01 us  [bubble_source(): lax.all_to_all(outgoing.reshape(devices, capacity, steps * depth), ('gx',...]
    ppermute x0 -> x7, starting transfers between devices: none -> 5.85 us  [incident_plane(): got = lax.ppermute(chosen[shift], 'gx', route)]
    add x1 -> x2, other arithmetic: 0.02 us -> 5.78 us  [body(): source[:, :, step, :] + forcing - divergence]
    all_to_all x1 -> x0, starting transfers between devices: 5.16 us -> none  [incident_plane(): rows = lax.all_to_all(chosen, 'gx', split_axis=0, concat_axis=0, tiled=True)]
    ppermute x8, starting transfers between devices: 22.2 us -> 20 us  [from_behind(): return lax.ppermute(block, axis, route)]
    unnamed x33 -> x27, local copies, waits for them, and re-layouts: 4.98 us -> 3.2 us
  transfers between devices with their start and end apart: 11 -> 17, of which waited for: 3 -> 6; matrix products, arithmetic and copies ran while one was open for 21% -> 24% of each run, Pallas kernels for 0% -> 0%
where the time goes in v5:
time: 168 us; the launch traced here: 165 us
  waiting for transfers between devices  64.3 us (38%)
  starting transfers between devices  37.6 us (22%)
  other arithmetic  29.2 us (17%)
  local copies, waits for them, and re-layouts  23 us (14%)
  matrix products  9.49 us (6%)
    ppermute x8, waiting for transfers between devices, from_behind(): return lax.ppermute(block, axis, route)  63.2 us
    ppermute x8, starting transfers between devices, from_behind(): return lax.ppermute(block, axis, route)  20 us
    sub x2, other arithmetic, body(): vel_z = vel_z - step_ratio * buoyancy * (next_z - pressure)  10.5 us
    add x2, other arithmetic, body(): pressure + step_ratio * stiffness * (source[:, :, step, :] + forcing - di...  6.21 us
    all_to_all x1, starting transfers between devices, bubble_source(): lax.all_to_all(out_cols.reshape(devices, capacity), ('gx', 'gy'), split_a...  5.91 us
    all_to_all x1, starting transfers between devices, bubble_source(): lax.all_to_all(outgoing.reshape(devices, capacity, steps * depth), ('gx',...  5.88 us
    ppermute x7, starting transfers between devices, incident_plane(): got = lax.ppermute(chosen[shift], 'gx', route)  5.85 us
    add x2, other arithmetic, body(): source[:, :, step, :] + forcing - divergence  5.78 us
  transfers between devices with their start and end apart: 17, of which 6 were waited for; matrix products, arithmetic and copies ran while one was open for 24% of the time, Pallas kernels for 0%

profile of v5, /device:TPU:18, one launch (start us, length us, event | category | flops | bytes accessed | tf_op | source)
XLA Modules:
  0.0 164.9 jit_solution(6474892283701991614)
XLA Ops:
  2.1 1.7 %reduce-window.6 = s32[32,6,128]{2,0,1:T(8,128)S(1)} reduce-window(s32[32,6,128]{2,0,1:T(8,128)S(1)} %fusion.28, s32[]{:T(128)} %constant.113.clone.1), window={size=1x1x128 pad=0_0x0_0x127_0}, to_apply=%region_0.0 | reduce-window | flops 3121152 | bytes 196612 | tf_op jit(solution)/shard_map/reduce-window
  5.7 5.9 %all-to-all-start = ((s32[32,1,48]{2,1,0:T(1,128)}), s32[32,1,48]{2,1,0:T(1,128)S(1)}, u32[]{:S(2)}, u32[]{:S(2)}) async-start(s32[32,1,48]{2,1,0:T(1,128)} %sub.109), calls=%async_computation | async-start | bytes 32768 | tf_op jit(solution)/shard_map/all_to_all | solution.py:44
  11.6 1.8 %copy.25 = bf16[96,8,2,512]{3,1,2,0:T(8,128)(2,1)S(1)} copy(bf16[96,8,2,512]{3,2,1,0:T(2,128)(2,1)} %bitcast.118) | data formatting | bytes 3145728
  13.4 4.0 %fusion.4 = bf16[1536,1024]{1,0:T(8,128)(2,1)} fusion(bf16[768,1024]{1,0:T(8,128)(2,1)S(1)} %bitcast.119, s32[768]{0:T(1024)S(1)} %add_add_fusion), kind=kOutput, calls=%fused_computation.8 | convolution fusion | flops 2418671616 | bytes 4721664 | tf_op jit(solution)/shard_map/dot_general | solution.py:38
  17.5 5.9 %all-to-all-start.1 = ((bf16[32,48,1024]{2,1,0:T(8,128)(2,1)}), bf16[32,48,1024]{2,1,0:T(8,128)(2,1)}, u32[]{:S(2)}, u32[]{:S(2)}) async-start(bf16[32,48,1024]{2,1,0:T(8,128)(2,1)} %bitcast.116), calls=%async_computation.1 | async-start | bytes 6291456 | tf_op jit(solution)/shard_map/all_to_all | solution.py:51
  23.4 2.2 %collective-permute-start.8 = (f32[3,32,512]{2,1,0:T(8,128)S(1)}, f32[3,32,512]{2,1,0:T(8,128)S(1)}, u32[]{:S(2)}, u32[]{:S(2)}) collective-permute-start(f32[3,32,512]{2,1,0:T(8,128)S(1)} %pad_maximum_fusion.1), channel_id=1, source_target_pairs={{0,4},{4,8},{8,12},{12,16},{16,20},{20,24},{24,28},{1,5},{5,9},{9,... | collective-permute-start | bytes 589832 | tf_op jit(solution)/shard_map/ppermute | solution.py:14
  27.9 1.5 collective-permute-start
  31.4 1.1 slice.208
  32.7 3.4 %collective-permute-start.10 = (f32[32,3,512]{2,1,0:T(4,128)S(1)}, f32[32,3,512]{2,1,0:T(4,128)}, u32[]{:S(2)}, u32[]{:S(2)}) collective-permute-start(f32[32,3,512]{2,1,0:T(4,128)S(1)} %pad_maximum_fusion), channel_id=1, source_target_pairs={{0,1},{1,2},{2,3},{4,5},{5,6},{6,7},{8,9},{9,10},{10,11},{12,13},{... | collective-permute-start | bytes 589832 | tf_op jit(solution)/shard_map/ppermute | solution.py:14
  36.1 1.5 slice.196
  37.6 1.9 %slice.214 = f32[32,32,511]{2,1,0:T(8,128)} slice(f32[32,32,512]{2,1,0:T(8,128)S(1)} %copy-done.2), slice={[0:32], [0:32], [1:512]} | slice | bytes 4186112 | tf_op jit(solution)/shard_map/slice | solution.py:119
  39.5 1.6 slice.205
  41.2 56.3 %collective-permute-done.8 = f32[3,32,512]{2,1,0:T(8,128)S(1)} collective-permute-done((f32[3,32,512]{2,1,0:T(8,128)S(1)}, f32[3,32,512]{2,1,0:T(8,128)S(1)}, u32[]{:S(2)}, u32[]{:S(2)}) %collective-permute-start.8) | collective-permute-done | bytes 196640 | tf_op jit(solution)/shard_map/ppermute | solution.py:14
  97.5 1.9 %collective-permute-start.7 = (f32[1,32,512]{2,1,0:T(8,128)S(1)}, f32[1,32,512]{2,1,0:T(8,128)S(1)}, u32[]{:S(2)}, u32[]{:S(2)}) collective-permute-start(f32[1,32,512]{2,1,0:T(8,128)S(1)} %get-tuple-element.36), channel_id=1, source_target_pairs={{4,0},{8,4},{12,8},{16,12},{20,16},{24,20},{28,24},{5,1},{9,5},{13... | collective-permute-start | bytes 196616 | tf_op jit(solution)/shard_map/ppermute | solution.py:14
  99.5 1.4 broadcast_select_fusion.2
  100.9 1.9 %collective-permute-start.9 = (f32[32,1,512]{2,1,0:T(1,128)S(1)}, f32[32,1,512]{2,1,0:T(1,128)S(1)}, u32[]{:S(2)}, u32[]{:S(2)}) collective-permute-start(f32[32,1,512]{2,1,0:T(1,128)S(1)} %get-tuple-element.35), channel_id=1, source_target_pairs={{1,0},{2,1},{3,2},{5,4},{6,5},{7,6},{9,8},{10,9},{11,10},{13,12},{... | collective-permute-start | bytes 196616 | tf_op jit(solution)/shard_map/ppermute | solution.py:14
  104.9 3.3 %collective-permute-done.9 = f32[32,1,512]{2,1,0:T(1,128)S(1)} collective-permute-done((f32[32,1,512]{2,1,0:T(1,128)S(1)}, f32[32,1,512]{2,1,0:T(1,128)S(1)}, u32[]{:S(2)}, u32[]{:S(2)}) %collective-permute-start.9) | collective-permute-done | bytes 65568 | tf_op jit(solution)/shard_map/ppermute | solution.py:14
  108.2 7.7 %multiply_subtract_fusion.1 = (f32[32,32,512]{2,1,0:T(8,128)}, f32[32,32,512]{2,1,0:T(8,128)}, f32[32,32,512]{2,1,0:T(8,128)S(1)}) fusion(f32[32,32,512]{2,1,0:T(8,128)} %param.15, f32[32,32,512]{2,1,0:T(8,128)S(1)} %copy-done.2, f32[32,32,511]{2,1,0:T(8,128)} %slice.214, f32[32,32,512]{2,1,0:T(8,128)} %param.16, f32[32,32,512]{2,1,0:T(8,128)} %param.14, ...), kind=kLoop, calls=%fused_computation.41 | loop fusion | flops 8388608 | bytes 23064576 | tf_op jit(solution)/shard_map/sub | solution.py:122
  115.9 1.3 copy-done.6
  117.2 1.5 slice.244
  118.6 4.6 %copy.20 = bf16[1536,1024]{0,1:T(8,128)(2,1)} copy(bf16[1536,1024]{1,0:T(8,128)(2,1)} %bitcast.4) | data formatting | bytes 6291456 | tf_op jit(solution)/shard_map/reshape | solution.py:62
  123.3 5.5 %fusion = f32[32,32,2,512]{3,1,2,0:T(8,128)S(1)} fusion(bf16[2,512,1536,1]{2,1,0,3:T(8,128)(2,1)} %bitcast.117, s32[1536]{0:T(1024)S(1)} %eq.78, s32[32,32]{1,0:T(8,128)S(1)} %multiply_add_fusion), kind=kOutput, calls=%fused_computation.2 | convolution fusion | flops 3222798336 | bytes 7350272 | tf_op jit(solution)/shard_map/dot_general | solution.py:61
  128.9 3.4 %collective-permute-start.1 = (bf16[32,512]{1,0:T(8,128)(2,1)S(1)}, bf16[32,512]{1,0:T(8,128)(2,1)S(1)}, u32[]{:S(2)}, u32[]{:S(2)}) collective-permute-start(bf16[32,512]{1,0:T(8,128)(2,1)S(1)} %get-tuple-element.43), channel_id=1, source_target_pairs={{0,8},{4,12},{8,16},{12,20},{16,24},{20,28},{24,0},{28,4},{1,9},{5... | collective-permute-start | bytes 98312 | tf_op jit(solution)/shard_map/ppermute | solution.py:79
  133.9 5.8 %fusion.31 = (f32[32,32,512]{2,1,0:T(8,128)S(1)}, f32[32,512]{1,0:T(8,128)S(1)}) fusion(f32[32,32,512]{2,1,0:T(8,128)S(1)} %get-tuple-element.29, f32[32,32,2,512]{3,1,2,0:T(8,128)S(1)} %fusion, bf16[32,512]{1,0:T(8,128)(2,1)S(1)} %collective-permute-done.6, f32[]{:T(128)} %bitcast.27, bf16[32,512]{1,0:T(8,128)(2,1)S(1)} %collective-permute-done.5, ...), kind=kLoop, calls=%fused_computation.60 | loop fusion | flops 393216 | bytes 458784 | tf_op jit(solution)/shard_map/add | solution.py:132
  139.7 2.6 %fusion.14 = f32[32,32,512]{2,1,0:T(8,128)S(1)} fusion(f32[32,32,512]{2,1,0:T(8,128)S(1)} %copy-done.2, f32[32,32,512]{2,1,0:T(8,128)S(1)} %fusion.38, f32[32,32,512]{2,1,0:T(8,128)S(1)} %copy-done.7, f32[31,32,512]{2,1,0:T(8,128)S(1)} %copy-done.11, f32[1,32,512]{2,1,0:T(8,128)S(1)} %get-tuple-element.21, f32[32,32,512]{2,1,0:T(8,128)S(1)} %copy-done.5, ...), kind=kLoop, calls=%fused_computation.22 | loop fusion | flops 7864320 | bytes 20967424 | tf_op jit(solution)/shard_map/add | solution.py:131
  142.3 2.0 %collective-permute-start.12 = (f32[1,32,512]{2,1,0:T(8,128)S(1)}, f32[1,32,512]{2,1,0:T(8,128)S(1)}, u32[]{:S(2)}, u32[]{:S(2)}) collective-permute-start(f32[1,32,512]{2,1,0:T(8,128)S(1)} %slice.253), channel_id=1, source_target_pairs={{0,4},{4,8},{8,12},{12,16},{16,20},{20,24},{24,28},{1,5},{5,9},{9,... | collective-permute-start | bytes 196616 | tf_op jit(solution)/shard_map/ppermute | solution.py:14
  144.3 3.0 %collective-permute-start.14 = (f32[32,1,512]{2,1,0:T(1,128)S(1)}, f32[32,1,512]{2,1,0:T(1,128)S(1)}, u32[]{:S(2)}, u32[]{:S(2)}) collective-permute-start(f32[32,1,512]{2,1,0:T(1,128)S(1)} %slice.257), channel_id=1, source_target_pairs={{0,1},{1,2},{2,3},{4,5},{5,6},{6,7},{8,9},{9,10},{10,11},{12,13},{... | collective-permute-start | bytes 196616 | tf_op jit(solution)/shard_map/ppermute | solution.py:14
  147.9 2.8 %collective-permute-start.11 = (f32[1,32,512]{2,1,0:T(8,128)S(1)}, f32[1,32,512]{2,1,0:T(8,128)S(1)}, u32[]{:S(2)}, u32[]{:S(2)}) collective-permute-start(f32[1,32,512]{2,1,0:T(8,128)S(1)} %get-tuple-element.34), channel_id=1, source_target_pairs={{4,0},{8,4},{12,8},{16,12},{20,16},{24,20},{28,24},{5,1},{9,5},{13... | collective-permute-start | bytes 196616 | tf_op jit(solution)/shard_map/ppermute | solution.py:14
  150.9 2.8 %collective-permute-start.13 = (f32[32,1,512]{2,1,0:T(1,128)S(1)}, f32[32,1,512]{2,1,0:T(1,128)S(1)}, u32[]{:S(2)}, u32[]{:S(2)}) collective-permute-start(f32[32,1,512]{2,1,0:T(1,128)S(1)} %get-tuple-element.32), channel_id=1, source_target_pairs={{1,0},{2,1},{3,2},{5,4},{6,5},{7,6},{9,8},{10,9},{11,10},{13,12},{... | collective-permute-start | bytes 196616 | tf_op jit(solution)/shard_map/ppermute | solution.py:14
  155.0 3.0 %collective-permute-done.13 = f32[32,1,512]{2,1,0:T(1,128)S(1)} collective-permute-done((f32[32,1,512]{2,1,0:T(1,128)S(1)}, f32[32,1,512]{2,1,0:T(1,128)S(1)}, u32[]{:S(2)}, u32[]{:S(2)}) %collective-permute-start.13) | collective-permute-done | bytes 65568 | tf_op jit(solution)/shard_map/ppermute | solution.py:14
  158.0 2.8 %multiply_subtract_fusion = (f32[32,32,512]{2,1,0:T(8,128)S(1)}, f32[32,32,512]{2,1,0:T(8,128)S(1)}, f32[32,32,512]{2,1,0:T(8,128)S(1)}) fusion(f32[32,32,512]{2,1,0:T(8,128)S(1)} %copy-done.4, f32[32,32,512]{2,1,0:T(8,128)S(1)} %fusion.14, f32[32,32,511]{2,1,0:T(8,128)S(1)} %slice.259, f32[32,32,512]{2,1,0:T(8,128)S(1)} %copy-done.3, ...), kind=kLoop, calls=%fused_computation.40 | loop fusion | flops 8388608 | bytes 23064576 | tf_op jit(solution)/shard_map/sub | solution.py:122
  161.1 3.7 %fusion.23 = f32[32,32,512]{2,1,0:T(8,128)} fusion(f32[32,32,512]{2,1,0:T(8,128)S(1)} %fusion.14, f32[32,32,512]{2,1,0:T(8,128)S(1)} %get-tuple-element.16, f32[32,32,512]{2,1,0:T(8,128)S(1)} %get-tuple-element.25, f32[31,32,512]{2,1,0:T(8,128)S(1)} %slice.254, f32[1,32,512]{2,1,0:T(8,128)S(1)} %get-tuple-element.33, ...), kind=kLoop, calls=%fused_computation.35 | loop fusion | flops 7864320 | bytes 20967424 | tf_op jit(solution)/shard_map/add | solution.py:131
  (91 shorter events, 13.8 us)
Async XLA Ops:
  0.6 25.9 %copy-start = (bf16[16,32,512]{2,1,0:T(8,128)(2,1)S(1)}, bf16[16,32,512]{2,1,0:T(8,128)(2,1)}, u32[]{:S(2)}) copy-start(bf16[16,32,512]{2,1,0:T(8,128)(2,1)} %param.20) | copy-start | bytes 1572868
  5.7 11.8 %all-to-all-start = ((s32[32,1,48]{2,1,0:T(1,128)}), s32[32,1,48]{2,1,0:T(1,128)S(1)}, u32[]{:S(2)}, u32[]{:S(2)}) async-start(s32[32,1,48]{2,1,0:T(1,128)} %sub.109), calls=%async_computation | async-start | bytes 32768 | tf_op jit(solution)/shard_map/all_to_all | solution.py:44
  17.4 5.9 %slice-start = ((f32[32,32,512]{2,1,0:T(8,128)}), f32[1,32,512]{2,1,0:T(8,128)S(1)}, s32[]{:S(2)}) async-start(f32[32,32,512]{2,1,0:T(8,128)} %param.12), calls=%async_computation.2 | async-start | bytes 131072 | tf_op jit(solution)/shard_map/slice | solution.py:98
  17.4 5.9 %slice-start.1 = ((f32[32,32,512]{2,1,0:T(8,128)}), f32[1,32,512]{2,1,0:T(8,128)S(1)}, s32[]{:S(2)}) async-start(f32[32,32,512]{2,1,0:T(8,128)} %param.16), calls=%async_computation.3 | async-start | bytes 131072 | tf_op jit(solution)/shard_map/slice | solution.py:98
  17.5 5.9 %slice-start.2 = ((f32[32,32,512]{2,1,0:T(8,128)}), f32[1,32,512]{2,1,0:T(8,128)S(1)}, s32[]{:S(2)}) async-start(f32[32,32,512]{2,1,0:T(8,128)} %param.13), calls=%async_computation.4 | async-start | bytes 131072 | tf_op jit(solution)/shard_map/slice | solution.py:98
  17.5 8.2 %copy-start.12 = (s32[8,8]{1,0:T(8,128)S(1)}, s32[8,8]{1,0:T(8,128)}, u32[]{:S(2)}) copy-start(s32[8,8]{1,0:T(8,128)} %param.21) | copy-start | bytes 772
  17.5 101.2 %all-to-all-start.1 = ((bf16[32,48,1024]{2,1,0:T(8,128)(2,1)}), bf16[32,48,1024]{2,1,0:T(8,128)(2,1)}, u32[]{:S(2)}, u32[]{:S(2)}) async-start(bf16[32,48,1024]{2,1,0:T(8,128)(2,1)} %bitcast.116), calls=%async_computation.1 | async-start | bytes 6291456 | tf_op jit(solution)/shard_map/all_to_all | solution.py:51
  23.4 8.0 %copy-start.2 = (f32[32,32,512]{2,1,0:T(8,128)S(1)}, f32[32,32,512]{2,1,0:T(8,128)}, u32[]{:S(2)}) copy-start(f32[32,32,512]{2,1,0:T(8,128)} %param.12) | copy-start | bytes 6291460
  23.4 74.1 %collective-permute-start.8 = (f32[3,32,512]{2,1,0:T(8,128)S(1)}, f32[3,32,512]{2,1,0:T(8,128)S(1)}, u32[]{:S(2)}, u32[]{:S(2)}) collective-permute-start(f32[3,32,512]{2,1,0:T(8,128)S(1)} %pad_maximum_fusion.1), channel_id=1, source_target_pairs={{0,4},{4,8},{8,12},{12,16},{16,20},{20,24},{24,28},{1,5},{5,9},{9,... | collective-permute-start | bytes 589832 | tf_op jit(solution)/shard_map/ppermute | solution.py:14
  27.9 100.9 %collective-permute-start = (bf16[32,512]{1,0:T(8,128)(2,1)}, bf16[32,512]{1,0:T(8,128)(2,1)S(1)}, u32[]{:S(2)}, u32[]{:S(2)}) collective-permute-start(bf16[32,512]{1,0:T(8,128)(2,1)} %get-tuple-element.37), channel_id=1, source_target_pairs={{0,4},{4,8},{8,12},{12,16},{16,20},{20,24},{24,28},{28,0},{1,5},{5... | collective-permute-start | bytes 98312 | tf_op jit(solution)/shard_map/ppermute | solution.py:79
  29.4 99.4 %collective-permute-start.6 = (bf16[32,512]{1,0:T(8,128)(2,1)}, bf16[32,512]{1,0:T(8,128)(2,1)S(1)}, u32[]{:S(2)}, u32[]{:S(2)}) collective-permute-start(bf16[32,512]{1,0:T(8,128)(2,1)} %get-tuple-element.38), channel_id=1, source_target_pairs={{0,28},{4,0},{8,4},{12,8},{16,12},{20,16},{24,20},{28,24},{1,29},{... | collective-permute-start | bytes 98312 | tf_op jit(solution)/shard_map/ppermute | solution.py:79
  29.7 103.1 %collective-permute-start.5 = (bf16[32,512]{1,0:T(8,128)(2,1)}, bf16[32,512]{1,0:T(8,128)(2,1)S(1)}, u32[]{:S(2)}, u32[]{:S(2)}) collective-permute-start(bf16[32,512]{1,0:T(8,128)(2,1)} %get-tuple-element.39), channel_id=1, source_target_pairs={{0,24},{4,28},{8,0},{12,4},{16,8},{20,12},{24,16},{28,20},{1,25},{... | collective-permute-start | bytes 98312 | tf_op jit(solution)/shard_map/ppermute | solution.py:79
  32.7 66.8 %collective-permute-start.10 = (f32[32,3,512]{2,1,0:T(4,128)S(1)}, f32[32,3,512]{2,1,0:T(4,128)}, u32[]{:S(2)}, u32[]{:S(2)}) collective-permute-start(f32[32,3,512]{2,1,0:T(4,128)S(1)} %pad_maximum_fusion), channel_id=1, source_target_pairs={{0,1},{1,2},{2,3},{4,5},{5,6},{6,7},{8,9},{9,10},{10,11},{12,13},{... | collective-permute-start | bytes 589832 | tf_op jit(solution)/shard_map/ppermute | solution.py:14
  97.5 7.3 %collective-permute-start.7 = (f32[1,32,512]{2,1,0:T(8,128)S(1)}, f32[1,32,512]{2,1,0:T(8,128)S(1)}, u32[]{:S(2)}, u32[]{:S(2)}) collective-permute-start(f32[1,32,512]{2,1,0:T(8,128)S(1)} %get-tuple-element.36), channel_id=1, source_target_pairs={{4,0},{8,4},{12,8},{16,12},{20,16},{24,20},{28,24},{5,1},{9,5},{13... | collective-permute-start | bytes 196616 | tf_op jit(solution)/shard_map/ppermute | solution.py:14
  100.9 7.3 %collective-permute-start.9 = (f32[32,1,512]{2,1,0:T(1,128)S(1)}, f32[32,1,512]{2,1,0:T(1,128)S(1)}, u32[]{:S(2)}, u32[]{:S(2)}) collective-permute-start(f32[32,1,512]{2,1,0:T(1,128)S(1)} %get-tuple-element.35), channel_id=1, source_target_pairs={{1,0},{2,1},{3,2},{5,4},{6,5},{7,6},{9,8},{10,9},{11,10},{13,12},{... | collective-permute-start | bytes 196616 | tf_op jit(solution)/shard_map/ppermute | solution.py:14
  104.8 27.9 %collective-permute-start.4 = (bf16[32,512]{1,0:T(8,128)(2,1)}, bf16[32,512]{1,0:T(8,128)(2,1)S(1)}, u32[]{:S(2)}, u32[]{:S(2)}) collective-permute-start(bf16[32,512]{1,0:T(8,128)(2,1)} %get-tuple-element.40), channel_id=1, source_target_pairs={{0,20},{4,24},{8,28},{12,0},{16,4},{20,8},{24,12},{28,16},{1,21},{... | collective-permute-start | bytes 98312 | tf_op jit(solution)/shard_map/ppermute | solution.py:79
  108.2 24.6 %collective-permute-start.3 = (bf16[32,512]{1,0:T(8,128)(2,1)}, bf16[32,512]{1,0:T(8,128)(2,1)S(1)}, u32[]{:S(2)}, u32[]{:S(2)}) collective-permute-start(bf16[32,512]{1,0:T(8,128)(2,1)} %get-tuple-element.41), channel_id=1, source_target_pairs={{0,16},{4,20},{8,24},{12,28},{16,0},{20,4},{24,8},{28,12},{1,17},{... | collective-permute-start | bytes 98312 | tf_op jit(solution)/shard_map/ppermute | solution.py:79
  123.3 16.4 %copy-start.11 = (f32[31,32,512]{2,1,0:T(8,128)S(1)}, f32[31,32,512]{2,1,0:T(8,128)}, u32[]{:S(2)}) copy-start(f32[31,32,512]{2,1,0:T(8,128)} %slice.244) | copy-start | bytes 6094852
  128.8 4.4 %collective-permute-start.2 = (bf16[32,512]{1,0:T(8,128)(2,1)S(1)}, bf16[32,512]{1,0:T(8,128)(2,1)S(1)}, u32[]{:S(2)}, u32[]{:S(2)}) collective-permute-start(bf16[32,512]{1,0:T(8,128)(2,1)S(1)} %get-tuple-element.42), channel_id=1, source_target_pairs={{0,12},{4,16},{8,20},{12,24},{16,28},{20,0},{24,4},{28,8},{1,13},{... | collective-permute-start | bytes 98312 | tf_op jit(solution)/shard_map/ppermute | solution.py:79
  128.9 5.0 %collective-permute-start.1 = (bf16[32,512]{1,0:T(8,128)(2,1)S(1)}, bf16[32,512]{1,0:T(8,128)(2,1)S(1)}, u32[]{:S(2)}, u32[]{:S(2)}) collective-permute-start(bf16[32,512]{1,0:T(8,128)(2,1)S(1)} %get-tuple-element.43), channel_id=1, source_target_pairs={{0,8},{4,12},{8,16},{12,20},{16,24},{20,28},{24,0},{28,4},{1,9},{5... | collective-permute-start | bytes 98312 | tf_op jit(solution)/shard_map/ppermute | solution.py:79
  132.3 7.4 %copy-start.3 = (f32[32,32,512]{2,1,0:T(8,128)S(1)}, f32[32,32,512]{2,1,0:T(8,128)}, u32[]{:S(2)}) copy-start(f32[32,32,512]{2,1,0:T(8,128)} %param.16) | copy-start | bytes 6291460
  132.3 7.4 %copy-start.4 = (f32[32,32,512]{2,1,0:T(8,128)S(1)}, f32[32,32,512]{2,1,0:T(8,128)}, u32[]{:S(2)}) copy-start(f32[32,32,512]{2,1,0:T(8,128)} %get-tuple-element.26) | copy-start | bytes 6291460
  132.3 7.4 %copy-start.5 = (f32[32,32,512]{2,1,0:T(8,128)S(1)}, f32[32,32,512]{2,1,0:T(8,128)}, u32[]{:S(2)}) copy-start(f32[32,32,512]{2,1,0:T(8,128)} %get-tuple-element.27) | copy-start | bytes 6291460
  132.3 7.4 %copy-start.7 = (f32[32,32,512]{2,1,0:T(8,128)S(1)}, f32[32,32,512]{2,1,0:T(8,128)}, u32[]{:S(2)}) copy-start(f32[32,32,512]{2,1,0:T(8,128)} %copy-done.6) | copy-start | bytes 6291460
  142.3 5.6 %collective-permute-start.12 = (f32[1,32,512]{2,1,0:T(8,128)S(1)}, f32[1,32,512]{2,1,0:T(8,128)S(1)}, u32[]{:S(2)}, u32[]{:S(2)}) collective-permute-start(f32[1,32,512]{2,1,0:T(8,128)S(1)} %slice.253), channel_id=1, source_target_pairs={{0,4},{4,8},{8,12},{12,16},{16,20},{20,24},{24,28},{1,5},{5,9},{9,... | collective-permute-start | bytes 196616 | tf_op jit(solution)/shard_map/ppermute | solution.py:14
  144.3 6.4 %collective-permute-start.14 = (f32[32,1,512]{2,1,0:T(1,128)S(1)}, f32[32,1,512]{2,1,0:T(1,128)S(1)}, u32[]{:S(2)}, u32[]{:S(2)}) collective-permute-start(f32[32,1,512]{2,1,0:T(1,128)S(1)} %slice.257), channel_id=1, source_target_pairs={{0,1},{1,2},{2,3},{4,5},{5,6},{6,7},{8,9},{9,10},{10,11},{12,13},{... | collective-permute-start | bytes 196616 | tf_op jit(solution)/shard_map/ppermute | solution.py:14
  147.9 7.1 %collective-permute-start.11 = (f32[1,32,512]{2,1,0:T(8,128)S(1)}, f32[1,32,512]{2,1,0:T(8,128)S(1)}, u32[]{:S(2)}, u32[]{:S(2)}) collective-permute-start(f32[1,32,512]{2,1,0:T(8,128)S(1)} %get-tuple-element.34), channel_id=1, source_target_pairs={{4,0},{8,4},{12,8},{16,12},{20,16},{24,20},{28,24},{5,1},{9,5},{13... | collective-permute-start | bytes 196616 | tf_op jit(solution)/shard_map/ppermute | solution.py:14
  150.9 7.1 %collective-permute-start.13 = (f32[32,1,512]{2,1,0:T(1,128)S(1)}, f32[32,1,512]{2,1,0:T(1,128)S(1)}, u32[]{:S(2)}, u32[]{:S(2)}) collective-permute-start(f32[32,1,512]{2,1,0:T(1,128)S(1)} %get-tuple-element.32), channel_id=1, source_target_pairs={{1,0},{2,1},{3,2},{5,4},{6,5},{7,6},{9,8},{10,9},{11,10},{13,12},{... | collective-permute-start | bytes 196616 | tf_op jit(solution)/shard_map/ppermute | solution.py:14
  160.8 4.0 %copy-start.8 = (f32[32,32,512]{2,1,0:T(8,128)}, f32[32,32,512]{2,1,0:T(8,128)S(1)}, u32[]{:S(2)}) copy-start(f32[32,32,512]{2,1,0:T(8,128)S(1)} %get-tuple-element.23) | copy-start | bytes 6291460
  160.8 4.0 %copy-start.9 = (f32[32,32,512]{2,1,0:T(8,128)}, f32[32,32,512]{2,1,0:T(8,128)S(1)}, u32[]{:S(2)}) copy-start(f32[32,32,512]{2,1,0:T(8,128)S(1)} %get-tuple-element.24) | copy-start | bytes 6291460
  160.8 4.0 %copy-start.10 = (f32[32,32,512]{2,1,0:T(8,128)}, f32[32,32,512]{2,1,0:T(8,128)S(1)}, u32[]{:S(2)}) copy-start(f32[32,32,512]{2,1,0:T(8,128)S(1)} %get-tuple-element.25) | copy-start | bytes 6291460
  161.1 3.7 %copy-start.1 = (bf16[16,32,512]{2,1,0:T(8,128)(2,1)S(1)}, bf16[16,32,512]{2,1,0:T(8,128)(2,1)}, u32[]{:S(2)}) copy-start(bf16[16,32,512]{2,1,0:T(8,128)(2,1)} %param.20) | copy-start | bytes 1572868
  (1 other events, 1.3 us)

commit v6 on v3

--- a/solution.py
+++ b/solution.py
@@ -35,12 +35,10 @@
     rank = jnp.sum(jnp.cumsum(owners, axis=0) * owners, axis=1) - 1
     slot_ids = dest * capacity + rank
     placed = slot_ids[None, :] == jnp.arange(slots, dtype=jnp.int32)[:, None]
-    outgoing = jnp.dot(
-        placed.astype(jnp.bfloat16),
-        waves.reshape(bubbles, steps * depth),
-        preferred_element_type=jnp.float32,
-    ).astype(jnp.bfloat16)
-    out_cols = jnp.max(jnp.where(placed, bubble_column[None, :] + 1, 0), axis=1) - 1
+    listed = jnp.arange(bubbles, dtype=jnp.int32)
+    holder = jnp.max(jnp.where(placed, listed[None, :] + 1, 0), axis=1) - 1
+    outgoing = jnp.take(waves.reshape(bubbles, steps * depth), jnp.maximum(holder, 0), axis=0)
+    out_cols = jnp.where(holder >= 0, jnp.take(bubble_column, jnp.maximum(holder, 0)), -1)
     in_cols = lax.all_to_all(
         out_cols.reshape(devices, capacity),
         ("gx", "gy"),

time: 162 us -> 170 us (1.049)
  local copies, waits for them, and re-layouts: 26.2 us -> 36.9 us
  matrix products: 10.9 us -> 5.48 us
  waiting for transfers between devices: 58.2 us -> 60.1 us
    gather x0 -> x2, local copies, waits for them, and re-layouts: none -> 11.7 us  [the longest x1 5.85 us: bubble_source(): jnp.take(bubble_column, jnp.maximum(holder, 0))]
    dot_general x1 -> x0, matrix products: 5.37 us -> none  [bubble_source(): jnp.dot(placed.astype(jnp.bfloat16), waves.reshape(bubbles, steps * depth...]
    dot_general x0 -> x1, local copies, waits for them, and re-layouts: none -> 4.67 us  [bubble_source(): jnp.dot(hits, incoming.reshape(slots, steps * depth), preferred_element_t...]
    reshape x1 -> x0, local copies, waits for them, and re-layouts: 4.66 us -> none  [bubble_source(): incoming.reshape(slots, steps * depth)]
    select_n x0 -> x2, other arithmetic: none -> 3.53 us  [the longest x1 3.53 us: bubble_source(): jnp.take(waves.reshape(bubbles, steps * depth), jnp.maximum(holder, 0), a...]
    all_to_all x1, waiting for transfers between devices: 1.11 us -> 2.96 us  [incident_plane(): rows = lax.all_to_all(chosen, 'gx', split_axis=0, concat_axis=0, tiled=True)]
    unnamed x33 -> x29, local copies, waits for them, and re-layouts: 4.98 us -> 5.21 us
where the time goes in v6:
time: 170 us; the launch traced here: 168 us
  waiting for transfers between devices  60.1 us (35%)
  starting transfers between devices  38.9 us (23%)
  local copies, waits for them, and re-layouts  36.9 us (22%)
  other arithmetic  25.6 us (15%)
  matrix products  5.48 us (3%)
    all_to_all x1, waiting for transfers between devices, bubble_source(): lax.all_to_all(outgoing.reshape(devices, capacity, steps * depth), ('gx',...  52.9 us
    ppermute x8, starting transfers between devices, from_behind(): return lax.ppermute(block, axis, route)  22.2 us
    sub x2, other arithmetic, body(): vel_z = vel_z - step_ratio * buoyancy * (next_z - pressure)  10.5 us
    add x2, other arithmetic, body(): pressure + step_ratio * stiffness * (source[:, :, step, :] + forcing - di...  6.18 us
    all_to_all x1, starting transfers between devices, bubble_source(): lax.all_to_all(out_cols.reshape(devices, capacity), ('gx', 'gy'), split_a...  5.91 us
    gather x1, local copies, waits for them, and re-layouts, bubble_source(): jnp.take(bubble_column, jnp.maximum(holder, 0))  5.85 us
    gather x1, local copies, waits for them, and re-layouts, bubble_source(): jnp.take(waves.reshape(bubbles, steps * depth), jnp.maximum(holder, 0), a...  5.83 us
    all_to_all x1, starting transfers between devices, bubble_source(): lax.all_to_all(outgoing.reshape(devices, capacity, steps * depth), ('gx',...  5.7 us
  transfers between devices with their start and end apart: 11, of which 3 were waited for; matrix products, arithmetic and copies ran while one was open for 21% of the time, Pallas kernels for 0%

profile of v6, /device:TPU:18, one launch (start us, length us, event | category | flops | bytes accessed | tf_op | source)
XLA Modules:
  0.0 168.3 jit_solution(18169486682512415435)
XLA Ops:
  1.4 1.7 %reduce-window.6 = s32[32,6,128]{2,0,1:T(8,128)S(1)} reduce-window(s32[32,6,128]{2,0,1:T(8,128)S(1)} %fusion.25, s32[]{:T(128)} %constant.116.clone.1), window={size=1x1x128 pad=0_0x0_0x127_0}, to_apply=%region_0.0 | reduce-window | flops 3121152 | bytes 196612 | tf_op jit(solution)/shard_map/reduce-window
  4.4 5.9 %gather_fusion = s32[1536]{0:T(1024)S(1)} fusion(s32[768]{0:T(1024)S(1)} %copy-done.2, s32[2048]{0:T(1024)S(1)} %pad_clamp_fusion), kind=kCustom, calls=%fused_computation | custom fusion | bytes 18432 | tf_op jit(solution)/shard_map/jit(_take)/gather | solution.py:41
  11.0 5.9 %all-to-all-start = ((s32[32,1,48]{2,1,0:T(1,128)}), s32[32,1,48]{2,1,0:T(1,128)S(1)}, u32[]{:S(2)}, u32[]{:S(2)}) async-start(s32[32,1,48]{2,1,0:T(1,128)} %reshape.212), calls=%async_computation | async-start | bytes 32768 | tf_op jit(solution)/shard_map/all_to_all | solution.py:42
  16.9 1.3 fusion.35
  18.2 2.5 %collective-permute-start.1 = (f32[32,1,512]{2,1,0:T(1,128)S(1)}, f32[32,1,512]{2,1,0:T(1,128)S(1)}, u32[]{:S(2)}, u32[]{:S(2)}) collective-permute-start(f32[32,1,512]{2,1,0:T(1,128)S(1)} %get-tuple-element.48), channel_id=1, source_target_pairs={{1,0},{2,1},{3,2},{5,4},{6,5},{7,6},{9,8},{10,9},{11,10},{13,12},{... | collective-permute-start | bytes 196616 | tf_op jit(solution)/shard_map/ppermute | solution.py:14
  20.7 1.5 fusion.36
  22.2 1.9 %collective-permute-start = (f32[1,32,512]{2,1,0:T(8,128)}, f32[1,32,512]{2,1,0:T(8,128)S(1)}, u32[]{:S(2)}, u32[]{:S(2)}) collective-permute-start(f32[1,32,512]{2,1,0:T(8,128)} %get-tuple-element.50), channel_id=1, source_target_pairs={{4,0},{8,4},{12,8},{16,12},{20,16},{24,20},{28,24},{5,1},{9,5},{13... | collective-permute-start | bytes 196616 | tf_op jit(solution)/shard_map/ppermute | solution.py:14
  24.2 2.4 %collective-permute-start.2 = (f32[3,32,512]{2,1,0:T(8,128)S(1)}, f32[3,32,512]{2,1,0:T(8,128)S(1)}, u32[]{:S(2)}, u32[]{:S(2)}) collective-permute-start(f32[3,32,512]{2,1,0:T(8,128)S(1)} %pad_maximum_fusion.1), channel_id=1, source_target_pairs={{0,4},{4,8},{8,12},{12,16},{16,20},{20,24},{24,28},{1,5},{5,9},{9,... | collective-permute-start | bytes 589832 | tf_op jit(solution)/shard_map/ppermute | solution.py:14
  27.7 1.1 slice.137
  29.0 4.3 %collective-permute-start.3 = (f32[32,3,512]{2,1,0:T(4,128)S(1)}, f32[32,3,512]{2,1,0:T(4,128)S(1)}, u32[]{:S(2)}, u32[]{:S(2)}) collective-permute-start(f32[32,3,512]{2,1,0:T(4,128)S(1)} %pad_maximum_fusion), channel_id=1, source_target_pairs={{0,1},{1,2},{2,3},{4,5},{5,6},{6,7},{8,9},{9,10},{10,11},{12,13},{... | collective-permute-start | bytes 589832 | tf_op jit(solution)/shard_map/ppermute | solution.py:14
  35.0 1.8 %copy.25 = bf16[96,8,2,512]{3,1,2,0:T(8,128)(2,1)S(1)} copy(bf16[96,8,2,512]{3,2,1,0:T(2,128)(2,1)} %bitcast.65) | data formatting | bytes 3145728
  36.8 5.8 %gather_fusion.1 = bf16[1536,1024]{1,0:T(8,128)(2,1)} fusion(bf16[768,1024]{1,0:T(8,128)(2,1)S(1)} %bitcast.58, s32[2048]{0:T(1024)S(1)} %pad_clamp_fusion), kind=kCustom, calls=%fused_computation.1 | custom fusion | bytes 6297600 | tf_op jit(solution)/shard_map/jit(_take)/gather | solution.py:40
  42.7 5.2 %all-to-all-start.2 = ((bf16[8,32,512]{2,1,0:T(8,128)(2,1)}), bf16[8,32,512]{2,1,0:T(8,128)(2,1)S(1)}, u32[]{:S(2)}, u32[]{:S(2)}) async-start(bf16[8,32,512]{2,1,0:T(8,128)(2,1)} %broadcast_select_fusion.1), calls=%async_computation.2 | async-start | bytes 524288 | tf_op jit(solution)/shard_map/all_to_all | solution.py:75
  47.8 3.5 %broadcast_select_fusion = bf16[1536,1024]{1,0:T(8,128)(2,1)} fusion(bf16[1536,1024]{1,0:T(8,128)(2,1)} %gather_fusion.1, pred[1536]{0:T(1024)(128)(4,1)S(1)} %broadcast_compare_fusion), kind=kLoop, calls=%fused_computation.10 | loop fusion | flops 1572864 | bytes 6292992 | tf_op jit(solution)/shard_map/jit(_take)/select_n | solution.py:40
  51.4 3.0 %all-to-all-done.2 = bf16[8,32,512]{2,1,0:T(8,128)(2,1)S(1)} async-done(((bf16[8,32,512]{2,1,0:T(8,128)(2,1)}), bf16[8,32,512]{2,1,0:T(8,128)(2,1)S(1)}, u32[]{:S(2)}, u32[]{:S(2)}) %all-to-all-start.2) | async-done | bytes 262176 | tf_op jit(solution)/shard_map/all_to_all | solution.py:75
  54.3 5.7 %all-to-all-start.1 = ((bf16[32,48,1024]{2,1,0:T(8,128)(2,1)}), bf16[32,48,1024]{2,1,0:T(8,128)(2,1)}, u32[]{:S(2)}, u32[]{:S(2)}) async-start(bf16[32,48,1024]{2,1,0:T(8,128)(2,1)} %bitcast.63), calls=%async_computation.1 | async-start | bytes 6291456 | tf_op jit(solution)/shard_map/all_to_all | solution.py:50
  60.1 1.5 slice.140
  61.6 1.7 %slice.145 = f32[32,31,512]{2,1,0:T(8,128)} slice(f32[32,32,512]{2,1,0:T(8,128)S(1)} %copy-done.3), slice={[0:32], [1:32], [0:512]} | slice | bytes 4063232 | tf_op jit(solution)/shard_map/slice | solution.py:113
  63.3 1.9 %slice.150 = f32[32,32,511]{2,1,0:T(8,128)} slice(f32[32,32,512]{2,1,0:T(8,128)S(1)} %copy-done.3), slice={[0:32], [0:32], [1:512]} | slice | bytes 4186112 | tf_op jit(solution)/shard_map/slice | solution.py:114
  65.3 7.7 %multiply_subtract_fusion.1 = (f32[32,32,512]{2,1,0:T(8,128)}, f32[32,32,512]{2,1,0:T(8,128)}, f32[32,32,512]{2,1,0:T(8,128)S(1)}) fusion(f32[32,32,512]{2,1,0:T(8,128)} %param.15, f32[32,32,512]{2,1,0:T(8,128)S(1)} %copy-done.3, f32[32,32,511]{2,1,0:T(8,128)} %slice.150, f32[32,32,512]{2,1,0:T(8,128)} %param.16, f32[32,32,512]{2,1,0:T(8,128)} %param.14, ...), kind=kLoop, calls=%fused_computation.40 | loop fusion | flops 8388608 | bytes 23064576 | tf_op jit(solution)/shard_map/sub | solution.py:117
  73.0 1.6 slice.171
  75.4 52.9 %all-to-all-done.1 = bf16[32,48,1024]{2,1,0:T(8,128)(2,1)} async-done(((bf16[32,48,1024]{2,1,0:T(8,128)(2,1)}), bf16[32,48,1024]{2,1,0:T(8,128)(2,1)}, u32[]{:S(2)}, u32[]{:S(2)}) %all-to-all-start.1) | async-done | bytes 3145760 | tf_op jit(solution)/shard_map/all_to_all | solution.py:50
  128.3 4.7 %copy.20 = bf16[1024,1536]{1,0:T(8,128)(2,1)} copy(bf16[1024,1536]{0,1:T(8,128)(2,1)} %bitcast.6) | data formatting | bytes 6291456 | tf_op jit(solution)/shard_map/dot_general | solution.py:60
  132.9 5.5 %fusion = f32[32,32,2,512]{3,1,2,0:T(8,128)S(1)} fusion(bf16[2,512,1536,1]{2,1,0,3:T(8,128)(2,1)} %bitcast.64, s32[1536]{0:T(1024)S(1)} %eq.76, s32[32,32]{1,0:T(8,128)S(1)} %multiply_add_fusion), kind=kOutput, calls=%fused_computation.3 | convolution fusion | flops 3222798336 | bytes 7350272 | tf_op jit(solution)/shard_map/dot_general | solution.py:60
  141.9 2.5 %fusion.11 = f32[32,32,512]{2,1,0:T(8,128)S(1)} fusion(f32[32,32,512]{2,1,0:T(8,128)S(1)} %copy-done.3, f32[32,32,512]{2,1,0:T(8,128)S(1)} %get-tuple-element.34, f32[32,32,512]{2,1,0:T(8,128)S(1)} %copy-done.8, f32[31,32,512]{2,1,0:T(8,128)S(1)} %copy-done.12, f32[1,32,512]{2,1,0:T(8,128)S(1)} %get-tuple-element.31, f32[32,32,512]{2,1,0:T(8,128)S(1)} %copy-done.6, ...), kind=kLoop, calls=%fused_computation.21 | loop fusion | flops 7864320 | bytes 20967424 | tf_op jit(solution)/shard_map/add | solution.py:126
  144.4 1.9 %collective-permute-start.5 = (f32[1,32,512]{2,1,0:T(8,128)S(1)}, f32[1,32,512]{2,1,0:T(8,128)S(1)}, u32[]{:S(2)}, u32[]{:S(2)}) collective-permute-start(f32[1,32,512]{2,1,0:T(8,128)S(1)} %slice.177), channel_id=1, source_target_pairs={{0,4},{4,8},{8,12},{12,16},{16,20},{20,24},{24,28},{1,5},{5,9},{9,... | collective-permute-start | bytes 196616 | tf_op jit(solution)/shard_map/ppermute | solution.py:14
  146.4 3.5 %collective-permute-start.7 = (f32[32,1,512]{2,1,0:T(1,128)S(1)}, f32[32,1,512]{2,1,0:T(1,128)S(1)}, u32[]{:S(2)}, u32[]{:S(2)}) collective-permute-start(f32[32,1,512]{2,1,0:T(1,128)S(1)} %slice.181), channel_id=1, source_target_pairs={{0,1},{1,2},{2,3},{4,5},{5,6},{6,7},{8,9},{9,10},{10,11},{12,13},{... | collective-permute-start | bytes 196616 | tf_op jit(solution)/shard_map/ppermute | solution.py:14
  150.1 3.3 %collective-permute-start.4 = (f32[1,32,512]{2,1,0:T(8,128)S(1)}, f32[1,32,512]{2,1,0:T(8,128)S(1)}, u32[]{:S(2)}, u32[]{:S(2)}) collective-permute-start(f32[1,32,512]{2,1,0:T(8,128)S(1)} %get-tuple-element.46), channel_id=1, source_target_pairs={{4,0},{8,4},{12,8},{16,12},{20,16},{24,20},{28,24},{5,1},{9,5},{13... | collective-permute-start | bytes 196616 | tf_op jit(solution)/shard_map/ppermute | solution.py:14
  153.6 2.3 %collective-permute-start.6 = (f32[32,1,512]{2,1,0:T(1,128)S(1)}, f32[32,1,512]{2,1,0:T(1,128)S(1)}, u32[]{:S(2)}, u32[]{:S(2)}) collective-permute-start(f32[32,1,512]{2,1,0:T(1,128)S(1)} %get-tuple-element.44), channel_id=1, source_target_pairs={{1,0},{2,1},{3,2},{5,4},{6,5},{7,6},{9,8},{10,9},{11,10},{13,12},{... | collective-permute-start | bytes 196616 | tf_op jit(solution)/shard_map/ppermute | solution.py:14
  157.1 4.2 %collective-permute-done.6 = f32[32,1,512]{2,1,0:T(1,128)S(1)} collective-permute-done((f32[32,1,512]{2,1,0:T(1,128)S(1)}, f32[32,1,512]{2,1,0:T(1,128)S(1)}, u32[]{:S(2)}, u32[]{:S(2)}) %collective-permute-start.6) | collective-permute-done | bytes 65568 | tf_op jit(solution)/shard_map/ppermute | solution.py:14
  161.3 2.8 %multiply_subtract_fusion = (f32[32,32,512]{2,1,0:T(8,128)S(1)}, f32[32,32,512]{2,1,0:T(8,128)S(1)}, f32[32,32,512]{2,1,0:T(8,128)S(1)}) fusion(f32[32,32,512]{2,1,0:T(8,128)S(1)} %copy-done.5, f32[32,32,512]{2,1,0:T(8,128)S(1)} %fusion.11, f32[32,32,511]{2,1,0:T(8,128)S(1)} %slice.183, f32[32,32,512]{2,1,0:T(8,128)S(1)} %copy-done.4, ...), kind=kLoop, calls=%fused_computation.39 | loop fusion | flops 8388608 | bytes 23064576 | tf_op jit(solution)/shard_map/sub | solution.py:117
  164.4 3.6 %fusion.20 = f32[32,32,512]{2,1,0:T(8,128)} fusion(f32[32,32,512]{2,1,0:T(8,128)S(1)} %fusion.11, f32[32,32,512]{2,1,0:T(8,128)S(1)} %get-tuple-element.33, f32[32,32,512]{2,1,0:T(8,128)S(1)} %get-tuple-element.37, f32[31,32,512]{2,1,0:T(8,128)S(1)} %slice.178, f32[1,32,512]{2,1,0:T(8,128)S(1)} %get-tuple-element.45, ...), kind=kLoop, calls=%fused_computation.34 | loop fusion | flops 7864320 | bytes 20967424 | tf_op jit(solution)/shard_map/add | solution.py:126
  (76 shorter events, 11.8 us)
Async XLA Ops:
  0.6 33.0 %copy-start = (bf16[16,32,512]{2,1,0:T(8,128)(2,1)S(1)}, bf16[16,32,512]{2,1,0:T(8,128)(2,1)}, u32[]{:S(2)}) copy-start(bf16[16,32,512]{2,1,0:T(8,128)(2,1)} %param.20) | copy-start | bytes 1572868
  0.6 3.7 %copy-start.2 = (s32[768]{0:T(1024)S(1)}, s32[768]{0:T(1024)}, u32[]{:S(2)}) copy-start(s32[768]{0:T(1024)} %param.19) | copy-start | bytes 9220
  4.3 19.8 %slice-start = ((f32[32,32,512]{2,1,0:T(8,128)}), f32[1,32,512]{2,1,0:T(8,128)S(1)}, s32[]{:S(2)}) async-start(f32[32,32,512]{2,1,0:T(8,128)} %param.16), calls=%async_computation.3 | async-start | bytes 131072 | tf_op jit(solution)/shard_map/slice | solution.py:93
  4.4 19.8 %slice-start.1 = ((f32[32,32,512]{2,1,0:T(8,128)}), f32[1,32,512]{2,1,0:T(8,128)S(1)}, s32[]{:S(2)}) async-start(f32[32,32,512]{2,1,0:T(8,128)} %param.13), calls=%async_computation.4 | async-start | bytes 131072 | tf_op jit(solution)/shard_map/slice | solution.py:93
  4.4 28.9 %copy-start.13 = (s32[8,8]{1,0:T(8,128)S(1)}, s32[8,8]{1,0:T(8,128)}, u32[]{:S(2)}) copy-start(s32[8,8]{1,0:T(8,128)} %param.21) | copy-start | bytes 772
  11.0 31.7 %all-to-all-start = ((s32[32,1,48]{2,1,0:T(1,128)}), s32[32,1,48]{2,1,0:T(1,128)S(1)}, u32[]{:S(2)}, u32[]{:S(2)}) async-start(s32[32,1,48]{2,1,0:T(1,128)} %reshape.212), calls=%async_computation | async-start | bytes 32768 | tf_op jit(solution)/shard_map/all_to_all | solution.py:42
  18.2 33.2 %collective-permute-start.1 = (f32[32,1,512]{2,1,0:T(1,128)S(1)}, f32[32,1,512]{2,1,0:T(1,128)S(1)}, u32[]{:S(2)}, u32[]{:S(2)}) collective-permute-start(f32[32,1,512]{2,1,0:T(1,128)S(1)} %get-tuple-element.48), channel_id=1, source_target_pairs={{1,0},{2,1},{3,2},{5,4},{6,5},{7,6},{9,8},{10,9},{11,10},{13,12},{... | collective-permute-start | bytes 196616 | tf_op jit(solution)/shard_map/ppermute | solution.py:14
  22.2 29.2 %collective-permute-start = (f32[1,32,512]{2,1,0:T(8,128)}, f32[1,32,512]{2,1,0:T(8,128)S(1)}, u32[]{:S(2)}, u32[]{:S(2)}) collective-permute-start(f32[1,32,512]{2,1,0:T(8,128)} %get-tuple-element.50), channel_id=1, source_target_pairs={{4,0},{8,4},{12,8},{16,12},{20,16},{24,20},{28,24},{5,1},{9,5},{13... | collective-permute-start | bytes 196616 | tf_op jit(solution)/shard_map/ppermute | solution.py:14
  24.2 27.2 %collective-permute-start.2 = (f32[3,32,512]{2,1,0:T(8,128)S(1)}, f32[3,32,512]{2,1,0:T(8,128)S(1)}, u32[]{:S(2)}, u32[]{:S(2)}) collective-permute-start(f32[3,32,512]{2,1,0:T(8,128)S(1)} %pad_maximum_fusion.1), channel_id=1, source_target_pairs={{0,4},{4,8},{8,12},{12,16},{16,20},{20,24},{24,28},{1,5},{5,9},{9,... | collective-permute-start | bytes 589832 | tf_op jit(solution)/shard_map/ppermute | solution.py:14
  29.0 22.4 %collective-permute-start.3 = (f32[32,3,512]{2,1,0:T(4,128)S(1)}, f32[32,3,512]{2,1,0:T(4,128)S(1)}, u32[]{:S(2)}, u32[]{:S(2)}) collective-permute-start(f32[32,3,512]{2,1,0:T(4,128)S(1)} %pad_maximum_fusion), channel_id=1, source_target_pairs={{0,1},{1,2},{2,3},{4,5},{5,6},{6,7},{8,9},{9,10},{10,11},{12,13},{... | collective-permute-start | bytes 589832 | tf_op jit(solution)/shard_map/ppermute | solution.py:14
  42.7 11.7 %all-to-all-start.2 = ((bf16[8,32,512]{2,1,0:T(8,128)(2,1)}), bf16[8,32,512]{2,1,0:T(8,128)(2,1)S(1)}, u32[]{:S(2)}, u32[]{:S(2)}) async-start(bf16[8,32,512]{2,1,0:T(8,128)(2,1)} %broadcast_select_fusion.1), calls=%async_computation.2 | async-start | bytes 524288 | tf_op jit(solution)/shard_map/all_to_all | solution.py:75
  54.3 5.7 %copy-start.3 = (f32[32,32,512]{2,1,0:T(8,128)S(1)}, f32[32,32,512]{2,1,0:T(8,128)}, u32[]{:S(2)}) copy-start(f32[32,32,512]{2,1,0:T(8,128)} %param.12) | copy-start | bytes 6291460
  54.3 73.9 %all-to-all-start.1 = ((bf16[32,48,1024]{2,1,0:T(8,128)(2,1)}), bf16[32,48,1024]{2,1,0:T(8,128)(2,1)}, u32[]{:S(2)}, u32[]{:S(2)}) async-start(bf16[32,48,1024]{2,1,0:T(8,128)(2,1)} %bitcast.63), calls=%async_computation.1 | async-start | bytes 6291456 | tf_op jit(solution)/shard_map/all_to_all | solution.py:50
  73.0 2.0 %copy-start.7 = (f32[32,32,512]{2,1,0:T(8,128)}, f32[32,32,512]{2,1,0:T(8,128)S(1)}, u32[]{:S(2)}) copy-start(f32[32,32,512]{2,1,0:T(8,128)S(1)} %get-tuple-element.42) | copy-start | bytes 6291460
  132.9 6.0 %copy-start.12 = (f32[31,32,512]{2,1,0:T(8,128)S(1)}, f32[31,32,512]{2,1,0:T(8,128)}, u32[]{:S(2)}) copy-start(f32[31,32,512]{2,1,0:T(8,128)} %slice.171) | copy-start | bytes 6094852
  138.4 1.6 copy-start.4
  138.4 2.2 %copy-start.5 = (f32[32,32,512]{2,1,0:T(8,128)S(1)}, f32[32,32,512]{2,1,0:T(8,128)}, u32[]{:S(2)}) copy-start(f32[32,32,512]{2,1,0:T(8,128)} %get-tuple-element.40) | copy-start | bytes 6291460
  138.4 2.8 %copy-start.6 = (f32[32,32,512]{2,1,0:T(8,128)S(1)}, f32[32,32,512]{2,1,0:T(8,128)}, u32[]{:S(2)}) copy-start(f32[32,32,512]{2,1,0:T(8,128)} %get-tuple-element.41) | copy-start | bytes 6291460
  138.5 3.4 %copy-start.8 = (f32[32,32,512]{2,1,0:T(8,128)S(1)}, f32[32,32,512]{2,1,0:T(8,128)}, u32[]{:S(2)}) copy-start(f32[32,32,512]{2,1,0:T(8,128)} %copy-done.7) | copy-start | bytes 6291460
  144.4 5.6 %collective-permute-start.5 = (f32[1,32,512]{2,1,0:T(8,128)S(1)}, f32[1,32,512]{2,1,0:T(8,128)S(1)}, u32[]{:S(2)}, u32[]{:S(2)}) collective-permute-start(f32[1,32,512]{2,1,0:T(8,128)S(1)} %slice.177), channel_id=1, source_target_pairs={{0,4},{4,8},{8,12},{12,16},{16,20},{20,24},{24,28},{1,5},{5,9},{9,... | collective-permute-start | bytes 196616 | tf_op jit(solution)/shard_map/ppermute | solution.py:14
  146.4 7.0 %collective-permute-start.7 = (f32[32,1,512]{2,1,0:T(1,128)S(1)}, f32[32,1,512]{2,1,0:T(1,128)S(1)}, u32[]{:S(2)}, u32[]{:S(2)}) collective-permute-start(f32[32,1,512]{2,1,0:T(1,128)S(1)} %slice.181), channel_id=1, source_target_pairs={{0,1},{1,2},{2,3},{4,5},{5,6},{6,7},{8,9},{9,10},{10,11},{12,13},{... | collective-permute-start | bytes 196616 | tf_op jit(solution)/shard_map/ppermute | solution.py:14
  150.1 7.1 %collective-permute-start.4 = (f32[1,32,512]{2,1,0:T(8,128)S(1)}, f32[1,32,512]{2,1,0:T(8,128)S(1)}, u32[]{:S(2)}, u32[]{:S(2)}) collective-permute-start(f32[1,32,512]{2,1,0:T(8,128)S(1)} %get-tuple-element.46), channel_id=1, source_target_pairs={{4,0},{8,4},{12,8},{16,12},{20,16},{24,20},{28,24},{5,1},{9,5},{13... | collective-permute-start | bytes 196616 | tf_op jit(solution)/shard_map/ppermute | solution.py:14
  153.6 7.7 %collective-permute-start.6 = (f32[32,1,512]{2,1,0:T(1,128)S(1)}, f32[32,1,512]{2,1,0:T(1,128)S(1)}, u32[]{:S(2)}, u32[]{:S(2)}) collective-permute-start(f32[32,1,512]{2,1,0:T(1,128)S(1)} %get-tuple-element.44), channel_id=1, source_target_pairs={{1,0},{2,1},{3,2},{5,4},{6,5},{7,6},{9,8},{10,9},{11,10},{13,12},{... | collective-permute-start | bytes 196616 | tf_op jit(solution)/shard_map/ppermute | solution.py:14
  164.1 4.0 %copy-start.9 = (f32[32,32,512]{2,1,0:T(8,128)}, f32[32,32,512]{2,1,0:T(8,128)S(1)}, u32[]{:S(2)}) copy-start(f32[32,32,512]{2,1,0:T(8,128)S(1)} %get-tuple-element.35) | copy-start | bytes 6291460
  164.1 4.0 %copy-start.10 = (f32[32,32,512]{2,1,0:T(8,128)}, f32[32,32,512]{2,1,0:T(8,128)S(1)}, u32[]{:S(2)}) copy-start(f32[32,32,512]{2,1,0:T(8,128)S(1)} %get-tuple-element.36) | copy-start | bytes 6291460
  164.1 3.9 %copy-start.11 = (f32[32,32,512]{2,1,0:T(8,128)}, f32[32,32,512]{2,1,0:T(8,128)S(1)}, u32[]{:S(2)}) copy-start(f32[32,32,512]{2,1,0:T(8,128)S(1)} %get-tuple-element.37) | copy-start | bytes 6291460
  164.4 3.7 %copy-start.1 = (bf16[16,32,512]{2,1,0:T(8,128)(2,1)S(1)}, bf16[16,32,512]{2,1,0:T(8,128)(2,1)}, u32[]{:S(2)}) copy-start(bf16[16,32,512]{2,1,0:T(8,128)(2,1)} %param.20) | copy-start | bytes 1572868

commit v7 on v3

--- a/solution.py
+++ b/solution.py
@@ -59,10 +59,7 @@
     hits = (
         jnp.arange(cells, dtype=jnp.int32)[:, None] == in_cols.reshape(slots)[None, :]
     ).astype(jnp.bfloat16)
-    source = jnp.dot(
-        hits, incoming.reshape(slots, steps * depth), preferred_element_type=jnp.float32
-    )
-    return source, ready
+    return hits, incoming.reshape(slots, steps, depth), ready
 
 
 def incident_plane(history, delays, size_y, depth):
@@ -99,10 +96,12 @@
     )
 
     ready = (above_x, above_y, below_x, below_y)
-    source, ready = bubble_source(waves, bubble_dest, bubble_column, size_x * size_y, ready)
+    hits, incoming, ready = bubble_source(
+        waves, bubble_dest, bubble_column, size_x * size_y, ready
+    )
     above_x, above_y, below_x, below_y = ready
+    history, _ = lax.optimization_barrier((history, incoming))
     incident = incident_plane(history, delays, size_y, depth)
-    source = source.reshape(size_x, size_y, steps, depth)
     p_bx, vx_bx, void_bx = below_x[0:1], below_x[1:2], below_x[2:3]
     p_by, vy_by, void_by = below_y[:, 0:1], below_y[:, 1:2], below_y[:, 2:3]
     b_bx, _ = material(void_bx)
@@ -110,7 +109,10 @@
     forcing = jnp.zeros_like(pressure).at[0].set(incident)
     z_edge = jnp.zeros((size_x, size_y, 1), jnp.float32)
 
+    wave_rows = incoming
     for step in range(steps):
+        source = jnp.dot(hits, wave_rows[:, step, :], preferred_element_type=jnp.float32)
+        source = source.reshape(size_x, size_y, depth)
         next_x = jnp.concatenate([pressure[1:], above_x], 0)
         next_y = jnp.concatenate([pressure[:, 1:], above_y], 1)
         next_z = jnp.concatenate([pressure[:, :, 1:], z_edge], 2)
@@ -126,9 +128,10 @@
         prev_z = jnp.concatenate([z_edge, vel_z[:, :, :-1]], 2)
         divergence = vel_x - prev_x + (vel_y - prev_y) + (vel_z - prev_z)
         pressure = pressure + step_ratio * stiffness * (
-            source[:, :, step, :] + forcing - divergence
+            source + forcing - divergence
         )
         if step + 1 < steps:
+            wave_rows, pressure = lax.optimization_barrier((wave_rows, pressure))
             above_x = from_behind(pressure[0:1], "gx", -1)
             above_y = from_behind(pressure[:, 0:1], "gy", -1)
             p_bx = from_behind(pressure[-1:], "gx", 1)

time: 162 us -> 169 us (1.043)
  other arithmetic: 24.5 us -> 32.7 us
  starting transfers between devices: 38.9 us -> 41.1 us
  matrix products: 10.9 us -> 8.98 us
    add x3 -> x4, other arithmetic: 6.19 us -> 12.8 us  [the longest x2 11.3 us: body(): pressure + step_ratio * stiffness * (source + forcing - divergence)]
    unnamed x33 -> x35, local copies, waits for them, and re-layouts: 4.98 us -> 0.5 us
    all_to_all x1, starting transfers between devices: 5.16 us -> 7.05 us  [incident_plane(): rows = lax.all_to_all(chosen, 'gx', split_axis=0, concat_axis=0, tiled=True)]
    slice x2, local copies, waits for them, and re-layouts: 1.82 us -> 3.53 us  [body(): prev_x = jnp.concatenate([lower_x, vel_x[:-1]], 0)]
    dot_general x1 -> x2, matrix products: 5.48 us -> 4.99 us  [body(): jnp.dot(hits, wave_rows[:, step, :], preferred_element_type=jnp.float32)]
  transfers between devices with their start and end apart: 11 -> 11, of which waited for: 3 -> 3; matrix products, arithmetic and copies ran while one was open for 21% -> 23% of each run, Pallas kernels for 0% -> 0%
where the time goes in v7:
time: 169 us; the launch traced here: 166 us
  waiting for transfers between devices  57 us (34%)
  starting transfers between devices  41.1 us (24%)
  other arithmetic  32.7 us (19%)
  local copies, waits for them, and re-layouts  25 us (15%)
  matrix products  8.98 us (5%)
    all_to_all x1, waiting for transfers between devices, bubble_source(): lax.all_to_all(outgoing.reshape(devices, capacity, steps * depth), ('gx',...  51.4 us
    ppermute x8, starting transfers between devices, from_behind(): return lax.ppermute(block, axis, route)  22.4 us
    sub x2, other arithmetic, body(): vel_z = vel_z - step_ratio * buoyancy * (next_z - pressure)  11.6 us
    add x2, other arithmetic, body(): pressure + step_ratio * stiffness * (source + forcing - divergence)  11.3 us
    all_to_all x1, starting transfers between devices, incident_plane(): rows = lax.all_to_all(chosen, 'gx', split_axis=0, concat_axis=0, tiled=True)  7.05 us
    reshape x1, local copies, waits for them, and re-layouts, bubble_source(): return (hits, incoming.reshape(slots, steps, depth), ready)  6.17 us
    all_to_all x1, starting transfers between devices, bubble_source(): lax.all_to_all(out_cols.reshape(devices, capacity), ('gx', 'gy'), split_a...  5.91 us
    all_to_all x1, starting transfers between devices, bubble_source(): lax.all_to_all(outgoing.reshape(devices, capacity, steps * depth), ('gx',...  5.77 us
  transfers between devices with their start and end apart: 11, of which 3 were waited for; matrix products, arithmetic and copies ran while one was open for 23% of the time, Pallas kernels for 0%

profile of v7, /device:TPU:18, one launch (start us, length us, event | category | flops | bytes accessed | tf_op | source)
XLA Modules:
  0.0 166.0 jit_solution(8899681231096058870)
XLA Ops:
  2.2 1.7 %reduce-window.6 = s32[32,6,128]{2,0,1:T(8,128)S(1)} reduce-window(s32[32,6,128]{2,0,1:T(8,128)S(1)} %fusion.31, s32[]{:T(128)} %constant.82.clone.1), window={size=1x1x128 pad=0_0x0_0x127_0}, to_apply=%region_0.0 | reduce-window | flops 3121152 | bytes 196612 | tf_op jit(solution)/shard_map/reduce-window
  5.8 5.9 %all-to-all-start = ((s32[32,1,48]{2,1,0:T(1,128)}), s32[32,1,48]{2,1,0:T(1,128)S(1)}, u32[]{:S(2)}, u32[]{:S(2)}) async-start(s32[32,1,48]{2,1,0:T(1,128)} %sub.122), calls=%async_computation | async-start | bytes 32768 | tf_op jit(solution)/shard_map/all_to_all | solution.py:44
  11.7 1.3 fusion.39
  13.0 2.5 %collective-permute-start.1 = (f32[32,1,512]{2,1,0:T(1,128)S(1)}, f32[32,1,512]{2,1,0:T(1,128)S(1)}, u32[]{:S(2)}, u32[]{:S(2)}) collective-permute-start(f32[32,1,512]{2,1,0:T(1,128)S(1)} %get-tuple-element.50), channel_id=1, source_target_pairs={{1,0},{2,1},{3,2},{5,4},{6,5},{7,6},{9,8},{10,9},{11,10},{13,12},{... | collective-permute-start | bytes 196616 | tf_op jit(solution)/shard_map/ppermute | solution.py:14
  15.5 0.9 fusion.40
  16.4 1.9 %collective-permute-start = (f32[1,32,512]{2,1,0:T(8,128)S(1)}, f32[1,32,512]{2,1,0:T(8,128)S(1)}, u32[]{:S(2)}, u32[]{:S(2)}) collective-permute-start(f32[1,32,512]{2,1,0:T(8,128)S(1)} %get-tuple-element.52), channel_id=1, source_target_pairs={{4,0},{8,4},{12,8},{16,12},{20,16},{24,20},{28,24},{5,1},{9,5},{13... | collective-permute-start | bytes 196616 | tf_op jit(solution)/shard_map/ppermute | solution.py:14
  20.1 2.4 %collective-permute-start.2 = (f32[3,32,512]{2,1,0:T(8,128)S(1)}, f32[3,32,512]{2,1,0:T(8,128)S(1)}, u32[]{:S(2)}, u32[]{:S(2)}) collective-permute-start(f32[3,32,512]{2,1,0:T(8,128)S(1)} %pad_maximum_fusion.1), channel_id=1, source_target_pairs={{0,4},{4,8},{8,12},{12,16},{16,20},{20,24},{24,28},{1,5},{5,9},{9,... | collective-permute-start | bytes 589832 | tf_op jit(solution)/shard_map/ppermute | solution.py:14
  22.4 1.1 slice.136
  23.6 1.1 slice.135
  24.8 4.3 %collective-permute-start.3 = (f32[32,3,512]{2,1,0:T(4,128)S(1)}, f32[32,3,512]{2,1,0:T(4,128)S(1)}, u32[]{:S(2)}, u32[]{:S(2)}) collective-permute-start(f32[32,3,512]{2,1,0:T(4,128)S(1)} %pad_maximum_fusion), channel_id=1, source_target_pairs={{0,1},{1,2},{2,3},{4,5},{5,6},{6,7},{8,9},{9,10},{10,11},{12,13},{... | collective-permute-start | bytes 589832 | tf_op jit(solution)/shard_map/ppermute | solution.py:14
  29.6 4.0 %fusion.5 = bf16[1536,1024]{1,0:T(8,128)(2,1)} fusion(bf16[768,1024]{1,0:T(8,128)(2,1)S(1)} %bitcast.45, s32[768]{0:T(1024)S(1)} %add_add_fusion), kind=kOutput, calls=%fused_computation.8 | convolution fusion | flops 2418671616 | bytes 4721664 | tf_op jit(solution)/shard_map/dot_general | solution.py:38
  33.6 2.2 %collective-permute-done.3 = f32[32,3,512]{2,1,0:T(4,128)S(1)} collective-permute-done((f32[32,3,512]{2,1,0:T(4,128)S(1)}, f32[32,3,512]{2,1,0:T(4,128)S(1)}, u32[]{:S(2)}, u32[]{:S(2)}) %collective-permute-start.3) | collective-permute-done | bytes 196640 | tf_op jit(solution)/shard_map/ppermute | solution.py:14
  35.8 5.8 %all-to-all-start.1 = ((bf16[32,48,1024]{2,1,0:T(8,128)(2,1)}), bf16[32,48,1024]{2,1,0:T(8,128)(2,1)}, u32[]{:S(2)}, u32[]{:S(2)}) async-start(bf16[32,48,1024]{2,1,0:T(8,128)(2,1)} %bitcast.43), calls=%async_computation.1 | async-start | bytes 6291456 | tf_op jit(solution)/shard_map/all_to_all | solution.py:52
  41.6 1.6 slice.138
  43.1 1.7 %slice.143 = f32[32,31,512]{2,1,0:T(8,128)} slice(f32[32,32,512]{2,1,0:T(8,128)S(1)} %copy-done.2), slice={[0:32], [1:32], [0:512]} | slice | bytes 4063232 | tf_op jit(solution)/shard_map/slice | solution.py:117
  44.8 1.9 %slice.148 = f32[32,32,511]{2,1,0:T(8,128)} slice(f32[32,32,512]{2,1,0:T(8,128)S(1)} %copy-done.2), slice={[0:32], [0:32], [1:512]} | slice | bytes 4186112 | tf_op jit(solution)/shard_map/slice | solution.py:118
  49.6 8.8 %multiply_subtract_fusion.1 = (f32[32,32,512]{2,1,0:T(8,128)}, f32[32,32,512]{2,1,0:T(8,128)}, f32[32,32,512]{2,1,0:T(8,128)}) fusion(f32[32,32,512]{2,1,0:T(8,128)} %param.15, f32[32,32,512]{2,1,0:T(8,128)S(1)} %copy-done.2, f32[32,32,511]{2,1,0:T(8,128)} %slice.148, f32[32,32,512]{2,1,0:T(8,128)} %param.16, f32[32,32,512]{2,1,0:T(8,128)} %param.14, ...), kind=kLoop, calls=%fused_computation.41 | loop fusion | flops 8388608 | bytes 23064576 | tf_op jit(solution)/shard_map/sub | solution.py:121
  58.4 51.4 %all-to-all-done.1 = bf16[32,48,1024]{2,1,0:T(8,128)(2,1)} async-done(((bf16[32,48,1024]{2,1,0:T(8,128)(2,1)}), bf16[32,48,1024]{2,1,0:T(8,128)(2,1)}, u32[]{:S(2)}, u32[]{:S(2)}) %all-to-all-start.1) | async-done | bytes 3145760 | tf_op jit(solution)/shard_map/all_to_all | solution.py:52
  109.8 6.2 %reshape.148 = bf16[1536,2,512]{2,1,0:T(2,128)(2,1)} reshape(bf16[32,48,1024]{2,1,0:T(8,128)(2,1)} %all-to-all-done.1) | data formatting | bytes 6291456 | tf_op jit(solution)/shard_map/reshape | solution.py:62
  117.5 7.1 %all-to-all-start.2 = ((bf16[8,32,512]{2,1,0:T(8,128)(2,1)}), bf16[8,32,512]{2,1,0:T(8,128)(2,1)S(1)}, u32[]{:S(2)}, u32[]{:S(2)}) async-start(bf16[8,32,512]{2,1,0:T(8,128)(2,1)} %broadcast_select_fusion), calls=%async_computation.2 | async-start | bytes 524288 | tf_op jit(solution)/shard_map/all_to_all | solution.py:74
  124.6 3.3 %slice.165 = f32[31,32,512]{2,1,0:T(8,128)} slice(f32[32,32,512]{2,1,0:T(8,128)} %get-tuple-element.44), slice={[0:31], [0:32], [0:512]} | slice | bytes 4063232 | tf_op jit(solution)/shard_map/slice | solution.py:126
  127.9 3.2 %fusion.2 = f32[32,32,512]{2,1,0:T(8,128)} fusion(s32[1536]{0:T(1024)S(1)} %eq.78, s32[32,32]{1,0:T(8,128)S(1)} %copy-done.14, bf16[1536,1,512]{2,1,0:T(2,128)(2,1)S(1)} %bitcast.42), kind=kOutput, calls=%fused_computation.3 | convolution fusion | flops 1612185600 | bytes 3680256 | tf_op jit(solution)/shard_map/dot_general | solution.py:114
  131.2 1.5 fusion.33
  132.7 7.6 %fusion.17 = f32[32,32,512]{2,1,0:T(8,128)S(1)} fusion(f32[32,32,512]{2,1,0:T(8,128)S(1)} %copy-done.2, f32[32,32,512]{2,1,0:T(8,128)} %fusion.33, f32[32,32,512]{2,1,0:T(8,128)} %get-tuple-element.44, f32[31,32,512]{2,1,0:T(8,128)} %slice.165, f32[1,32,512]{2,1,0:T(8,128)S(1)} %get-tuple-element.37, f32[32,32,512]{2,1,0:T(8,128)} %get-tuple-element.43, ...), kind=kLoop, calls=%fused_computation.22 | loop fusion | flops 7864320 | bytes 20967424 | tf_op jit(solution)/shard_map/add | solution.py:130
  140.9 2.2 %collective-permute-start.5 = (f32[1,32,512]{2,1,0:T(8,128)S(1)}, f32[1,32,512]{2,1,0:T(8,128)S(1)}, u32[]{:S(2)}, u32[]{:S(2)}) collective-permute-start(f32[1,32,512]{2,1,0:T(8,128)S(1)} %slice.153), channel_id=1, source_target_pairs={{0,4},{4,8},{8,12},{12,16},{16,20},{20,24},{24,28},{1,5},{5,9},{9,... | collective-permute-start | bytes 196616 | tf_op jit(solution)/shard_map/ppermute | solution.py:14
  143.1 1.8 %fusion = f32[32,32,512]{2,1,0:T(8,128)S(1)} fusion(s32[1536]{0:T(1024)S(1)} %eq.78, s32[32,32]{1,0:T(8,128)S(1)} %copy-done.14, bf16[1536,2,512]{2,0,1:T(8,128)(2,1)S(1)} %copy.19), kind=kOutput, calls=%fused_computation.1 | convolution fusion | flops 1612185600 | bytes 3694592 | tf_op jit(solution)/shard_map/dot_general | solution.py:114
  145.0 2.9 %collective-permute-start.7 = (f32[32,1,512]{2,1,0:T(1,128)S(1)}, f32[32,1,512]{2,1,0:T(1,128)S(1)}, u32[]{:S(2)}, u32[]{:S(2)}) collective-permute-start(f32[32,1,512]{2,1,0:T(1,128)S(1)} %slice.157), channel_id=1, source_target_pairs={{0,1},{1,2},{2,3},{4,5},{5,6},{6,7},{8,9},{9,10},{10,11},{12,13},{... | collective-permute-start | bytes 196616 | tf_op jit(solution)/shard_map/ppermute | solution.py:14
  148.0 3.2 %collective-permute-start.4 = (f32[1,32,512]{2,1,0:T(8,128)S(1)}, f32[1,32,512]{2,1,0:T(8,128)S(1)}, u32[]{:S(2)}, u32[]{:S(2)}) collective-permute-start(f32[1,32,512]{2,1,0:T(8,128)S(1)} %get-tuple-element.48), channel_id=1, source_target_pairs={{4,0},{8,4},{12,8},{16,12},{20,16},{24,20},{28,24},{5,1},{9,5},{13... | collective-permute-start | bytes 196616 | tf_op jit(solution)/shard_map/ppermute | solution.py:14
  151.4 2.9 %collective-permute-start.6 = (f32[32,1,512]{2,1,0:T(1,128)S(1)}, f32[32,1,512]{2,1,0:T(1,128)S(1)}, u32[]{:S(2)}, u32[]{:S(2)}) collective-permute-start(f32[32,1,512]{2,1,0:T(1,128)S(1)} %get-tuple-element.46), channel_id=1, source_target_pairs={{1,0},{2,1},{3,2},{5,4},{6,5},{7,6},{9,8},{10,9},{11,10},{13,12},{... | collective-permute-start | bytes 196616 | tf_op jit(solution)/shard_map/ppermute | solution.py:14
  155.7 3.4 %collective-permute-done.6 = f32[32,1,512]{2,1,0:T(1,128)S(1)} collective-permute-done((f32[32,1,512]{2,1,0:T(1,128)S(1)}, f32[32,1,512]{2,1,0:T(1,128)S(1)}, u32[]{:S(2)}, u32[]{:S(2)}) %collective-permute-start.6) | collective-permute-done | bytes 65568 | tf_op jit(solution)/shard_map/ppermute | solution.py:14
  159.1 2.8 %multiply_subtract_fusion = (f32[32,32,512]{2,1,0:T(8,128)S(1)}, f32[32,32,512]{2,1,0:T(8,128)S(1)}, f32[32,32,512]{2,1,0:T(8,128)S(1)}) fusion(f32[32,32,512]{2,1,0:T(8,128)S(1)} %copy-done.4, f32[32,32,512]{2,1,0:T(8,128)S(1)} %fusion.17, f32[32,32,511]{2,1,0:T(8,128)S(1)} %slice.159, f32[32,32,512]{2,1,0:T(8,128)S(1)} %copy-done.3, ...), kind=kLoop, calls=%fused_computation.40 | loop fusion | flops 8388608 | bytes 23064576 | tf_op jit(solution)/shard_map/sub | solution.py:121
  162.2 3.6 %fusion.26 = f32[32,32,512]{2,1,0:T(8,128)} fusion(f32[32,32,512]{2,1,0:T(8,128)S(1)} %fusion.17, f32[32,32,512]{2,1,0:T(8,128)S(1)} %fusion.32, f32[32,32,512]{2,1,0:T(8,128)S(1)} %get-tuple-element.41, f32[31,32,512]{2,1,0:T(8,128)S(1)} %slice.169, f32[1,32,512]{2,1,0:T(8,128)S(1)} %get-tuple-element.47, f32[32,32,512]{2,1,0:T(8,128)S(1)} %get-tuple-element.40, ...), kind=kLoop, calls=%fused_computation.35 | loop fusion | flops 7864320 | bytes 20967424 | tf_op jit(solution)/shard_map/add | solution.py:130
  (78 shorter events, 12.5 us)
Async XLA Ops:
  0.6 115.3 %copy-start = (bf16[16,32,512]{2,1,0:T(8,128)(2,1)S(1)}, bf16[16,32,512]{2,1,0:T(8,128)(2,1)}, u32[]{:S(2)}) copy-start(bf16[16,32,512]{2,1,0:T(8,128)(2,1)} %param.20) | copy-start | bytes 1572868
  0.6 28.5 %copy-start.12 = (bf16[768,2,512]{2,1,0:T(2,128)(2,1)S(1)}, bf16[768,2,512]{2,1,0:T(2,128)(2,1)}, u32[]{:S(2)}) copy-start(bf16[768,2,512]{2,1,0:T(2,128)(2,1)} %param.17) | copy-start | bytes 4718596
  5.8 27.8 %all-to-all-start = ((s32[32,1,48]{2,1,0:T(1,128)}), s32[32,1,48]{2,1,0:T(1,128)S(1)}, u32[]{:S(2)}, u32[]{:S(2)}) async-start(s32[32,1,48]{2,1,0:T(1,128)} %sub.122), calls=%async_computation | async-start | bytes 32768 | tf_op jit(solution)/shard_map/all_to_all | solution.py:44
  13.0 20.5 %collective-permute-start.1 = (f32[32,1,512]{2,1,0:T(1,128)S(1)}, f32[32,1,512]{2,1,0:T(1,128)S(1)}, u32[]{:S(2)}, u32[]{:S(2)}) collective-permute-start(f32[32,1,512]{2,1,0:T(1,128)S(1)} %get-tuple-element.50), channel_id=1, source_target_pairs={{1,0},{2,1},{3,2},{5,4},{6,5},{7,6},{9,8},{10,9},{11,10},{13,12},{... | collective-permute-start | bytes 196616 | tf_op jit(solution)/shard_map/ppermute | solution.py:14
  16.4 17.2 %collective-permute-start = (f32[1,32,512]{2,1,0:T(8,128)S(1)}, f32[1,32,512]{2,1,0:T(8,128)S(1)}, u32[]{:S(2)}, u32[]{:S(2)}) collective-permute-start(f32[1,32,512]{2,1,0:T(8,128)S(1)} %get-tuple-element.52), channel_id=1, source_target_pairs={{4,0},{8,4},{12,8},{16,12},{20,16},{24,20},{28,24},{5,1},{9,5},{13... | collective-permute-start | bytes 196616 | tf_op jit(solution)/shard_map/ppermute | solution.py:14
  20.1 13.5 %collective-permute-start.2 = (f32[3,32,512]{2,1,0:T(8,128)S(1)}, f32[3,32,512]{2,1,0:T(8,128)S(1)}, u32[]{:S(2)}, u32[]{:S(2)}) collective-permute-start(f32[3,32,512]{2,1,0:T(8,128)S(1)} %pad_maximum_fusion.1), channel_id=1, source_target_pairs={{0,4},{4,8},{8,12},{12,16},{16,20},{20,24},{24,28},{1,5},{5,9},{9,... | collective-permute-start | bytes 589832 | tf_op jit(solution)/shard_map/ppermute | solution.py:14
  24.8 10.9 %collective-permute-start.3 = (f32[32,3,512]{2,1,0:T(4,128)S(1)}, f32[32,3,512]{2,1,0:T(4,128)S(1)}, u32[]{:S(2)}, u32[]{:S(2)}) collective-permute-start(f32[32,3,512]{2,1,0:T(4,128)S(1)} %pad_maximum_fusion), channel_id=1, source_target_pairs={{0,1},{1,2},{2,3},{4,5},{5,6},{6,7},{8,9},{9,10},{10,11},{12,13},{... | collective-permute-start | bytes 589832 | tf_op jit(solution)/shard_map/ppermute | solution.py:14
  35.8 5.8 %copy-start.2 = (f32[32,32,512]{2,1,0:T(8,128)S(1)}, f32[32,32,512]{2,1,0:T(8,128)}, u32[]{:S(2)}) copy-start(f32[32,32,512]{2,1,0:T(8,128)} %param.12) | copy-start | bytes 6291460
  35.8 74.0 %all-to-all-start.1 = ((bf16[32,48,1024]{2,1,0:T(8,128)(2,1)}), bf16[32,48,1024]{2,1,0:T(8,128)(2,1)}, u32[]{:S(2)}, u32[]{:S(2)}) async-start(bf16[32,48,1024]{2,1,0:T(8,128)(2,1)} %bitcast.43), calls=%async_computation.1 | async-start | bytes 6291456 | tf_op jit(solution)/shard_map/all_to_all | solution.py:52
  44.8 1.9 %copy-start.13 = (s32[8,8]{1,0:T(8,128)S(1)}, s32[8,8]{1,0:T(8,128)}, u32[]{:S(2)}) copy-start(s32[8,8]{1,0:T(8,128)} %param.21) | copy-start | bytes 772
  58.4 58.3 %copy-start.15 = (pred[8]{0:T(512)(128)(4,1)S(1)}, pred[8]{0:T(512)(128)(4,1)}, u32[]{:S(2)}) copy-start(pred[8]{0:T(512)(128)(4,1)} %and_reduce_fusion) | copy-start | bytes 28
  117.5 13.6 %all-to-all-start.2 = ((bf16[8,32,512]{2,1,0:T(8,128)(2,1)}), bf16[8,32,512]{2,1,0:T(8,128)(2,1)S(1)}, u32[]{:S(2)}, u32[]{:S(2)}) async-start(bf16[8,32,512]{2,1,0:T(8,128)(2,1)} %broadcast_select_fusion), calls=%async_computation.2 | async-start | bytes 524288 | tf_op jit(solution)/shard_map/all_to_all | solution.py:74
  124.6 3.4 %copy-start.14 = (s32[32,32]{1,0:T(8,128)S(1)}, s32[32,32]{1,0:T(8,128)}, u32[]{:S(2)}) copy-start(s32[32,32]{1,0:T(8,128)} %multiply_add_fusion) | copy-start | bytes 12292
  124.6 3.3 %copy-start.10 = (bf16[1536,2,512]{2,1,0:T(2,128)(2,1)S(1)}, bf16[1536,2,512]{2,1,0:T(2,128)(2,1)}, u32[]{:S(2)}) copy-start(bf16[1536,2,512]{2,1,0:T(2,128)(2,1)} %reshape.148) | copy-start | bytes 9437188
  127.9 3.2 %copy-start.16 = (f32[8]{0:T(128)S(1)}, f32[8]{0:T(128)}, u32[]{:S(2)}) copy-start(f32[8]{0:T(128)} %fusion.38) | copy-start | bytes 100
  132.7 7.6 %copy-start.11 = (bf16[1536,2,512]{2,1,0:T(2,128)(2,1)S(1)}, bf16[1536,2,512]{2,1,0:T(2,128)(2,1)}, u32[]{:S(2)}) copy-start(bf16[1536,2,512]{2,1,0:T(2,128)(2,1)} %reshape.148) | copy-start | bytes 9437188
  140.9 7.1 %collective-permute-start.5 = (f32[1,32,512]{2,1,0:T(8,128)S(1)}, f32[1,32,512]{2,1,0:T(8,128)S(1)}, u32[]{:S(2)}, u32[]{:S(2)}) collective-permute-start(f32[1,32,512]{2,1,0:T(8,128)S(1)} %slice.153), channel_id=1, source_target_pairs={{0,4},{4,8},{8,12},{12,16},{16,20},{20,24},{24,28},{1,5},{5,9},{9,... | collective-permute-start | bytes 196616 | tf_op jit(solution)/shard_map/ppermute | solution.py:14
  145.0 6.2 %collective-permute-start.7 = (f32[32,1,512]{2,1,0:T(1,128)S(1)}, f32[32,1,512]{2,1,0:T(1,128)S(1)}, u32[]{:S(2)}, u32[]{:S(2)}) collective-permute-start(f32[32,1,512]{2,1,0:T(1,128)S(1)} %slice.157), channel_id=1, source_target_pairs={{0,1},{1,2},{2,3},{4,5},{5,6},{6,7},{8,9},{9,10},{10,11},{12,13},{... | collective-permute-start | bytes 196616 | tf_op jit(solution)/shard_map/ppermute | solution.py:14
  148.0 7.6 %collective-permute-start.4 = (f32[1,32,512]{2,1,0:T(8,128)S(1)}, f32[1,32,512]{2,1,0:T(8,128)S(1)}, u32[]{:S(2)}, u32[]{:S(2)}) collective-permute-start(f32[1,32,512]{2,1,0:T(8,128)S(1)} %get-tuple-element.48), channel_id=1, source_target_pairs={{4,0},{8,4},{12,8},{16,12},{20,16},{24,20},{28,24},{5,1},{9,5},{13... | collective-permute-start | bytes 196616 | tf_op jit(solution)/shard_map/ppermute | solution.py:14
  151.4 7.6 %collective-permute-start.6 = (f32[32,1,512]{2,1,0:T(1,128)S(1)}, f32[32,1,512]{2,1,0:T(1,128)S(1)}, u32[]{:S(2)}, u32[]{:S(2)}) collective-permute-start(f32[32,1,512]{2,1,0:T(1,128)S(1)} %get-tuple-element.46), channel_id=1, source_target_pairs={{1,0},{2,1},{3,2},{5,4},{6,5},{7,6},{9,8},{10,9},{11,10},{13,12},{... | collective-permute-start | bytes 196616 | tf_op jit(solution)/shard_map/ppermute | solution.py:14
  154.6 4.4 %copy-start.5 = (f32[32,32,512]{2,1,0:T(8,128)S(1)}, f32[32,32,512]{2,1,0:T(8,128)}, u32[]{:S(2)}) copy-start(f32[32,32,512]{2,1,0:T(8,128)} %get-tuple-element.43) | copy-start | bytes 6291460
  154.6 4.4 %copy-start.6 = (f32[32,32,512]{2,1,0:T(8,128)S(1)}, f32[32,32,512]{2,1,0:T(8,128)}, u32[]{:S(2)}) copy-start(f32[32,32,512]{2,1,0:T(8,128)} %get-tuple-element.44) | copy-start | bytes 6291460
  155.2 3.8 %copy-start.3 = (f32[32,32,512]{2,1,0:T(8,128)S(1)}, f32[32,32,512]{2,1,0:T(8,128)}, u32[]{:S(2)}) copy-start(f32[32,32,512]{2,1,0:T(8,128)} %param.16) | copy-start | bytes 6291460
  155.3 3.8 %copy-start.4 = (f32[32,32,512]{2,1,0:T(8,128)S(1)}, f32[32,32,512]{2,1,0:T(8,128)}, u32[]{:S(2)}) copy-start(f32[32,32,512]{2,1,0:T(8,128)} %get-tuple-element.42) | copy-start | bytes 6291460
  161.9 4.0 %copy-start.7 = (f32[32,32,512]{2,1,0:T(8,128)}, f32[32,32,512]{2,1,0:T(8,128)S(1)}, u32[]{:S(2)}) copy-start(f32[32,32,512]{2,1,0:T(8,128)S(1)} %get-tuple-element.39) | copy-start | bytes 6291460
  161.9 4.0 %copy-start.8 = (f32[32,32,512]{2,1,0:T(8,128)}, f32[32,32,512]{2,1,0:T(8,128)S(1)}, u32[]{:S(2)}) copy-start(f32[32,32,512]{2,1,0:T(8,128)S(1)} %get-tuple-element.40) | copy-start | bytes 6291460
  161.9 3.9 %copy-start.9 = (f32[32,32,512]{2,1,0:T(8,128)}, f32[32,32,512]{2,1,0:T(8,128)S(1)}, u32[]{:S(2)}) copy-start(f32[32,32,512]{2,1,0:T(8,128)S(1)} %get-tuple-element.41) | copy-start | bytes 6291460
  162.2 3.7 %copy-start.1 = (bf16[16,32,512]{2,1,0:T(8,128)(2,1)S(1)}, bf16[16,32,512]{2,1,0:T(8,128)(2,1)}, u32[]{:S(2)}) copy-start(bf16[16,32,512]{2,1,0:T(8,128)(2,1)} %param.20) | copy-start | bytes 1572868

commit v8 on v3

--- a/solution.py
+++ b/solution.py
@@ -62,7 +62,7 @@
     source = jnp.dot(
         hits, incoming.reshape(slots, steps * depth), preferred_element_type=jnp.float32
     )
-    return source, ready
+    return source, incoming, ready
 
 
 def incident_plane(history, delays, size_y, depth):
@@ -99,8 +99,11 @@
     )
 
     ready = (above_x, above_y, below_x, below_y)
-    source, ready = bubble_source(waves, bubble_dest, bubble_column, size_x * size_y, ready)
+    source, incoming, ready = bubble_source(
+        waves, bubble_dest, bubble_column, size_x * size_y, ready
+    )
     above_x, above_y, below_x, below_y = ready
+    history, _ = lax.optimization_barrier((history, incoming))
     incident = incident_plane(history, delays, size_y, depth)
     source = source.reshape(size_x, size_y, steps, depth)
     p_bx, vx_bx, void_bx = below_x[0:1], below_x[1:2], below_x[2:3]

time: 162 us -> 170 us (1.049)
  other arithmetic: 24.5 us -> 29.6 us
  local copies, waits for them, and re-layouts: 26.2 us -> 29.5 us
    add x2, other arithmetic: 6.18 us -> 11.4 us  [body(): pressure + step_ratio * stiffness * (source[:, :, step, :] + forcing - di...]
    squeeze x1, local copies, waits for them, and re-layouts: 0.44 us -> 2.51 us  [body(): source[:, :, step, :] + forcing - divergence]
    all_to_all x1, starting transfers between devices: 5.16 us -> 7.06 us  [incident_plane(): rows = lax.all_to_all(chosen, 'gx', split_axis=0, concat_axis=0, tiled=True)]
    ppermute x8, waiting for transfers between devices: 4.22 us -> 6.03 us  [from_behind(): return lax.ppermute(block, axis, route)]
    unnamed x33 -> x35, local copies, waits for them, and re-layouts: 4.98 us -> 6.47 us
  transfers between devices with their start and end apart: 11 -> 11, of which waited for: 3 -> 5; matrix products, arithmetic and copies ran while one was open for 21% -> 24% of each run, Pallas kernels for 0% -> 0%
where the time goes in v8:
time: 170 us; the launch traced here: 169 us
  waiting for transfers between devices  58.6 us (34%)
  starting transfers between devices  40.2 us (24%)
  other arithmetic  29.6 us (17%)
  local copies, waits for them, and re-layouts  29.5 us (17%)
  matrix products  9.35 us (6%)
    all_to_all x1, waiting for transfers between devices, bubble_source(): lax.all_to_all(outgoing.reshape(devices, capacity, steps * depth), ('gx',...  52.6 us
    ppermute x8, starting transfers between devices, from_behind(): return lax.ppermute(block, axis, route)  21.5 us
    add x2, other arithmetic, body(): pressure + step_ratio * stiffness * (source[:, :, step, :] + forcing - di...  11.4 us
    sub x2, other arithmetic, body(): vel_z = vel_z - step_ratio * buoyancy * (next_z - pressure)  10.6 us
    all_to_all x1, starting transfers between devices, incident_plane(): rows = lax.all_to_all(chosen, 'gx', split_axis=0, concat_axis=0, tiled=True)  7.06 us
    unnamed x35, local copies, waits for them, and re-layouts  6.47 us
    ppermute x8, waiting for transfers between devices, from_behind(): return lax.ppermute(block, axis, route)  6.03 us
    all_to_all x1, starting transfers between devices, bubble_source(): lax.all_to_all(out_cols.reshape(devices, capacity), ('gx', 'gy'), split_a...  5.91 us
  transfers between devices with their start and end apart: 11, of which 5 were waited for; matrix products, arithmetic and copies ran while one was open for 24% of the time, Pallas kernels for 0%

profile of v8, /device:TPU:18, one launch (start us, length us, event | category | flops | bytes accessed | tf_op | source)
XLA Modules:
  0.0 168.5 jit_solution(5960618065893051399)
XLA Ops:
  2.2 1.7 %reduce-window.6 = s32[32,6,128]{2,0,1:T(8,128)S(1)} reduce-window(s32[32,6,128]{2,0,1:T(8,128)S(1)} %fusion.28, s32[]{:T(128)} %constant.87.clone.1), window={size=1x1x128 pad=0_0x0_0x127_0}, to_apply=%region_0.0 | reduce-window | flops 3121152 | bytes 196612 | tf_op jit(solution)/shard_map/reduce-window
  5.8 5.9 %all-to-all-start = ((s32[32,1,48]{2,1,0:T(1,128)}), s32[32,1,48]{2,1,0:T(1,128)S(1)}, u32[]{:S(2)}, u32[]{:S(2)}) async-start(s32[32,1,48]{2,1,0:T(1,128)} %sub.123), calls=%async_computation | async-start | bytes 32768 | tf_op jit(solution)/shard_map/all_to_all | solution.py:44
  11.7 1.3 fusion.38
  13.0 2.5 %collective-permute-start.1 = (f32[32,1,512]{2,1,0:T(1,128)S(1)}, f32[32,1,512]{2,1,0:T(1,128)S(1)}, u32[]{:S(2)}, u32[]{:S(2)}) collective-permute-start(f32[32,1,512]{2,1,0:T(1,128)S(1)} %get-tuple-element.50), channel_id=1, source_target_pairs={{1,0},{2,1},{3,2},{5,4},{6,5},{7,6},{9,8},{10,9},{11,10},{13,12},{... | collective-permute-start | bytes 196616 | tf_op jit(solution)/shard_map/ppermute | solution.py:14
  16.4 1.9 %collective-permute-start = (f32[1,32,512]{2,1,0:T(8,128)S(1)}, f32[1,32,512]{2,1,0:T(8,128)S(1)}, u32[]{:S(2)}, u32[]{:S(2)}) collective-permute-start(f32[1,32,512]{2,1,0:T(8,128)S(1)} %get-tuple-element.52), channel_id=1, source_target_pairs={{4,0},{8,4},{12,8},{16,12},{20,16},{24,20},{28,24},{5,1},{9,5},{13... | collective-permute-start | bytes 196616 | tf_op jit(solution)/shard_map/ppermute | solution.py:14
  20.1 2.4 %collective-permute-start.2 = (f32[3,32,512]{2,1,0:T(8,128)S(1)}, f32[3,32,512]{2,1,0:T(8,128)S(1)}, u32[]{:S(2)}, u32[]{:S(2)}) collective-permute-start(f32[3,32,512]{2,1,0:T(8,128)S(1)} %pad_maximum_fusion.1), channel_id=1, source_target_pairs={{0,4},{4,8},{8,12},{12,16},{16,20},{20,24},{24,28},{1,5},{5,9},{9,... | collective-permute-start | bytes 589832 | tf_op jit(solution)/shard_map/ppermute | solution.py:14
  22.4 1.1 slice.138
  24.8 4.3 %collective-permute-start.3 = (f32[32,3,512]{2,1,0:T(4,128)S(1)}, f32[32,3,512]{2,1,0:T(4,128)S(1)}, u32[]{:S(2)}, u32[]{:S(2)}) collective-permute-start(f32[32,3,512]{2,1,0:T(4,128)S(1)} %pad_maximum_fusion), channel_id=1, source_target_pairs={{0,1},{1,2},{2,3},{4,5},{5,6},{6,7},{8,9},{9,10},{10,11},{12,13},{... | collective-permute-start | bytes 589832 | tf_op jit(solution)/shard_map/ppermute | solution.py:14
  29.6 4.0 %fusion.4 = bf16[1536,1024]{1,0:T(8,128)(2,1)} fusion(bf16[768,1024]{1,0:T(8,128)(2,1)S(1)} %bitcast.66, s32[768]{0:T(1024)S(1)} %add_add_fusion), kind=kOutput, calls=%fused_computation.7 | convolution fusion | flops 2418671616 | bytes 4721664 | tf_op jit(solution)/shard_map/dot_general | solution.py:38
  33.6 2.2 %collective-permute-done.3 = f32[32,3,512]{2,1,0:T(4,128)S(1)} collective-permute-done((f32[32,3,512]{2,1,0:T(4,128)S(1)}, f32[32,3,512]{2,1,0:T(4,128)S(1)}, u32[]{:S(2)}, u32[]{:S(2)}) %collective-permute-start.3) | collective-permute-done | bytes 196640 | tf_op jit(solution)/shard_map/ppermute | solution.py:14
  36.5 5.8 %all-to-all-start.1 = ((bf16[32,48,1024]{2,1,0:T(8,128)(2,1)}), bf16[32,48,1024]{2,1,0:T(8,128)(2,1)}, u32[]{:S(2)}, u32[]{:S(2)}) async-start(bf16[32,48,1024]{2,1,0:T(8,128)(2,1)} %bitcast.63), calls=%async_computation.1 | async-start | bytes 6291456 | tf_op jit(solution)/shard_map/all_to_all | solution.py:52
  42.3 1.5 slice.140
  43.8 1.7 %slice.145 = f32[32,31,512]{2,1,0:T(8,128)} slice(f32[32,32,512]{2,1,0:T(8,128)S(1)} %copy-done.2), slice={[0:32], [1:32], [0:512]} | slice | bytes 4063232 | tf_op jit(solution)/shard_map/slice | solution.py:118
  45.5 1.9 %slice.150 = f32[32,32,511]{2,1,0:T(8,128)} slice(f32[32,32,512]{2,1,0:T(8,128)S(1)} %copy-done.2), slice={[0:32], [0:32], [1:512]} | slice | bytes 4186112 | tf_op jit(solution)/shard_map/slice | solution.py:119
  47.9 7.8 %multiply_subtract_fusion.1 = (f32[32,32,512]{2,1,0:T(8,128)}, f32[32,32,512]{2,1,0:T(8,128)}, f32[32,32,512]{2,1,0:T(8,128)S(1)}) fusion(f32[32,32,512]{2,1,0:T(8,128)} %param.15, f32[32,32,512]{2,1,0:T(8,128)S(1)} %copy-done.2, f32[32,32,511]{2,1,0:T(8,128)} %slice.150, f32[32,32,512]{2,1,0:T(8,128)} %param.16, f32[32,32,512]{2,1,0:T(8,128)} %param.14, ...), kind=kLoop, calls=%fused_computation.40 | loop fusion | flops 8388608 | bytes 23064576 | tf_op jit(solution)/shard_map/sub | solution.py:122
  55.7 1.5 slice.167
  57.9 52.6 %all-to-all-done.1 = bf16[32,48,1024]{2,1,0:T(8,128)(2,1)} async-done(((bf16[32,48,1024]{2,1,0:T(8,128)(2,1)}), bf16[32,48,1024]{2,1,0:T(8,128)(2,1)}, u32[]{:S(2)}, u32[]{:S(2)}) %all-to-all-start.1) | async-done | bytes 3145760 | tf_op jit(solution)/shard_map/all_to_all | solution.py:52
  111.9 7.1 %all-to-all-start.2 = ((bf16[8,32,512]{2,1,0:T(8,128)(2,1)}), bf16[8,32,512]{2,1,0:T(8,128)(2,1)S(1)}, u32[]{:S(2)}, u32[]{:S(2)}) async-start(bf16[8,32,512]{2,1,0:T(8,128)(2,1)} %broadcast_select_fusion), calls=%async_computation.2 | async-start | bytes 524288 | tf_op jit(solution)/shard_map/all_to_all | solution.py:77
  118.9 4.7 %copy.20 = bf16[1536,1024]{0,1:T(8,128)(2,1)} copy(bf16[1536,1024]{1,0:T(8,128)(2,1)} %bitcast.5) | data formatting | bytes 6291456 | tf_op jit(solution)/shard_map/reshape | solution.py:63
  123.6 5.3 %fusion = f32[32,32,2,512]{3,1,2,0:T(8,128)S(1)} fusion(bf16[2,512,1536,1]{2,1,0,3:T(8,128)(2,1)} %bitcast.64, s32[1536]{0:T(1024)S(1)} %eq.76, s32[32,32]{1,0:T(8,128)S(1)} %multiply_add_fusion), kind=kOutput, calls=%fused_computation.1 | convolution fusion | flops 3222798336 | bytes 7350272 | tf_op jit(solution)/shard_map/dot_general | solution.py:62
  129.0 1.9 %copy-done.12 = f32[32,32,2,512]{3,1,2,0:T(8,128)} copy-done((f32[32,32,2,512]{3,1,2,0:T(8,128)}, f32[32,32,2,512]{3,1,2,0:T(8,128)S(1)}, u32[]{:S(2)}) %copy-start.12) | copy-done | bytes 4194328
  130.9 2.5 %slice_bitcast_fusion = (f32[32,32,512]{2,1,0:T(8,128)}, f32[32,32,512]{2,1,0:T(8,128)}) fusion(f32[32,32,2,512]{3,1,2,0:T(8,128)S(1)} %fusion), kind=kLoop, calls=%fused_computation.11 | loop fusion | bytes 8388608 | tf_op jit(solution)/shard_map/squeeze | solution.py:132
  133.5 1.5 fusion.30
  135.1 7.8 %fusion.14 = f32[32,32,512]{2,1,0:T(8,128)S(1)} fusion(f32[32,32,512]{2,1,0:T(8,128)S(1)} %copy-done.2, f32[32,32,512]{2,1,0:T(8,128)} %get-tuple-element.36, f32[32,32,512]{2,1,0:T(8,128)} %copy-done.6, f32[31,32,512]{2,1,0:T(8,128)} %slice.167, f32[1,32,512]{2,1,0:T(8,128)S(1)} %get-tuple-element.33, f32[32,32,512]{2,1,0:T(8,128)} %get-tuple-element.43, ...), kind=kLoop, calls=%fused_computation.21 | loop fusion | flops 7864320 | bytes 20967424 | tf_op jit(solution)/shard_map/add | solution.py:131
  142.9 2.1 %collective-permute-start.5 = (f32[1,32,512]{2,1,0:T(8,128)S(1)}, f32[1,32,512]{2,1,0:T(8,128)S(1)}, u32[]{:S(2)}, u32[]{:S(2)}) collective-permute-start(f32[1,32,512]{2,1,0:T(8,128)S(1)} %slice.173), channel_id=1, source_target_pairs={{0,4},{4,8},{8,12},{12,16},{16,20},{20,24},{24,28},{1,5},{5,9},{9,... | collective-permute-start | bytes 196616 | tf_op jit(solution)/shard_map/ppermute | solution.py:14
  145.0 2.9 %collective-permute-start.7 = (f32[32,1,512]{2,1,0:T(1,128)S(1)}, f32[32,1,512]{2,1,0:T(1,128)S(1)}, u32[]{:S(2)}, u32[]{:S(2)}) collective-permute-start(f32[32,1,512]{2,1,0:T(1,128)S(1)} %slice.177), channel_id=1, source_target_pairs={{0,1},{1,2},{2,3},{4,5},{5,6},{6,7},{8,9},{9,10},{10,11},{12,13},{... | collective-permute-start | bytes 196616 | tf_op jit(solution)/shard_map/ppermute | solution.py:14
  148.5 2.7 %collective-permute-start.4 = (f32[1,32,512]{2,1,0:T(8,128)S(1)}, f32[1,32,512]{2,1,0:T(8,128)S(1)}, u32[]{:S(2)}, u32[]{:S(2)}) collective-permute-start(f32[1,32,512]{2,1,0:T(8,128)S(1)} %get-tuple-element.48), channel_id=1, source_target_pairs={{4,0},{8,4},{12,8},{16,12},{20,16},{24,20},{28,24},{5,1},{9,5},{13... | collective-permute-start | bytes 196616 | tf_op jit(solution)/shard_map/ppermute | solution.py:14
  151.7 2.7 %collective-permute-start.6 = (f32[32,1,512]{2,1,0:T(1,128)S(1)}, f32[32,1,512]{2,1,0:T(1,128)S(1)}, u32[]{:S(2)}, u32[]{:S(2)}) collective-permute-start(f32[32,1,512]{2,1,0:T(1,128)S(1)} %get-tuple-element.46), channel_id=1, source_target_pairs={{1,0},{2,1},{3,2},{5,4},{6,5},{7,6},{9,8},{10,9},{11,10},{13,12},{... | collective-permute-start | bytes 196616 | tf_op jit(solution)/shard_map/ppermute | solution.py:14
  155.7 3.1 %collective-permute-done.6 = f32[32,1,512]{2,1,0:T(1,128)S(1)} collective-permute-done((f32[32,1,512]{2,1,0:T(1,128)S(1)}, f32[32,1,512]{2,1,0:T(1,128)S(1)}, u32[]{:S(2)}, u32[]{:S(2)}) %collective-permute-start.6) | collective-permute-done | bytes 65568 | tf_op jit(solution)/shard_map/ppermute | solution.py:14
  158.8 2.8 %multiply_subtract_fusion = (f32[32,32,512]{2,1,0:T(8,128)S(1)}, f32[32,32,512]{2,1,0:T(8,128)S(1)}, f32[32,32,512]{2,1,0:T(8,128)S(1)}) fusion(f32[32,32,512]{2,1,0:T(8,128)S(1)} %copy-done.4, f32[32,32,512]{2,1,0:T(8,128)S(1)} %fusion.14, f32[32,32,511]{2,1,0:T(8,128)S(1)} %slice.179, f32[32,32,512]{2,1,0:T(8,128)S(1)} %copy-done.3, ...), kind=kLoop, calls=%fused_computation.39 | loop fusion | flops 8388608 | bytes 23064576 | tf_op jit(solution)/shard_map/sub | solution.py:122
  161.9 2.9 %copy-done.11 = f32[32,32,512]{2,1,0:T(8,128)S(1)} copy-done((f32[32,32,512]{2,1,0:T(8,128)S(1)}, f32[32,32,512]{2,1,0:T(8,128)}, u32[]{:S(2)}) %copy-start.11) | copy-done | bytes 2097176
  164.8 3.5 %fusion.23 = f32[32,32,512]{2,1,0:T(8,128)} fusion(f32[32,32,512]{2,1,0:T(8,128)S(1)} %fusion.14, f32[32,32,512]{2,1,0:T(8,128)S(1)} %copy-done.11, f32[32,32,512]{2,1,0:T(8,128)S(1)} %get-tuple-element.39, f32[31,32,512]{2,1,0:T(8,128)S(1)} %slice.174, f32[1,32,512]{2,1,0:T(8,128)S(1)} %get-tuple-element.47, f32[32,32,512]{2,1,0:T(8,128)S(1)} %get-tuple-element.38, ...), kind=kLoop, calls=%fused_computation.34 | loop fusion | flops 7864320 | bytes 20967424 | tf_op jit(solution)/shard_map/add | solution.py:131
  (76 shorter events, 13.6 us)
Async XLA Ops:
  0.6 109.9 %copy-start = (bf16[16,32,512]{2,1,0:T(8,128)(2,1)S(1)}, bf16[16,32,512]{2,1,0:T(8,128)(2,1)}, u32[]{:S(2)}) copy-start(bf16[16,32,512]{2,1,0:T(8,128)(2,1)} %param.20) | copy-start | bytes 1572868
  0.6 28.5 %copy-start.13 = (bf16[768,2,512]{2,1,0:T(2,128)(2,1)S(1)}, bf16[768,2,512]{2,1,0:T(2,128)(2,1)}, u32[]{:S(2)}) copy-start(bf16[768,2,512]{2,1,0:T(2,128)(2,1)} %param.17) | copy-start | bytes 4718596
  5.8 27.8 %all-to-all-start = ((s32[32,1,48]{2,1,0:T(1,128)}), s32[32,1,48]{2,1,0:T(1,128)S(1)}, u32[]{:S(2)}, u32[]{:S(2)}) async-start(s32[32,1,48]{2,1,0:T(1,128)} %sub.123), calls=%async_computation | async-start | bytes 32768 | tf_op jit(solution)/shard_map/all_to_all | solution.py:44
  13.0 20.6 %collective-permute-start.1 = (f32[32,1,512]{2,1,0:T(1,128)S(1)}, f32[32,1,512]{2,1,0:T(1,128)S(1)}, u32[]{:S(2)}, u32[]{:S(2)}) collective-permute-start(f32[32,1,512]{2,1,0:T(1,128)S(1)} %get-tuple-element.50), channel_id=1, source_target_pairs={{1,0},{2,1},{3,2},{5,4},{6,5},{7,6},{9,8},{10,9},{11,10},{13,12},{... | collective-permute-start | bytes 196616 | tf_op jit(solution)/shard_map/ppermute | solution.py:14
  16.4 17.2 %collective-permute-start = (f32[1,32,512]{2,1,0:T(8,128)S(1)}, f32[1,32,512]{2,1,0:T(8,128)S(1)}, u32[]{:S(2)}, u32[]{:S(2)}) collective-permute-start(f32[1,32,512]{2,1,0:T(8,128)S(1)} %get-tuple-element.52), channel_id=1, source_target_pairs={{4,0},{8,4},{12,8},{16,12},{20,16},{24,20},{28,24},{5,1},{9,5},{13... | collective-permute-start | bytes 196616 | tf_op jit(solution)/shard_map/ppermute | solution.py:14
  20.1 13.5 %collective-permute-start.2 = (f32[3,32,512]{2,1,0:T(8,128)S(1)}, f32[3,32,512]{2,1,0:T(8,128)S(1)}, u32[]{:S(2)}, u32[]{:S(2)}) collective-permute-start(f32[3,32,512]{2,1,0:T(8,128)S(1)} %pad_maximum_fusion.1), channel_id=1, source_target_pairs={{0,4},{4,8},{8,12},{12,16},{16,20},{20,24},{24,28},{1,5},{5,9},{9,... | collective-permute-start | bytes 589832 | tf_op jit(solution)/shard_map/ppermute | solution.py:14
  24.8 10.9 %collective-permute-start.3 = (f32[32,3,512]{2,1,0:T(4,128)S(1)}, f32[32,3,512]{2,1,0:T(4,128)S(1)}, u32[]{:S(2)}, u32[]{:S(2)}) collective-permute-start(f32[32,3,512]{2,1,0:T(4,128)S(1)} %pad_maximum_fusion), channel_id=1, source_target_pairs={{0,1},{1,2},{2,3},{4,5},{5,6},{6,7},{8,9},{9,10},{10,11},{12,13},{... | collective-permute-start | bytes 589832 | tf_op jit(solution)/shard_map/ppermute | solution.py:14
  35.8 0.7 copy-start.14
  35.8 6.5 %copy-start.2 = (f32[32,32,512]{2,1,0:T(8,128)S(1)}, f32[32,32,512]{2,1,0:T(8,128)}, u32[]{:S(2)}) copy-start(f32[32,32,512]{2,1,0:T(8,128)} %param.12) | copy-start | bytes 6291460
  36.5 74.0 %all-to-all-start.1 = ((bf16[32,48,1024]{2,1,0:T(8,128)(2,1)}), bf16[32,48,1024]{2,1,0:T(8,128)(2,1)}, u32[]{:S(2)}, u32[]{:S(2)}) async-start(bf16[32,48,1024]{2,1,0:T(8,128)(2,1)} %bitcast.63), calls=%async_computation.1 | async-start | bytes 6291456 | tf_op jit(solution)/shard_map/all_to_all | solution.py:52
  45.5 1.9 %copy-start.16 = (s32[8,8]{1,0:T(8,128)S(1)}, s32[8,8]{1,0:T(8,128)}, u32[]{:S(2)}) copy-start(s32[8,8]{1,0:T(8,128)} %param.21) | copy-start | bytes 772
  55.7 2.0 %copy-start.6 = (f32[32,32,512]{2,1,0:T(8,128)}, f32[32,32,512]{2,1,0:T(8,128)S(1)}, u32[]{:S(2)}) copy-start(f32[32,32,512]{2,1,0:T(8,128)S(1)} %get-tuple-element.44) | copy-start | bytes 6291460
  55.7 2.0 %copy-start.15 = (f32[32,3,512]{2,1,0:T(4,128)S(1)}, f32[32,3,512]{2,1,0:T(4,128)}, u32[]{:S(2)}) copy-start(f32[32,3,512]{2,1,0:T(4,128)} %copy-done.14) | copy-start | bytes 589828
  111.9 21.5 %all-to-all-start.2 = ((bf16[8,32,512]{2,1,0:T(8,128)(2,1)}), bf16[8,32,512]{2,1,0:T(8,128)(2,1)S(1)}, u32[]{:S(2)}, u32[]{:S(2)}) async-start(bf16[8,32,512]{2,1,0:T(8,128)(2,1)} %broadcast_select_fusion), calls=%async_computation.2 | async-start | bytes 524288 | tf_op jit(solution)/shard_map/all_to_all | solution.py:77
  128.9 1.9 %copy-start.12 = (f32[32,32,2,512]{3,1,2,0:T(8,128)}, f32[32,32,2,512]{3,1,2,0:T(8,128)S(1)}, u32[]{:S(2)}) copy-start(f32[32,32,2,512]{3,1,2,0:T(8,128)S(1)} %fusion) | copy-start | bytes 12582916
  142.9 5.6 %collective-permute-start.5 = (f32[1,32,512]{2,1,0:T(8,128)S(1)}, f32[1,32,512]{2,1,0:T(8,128)S(1)}, u32[]{:S(2)}, u32[]{:S(2)}) collective-permute-start(f32[1,32,512]{2,1,0:T(8,128)S(1)} %slice.173), channel_id=1, source_target_pairs={{0,4},{4,8},{8,12},{12,16},{16,20},{20,24},{24,28},{1,5},{5,9},{9,... | collective-permute-start | bytes 196616 | tf_op jit(solution)/shard_map/ppermute | solution.py:14
  145.0 6.5 %collective-permute-start.7 = (f32[32,1,512]{2,1,0:T(1,128)S(1)}, f32[32,1,512]{2,1,0:T(1,128)S(1)}, u32[]{:S(2)}, u32[]{:S(2)}) collective-permute-start(f32[32,1,512]{2,1,0:T(1,128)S(1)} %slice.177), channel_id=1, source_target_pairs={{0,1},{1,2},{2,3},{4,5},{5,6},{6,7},{8,9},{9,10},{10,11},{12,13},{... | collective-permute-start | bytes 196616 | tf_op jit(solution)/shard_map/ppermute | solution.py:14
  148.5 7.1 %collective-permute-start.4 = (f32[1,32,512]{2,1,0:T(8,128)S(1)}, f32[1,32,512]{2,1,0:T(8,128)S(1)}, u32[]{:S(2)}, u32[]{:S(2)}) collective-permute-start(f32[1,32,512]{2,1,0:T(8,128)S(1)} %get-tuple-element.48), channel_id=1, source_target_pairs={{4,0},{8,4},{12,8},{16,12},{20,16},{24,20},{28,24},{5,1},{9,5},{13... | collective-permute-start | bytes 196616 | tf_op jit(solution)/shard_map/ppermute | solution.py:14
  151.7 7.1 %collective-permute-start.6 = (f32[32,1,512]{2,1,0:T(1,128)S(1)}, f32[32,1,512]{2,1,0:T(1,128)S(1)}, u32[]{:S(2)}, u32[]{:S(2)}) collective-permute-start(f32[32,1,512]{2,1,0:T(1,128)S(1)} %get-tuple-element.46), channel_id=1, source_target_pairs={{1,0},{2,1},{3,2},{5,4},{6,5},{7,6},{9,8},{10,9},{11,10},{13,12},{... | collective-permute-start | bytes 196616 | tf_op jit(solution)/shard_map/ppermute | solution.py:14
  154.6 4.1 %copy-start.5 = (f32[32,32,512]{2,1,0:T(8,128)S(1)}, f32[32,32,512]{2,1,0:T(8,128)}, u32[]{:S(2)}) copy-start(f32[32,32,512]{2,1,0:T(8,128)} %get-tuple-element.43) | copy-start | bytes 6291460
  154.6 4.1 %copy-start.7 = (f32[32,32,512]{2,1,0:T(8,128)S(1)}, f32[32,32,512]{2,1,0:T(8,128)}, u32[]{:S(2)}) copy-start(f32[32,32,512]{2,1,0:T(8,128)} %copy-done.6) | copy-start | bytes 6291460
  155.2 3.5 %copy-start.3 = (f32[32,32,512]{2,1,0:T(8,128)S(1)}, f32[32,32,512]{2,1,0:T(8,128)}, u32[]{:S(2)}) copy-start(f32[32,32,512]{2,1,0:T(8,128)} %param.16) | copy-start | bytes 6291460
  155.3 3.5 %copy-start.4 = (f32[32,32,512]{2,1,0:T(8,128)S(1)}, f32[32,32,512]{2,1,0:T(8,128)}, u32[]{:S(2)}) copy-start(f32[32,32,512]{2,1,0:T(8,128)} %get-tuple-element.42) | copy-start | bytes 6291460
  161.6 6.7 %copy-start.8 = (f32[32,32,512]{2,1,0:T(8,128)}, f32[32,32,512]{2,1,0:T(8,128)S(1)}, u32[]{:S(2)}) copy-start(f32[32,32,512]{2,1,0:T(8,128)S(1)} %get-tuple-element.37) | copy-start | bytes 6291460
  161.6 6.7 %copy-start.9 = (f32[32,32,512]{2,1,0:T(8,128)}, f32[32,32,512]{2,1,0:T(8,128)S(1)}, u32[]{:S(2)}) copy-start(f32[32,32,512]{2,1,0:T(8,128)S(1)} %get-tuple-element.38) | copy-start | bytes 6291460
  161.6 6.7 %copy-start.10 = (f32[32,32,512]{2,1,0:T(8,128)}, f32[32,32,512]{2,1,0:T(8,128)S(1)}, u32[]{:S(2)}) copy-start(f32[32,32,512]{2,1,0:T(8,128)S(1)} %get-tuple-element.39) | copy-start | bytes 6291460
  161.6 3.2 %copy-start.11 = (f32[32,32,512]{2,1,0:T(8,128)S(1)}, f32[32,32,512]{2,1,0:T(8,128)}, u32[]{:S(2)}) copy-start(f32[32,32,512]{2,1,0:T(8,128)} %get-tuple-element.35) | copy-start | bytes 6291460
  164.8 3.6 %copy-start.1 = (bf16[16,32,512]{2,1,0:T(8,128)(2,1)S(1)}, bf16[16,32,512]{2,1,0:T(8,128)(2,1)}, u32[]{:S(2)}) copy-start(bf16[16,32,512]{2,1,0:T(8,128)(2,1)} %param.20) | copy-start | bytes 1572868

commit v9 on v3

--- a/solution.py
+++ b/solution.py
@@ -48,7 +48,6 @@
         concat_axis=0,
         tiled=True,
     )
-    in_cols, outgoing, ready = lax.optimization_barrier((in_cols, outgoing, ready))
     incoming = lax.all_to_all(
         outgoing.reshape(devices, capacity, steps * depth),
         ("gx", "gy"),

time: 162 us -> 168 us (1.037)
  waiting for transfers between devices: 58.2 us -> 69.4 us
  local copies, waits for them, and re-layouts: 26.2 us -> 23.6 us
  starting transfers between devices: 38.9 us -> 36.9 us
    ppermute x8, waiting for transfers between devices: 4.22 us -> 68.2 us  [from_behind(): return lax.ppermute(block, axis, route)]
    all_to_all x1, waiting for transfers between devices: 52.9 us -> 0.01 us  [bubble_source(): lax.all_to_all(outgoing.reshape(devices, capacity, steps * depth), ('gx',...]
    ppermute x8, starting transfers between devices: 22.2 us -> 18.4 us  [from_behind(): return lax.ppermute(block, axis, route)]
    all_to_all x1, starting transfers between devices: 5.68 us -> 7.41 us  [bubble_source(): lax.all_to_all(outgoing.reshape(devices, capacity, steps * depth), ('gx',...]
    unnamed x33 -> x27, local copies, waits for them, and re-layouts: 4.98 us -> 5.89 us
  transfers between devices with their start and end apart: 11 -> 11, of which waited for: 3 -> 6; matrix products, arithmetic and copies ran while one was open for 21% -> 18% of each run, Pallas kernels for 0% -> 0%
where the time goes in v9:
time: 168 us; the launch traced here: 167 us
  waiting for transfers between devices  69.4 us (41%)
  starting transfers between devices  36.9 us (22%)
  other arithmetic  24.9 us (15%)
  local copies, waits for them, and re-layouts  23.6 us (14%)
  matrix products  10.8 us (6%)
    ppermute x8, waiting for transfers between devices, from_behind(): return lax.ppermute(block, axis, route)  68.2 us
    ppermute x8, starting transfers between devices, from_behind(): return lax.ppermute(block, axis, route)  18.4 us
    sub x2, other arithmetic, body(): vel_z = vel_z - step_ratio * buoyancy * (next_z - pressure)  10.5 us
    all_to_all x1, starting transfers between devices, bubble_source(): lax.all_to_all(outgoing.reshape(devices, capacity, steps * depth), ('gx',...  7.41 us
    add x2, other arithmetic, body(): pressure + step_ratio * stiffness * (source[:, :, step, :] + forcing - di...  6.19 us
    all_to_all x1, starting transfers between devices, bubble_source(): lax.all_to_all(out_cols.reshape(devices, capacity), ('gx', 'gy'), split_a...  5.91 us
    unnamed x27, local copies, waits for them, and re-layouts  5.89 us
    dot_general x1, matrix products, bubble_source(): jnp.dot(hits, incoming.reshape(slots, steps * depth), preferred_element_t...  5.48 us
  transfers between devices with their start and end apart: 11, of which 6 were waited for; matrix products, arithmetic and copies ran while one was open for 18% of the time, Pallas kernels for 0%

profile of v9, /device:TPU:18, one launch (start us, length us, event | category | flops | bytes accessed | tf_op | source)
XLA Modules:
  0.0 166.8 jit_solution(3760669196608752940)
XLA Ops:
  2.2 1.7 %reduce-window.6 = s32[32,6,128]{2,0,1:T(8,128)S(1)} reduce-window(s32[32,6,128]{2,0,1:T(8,128)S(1)} %fusion.28, s32[]{:T(128)} %constant.87.clone.1), window={size=1x1x128 pad=0_0x0_0x127_0}, to_apply=%region_0.0 | reduce-window | flops 3121152 | bytes 196612 | tf_op jit(solution)/shard_map/reduce-window
  5.8 5.9 %all-to-all-start = ((s32[32,1,48]{2,1,0:T(1,128)}), s32[32,1,48]{2,1,0:T(1,128)S(1)}, u32[]{:S(2)}, u32[]{:S(2)}) async-start(s32[32,1,48]{2,1,0:T(1,128)} %sub.123), calls=%async_computation | async-start | bytes 32768 | tf_op jit(solution)/shard_map/all_to_all | solution.py:44
  14.8 1.6 copy.25
  16.4 5.2 %all-to-all-start.2 = ((bf16[8,32,512]{2,1,0:T(8,128)(2,1)}), bf16[8,32,512]{2,1,0:T(8,128)(2,1)S(1)}, u32[]{:S(2)}, u32[]{:S(2)}) async-start(bf16[8,32,512]{2,1,0:T(8,128)(2,1)} %broadcast_select_fusion), calls=%async_computation.2 | async-start | bytes 524288 | tf_op jit(solution)/shard_map/all_to_all | solution.py:76
  21.6 5.4 %fusion.4 = bf16[1536,1024]{1,0:T(8,128)(2,1)} fusion(bf16[768,1024]{1,0:T(8,128)(2,1)} %bitcast.65, s32[768]{0:T(1024)S(1)} %add_add_fusion), kind=kOutput, calls=%fused_computation.7 | convolution fusion | flops 2418671616 | bytes 4721664 | tf_op jit(solution)/shard_map/dot_general | solution.py:38
  26.9 1.1 all-to-all-done.2
  28.1 7.4 %all-to-all-start.1 = ((bf16[32,48,1024]{2,1,0:T(8,128)(2,1)}), bf16[32,48,1024]{2,1,0:T(8,128)(2,1)}, u32[]{:S(2)}, u32[]{:S(2)}) async-start(bf16[32,48,1024]{2,1,0:T(8,128)(2,1)} %bitcast.62), calls=%async_computation.1 | async-start | bytes 6291456 | tf_op jit(solution)/shard_map/all_to_all | solution.py:51
  35.6 2.1 %collective-permute-start.1 = (f32[3,32,512]{2,1,0:T(8,128)S(1)}, f32[3,32,512]{2,1,0:T(8,128)S(1)}, u32[]{:S(2)}, u32[]{:S(2)}) collective-permute-start(f32[3,32,512]{2,1,0:T(8,128)S(1)} %pad_maximum_fusion.1), channel_id=1, source_target_pairs={{0,4},{4,8},{8,12},{12,16},{16,20},{20,24},{24,28},{1,5},{5,9},{9,... | collective-permute-start | bytes 589832 | tf_op jit(solution)/shard_map/ppermute | solution.py:14
  37.6 1.1 slice.145
  38.8 1.1 slice.144
  40.1 3.4 %collective-permute-start.3 = (f32[32,3,512]{2,1,0:T(4,128)S(1)}, f32[32,3,512]{2,1,0:T(4,128)S(1)}, u32[]{:S(2)}, u32[]{:S(2)}) collective-permute-start(f32[32,3,512]{2,1,0:T(4,128)S(1)} %pad_maximum_fusion), channel_id=1, source_target_pairs={{0,1},{1,2},{2,3},{4,5},{5,6},{6,7},{8,9},{9,10},{10,11},{12,13},{... | collective-permute-start | bytes 589832 | tf_op jit(solution)/shard_map/ppermute | solution.py:14
  43.5 1.6 slice.132
  45.1 1.9 %slice.150 = f32[32,32,511]{2,1,0:T(8,128)} slice(f32[32,32,512]{2,1,0:T(8,128)S(1)} %copy-done.2), slice={[0:32], [0:32], [1:512]} | slice | bytes 4186112 | tf_op jit(solution)/shard_map/slice | solution.py:115
  47.0 1.7 %slice.141 = f32[32,31,512]{2,1,0:T(8,128)} slice(f32[32,32,512]{2,1,0:T(8,128)S(1)} %copy-done.2), slice={[0:32], [1:32], [0:512]} | slice | bytes 4063232 | tf_op jit(solution)/shard_map/slice | solution.py:114
  48.7 59.5 %collective-permute-done.1 = f32[3,32,512]{2,1,0:T(8,128)S(1)} collective-permute-done((f32[3,32,512]{2,1,0:T(8,128)S(1)}, f32[3,32,512]{2,1,0:T(8,128)S(1)}, u32[]{:S(2)}, u32[]{:S(2)}) %collective-permute-start.1) | collective-permute-done | bytes 196640 | tf_op jit(solution)/shard_map/ppermute | solution.py:14
  108.2 1.9 %collective-permute-start = (f32[1,32,512]{2,1,0:T(8,128)S(1)}, f32[1,32,512]{2,1,0:T(8,128)S(1)}, u32[]{:S(2)}, u32[]{:S(2)}) collective-permute-start(f32[1,32,512]{2,1,0:T(8,128)S(1)} %get-tuple-element.36), channel_id=1, source_target_pairs={{4,0},{8,4},{12,8},{16,12},{20,16},{24,20},{28,24},{5,1},{9,5},{13... | collective-permute-start | bytes 196616 | tf_op jit(solution)/shard_map/ppermute | solution.py:14
  110.4 2.1 %collective-permute-start.2 = (f32[32,1,512]{2,1,0:T(1,128)S(1)}, f32[32,1,512]{2,1,0:T(1,128)S(1)}, u32[]{:S(2)}, u32[]{:S(2)}) collective-permute-start(f32[32,1,512]{2,1,0:T(1,128)S(1)} %get-tuple-element.35), channel_id=1, source_target_pairs={{1,0},{2,1},{3,2},{5,4},{6,5},{7,6},{9,8},{10,9},{11,10},{13,12},{... | collective-permute-start | bytes 196616 | tf_op jit(solution)/shard_map/ppermute | solution.py:14
  113.8 3.9 %collective-permute-done.2 = f32[32,1,512]{2,1,0:T(1,128)S(1)} collective-permute-done((f32[32,1,512]{2,1,0:T(1,128)S(1)}, f32[32,1,512]{2,1,0:T(1,128)S(1)}, u32[]{:S(2)}, u32[]{:S(2)}) %collective-permute-start.2) | collective-permute-done | bytes 65568 | tf_op jit(solution)/shard_map/ppermute | solution.py:14
  117.7 7.7 %multiply_subtract_fusion.1 = (f32[32,32,512]{2,1,0:T(8,128)}, f32[32,32,512]{2,1,0:T(8,128)}, f32[32,32,512]{2,1,0:T(8,128)S(1)}) fusion(f32[32,32,512]{2,1,0:T(8,128)} %param.15, f32[32,32,512]{2,1,0:T(8,128)S(1)} %copy-done.2, f32[32,32,511]{2,1,0:T(8,128)} %slice.150, f32[32,32,512]{2,1,0:T(8,128)} %param.16, f32[32,32,512]{2,1,0:T(8,128)} %param.14, ...), kind=kLoop, calls=%fused_computation.40 | loop fusion | flops 8388608 | bytes 23064576 | tf_op jit(solution)/shard_map/sub | solution.py:118
  125.4 1.3 copy-done.6
  126.7 1.5 slice.170
  128.3 4.7 %copy.20 = bf16[1536,1024]{0,1:T(8,128)(2,1)} copy(bf16[1536,1024]{1,0:T(8,128)(2,1)} %bitcast.4) | data formatting | bytes 6291456 | tf_op jit(solution)/shard_map/reshape | solution.py:62
  133.0 5.5 %fusion = f32[32,32,2,512]{3,1,2,0:T(8,128)S(1)} fusion(bf16[2,512,1536,1]{2,1,0,3:T(8,128)(2,1)} %bitcast.63, s32[1536]{0:T(1024)S(1)} %eq.76, s32[32,32]{1,0:T(8,128)S(1)} %multiply_add_fusion), kind=kOutput, calls=%fused_computation.1 | convolution fusion | flops 3222798336 | bytes 7350272 | tf_op jit(solution)/shard_map/dot_general | solution.py:61
  141.9 2.5 %fusion.14 = f32[32,32,512]{2,1,0:T(8,128)S(1)} fusion(f32[32,32,512]{2,1,0:T(8,128)S(1)} %copy-done.2, f32[32,32,512]{2,1,0:T(8,128)S(1)} %get-tuple-element.22, f32[32,32,512]{2,1,0:T(8,128)S(1)} %copy-done.7, f32[31,32,512]{2,1,0:T(8,128)S(1)} %copy-done.11, f32[1,32,512]{2,1,0:T(8,128)S(1)} %get-tuple-element.19, f32[32,32,512]{2,1,0:T(8,128)S(1)} %copy-done.5, ...), kind=kLoop, calls=%fused_computation.21 | loop fusion | flops 7864320 | bytes 20967424 | tf_op jit(solution)/shard_map/add | solution.py:127
  144.5 1.9 %collective-permute-start.5 = (f32[1,32,512]{2,1,0:T(8,128)S(1)}, f32[1,32,512]{2,1,0:T(8,128)S(1)}, u32[]{:S(2)}, u32[]{:S(2)}) collective-permute-start(f32[1,32,512]{2,1,0:T(8,128)S(1)} %slice.179), channel_id=1, source_target_pairs={{0,4},{4,8},{8,12},{12,16},{16,20},{20,24},{24,28},{1,5},{5,9},{9,... | collective-permute-start | bytes 196616 | tf_op jit(solution)/shard_map/ppermute | solution.py:14
  146.5 1.9 %collective-permute-start.7 = (f32[32,1,512]{2,1,0:T(1,128)S(1)}, f32[32,1,512]{2,1,0:T(1,128)S(1)}, u32[]{:S(2)}, u32[]{:S(2)}) collective-permute-start(f32[32,1,512]{2,1,0:T(1,128)S(1)} %slice.183), channel_id=1, source_target_pairs={{0,1},{1,2},{2,3},{4,5},{5,6},{6,7},{8,9},{9,10},{10,11},{12,13},{... | collective-permute-start | bytes 196616 | tf_op jit(solution)/shard_map/ppermute | solution.py:14
  148.4 1.7 collective-permute-done.5
  150.1 2.0 %collective-permute-start.4 = (f32[1,32,512]{2,1,0:T(8,128)S(1)}, f32[1,32,512]{2,1,0:T(8,128)S(1)}, u32[]{:S(2)}, u32[]{:S(2)}) collective-permute-start(f32[1,32,512]{2,1,0:T(8,128)S(1)} %get-tuple-element.34), channel_id=1, source_target_pairs={{4,0},{8,4},{12,8},{16,12},{20,16},{24,20},{28,24},{5,1},{9,5},{13... | collective-permute-start | bytes 196616 | tf_op jit(solution)/shard_map/ppermute | solution.py:14
  152.8 3.1 %collective-permute-start.6 = (f32[32,1,512]{2,1,0:T(1,128)S(1)}, f32[32,1,512]{2,1,0:T(1,128)S(1)}, u32[]{:S(2)}, u32[]{:S(2)}) collective-permute-start(f32[32,1,512]{2,1,0:T(1,128)S(1)} %get-tuple-element.32), channel_id=1, source_target_pairs={{1,0},{2,1},{3,2},{5,4},{6,5},{7,6},{9,8},{10,9},{11,10},{13,12},{... | collective-permute-start | bytes 196616 | tf_op jit(solution)/shard_map/ppermute | solution.py:14
  157.2 2.7 %collective-permute-done.6 = f32[32,1,512]{2,1,0:T(1,128)S(1)} collective-permute-done((f32[32,1,512]{2,1,0:T(1,128)S(1)}, f32[32,1,512]{2,1,0:T(1,128)S(1)}, u32[]{:S(2)}, u32[]{:S(2)}) %collective-permute-start.6) | collective-permute-done | bytes 65568 | tf_op jit(solution)/shard_map/ppermute | solution.py:14
  159.9 2.8 %multiply_subtract_fusion = (f32[32,32,512]{2,1,0:T(8,128)S(1)}, f32[32,32,512]{2,1,0:T(8,128)S(1)}, f32[32,32,512]{2,1,0:T(8,128)S(1)}) fusion(f32[32,32,512]{2,1,0:T(8,128)S(1)} %copy-done.4, f32[32,32,512]{2,1,0:T(8,128)S(1)} %fusion.14, f32[32,32,511]{2,1,0:T(8,128)S(1)} %slice.185, f32[32,32,512]{2,1,0:T(8,128)S(1)} %copy-done.3, ...), kind=kLoop, calls=%fused_computation.39 | loop fusion | flops 8388608 | bytes 23064576 | tf_op jit(solution)/shard_map/sub | solution.py:118
  163.0 3.7 %fusion.23 = f32[32,32,512]{2,1,0:T(8,128)} fusion(f32[32,32,512]{2,1,0:T(8,128)S(1)} %fusion.14, f32[32,32,512]{2,1,0:T(8,128)S(1)} %get-tuple-element.21, f32[32,32,512]{2,1,0:T(8,128)S(1)} %get-tuple-element.25, f32[31,32,512]{2,1,0:T(8,128)S(1)} %slice.180, f32[1,32,512]{2,1,0:T(8,128)S(1)} %get-tuple-element.33, ...), kind=kLoop, calls=%fused_computation.34 | loop fusion | flops 7864320 | bytes 20967424 | tf_op jit(solution)/shard_map/add | solution.py:127
  (73 shorter events, 14.2 us)
Async XLA Ops:
  0.6 12.8 %copy-start = (bf16[16,32,512]{2,1,0:T(8,128)(2,1)S(1)}, bf16[16,32,512]{2,1,0:T(8,128)(2,1)}, u32[]{:S(2)}) copy-start(bf16[16,32,512]{2,1,0:T(8,128)(2,1)} %param.20) | copy-start | bytes 1572868
  0.6 14.2 %copy-start.12 = (bf16[768,2,512]{2,1,0:T(2,128)(2,1)S(1)}, bf16[768,2,512]{2,1,0:T(2,128)(2,1)}, u32[]{:S(2)}) copy-start(bf16[768,2,512]{2,1,0:T(2,128)(2,1)} %param.17) | copy-start | bytes 4718596
  5.8 10.6 %all-to-all-start = ((s32[32,1,48]{2,1,0:T(1,128)}), s32[32,1,48]{2,1,0:T(1,128)S(1)}, u32[]{:S(2)}, u32[]{:S(2)}) async-start(s32[32,1,48]{2,1,0:T(1,128)} %sub.123), calls=%async_computation | async-start | bytes 32768 | tf_op jit(solution)/shard_map/all_to_all | solution.py:44
  16.4 11.7 %all-to-all-start.2 = ((bf16[8,32,512]{2,1,0:T(8,128)(2,1)}), bf16[8,32,512]{2,1,0:T(8,128)(2,1)S(1)}, u32[]{:S(2)}, u32[]{:S(2)}) async-start(bf16[8,32,512]{2,1,0:T(8,128)(2,1)} %broadcast_select_fusion), calls=%async_computation.2 | async-start | bytes 524288 | tf_op jit(solution)/shard_map/all_to_all | solution.py:76
  28.1 7.4 %slice-start = ((f32[32,32,512]{2,1,0:T(8,128)}), f32[1,32,512]{2,1,0:T(8,128)S(1)}, s32[]{:S(2)}) async-start(f32[32,32,512]{2,1,0:T(8,128)} %param.12), calls=%async_computation.3 | async-start | bytes 131072 | tf_op jit(solution)/shard_map/slice | solution.py:94
  28.1 7.4 %slice-start.1 = ((f32[32,32,512]{2,1,0:T(8,128)}), f32[1,32,512]{2,1,0:T(8,128)S(1)}, s32[]{:S(2)}) async-start(f32[32,32,512]{2,1,0:T(8,128)} %param.16), calls=%async_computation.4 | async-start | bytes 131072 | tf_op jit(solution)/shard_map/slice | solution.py:94
  28.1 7.4 %slice-start.2 = ((f32[32,32,512]{2,1,0:T(8,128)}), f32[1,32,512]{2,1,0:T(8,128)S(1)}, s32[]{:S(2)}) async-start(f32[32,32,512]{2,1,0:T(8,128)} %param.13), calls=%async_computation.5 | async-start | bytes 131072 | tf_op jit(solution)/shard_map/slice | solution.py:94
  28.1 10.7 %copy-start.2 = (f32[32,32,512]{2,1,0:T(8,128)S(1)}, f32[32,32,512]{2,1,0:T(8,128)}, u32[]{:S(2)}) copy-start(f32[32,32,512]{2,1,0:T(8,128)} %param.12) | copy-start | bytes 6291460
  28.1 100.2 %all-to-all-start.1 = ((bf16[32,48,1024]{2,1,0:T(8,128)(2,1)}), bf16[32,48,1024]{2,1,0:T(8,128)(2,1)}, u32[]{:S(2)}, u32[]{:S(2)}) async-start(bf16[32,48,1024]{2,1,0:T(8,128)(2,1)} %bitcast.62), calls=%async_computation.1 | async-start | bytes 6291456 | tf_op jit(solution)/shard_map/all_to_all | solution.py:51
  35.6 72.6 %collective-permute-start.1 = (f32[3,32,512]{2,1,0:T(8,128)S(1)}, f32[3,32,512]{2,1,0:T(8,128)S(1)}, u32[]{:S(2)}, u32[]{:S(2)}) collective-permute-start(f32[3,32,512]{2,1,0:T(8,128)S(1)} %pad_maximum_fusion.1), channel_id=1, source_target_pairs={{0,4},{4,8},{8,12},{12,16},{16,20},{20,24},{24,28},{1,5},{5,9},{9,... | collective-permute-start | bytes 589832 | tf_op jit(solution)/shard_map/ppermute | solution.py:14
  40.1 70.0 %collective-permute-start.3 = (f32[32,3,512]{2,1,0:T(4,128)S(1)}, f32[32,3,512]{2,1,0:T(4,128)S(1)}, u32[]{:S(2)}, u32[]{:S(2)}) collective-permute-start(f32[32,3,512]{2,1,0:T(4,128)S(1)} %pad_maximum_fusion), channel_id=1, source_target_pairs={{0,1},{1,2},{2,3},{4,5},{5,6},{6,7},{8,9},{9,10},{10,11},{12,13},{... | collective-permute-start | bytes 589832 | tf_op jit(solution)/shard_map/ppermute | solution.py:14
  108.2 5.6 %collective-permute-start = (f32[1,32,512]{2,1,0:T(8,128)S(1)}, f32[1,32,512]{2,1,0:T(8,128)S(1)}, u32[]{:S(2)}, u32[]{:S(2)}) collective-permute-start(f32[1,32,512]{2,1,0:T(8,128)S(1)} %get-tuple-element.36), channel_id=1, source_target_pairs={{4,0},{8,4},{12,8},{16,12},{20,16},{24,20},{28,24},{5,1},{9,5},{13... | collective-permute-start | bytes 196616 | tf_op jit(solution)/shard_map/ppermute | solution.py:14
  110.4 7.3 %collective-permute-start.2 = (f32[32,1,512]{2,1,0:T(1,128)S(1)}, f32[32,1,512]{2,1,0:T(1,128)S(1)}, u32[]{:S(2)}, u32[]{:S(2)}) collective-permute-start(f32[32,1,512]{2,1,0:T(1,128)S(1)} %get-tuple-element.35), channel_id=1, source_target_pairs={{1,0},{2,1},{3,2},{5,4},{6,5},{7,6},{9,8},{10,9},{11,10},{13,12},{... | collective-permute-start | bytes 196616 | tf_op jit(solution)/shard_map/ppermute | solution.py:14
  125.4 1.3 copy-start.6
  133.0 6.0 %copy-start.11 = (f32[31,32,512]{2,1,0:T(8,128)S(1)}, f32[31,32,512]{2,1,0:T(8,128)}, u32[]{:S(2)}) copy-start(f32[31,32,512]{2,1,0:T(8,128)} %slice.170) | copy-start | bytes 6094852
  138.5 1.6 copy-start.3
  138.5 2.2 %copy-start.4 = (f32[32,32,512]{2,1,0:T(8,128)S(1)}, f32[32,32,512]{2,1,0:T(8,128)}, u32[]{:S(2)}) copy-start(f32[32,32,512]{2,1,0:T(8,128)} %get-tuple-element.28) | copy-start | bytes 6291460
  138.5 2.8 %copy-start.5 = (f32[32,32,512]{2,1,0:T(8,128)S(1)}, f32[32,32,512]{2,1,0:T(8,128)}, u32[]{:S(2)}) copy-start(f32[32,32,512]{2,1,0:T(8,128)} %get-tuple-element.29) | copy-start | bytes 6291460
  138.5 3.4 %copy-start.7 = (f32[32,32,512]{2,1,0:T(8,128)S(1)}, f32[32,32,512]{2,1,0:T(8,128)}, u32[]{:S(2)}) copy-start(f32[32,32,512]{2,1,0:T(8,128)} %copy-done.6) | copy-start | bytes 6291460
  144.5 5.6 %collective-permute-start.5 = (f32[1,32,512]{2,1,0:T(8,128)S(1)}, f32[1,32,512]{2,1,0:T(8,128)S(1)}, u32[]{:S(2)}, u32[]{:S(2)}) collective-permute-start(f32[1,32,512]{2,1,0:T(8,128)S(1)} %slice.179), channel_id=1, source_target_pairs={{0,4},{4,8},{8,12},{12,16},{16,20},{20,24},{24,28},{1,5},{5,9},{9,... | collective-permute-start | bytes 196616 | tf_op jit(solution)/shard_map/ppermute | solution.py:14
  146.5 6.2 %collective-permute-start.7 = (f32[32,1,512]{2,1,0:T(1,128)S(1)}, f32[32,1,512]{2,1,0:T(1,128)S(1)}, u32[]{:S(2)}, u32[]{:S(2)}) collective-permute-start(f32[32,1,512]{2,1,0:T(1,128)S(1)} %slice.183), channel_id=1, source_target_pairs={{0,1},{1,2},{2,3},{4,5},{5,6},{6,7},{8,9},{9,10},{10,11},{12,13},{... | collective-permute-start | bytes 196616 | tf_op jit(solution)/shard_map/ppermute | solution.py:14
  150.1 7.1 %collective-permute-start.4 = (f32[1,32,512]{2,1,0:T(8,128)S(1)}, f32[1,32,512]{2,1,0:T(8,128)S(1)}, u32[]{:S(2)}, u32[]{:S(2)}) collective-permute-start(f32[1,32,512]{2,1,0:T(8,128)S(1)} %get-tuple-element.34), channel_id=1, source_target_pairs={{4,0},{8,4},{12,8},{16,12},{20,16},{24,20},{28,24},{5,1},{9,5},{13... | collective-permute-start | bytes 196616 | tf_op jit(solution)/shard_map/ppermute | solution.py:14
  152.8 7.1 %collective-permute-start.6 = (f32[32,1,512]{2,1,0:T(1,128)S(1)}, f32[32,1,512]{2,1,0:T(1,128)S(1)}, u32[]{:S(2)}, u32[]{:S(2)}) collective-permute-start(f32[32,1,512]{2,1,0:T(1,128)S(1)} %get-tuple-element.32), channel_id=1, source_target_pairs={{1,0},{2,1},{3,2},{5,4},{6,5},{7,6},{9,8},{10,9},{11,10},{13,12},{... | collective-permute-start | bytes 196616 | tf_op jit(solution)/shard_map/ppermute | solution.py:14
  162.7 4.0 %copy-start.8 = (f32[32,32,512]{2,1,0:T(8,128)}, f32[32,32,512]{2,1,0:T(8,128)S(1)}, u32[]{:S(2)}) copy-start(f32[32,32,512]{2,1,0:T(8,128)S(1)} %get-tuple-element.23) | copy-start | bytes 6291460
  162.7 4.0 %copy-start.9 = (f32[32,32,512]{2,1,0:T(8,128)}, f32[32,32,512]{2,1,0:T(8,128)S(1)}, u32[]{:S(2)}) copy-start(f32[32,32,512]{2,1,0:T(8,128)S(1)} %get-tuple-element.24) | copy-start | bytes 6291460
  162.7 4.0 %copy-start.10 = (f32[32,32,512]{2,1,0:T(8,128)}, f32[32,32,512]{2,1,0:T(8,128)S(1)}, u32[]{:S(2)}) copy-start(f32[32,32,512]{2,1,0:T(8,128)S(1)} %get-tuple-element.25) | copy-start | bytes 6291460
  163.0 3.7 %copy-start.1 = (bf16[16,32,512]{2,1,0:T(8,128)(2,1)S(1)}, bf16[16,32,512]{2,1,0:T(8,128)(2,1)}, u32[]{:S(2)}) copy-start(bf16[16,32,512]{2,1,0:T(8,128)(2,1)} %param.20) | copy-start | bytes 1572868

commit v10 on v3

--- a/solution.py
+++ b/solution.py
@@ -12,6 +12,10 @@
     devices = range(lax.axis_size(axis))
     route = [(i - distance, i) for i in devices if i - distance in devices]
     return lax.ppermute(block, axis, route)
+
+
+def y_plane_from_behind(plane, axis, distance):
+    return from_behind(plane, axis, distance)[:, None, :]
 
 
 def material(void_frac):
@@ -90,13 +94,14 @@
     buoyancy, stiffness = material(void_frac)
 
     above_x = from_behind(pressure[0:1], "gx", -1)
-    above_y = from_behind(pressure[:, 0:1], "gy", -1)
+    above_y = y_plane_from_behind(pressure[:, 0], "gy", -1)
     below_x = from_behind(
         jnp.concatenate([pressure[-1:], vel_x[-1:], void_frac[-1:]], 0), "gx", 1
     )
     below_y = from_behind(
-        jnp.concatenate([pressure[:, -1:], vel_y[:, -1:], void_frac[:, -1:]], 1), "gy", 1
+        jnp.stack([pressure[:, -1], vel_y[:, -1], void_frac[:, -1]], 0), "gy", 1
     )
+    below_y = jnp.moveaxis(below_y, 0, 1)
 
     ready = (above_x, above_y, below_x, below_y)
     source, ready = bubble_source(waves, bubble_dest, bubble_column, size_x * size_y, ready)
@@ -130,9 +135,9 @@
         )
         if step + 1 < steps:
             above_x = from_behind(pressure[0:1], "gx", -1)
-            above_y = from_behind(pressure[:, 0:1], "gy", -1)
+            above_y = y_plane_from_behind(pressure[:, 0], "gy", -1)
             p_bx = from_behind(pressure[-1:], "gx", 1)
-            p_by = from_behind(pressure[:, -1:], "gy", 1)
+            p_by = y_plane_from_behind(pressure[:, -1], "gy", 1)
     return (pressure, vel_x, vel_y, vel_z)
 
 

time: 162 us -> 157 us (0.969)
  the two profiles are of different devices: /device:TPU:18 before, /device:TPU:21 now
where the time goes in v10:
time: 157 us
  waiting for transfers between devices  54.8 us (35%)
  starting transfers between devices  42.7 us (27%)
  local copies, waits for them, and re-layouts  24.7 us (16%)
  other arithmetic  22.3 us (14%)
  matrix products  10.9 us (7%)
    all_to_all x1, waiting for transfers between devices, bubble_source(): lax.all_to_all(outgoing.reshape(devices, capacity, steps * depth), ('gx',...  52.4 us
    ppermute x8, starting transfers between devices, from_behind(): return lax.ppermute(block, axis, route)  24.9 us
    sub x2, other arithmetic, body(): vel_z = vel_z - step_ratio * buoyancy * (next_z - pressure)  10.5 us
    all_to_all x1, starting transfers between devices, bubble_source(): lax.all_to_all(outgoing.reshape(devices, capacity, steps * depth), ('gx',...  7.57 us
    all_to_all x1, starting transfers between devices, bubble_source(): lax.all_to_all(out_cols.reshape(devices, capacity), ('gx', 'gy'), split_a...  6.2 us
    add x2, other arithmetic, body(): pressure + step_ratio * stiffness * (source[:, :, step, :] + forcing - di...  6.19 us
    dot_general x1, matrix products, bubble_source(): jnp.dot(hits, incoming.reshape(slots, steps * depth), preferred_element_t...  5.48 us
    dot_general x1, matrix products, bubble_source(): jnp.dot(placed.astype(jnp.bfloat16), waves.reshape(bubbles, steps * depth...  5.39 us
  transfers between devices with their start and end apart: 11, of which 3 were waited for; matrix products, arithmetic and copies ran while one was open for 19% of the time, Pallas kernels for 0%

profile of v10, /device:TPU:21, one launch (start us, length us, event | category | flops | bytes accessed | tf_op | source)
XLA Modules:
  0.0 156.7 jit_solution(867040097709782272)
XLA Ops:
  0.7 0.8 broadcast_add_fusion.1
  2.3 1.7 %reduce-window.6 = s32[32,6,128]{2,0,1:T(8,128)S(1)} reduce-window(s32[32,6,128]{2,0,1:T(8,128)S(1)} %fusion.28, s32[]{:T(128)} %constant.87.clone.1), window={size=1x1x128 pad=0_0x0_0x127_0}, to_apply=%region_0.0 | reduce-window | flops 3121152 | bytes 196612 | tf_op jit(solution)/shard_map/reduce-window
  5.8 6.2 %all-to-all-start = ((s32[32,1,48]{2,1,0:T(1,128)}), s32[32,1,48]{2,1,0:T(1,128)S(1)}, u32[]{:S(2)}, u32[]{:S(2)}) async-start(s32[32,1,48]{2,1,0:T(1,128)} %sub.123), calls=%async_computation | async-start | bytes 32768 | tf_op jit(solution)/shard_map/all_to_all | solution.py:48
  12.0 0.9 fusion.43
  12.9 2.3 %collective-permute-start = (f32[1,32,512]{2,1,0:T(8,128)S(1)}, f32[1,32,512]{2,1,0:T(8,128)S(1)}, u32[]{:S(2)}, u32[]{:S(2)}) collective-permute-start(f32[1,32,512]{2,1,0:T(8,128)S(1)} %get-tuple-element.49), channel_id=1, source_target_pairs={{4,0},{8,4},{12,8},{16,12},{20,16},{24,20},{28,24},{5,1},{9,5},{13... | collective-permute-start | bytes 196616 | tf_op jit(solution)/shard_map/ppermute | solution.py:14
  15.2 1.3 fusion.42
  16.5 3.1 %collective-permute-start.1 = (f32[32,512]{1,0:T(8,128)S(1)}, f32[32,512]{1,0:T(8,128)S(1)}, u32[]{:S(2)}, u32[]{:S(2)}) collective-permute-start(f32[32,512]{1,0:T(8,128)S(1)} %bitcast.101), channel_id=1, source_target_pairs={{1,0},{2,1},{3,2},{5,4},{6,5},{7,6},{9,8},{10,9},{11,10},{13,12},{... | collective-permute-start | bytes 196616 | tf_op jit(solution)/shard_map/ppermute | solution.py:14
  19.6 1.1 slice.137
  20.8 1.1 slice.138
  21.9 2.2 %collective-permute-start.3 = (f32[3,32,512]{2,1,0:T(8,128)S(1)}, f32[3,32,512]{2,1,0:T(8,128)S(1)}, u32[]{:S(2)}, u32[]{:S(2)}) collective-permute-start(f32[3,32,512]{2,1,0:T(8,128)S(1)} %pad_maximum_fusion.1), channel_id=1, source_target_pairs={{0,1},{1,2},{2,3},{4,5},{5,6},{6,7},{8,9},{9,10},{10,11},{12,13},{... | collective-permute-start | bytes 589832 | tf_op jit(solution)/shard_map/ppermute | solution.py:14
  24.2 3.9 %collective-permute-start.2 = (f32[3,32,512]{2,1,0:T(8,128)S(1)}, f32[3,32,512]{2,1,0:T(8,128)S(1)}, u32[]{:S(2)}, u32[]{:S(2)}) collective-permute-start(f32[3,32,512]{2,1,0:T(8,128)S(1)} %pad_maximum_fusion), channel_id=1, source_target_pairs={{0,4},{4,8},{8,12},{12,16},{16,20},{20,24},{24,28},{1,5},{5,9},{9,... | collective-permute-start | bytes 589832 | tf_op jit(solution)/shard_map/ppermute | solution.py:14
  29.8 1.6 %copy.58 = bf16[96,8,2,512]{3,1,2,0:T(8,128)(2,1)} copy(bf16[96,8,2,512]{3,2,1,0:T(2,128)(2,1)S(1)} %bitcast.92) | data formatting | bytes 3145728
  31.4 4.0 %all-to-all-start.2 = ((bf16[8,32,512]{2,1,0:T(8,128)(2,1)}), bf16[8,32,512]{2,1,0:T(8,128)(2,1)S(1)}, u32[]{:S(2)}, u32[]{:S(2)}) async-start(bf16[8,32,512]{2,1,0:T(8,128)(2,1)} %broadcast_select_fusion), calls=%async_computation.2 | async-start | bytes 524288 | tf_op jit(solution)/shard_map/all_to_all | solution.py:81
  35.3 5.4 %fusion.4 = bf16[1536,1024]{1,0:T(8,128)(2,1)} fusion(bf16[768,1024]{1,0:T(8,128)(2,1)} %bitcast.93, s32[768]{0:T(1024)S(1)} %add_add_fusion), kind=kOutput, calls=%fused_computation.7 | convolution fusion | flops 2418671616 | bytes 4721664 | tf_op jit(solution)/shard_map/dot_general | solution.py:42
  40.9 7.6 %all-to-all-start.1 = ((bf16[32,48,1024]{2,1,0:T(8,128)(2,1)}), bf16[32,48,1024]{2,1,0:T(8,128)(2,1)}, u32[]{:S(2)}, u32[]{:S(2)}) async-start(bf16[32,48,1024]{2,1,0:T(8,128)(2,1)} %bitcast.90), calls=%async_computation.1 | async-start | bytes 6291456 | tf_op jit(solution)/shard_map/all_to_all | solution.py:56
  48.5 1.5 slice.140
  50.0 1.9 %slice.150 = f32[32,32,511]{2,1,0:T(8,128)} slice(f32[32,32,512]{2,1,0:T(8,128)S(1)} %copy-done.2), slice={[0:32], [0:32], [1:512]} | slice | bytes 4186112 | tf_op jit(solution)/shard_map/slice | solution.py:121
  51.9 1.7 %slice.145 = f32[32,31,512]{2,1,0:T(8,128)} slice(f32[32,32,512]{2,1,0:T(8,128)S(1)} %copy-done.2), slice={[0:32], [1:32], [0:512]} | slice | bytes 4063232 | tf_op jit(solution)/shard_map/slice | solution.py:120
  53.9 7.7 %multiply_subtract_fusion.1 = (f32[32,32,512]{2,1,0:T(8,128)}, f32[32,32,512]{2,1,0:T(8,128)}, f32[32,32,512]{2,1,0:T(8,128)S(1)}) fusion(f32[32,32,512]{2,1,0:T(8,128)} %param.15, f32[32,32,512]{2,1,0:T(8,128)S(1)} %copy-done.2, f32[32,32,511]{2,1,0:T(8,128)} %slice.150, f32[32,32,512]{2,1,0:T(8,128)} %param.16, f32[32,32,512]{2,1,0:T(8,128)} %param.14, ...), kind=kLoop, calls=%fused_computation.40 | loop fusion | flops 8388608 | bytes 23064576 | tf_op jit(solution)/shard_map/sub | solution.py:124
  61.6 1.6 slice.167
  63.7 52.4 %all-to-all-done.1 = bf16[32,48,1024]{2,1,0:T(8,128)(2,1)} async-done(((bf16[32,48,1024]{2,1,0:T(8,128)(2,1)}), bf16[32,48,1024]{2,1,0:T(8,128)(2,1)}, u32[]{:S(2)}, u32[]{:S(2)}) %all-to-all-start.1) | async-done | bytes 3145760 | tf_op jit(solution)/shard_map/all_to_all | solution.py:56
  116.1 4.7 %copy.42 = bf16[1536,1024]{0,1:T(8,128)(2,1)} copy(bf16[1536,1024]{1,0:T(8,128)(2,1)} %bitcast.11) | data formatting | bytes 6291456 | tf_op jit(solution)/shard_map/reshape | solution.py:67
  120.8 5.5 %fusion = f32[32,32,2,512]{3,1,2,0:T(8,128)S(1)} fusion(bf16[2,512,1536,1]{2,1,0,3:T(8,128)(2,1)} %bitcast.91, s32[1536]{0:T(1024)S(1)} %eq.76, s32[32,32]{1,0:T(8,128)S(1)} %multiply_add_fusion), kind=kOutput, calls=%fused_computation.1 | convolution fusion | flops 3222798336 | bytes 7350272 | tf_op jit(solution)/shard_map/dot_general | solution.py:66
  126.8 1.1 copy-done.3
  129.7 2.5 %fusion.14 = f32[32,32,512]{2,1,0:T(8,128)S(1)} fusion(f32[32,32,512]{2,1,0:T(8,128)S(1)} %copy-done.2, f32[32,32,512]{2,1,0:T(8,128)S(1)} %get-tuple-element.33, f32[32,32,512]{2,1,0:T(8,128)S(1)} %copy-done.7, f32[31,32,512]{2,1,0:T(8,128)S(1)} %copy-done.11, f32[1,32,512]{2,1,0:T(8,128)S(1)} %get-tuple-element.30, f32[32,32,512]{2,1,0:T(8,128)S(1)} %copy-done.5, ...), kind=kLoop, calls=%fused_computation.21 | loop fusion | flops 7864320 | bytes 20967424 | tf_op jit(solution)/shard_map/add | solution.py:133
  132.4 3.1 %collective-permute-start.7 = (f32[32,512]{1,0:T(8,128)S(1)}, f32[32,512]{1,0:T(8,128)S(1)}, u32[]{:S(2)}, u32[]{:S(2)}) collective-permute-start(f32[32,512]{1,0:T(8,128)S(1)} %bitcast.102), channel_id=1, source_target_pairs={{0,1},{1,2},{2,3},{4,5},{5,6},{6,7},{8,9},{9,10},{10,11},{12,13},{... | collective-permute-start | bytes 196616 | tf_op jit(solution)/shard_map/ppermute | solution.py:14
  135.5 5.6 %collective-permute-start.5 = (f32[1,32,512]{2,1,0:T(8,128)S(1)}, f32[1,32,512]{2,1,0:T(8,128)S(1)}, u32[]{:S(2)}, u32[]{:S(2)}) collective-permute-start(f32[1,32,512]{2,1,0:T(8,128)S(1)} %slice.173), channel_id=1, source_target_pairs={{0,4},{4,8},{8,12},{12,16},{16,20},{20,24},{24,28},{1,5},{5,9},{9,... | collective-permute-start | bytes 196616 | tf_op jit(solution)/shard_map/ppermute | solution.py:14
  141.2 2.9 %collective-permute-start.6 = (f32[32,512]{1,0:T(8,128)S(1)}, f32[32,512]{1,0:T(8,128)S(1)}, u32[]{:S(2)}, u32[]{:S(2)}) collective-permute-start(f32[32,512]{1,0:T(8,128)S(1)} %get-tuple-element.51), channel_id=1, source_target_pairs={{1,0},{2,1},{3,2},{5,4},{6,5},{7,6},{9,8},{10,9},{11,10},{13,12},{... | collective-permute-start | bytes 196616 | tf_op jit(solution)/shard_map/ppermute | solution.py:14
  144.2 1.9 %collective-permute-start.4 = (f32[1,32,512]{2,1,0:T(8,128)S(1)}, f32[1,32,512]{2,1,0:T(8,128)S(1)}, u32[]{:S(2)}, u32[]{:S(2)}) collective-permute-start(f32[1,32,512]{2,1,0:T(8,128)S(1)} %get-tuple-element.45), channel_id=1, source_target_pairs={{4,0},{8,4},{12,8},{16,12},{20,16},{24,20},{28,24},{5,1},{9,5},{13... | collective-permute-start | bytes 196616 | tf_op jit(solution)/shard_map/ppermute | solution.py:14
  147.5 2.3 %collective-permute-done.4 = f32[1,32,512]{2,1,0:T(8,128)S(1)} collective-permute-done((f32[1,32,512]{2,1,0:T(8,128)S(1)}, f32[1,32,512]{2,1,0:T(8,128)S(1)}, u32[]{:S(2)}, u32[]{:S(2)}) %collective-permute-start.4) | collective-permute-done | bytes 65568 | tf_op jit(solution)/shard_map/ppermute | solution.py:14
  149.7 2.8 %multiply_subtract_fusion = (f32[32,32,512]{2,1,0:T(8,128)S(1)}, f32[32,32,512]{2,1,0:T(8,128)S(1)}, f32[32,32,512]{2,1,0:T(8,128)S(1)}) fusion(f32[32,32,512]{2,1,0:T(8,128)S(1)} %copy-done.4, f32[32,32,512]{2,1,0:T(8,128)S(1)} %fusion.14, f32[32,32,511]{2,1,0:T(8,128)S(1)} %slice.179, f32[32,32,512]{2,1,0:T(8,128)S(1)} %copy-done.3, ...), kind=kLoop, calls=%fused_computation.39 | loop fusion | flops 8388608 | bytes 23064576 | tf_op jit(solution)/shard_map/sub | solution.py:124
  152.9 3.7 %fusion.23 = f32[32,32,512]{2,1,0:T(8,128)} fusion(f32[32,32,512]{2,1,0:T(8,128)S(1)} %fusion.14, f32[32,32,512]{2,1,0:T(8,128)S(1)} %get-tuple-element.32, f32[32,32,512]{2,1,0:T(8,128)S(1)} %get-tuple-element.36, f32[31,32,512]{2,1,0:T(8,128)S(1)} %slice.174, f32[1,32,512]{2,1,0:T(8,128)S(1)} %get-tuple-element.44, ...), kind=kLoop, calls=%fused_computation.34 | loop fusion | flops 7864320 | bytes 20967424 | tf_op jit(solution)/shard_map/add | solution.py:133
  (81 shorter events, 9.5 us)
Async XLA Ops:
  0.6 27.8 %copy-start = (bf16[16,32,512]{2,1,0:T(8,128)(2,1)S(1)}, bf16[16,32,512]{2,1,0:T(8,128)(2,1)}, u32[]{:S(2)}) copy-start(bf16[16,32,512]{2,1,0:T(8,128)(2,1)} %param.20) | copy-start | bytes 1572868
  0.6 23.5 %slice-start = ((f32[32,32,512]{2,1,0:T(8,128)}), f32[1,32,512]{2,1,0:T(8,128)S(1)}, s32[]{:S(2)}) async-start(f32[32,32,512]{2,1,0:T(8,128)} %param.16), calls=%async_computation.3 | async-start | bytes 131072 | tf_op jit(solution)/shard_map/slice | solution.py:99
  0.7 23.5 %slice-start.1 = ((f32[32,32,512]{2,1,0:T(8,128)}), f32[1,32,512]{2,1,0:T(8,128)S(1)}, s32[]{:S(2)}) async-start(f32[32,32,512]{2,1,0:T(8,128)} %param.13), calls=%async_computation.4 | async-start | bytes 131072 | tf_op jit(solution)/shard_map/slice | solution.py:99
  0.7 27.4 %copy-start.13 = (s32[8,8]{1,0:T(8,128)S(1)}, s32[8,8]{1,0:T(8,128)}, u32[]{:S(2)}) copy-start(s32[8,8]{1,0:T(8,128)} %param.21) | copy-start | bytes 772
  0.7 29.1 %copy-start.12 = (bf16[768,2,512]{2,1,0:T(2,128)(2,1)S(1)}, bf16[768,2,512]{2,1,0:T(2,128)(2,1)}, u32[]{:S(2)}) copy-start(bf16[768,2,512]{2,1,0:T(2,128)(2,1)} %param.17) | copy-start | bytes 4718596
  5.8 25.6 %all-to-all-start = ((s32[32,1,48]{2,1,0:T(1,128)}), s32[32,1,48]{2,1,0:T(1,128)S(1)}, u32[]{:S(2)}, u32[]{:S(2)}) async-start(s32[32,1,48]{2,1,0:T(1,128)} %sub.123), calls=%async_computation | async-start | bytes 32768 | tf_op jit(solution)/shard_map/all_to_all | solution.py:48
  12.9 27.8 %collective-permute-start = (f32[1,32,512]{2,1,0:T(8,128)S(1)}, f32[1,32,512]{2,1,0:T(8,128)S(1)}, u32[]{:S(2)}, u32[]{:S(2)}) collective-permute-start(f32[1,32,512]{2,1,0:T(8,128)S(1)} %get-tuple-element.49), channel_id=1, source_target_pairs={{4,0},{8,4},{12,8},{16,12},{20,16},{24,20},{28,24},{5,1},{9,5},{13... | collective-permute-start | bytes 196616 | tf_op jit(solution)/shard_map/ppermute | solution.py:14
  16.5 24.2 %collective-permute-start.1 = (f32[32,512]{1,0:T(8,128)S(1)}, f32[32,512]{1,0:T(8,128)S(1)}, u32[]{:S(2)}, u32[]{:S(2)}) collective-permute-start(f32[32,512]{1,0:T(8,128)S(1)} %bitcast.101), channel_id=1, source_target_pairs={{1,0},{2,1},{3,2},{5,4},{6,5},{7,6},{9,8},{10,9},{11,10},{13,12},{... | collective-permute-start | bytes 196616 | tf_op jit(solution)/shard_map/ppermute | solution.py:14
  21.9 18.8 %collective-permute-start.3 = (f32[3,32,512]{2,1,0:T(8,128)S(1)}, f32[3,32,512]{2,1,0:T(8,128)S(1)}, u32[]{:S(2)}, u32[]{:S(2)}) collective-permute-start(f32[3,32,512]{2,1,0:T(8,128)S(1)} %pad_maximum_fusion.1), channel_id=1, source_target_pairs={{0,1},{1,2},{2,3},{4,5},{5,6},{6,7},{8,9},{9,10},{10,11},{12,13},{... | collective-permute-start | bytes 589832 | tf_op jit(solution)/shard_map/ppermute | solution.py:14
  24.2 16.6 %collective-permute-start.2 = (f32[3,32,512]{2,1,0:T(8,128)S(1)}, f32[3,32,512]{2,1,0:T(8,128)S(1)}, u32[]{:S(2)}, u32[]{:S(2)}) collective-permute-start(f32[3,32,512]{2,1,0:T(8,128)S(1)} %pad_maximum_fusion), channel_id=1, source_target_pairs={{0,4},{4,8},{8,12},{12,16},{16,20},{20,24},{24,28},{1,5},{5,9},{9,... | collective-permute-start | bytes 589832 | tf_op jit(solution)/shard_map/ppermute | solution.py:14
  31.4 9.5 %all-to-all-start.2 = ((bf16[8,32,512]{2,1,0:T(8,128)(2,1)}), bf16[8,32,512]{2,1,0:T(8,128)(2,1)S(1)}, u32[]{:S(2)}, u32[]{:S(2)}) async-start(bf16[8,32,512]{2,1,0:T(8,128)(2,1)} %broadcast_select_fusion), calls=%async_computation.2 | async-start | bytes 524288 | tf_op jit(solution)/shard_map/all_to_all | solution.py:81
  40.9 7.6 %copy-start.2 = (f32[32,32,512]{2,1,0:T(8,128)S(1)}, f32[32,32,512]{2,1,0:T(8,128)}, u32[]{:S(2)}) copy-start(f32[32,32,512]{2,1,0:T(8,128)} %param.12) | copy-start | bytes 6291460
  40.9 75.2 %all-to-all-start.1 = ((bf16[32,48,1024]{2,1,0:T(8,128)(2,1)}), bf16[32,48,1024]{2,1,0:T(8,128)(2,1)}, u32[]{:S(2)}, u32[]{:S(2)}) async-start(bf16[32,48,1024]{2,1,0:T(8,128)(2,1)} %bitcast.90), calls=%async_computation.1 | async-start | bytes 6291456 | tf_op jit(solution)/shard_map/all_to_all | solution.py:56
  61.6 2.0 %copy-start.6 = (f32[32,32,512]{2,1,0:T(8,128)}, f32[32,32,512]{2,1,0:T(8,128)S(1)}, u32[]{:S(2)}) copy-start(f32[32,32,512]{2,1,0:T(8,128)S(1)} %get-tuple-element.41) | copy-start | bytes 6291460
  120.8 6.0 %copy-start.11 = (f32[31,32,512]{2,1,0:T(8,128)S(1)}, f32[31,32,512]{2,1,0:T(8,128)}, u32[]{:S(2)}) copy-start(f32[31,32,512]{2,1,0:T(8,128)} %slice.167) | copy-start | bytes 6094852
  126.3 1.6 %copy-start.3 = (f32[32,32,512]{2,1,0:T(8,128)S(1)}, f32[32,32,512]{2,1,0:T(8,128)}, u32[]{:S(2)}) copy-start(f32[32,32,512]{2,1,0:T(8,128)} %param.16) | copy-start | bytes 6291460
  126.3 2.2 %copy-start.4 = (f32[32,32,512]{2,1,0:T(8,128)S(1)}, f32[32,32,512]{2,1,0:T(8,128)}, u32[]{:S(2)}) copy-start(f32[32,32,512]{2,1,0:T(8,128)} %get-tuple-element.39) | copy-start | bytes 6291460
  126.3 2.8 %copy-start.5 = (f32[32,32,512]{2,1,0:T(8,128)S(1)}, f32[32,32,512]{2,1,0:T(8,128)}, u32[]{:S(2)}) copy-start(f32[32,32,512]{2,1,0:T(8,128)} %get-tuple-element.40) | copy-start | bytes 6291460
  126.3 3.4 %copy-start.7 = (f32[32,32,512]{2,1,0:T(8,128)S(1)}, f32[32,32,512]{2,1,0:T(8,128)}, u32[]{:S(2)}) copy-start(f32[32,32,512]{2,1,0:T(8,128)} %copy-done.6) | copy-start | bytes 6291460
  132.4 8.7 %collective-permute-start.7 = (f32[32,512]{1,0:T(8,128)S(1)}, f32[32,512]{1,0:T(8,128)S(1)}, u32[]{:S(2)}, u32[]{:S(2)}) collective-permute-start(f32[32,512]{1,0:T(8,128)S(1)} %bitcast.102), channel_id=1, source_target_pairs={{0,1},{1,2},{2,3},{4,5},{5,6},{6,7},{8,9},{9,10},{10,11},{12,13},{... | collective-permute-start | bytes 196616 | tf_op jit(solution)/shard_map/ppermute | solution.py:14
  135.5 8.6 %collective-permute-start.5 = (f32[1,32,512]{2,1,0:T(8,128)S(1)}, f32[1,32,512]{2,1,0:T(8,128)S(1)}, u32[]{:S(2)}, u32[]{:S(2)}) collective-permute-start(f32[1,32,512]{2,1,0:T(8,128)S(1)} %slice.173), channel_id=1, source_target_pairs={{0,4},{4,8},{8,12},{12,16},{16,20},{20,24},{24,28},{1,5},{5,9},{9,... | collective-permute-start | bytes 196616 | tf_op jit(solution)/shard_map/ppermute | solution.py:14
  141.2 6.2 %collective-permute-start.6 = (f32[32,512]{1,0:T(8,128)S(1)}, f32[32,512]{1,0:T(8,128)S(1)}, u32[]{:S(2)}, u32[]{:S(2)}) collective-permute-start(f32[32,512]{1,0:T(8,128)S(1)} %get-tuple-element.51), channel_id=1, source_target_pairs={{1,0},{2,1},{3,2},{5,4},{6,5},{7,6},{9,8},{10,9},{11,10},{13,12},{... | collective-permute-start | bytes 196616 | tf_op jit(solution)/shard_map/ppermute | solution.py:14
  144.2 5.6 %collective-permute-start.4 = (f32[1,32,512]{2,1,0:T(8,128)S(1)}, f32[1,32,512]{2,1,0:T(8,128)S(1)}, u32[]{:S(2)}, u32[]{:S(2)}) collective-permute-start(f32[1,32,512]{2,1,0:T(8,128)S(1)} %get-tuple-element.45), channel_id=1, source_target_pairs={{4,0},{8,4},{12,8},{16,12},{20,16},{24,20},{28,24},{5,1},{9,5},{13... | collective-permute-start | bytes 196616 | tf_op jit(solution)/shard_map/ppermute | solution.py:14
  152.6 4.0 %copy-start.8 = (f32[32,32,512]{2,1,0:T(8,128)}, f32[32,32,512]{2,1,0:T(8,128)S(1)}, u32[]{:S(2)}) copy-start(f32[32,32,512]{2,1,0:T(8,128)S(1)} %get-tuple-element.34) | copy-start | bytes 6291460
  152.6 4.0 %copy-start.9 = (f32[32,32,512]{2,1,0:T(8,128)}, f32[32,32,512]{2,1,0:T(8,128)S(1)}, u32[]{:S(2)}) copy-start(f32[32,32,512]{2,1,0:T(8,128)S(1)} %get-tuple-element.35) | copy-start | bytes 6291460
  152.6 4.0 %copy-start.10 = (f32[32,32,512]{2,1,0:T(8,128)}, f32[32,32,512]{2,1,0:T(8,128)S(1)}, u32[]{:S(2)}) copy-start(f32[32,32,512]{2,1,0:T(8,128)S(1)} %get-tuple-element.36) | copy-start | bytes 6291460
  152.9 3.7 %copy-start.1 = (bf16[16,32,512]{2,1,0:T(8,128)(2,1)S(1)}, bf16[16,32,512]{2,1,0:T(8,128)(2,1)}, u32[]{:S(2)}) copy-start(bf16[16,32,512]{2,1,0:T(8,128)(2,1)} %param.20) | copy-start | bytes 1572868

commit v11 on v10

--- a/solution.py
+++ b/solution.py
@@ -11,7 +11,8 @@
 def from_behind(block, axis, distance):
     devices = range(lax.axis_size(axis))
     route = [(i - distance, i) for i in devices if i - distance in devices]
-    return lax.ppermute(block, axis, route)
+    sent = lax.ppermute(block.astype(jnp.bfloat16), axis, route)
+    return sent.astype(jnp.float32)
 
 
 def y_plane_from_behind(plane, axis, distance):

time: 157 us -> 159 us (1.013)
  the two profiles are of different devices: /device:TPU:21 before, /device:TPU:3 now
where the time goes in v11:
time: 159 us
  waiting for transfers between devices  58.6 us (37%)
  starting transfers between devices  37.8 us (24%)
  local copies, waits for them, and re-layouts  26 us (16%)
  other arithmetic  24.1 us (15%)
  matrix products  10.8 us (7%)
    all_to_all x1, waiting for transfers between devices, bubble_source(): lax.all_to_all(outgoing.reshape(devices, capacity, steps * depth), ('gx',...  55.4 us
    ppermute x8, starting transfers between devices, from_behind(): sent = lax.ppermute(block.astype(jnp.bfloat16), axis, route)  23.1 us
    sub x1, other arithmetic, body(): vel_x = vel_x - step_ratio * buoyancy * (next_x - pressure)  7.71 us
    unnamed x36, local copies, waits for them, and re-layouts  6.55 us
    all_to_all x1, starting transfers between devices, bubble_source(): lax.all_to_all(out_cols.reshape(devices, capacity), ('gx', 'gy'), split_a...  6.3 us
    another operation x5, other arithmetic  6.24 us
    dot_general x1, matrix products, bubble_source(): jnp.dot(hits, incoming.reshape(slots, steps * depth), preferred_element_t...  5.48 us
    dot_general x1, matrix products, bubble_source(): jnp.dot(placed.astype(jnp.bfloat16), waves.reshape(bubbles, steps * depth...  5.37 us
  transfers between devices with their start and end apart: 11, of which 2 were waited for; matrix products, arithmetic and copies ran while one was open for 24% of the time, Pallas kernels for 0%

profile of v11, /device:TPU:3, one launch (start us, length us, event | category | flops | bytes accessed | tf_op | source)
XLA Modules:
  0.0 158.6 jit_solution(14249316015764877626)
XLA Ops:
  0.7 1.0 slice.219
  1.7 2.6 %collective-permute-start = (bf16[1,32,512]{2,1,0:T(8,128)(2,1)S(1)}, bf16[1,32,512]{2,1,0:T(8,128)(2,1)S(1)}, u32[]{:S(2)}, u32[]{:S(2)}) collective-permute-start(bf16[1,32,512]{2,1,0:T(8,128)(2,1)S(1)} %slice.219), channel_id=1, source_target_pairs={{4,0},{8,4},{12,8},{16,12},{20,16},{24,20},{28,24},{5,1},{9,5},{13... | collective-permute-start | bytes 98312 | tf_op jit(solution)/shard_map/ppermute | solution.py:14
  4.2 1.1 slice.140
  5.3 1.9 %collective-permute-start.1 = (bf16[32,512]{1,0:T(8,128)(2,1)S(1)}, bf16[32,512]{1,0:T(8,128)(2,1)S(1)}, u32[]{:S(2)}, u32[]{:S(2)}) collective-permute-start(bf16[32,512]{1,0:T(8,128)(2,1)S(1)} %bitcast.96), channel_id=1, source_target_pairs={{1,0},{2,1},{3,2},{5,4},{6,5},{7,6},{9,8},{10,9},{11,10},{13,12},{... | collective-permute-start | bytes 98312 | tf_op jit(solution)/shard_map/ppermute | solution.py:14
  8.7 1.7 %reduce-window.6 = s32[32,6,128]{2,0,1:T(8,128)S(1)} reduce-window(s32[32,6,128]{2,0,1:T(8,128)S(1)} %fusion.28, s32[]{:T(128)} %constant.87.clone.1), window={size=1x1x128 pad=0_0x0_0x127_0}, to_apply=%region_0.0 | reduce-window | flops 3121152 | bytes 196612 | tf_op jit(solution)/shard_map/reduce-window
  12.3 6.3 %all-to-all-start = ((s32[32,1,48]{2,1,0:T(1,128)}), s32[32,1,48]{2,1,0:T(1,128)S(1)}, u32[]{:S(2)}, u32[]{:S(2)}) async-start(s32[32,1,48]{2,1,0:T(1,128)} %sub.123), calls=%async_computation | async-start | bytes 32768 | tf_op jit(solution)/shard_map/all_to_all | solution.py:49
  18.6 1.7 %convert.31 = bf16[32,32,512]{2,1,0:T(8,128)(2,1)S(1)} convert(f32[32,32,512]{2,1,0:T(8,128)} %param.12) | non-fusion elementwise | flops 524288 | bytes 3145728 | tf_op jit(solution)/shard_map/convert.20
  21.4 3.5 %collective-permute-start.2 = (bf16[3,32,512]{2,1,0:T(8,128)(2,1)S(1)}, bf16[3,32,512]{2,1,0:T(8,128)(2,1)S(1)}, u32[]{:S(2)}, u32[]{:S(2)}) collective-permute-start(bf16[3,32,512]{2,1,0:T(8,128)(2,1)S(1)} %pad_maximum_fusion), channel_id=1, source_target_pairs={{0,4},{4,8},{8,12},{12,16},{16,20},{20,24},{24,28},{1,5},{5,9},{9,... | collective-permute-start | bytes 294920 | tf_op jit(solution)/shard_map/ppermute | solution.py:14
  25.0 1.1 slice.178
  26.2 3.1 %collective-permute-start.3 = (bf16[3,32,512]{2,1,0:T(8,128)(2,1)S(1)}, bf16[3,32,512]{2,1,0:T(8,128)(2,1)S(1)}, u32[]{:S(2)}, u32[]{:S(2)}) collective-permute-start(bf16[3,32,512]{2,1,0:T(8,128)(2,1)S(1)} %pad_maximum_fusion.1), channel_id=1, source_target_pairs={{0,1},{1,2},{2,3},{4,5},{5,6},{6,7},{8,9},{9,10},{10,11},{12,13},{... | collective-permute-start | bytes 294920 | tf_op jit(solution)/shard_map/ppermute | solution.py:14
  31.1 1.6 copy.187
  32.6 4.0 %all-to-all-start.2 = ((bf16[8,32,512]{2,1,0:T(8,128)(2,1)}), bf16[8,32,512]{2,1,0:T(8,128)(2,1)S(1)}, u32[]{:S(2)}, u32[]{:S(2)}) async-start(bf16[8,32,512]{2,1,0:T(8,128)(2,1)} %broadcast_select_fusion), calls=%async_computation.2 | async-start | bytes 524288 | tf_op jit(solution)/shard_map/all_to_all | solution.py:82
  36.6 5.4 %fusion.4 = bf16[1536,1024]{1,0:T(8,128)(2,1)} fusion(bf16[768,1024]{1,0:T(8,128)(2,1)} %bitcast.92, s32[768]{0:T(1024)S(1)} %add_add_fusion), kind=kOutput, calls=%fused_computation.7 | convolution fusion | flops 2418671616 | bytes 4721664 | tf_op jit(solution)/shard_map/dot_general | solution.py:43
  42.1 3.2 %all-to-all-done.2 = bf16[8,32,512]{2,1,0:T(8,128)(2,1)S(1)} async-done(((bf16[8,32,512]{2,1,0:T(8,128)(2,1)}), bf16[8,32,512]{2,1,0:T(8,128)(2,1)S(1)}, u32[]{:S(2)}, u32[]{:S(2)}) %all-to-all-start.2) | async-done | bytes 262176 | tf_op jit(solution)/shard_map/all_to_all | solution.py:82
  45.3 4.5 %all-to-all-start.1 = ((bf16[32,48,1024]{2,1,0:T(8,128)(2,1)}), bf16[32,48,1024]{2,1,0:T(8,128)(2,1)}, u32[]{:S(2)}, u32[]{:S(2)}) async-start(bf16[32,48,1024]{2,1,0:T(8,128)(2,1)} %bitcast.89), calls=%async_computation.1 | async-start | bytes 6291456 | tf_op jit(solution)/shard_map/all_to_all | solution.py:57
  49.8 1.5 slice.148
  51.3 1.7 %slice.153 = f32[32,31,512]{2,1,0:T(8,128)} slice(f32[32,32,512]{2,1,0:T(8,128)S(1)} %copy-done.2), slice={[0:32], [1:32], [0:512]} | slice | bytes 4063232 | tf_op jit(solution)/shard_map/slice | solution.py:121
  53.1 1.9 %slice.158 = f32[32,32,511]{2,1,0:T(8,128)} slice(f32[32,32,512]{2,1,0:T(8,128)S(1)} %copy-done.2), slice={[0:32], [0:32], [1:512]} | slice | bytes 4186112 | tf_op jit(solution)/shard_map/slice | solution.py:122
  55.2 7.7 %fusion.9 = (f32[32,32,512]{2,1,0:T(8,128)S(1)}, f32[32,32,512]{2,1,0:T(8,128)}, f32[32,32,512]{2,1,0:T(8,128)}) fusion(f32[32,32,512]{2,1,0:T(8,128)} %param.13, f32[32,32,512]{2,1,0:T(8,128)S(1)} %copy-done.2, f32[1,32,512]{2,1,0:T(8,128)S(1)} %convert_element_type.64, f32[31,32,512]{2,1,0:T(8,128)} %slice.148, f32[32,32,512]{2,1,0:T(8,128)} %param.16, ...), kind=kLoop, calls=%fused_computation.15 | loop fusion | flops 8388608 | bytes 23064576 | tf_op jit(solution)/shard_map/sub | solution.py:123
  62.9 1.6 slice.181
  65.0 55.4 %all-to-all-done.1 = bf16[32,48,1024]{2,1,0:T(8,128)(2,1)} async-done(((bf16[32,48,1024]{2,1,0:T(8,128)(2,1)}), bf16[32,48,1024]{2,1,0:T(8,128)(2,1)}, u32[]{:S(2)}, u32[]{:S(2)}) %all-to-all-start.1) | async-done | bytes 3145760 | tf_op jit(solution)/shard_map/all_to_all | solution.py:57
  120.4 4.6 %copy.170 = bf16[1536,1024]{0,1:T(8,128)(2,1)} copy(bf16[1536,1024]{1,0:T(8,128)(2,1)} %bitcast.8) | data formatting | bytes 6291456 | tf_op jit(solution)/shard_map/reshape | solution.py:68
  125.0 5.5 %fusion = f32[32,32,2,512]{3,1,2,0:T(8,128)S(1)} fusion(bf16[2,512,1536,1]{2,1,0,3:T(8,128)(2,1)} %bitcast.90, s32[1536]{0:T(1024)S(1)} %eq.76, s32[32,32]{1,0:T(8,128)S(1)} %multiply_add_fusion), kind=kOutput, calls=%fused_computation.1 | convolution fusion | flops 3222798336 | bytes 7350272 | tf_op jit(solution)/shard_map/dot_general | solution.py:67
  131.1 1.1 copy-done.4
  134.0 2.6 %fusion.44 = (bf16[32,32,512]{2,1,0:T(8,128)(2,1)S(1)}, f32[32,32,512]{2,1,0:T(8,128)S(1)}) fusion(f32[32,32,512]{2,1,0:T(8,128)S(1)} %copy-done.2, f32[32,32,512]{2,1,0:T(8,128)S(1)} %get-tuple-element.47, f32[32,32,512]{2,1,0:T(8,128)S(1)} %copy-done.6, f32[32,32,511]{2,1,0:T(8,128)S(1)} %bitcast.86, f32[32,32,512]{2,1,0:T(8,128)S(1)} %copy-done.5, ...), kind=kLoop, calls=%fused_computation.99 | loop fusion | flops 8388608 | bytes 22016000 | tf_op jit(solution)/shard_map/convert.5
  136.6 2.1 %collective-permute-start.6 = (bf16[32,512]{1,0:T(8,128)(2,1)S(1)}, bf16[32,512]{1,0:T(8,128)(2,1)S(1)}, u32[]{:S(2)}, u32[]{:S(2)}) collective-permute-start(bf16[32,512]{1,0:T(8,128)(2,1)S(1)} %bitcast.98), channel_id=1, source_target_pairs={{1,0},{2,1},{3,2},{5,4},{6,5},{7,6},{9,8},{10,9},{11,10},{13,12},{... | collective-permute-start | bytes 98312 | tf_op jit(solution)/shard_map/ppermute | solution.py:14
  140.1 3.1 %collective-permute-start.4 = (bf16[1,32,512]{2,1,0:T(8,128)(2,1)S(1)}, bf16[1,32,512]{2,1,0:T(8,128)(2,1)S(1)}, u32[]{:S(2)}, u32[]{:S(2)}) collective-permute-start(bf16[1,32,512]{2,1,0:T(8,128)(2,1)S(1)} %slice.218), channel_id=1, source_target_pairs={{4,0},{8,4},{12,8},{16,12},{20,16},{24,20},{28,24},{5,1},{9,5},{13... | collective-permute-start | bytes 98312 | tf_op jit(solution)/shard_map/ppermute | solution.py:14
  143.2 4.0 %collective-permute-start.7 = (bf16[32,512]{1,0:T(8,128)(2,1)S(1)}, bf16[32,512]{1,0:T(8,128)(2,1)S(1)}, u32[]{:S(2)}, u32[]{:S(2)}) collective-permute-start(bf16[32,512]{1,0:T(8,128)(2,1)S(1)} %bitcast.97), channel_id=1, source_target_pairs={{0,1},{1,2},{2,3},{4,5},{5,6},{6,7},{8,9},{9,10},{10,11},{12,13},{... | collective-permute-start | bytes 98312 | tf_op jit(solution)/shard_map/ppermute | solution.py:14
  147.3 2.8 %collective-permute-start.5 = (bf16[1,32,512]{2,1,0:T(8,128)(2,1)S(1)}, bf16[1,32,512]{2,1,0:T(8,128)(2,1)S(1)}, u32[]{:S(2)}, u32[]{:S(2)}) collective-permute-start(bf16[1,32,512]{2,1,0:T(8,128)(2,1)S(1)} %slice.187), channel_id=1, source_target_pairs={{0,4},{4,8},{8,12},{12,16},{16,20},{20,24},{24,28},{1,5},{5,9},{9,... | collective-permute-start | bytes 98312 | tf_op jit(solution)/shard_map/ppermute | solution.py:14
  150.2 2.8 %multiply_subtract_fusion = (f32[32,32,512]{2,1,0:T(8,128)S(1)}, f32[32,32,512]{2,1,0:T(8,128)S(1)}, f32[32,32,512]{2,1,0:T(8,128)S(1)}) fusion(f32[32,32,512]{2,1,0:T(8,128)S(1)} %copy-done.6, f32[32,32,512]{2,1,0:T(8,128)S(1)} %get-tuple-element.41, f32[32,32,511]{2,1,0:T(8,128)S(1)} %slice.193, f32[32,32,512]{2,1,0:T(8,128)S(1)} %copy-done.4, ...), kind=kLoop, calls=%fused_computation.39 | loop fusion | flops 8388608 | bytes 23064576 | tf_op jit(solution)/shard_map/sub | solution.py:125
  153.5 0.9 copy-done.9
  155.1 3.6 %fusion.23 = f32[32,32,512]{2,1,0:T(8,128)} fusion(f32[32,32,512]{2,1,0:T(8,128)S(1)} %get-tuple-element.41, f32[32,32,512]{2,1,0:T(8,128)S(1)} %get-tuple-element.46, f32[32,32,512]{2,1,0:T(8,128)S(1)} %get-tuple-element.50, f32[31,32,512]{2,1,0:T(8,128)S(1)} %slice.188, f32[1,32,512]{2,1,0:T(8,128)S(1)} %subtract_select_fusion, ...), kind=kLoop, calls=%fused_computation.34 | loop fusion | flops 7864320 | bytes 20967424 | tf_op jit(solution)/shard_map/add | solution.py:134
  (92 shorter events, 11.9 us)
Async XLA Ops:
  0.6 29.1 %copy-start = (bf16[16,32,512]{2,1,0:T(8,128)(2,1)S(1)}, bf16[16,32,512]{2,1,0:T(8,128)(2,1)}, u32[]{:S(2)}) copy-start(bf16[16,32,512]{2,1,0:T(8,128)(2,1)} %param.20) | copy-start | bytes 1572868
  0.6 20.5 %copy-start.3 = (f32[32,32,512]{2,1,0:T(8,128)S(1)}, f32[32,32,512]{2,1,0:T(8,128)}, u32[]{:S(2)}) copy-start(f32[32,32,512]{2,1,0:T(8,128)} %param.16) | copy-start | bytes 6291460
  1.7 40.3 %collective-permute-start = (bf16[1,32,512]{2,1,0:T(8,128)(2,1)S(1)}, bf16[1,32,512]{2,1,0:T(8,128)(2,1)S(1)}, u32[]{:S(2)}, u32[]{:S(2)}) collective-permute-start(bf16[1,32,512]{2,1,0:T(8,128)(2,1)S(1)} %slice.219), channel_id=1, source_target_pairs={{4,0},{8,4},{12,8},{16,12},{20,16},{24,20},{28,24},{5,1},{9,5},{13... | collective-permute-start | bytes 98312 | tf_op jit(solution)/shard_map/ppermute | solution.py:14
  5.3 36.7 %collective-permute-start.1 = (bf16[32,512]{1,0:T(8,128)(2,1)S(1)}, bf16[32,512]{1,0:T(8,128)(2,1)S(1)}, u32[]{:S(2)}, u32[]{:S(2)}) collective-permute-start(bf16[32,512]{1,0:T(8,128)(2,1)S(1)} %bitcast.96), channel_id=1, source_target_pairs={{1,0},{2,1},{3,2},{5,4},{6,5},{7,6},{9,8},{10,9},{11,10},{13,12},{... | collective-permute-start | bytes 98312 | tf_op jit(solution)/shard_map/ppermute | solution.py:14
  12.3 20.4 %all-to-all-start = ((s32[32,1,48]{2,1,0:T(1,128)}), s32[32,1,48]{2,1,0:T(1,128)S(1)}, u32[]{:S(2)}, u32[]{:S(2)}) async-start(s32[32,1,48]{2,1,0:T(1,128)} %sub.123), calls=%async_computation | async-start | bytes 32768 | tf_op jit(solution)/shard_map/all_to_all | solution.py:49
  21.2 8.1 %copy-start.14 = (s32[8,8]{1,0:T(8,128)S(1)}, s32[8,8]{1,0:T(8,128)}, u32[]{:S(2)}) copy-start(s32[8,8]{1,0:T(8,128)} %param.21) | copy-start | bytes 772
  21.3 9.8 %copy-start.13 = (bf16[768,2,512]{2,1,0:T(2,128)(2,1)S(1)}, bf16[768,2,512]{2,1,0:T(2,128)(2,1)}, u32[]{:S(2)}) copy-start(bf16[768,2,512]{2,1,0:T(2,128)(2,1)} %param.17) | copy-start | bytes 4718596
  21.4 20.7 %collective-permute-start.2 = (bf16[3,32,512]{2,1,0:T(8,128)(2,1)S(1)}, bf16[3,32,512]{2,1,0:T(8,128)(2,1)S(1)}, u32[]{:S(2)}, u32[]{:S(2)}) collective-permute-start(bf16[3,32,512]{2,1,0:T(8,128)(2,1)S(1)} %pad_maximum_fusion), channel_id=1, source_target_pairs={{0,4},{4,8},{8,12},{12,16},{16,20},{20,24},{24,28},{1,5},{5,9},{9,... | collective-permute-start | bytes 294920 | tf_op jit(solution)/shard_map/ppermute | solution.py:14
  26.2 15.9 %collective-permute-start.3 = (bf16[3,32,512]{2,1,0:T(8,128)(2,1)S(1)}, bf16[3,32,512]{2,1,0:T(8,128)(2,1)S(1)}, u32[]{:S(2)}, u32[]{:S(2)}) collective-permute-start(bf16[3,32,512]{2,1,0:T(8,128)(2,1)S(1)} %pad_maximum_fusion.1), channel_id=1, source_target_pairs={{0,1},{1,2},{2,3},{4,5},{5,6},{6,7},{8,9},{9,10},{10,11},{12,13},{... | collective-permute-start | bytes 294920 | tf_op jit(solution)/shard_map/ppermute | solution.py:14
  32.6 12.7 %all-to-all-start.2 = ((bf16[8,32,512]{2,1,0:T(8,128)(2,1)}), bf16[8,32,512]{2,1,0:T(8,128)(2,1)S(1)}, u32[]{:S(2)}, u32[]{:S(2)}) async-start(bf16[8,32,512]{2,1,0:T(8,128)(2,1)} %broadcast_select_fusion), calls=%async_computation.2 | async-start | bytes 524288 | tf_op jit(solution)/shard_map/all_to_all | solution.py:82
  45.3 4.5 %copy-start.2 = (f32[32,32,512]{2,1,0:T(8,128)S(1)}, f32[32,32,512]{2,1,0:T(8,128)}, u32[]{:S(2)}) copy-start(f32[32,32,512]{2,1,0:T(8,128)} %param.12) | copy-start | bytes 6291460
  45.3 75.0 %all-to-all-start.1 = ((bf16[32,48,1024]{2,1,0:T(8,128)(2,1)}), bf16[32,48,1024]{2,1,0:T(8,128)(2,1)}, u32[]{:S(2)}, u32[]{:S(2)}) async-start(bf16[32,48,1024]{2,1,0:T(8,128)(2,1)} %bitcast.89), calls=%async_computation.1 | async-start | bytes 6291456 | tf_op jit(solution)/shard_map/all_to_all | solution.py:57
  62.9 2.0 %copy-start.7 = (f32[32,32,512]{2,1,0:T(8,128)}, f32[32,32,512]{2,1,0:T(8,128)S(1)}, u32[]{:S(2)}) copy-start(f32[32,32,512]{2,1,0:T(8,128)S(1)} %get-tuple-element.53) | copy-start | bytes 6291460
  125.0 6.0 %copy-start.12 = (f32[31,32,512]{2,1,0:T(8,128)S(1)}, f32[31,32,512]{2,1,0:T(8,128)}, u32[]{:S(2)}) copy-start(f32[31,32,512]{2,1,0:T(8,128)} %slice.181) | copy-start | bytes 6094852
  130.5 1.6 %copy-start.4 = (f32[32,32,512]{2,1,0:T(8,128)S(1)}, f32[32,32,512]{2,1,0:T(8,128)}, u32[]{:S(2)}) copy-start(f32[32,32,512]{2,1,0:T(8,128)} %param.16) | copy-start | bytes 6291460
  130.5 2.2 %copy-start.5 = (f32[32,32,512]{2,1,0:T(8,128)S(1)}, f32[32,32,512]{2,1,0:T(8,128)}, u32[]{:S(2)}) copy-start(f32[32,32,512]{2,1,0:T(8,128)} %get-tuple-element.54) | copy-start | bytes 6291460
  130.5 2.8 %copy-start.6 = (f32[32,32,512]{2,1,0:T(8,128)S(1)}, f32[32,32,512]{2,1,0:T(8,128)}, u32[]{:S(2)}) copy-start(f32[32,32,512]{2,1,0:T(8,128)} %get-tuple-element.55) | copy-start | bytes 6291460
  130.6 3.4 %copy-start.8 = (f32[32,32,512]{2,1,0:T(8,128)S(1)}, f32[32,32,512]{2,1,0:T(8,128)}, u32[]{:S(2)}) copy-start(f32[32,32,512]{2,1,0:T(8,128)} %copy-done.7) | copy-start | bytes 6291460
  136.6 13.4 %collective-permute-start.6 = (bf16[32,512]{1,0:T(8,128)(2,1)S(1)}, bf16[32,512]{1,0:T(8,128)(2,1)S(1)}, u32[]{:S(2)}, u32[]{:S(2)}) collective-permute-start(bf16[32,512]{1,0:T(8,128)(2,1)S(1)} %bitcast.98), channel_id=1, source_target_pairs={{1,0},{2,1},{3,2},{5,4},{6,5},{7,6},{9,8},{10,9},{11,10},{13,12},{... | collective-permute-start | bytes 98312 | tf_op jit(solution)/shard_map/ppermute | solution.py:14
  140.1 10.0 %collective-permute-start.4 = (bf16[1,32,512]{2,1,0:T(8,128)(2,1)S(1)}, bf16[1,32,512]{2,1,0:T(8,128)(2,1)S(1)}, u32[]{:S(2)}, u32[]{:S(2)}) collective-permute-start(bf16[1,32,512]{2,1,0:T(8,128)(2,1)S(1)} %slice.218), channel_id=1, source_target_pairs={{4,0},{8,4},{12,8},{16,12},{20,16},{24,20},{28,24},{5,1},{9,5},{13... | collective-permute-start | bytes 98312 | tf_op jit(solution)/shard_map/ppermute | solution.py:14
  143.2 9.9 %collective-permute-start.7 = (bf16[32,512]{1,0:T(8,128)(2,1)S(1)}, bf16[32,512]{1,0:T(8,128)(2,1)S(1)}, u32[]{:S(2)}, u32[]{:S(2)}) collective-permute-start(bf16[32,512]{1,0:T(8,128)(2,1)S(1)} %bitcast.97), channel_id=1, source_target_pairs={{0,1},{1,2},{2,3},{4,5},{5,6},{6,7},{8,9},{9,10},{10,11},{12,13},{... | collective-permute-start | bytes 98312 | tf_op jit(solution)/shard_map/ppermute | solution.py:14
  147.3 6.2 %collective-permute-start.5 = (bf16[1,32,512]{2,1,0:T(8,128)(2,1)S(1)}, bf16[1,32,512]{2,1,0:T(8,128)(2,1)S(1)}, u32[]{:S(2)}, u32[]{:S(2)}) collective-permute-start(bf16[1,32,512]{2,1,0:T(8,128)(2,1)S(1)} %slice.187), channel_id=1, source_target_pairs={{0,4},{4,8},{8,12},{12,16},{16,20},{20,24},{24,28},{1,5},{5,9},{9,... | collective-permute-start | bytes 98312 | tf_op jit(solution)/shard_map/ppermute | solution.py:14
  153.0 1.3 copy-start.9
  153.0 2.0 %copy-start.10 = (f32[32,32,512]{2,1,0:T(8,128)}, f32[32,32,512]{2,1,0:T(8,128)S(1)}, u32[]{:S(2)}) copy-start(f32[32,32,512]{2,1,0:T(8,128)S(1)} %get-tuple-element.49) | copy-start | bytes 6291460
  153.1 5.6 %copy-start.11 = (f32[32,32,512]{2,1,0:T(8,128)}, f32[32,32,512]{2,1,0:T(8,128)S(1)}, u32[]{:S(2)}) copy-start(f32[32,32,512]{2,1,0:T(8,128)S(1)} %get-tuple-element.50) | copy-start | bytes 6291460
  155.0 3.6 %copy-start.1 = (bf16[16,32,512]{2,1,0:T(8,128)(2,1)S(1)}, bf16[16,32,512]{2,1,0:T(8,128)(2,1)}, u32[]{:S(2)}) copy-start(bf16[16,32,512]{2,1,0:T(8,128)(2,1)} %param.20) | copy-start | bytes 1572868

commit v12 on v10

--- a/solution.py
+++ b/solution.py
@@ -66,7 +66,7 @@
     source = jnp.dot(
         hits, incoming.reshape(slots, steps * depth), preferred_element_type=jnp.float32
     )
-    return source, ready
+    return source, incoming, ready
 
 
 def incident_plane(history, delays, size_y, depth):
@@ -104,8 +104,11 @@
     below_y = jnp.moveaxis(below_y, 0, 1)
 
     ready = (above_x, above_y, below_x, below_y)
-    source, ready = bubble_source(waves, bubble_dest, bubble_column, size_x * size_y, ready)
+    source, incoming, ready = bubble_source(
+        waves, bubble_dest, bubble_column, size_x * size_y, ready
+    )
     above_x, above_y, below_x, below_y = ready
+    history, _ = lax.optimization_barrier((history, incoming))
     incident = incident_plane(history, delays, size_y, depth)
     source = source.reshape(size_x, size_y, steps, depth)
     p_bx, vx_bx, void_bx = below_x[0:1], below_x[1:2], below_x[2:3]
@@ -130,8 +133,10 @@
         prev_y = jnp.concatenate([lower_y, vel_y[:, :-1]], 1)
         prev_z = jnp.concatenate([z_edge, vel_z[:, :, :-1]], 2)
         divergence = vel_x - prev_x + (vel_y - prev_y) + (vel_z - prev_z)
+        if step + 1 < steps:
+            divergence = lax.optimization_barrier(divergence)
         pressure = pressure + step_ratio * stiffness * (
-            source[:, :, step, :] + forcing - divergence
+            source[:, :, step, :] - divergence + forcing
         )
         if step + 1 < steps:
             above_x = from_behind(pressure[0:1], "gx", -1)

time: 157 us -> 157 us (level)
  the two profiles are of different devices: /device:TPU:21 before, /device:TPU:18 now
where the time goes in v12:
time: 157 us; the launch traced here: 155 us
  waiting for transfers between devices  53.2 us (34%)
  starting transfers between devices  38.2 us (24%)
  other arithmetic  28 us (18%)
  local copies, waits for them, and re-layouts  25.3 us (16%)
  matrix products  9.53 us (6%)
    all_to_all x1, waiting for transfers between devices, bubble_source(): lax.all_to_all(outgoing.reshape(devices, capacity, steps * depth), ('gx',...  50.3 us
    ppermute x8, starting transfers between devices, from_behind(): return lax.ppermute(block, axis, route)  20.3 us
    sub x2, other arithmetic, body(): vel_z = vel_z - step_ratio * buoyancy * (next_z - pressure)  8.61 us
    unnamed x42, local copies, waits for them, and re-layouts  7.41 us
    all_to_all x1, starting transfers between devices, incident_plane(): rows = lax.all_to_all(chosen, 'gx', split_axis=0, concat_axis=0, tiled=True)  7.06 us
    all_to_all x1, starting transfers between devices, bubble_source(): lax.all_to_all(out_cols.reshape(devices, capacity), ('gx', 'gy'), split_a...  5.91 us
    dot_general x1, matrix products, bubble_source(): jnp.dot(hits, incoming.reshape(slots, steps * depth), preferred_element_t...  5.48 us
    add x2, other arithmetic, body(): pressure + step_ratio * stiffness * (source[:, :, step, :] - divergence +...  5.09 us
  transfers between devices with their start and end apart: 11, of which 5 were waited for; matrix products, arithmetic and copies ran while one was open for 24% of the time, Pallas kernels for 0%

profile of v12, /device:TPU:18, one launch (start us, length us, event | category | flops | bytes accessed | tf_op | source)
XLA Modules:
  0.0 155.4 jit_solution(2902041281432155459)
XLA Ops:
  2.2 1.7 %reduce-window.6 = s32[32,6,128]{2,0,1:T(8,128)S(1)} reduce-window(s32[32,6,128]{2,0,1:T(8,128)S(1)} %fusion.24, s32[]{:T(128)} %constant.85.clone.1), window={size=1x1x128 pad=0_0x0_0x127_0}, to_apply=%region_0.0 | reduce-window | flops 3121152 | bytes 196612 | tf_op jit(solution)/shard_map/reduce-window
  5.8 5.9 %all-to-all-start = ((s32[32,1,48]{2,1,0:T(1,128)}), s32[32,1,48]{2,1,0:T(1,128)S(1)}, u32[]{:S(2)}, u32[]{:S(2)}) async-start(s32[32,1,48]{2,1,0:T(1,128)} %sub.127), calls=%async_computation | async-start | bytes 32768 | tf_op jit(solution)/shard_map/all_to_all | solution.py:48
  12.6 2.2 %collective-permute-start = (f32[1,32,512]{2,1,0:T(8,128)S(1)}, f32[1,32,512]{2,1,0:T(8,128)S(1)}, u32[]{:S(2)}, u32[]{:S(2)}) collective-permute-start(f32[1,32,512]{2,1,0:T(8,128)S(1)} %get-tuple-element.47), channel_id=1, source_target_pairs={{4,0},{8,4},{12,8},{16,12},{20,16},{24,20},{28,24},{5,1},{9,5},{13... | collective-permute-start | bytes 196616 | tf_op jit(solution)/shard_map/ppermute | solution.py:14
  14.9 1.3 fusion.36
  16.2 2.5 %collective-permute-start.1 = (f32[32,512]{1,0:T(8,128)S(1)}, f32[32,512]{1,0:T(8,128)S(1)}, u32[]{:S(2)}, u32[]{:S(2)}) collective-permute-start(f32[32,512]{1,0:T(8,128)S(1)} %bitcast.93), channel_id=1, source_target_pairs={{1,0},{2,1},{3,2},{5,4},{6,5},{7,6},{9,8},{10,9},{11,10},{13,12},{... | collective-permute-start | bytes 196616 | tf_op jit(solution)/shard_map/ppermute | solution.py:14
  18.7 1.1 slice.135
  19.8 1.1 slice.136
  20.9 4.3 %collective-permute-start.3 = (f32[3,32,512]{2,1,0:T(8,128)S(1)}, f32[3,32,512]{2,1,0:T(8,128)S(1)}, u32[]{:S(2)}, u32[]{:S(2)}) collective-permute-start(f32[3,32,512]{2,1,0:T(8,128)S(1)} %pad_maximum_fusion.1), channel_id=1, source_target_pairs={{0,1},{1,2},{2,3},{4,5},{5,6},{6,7},{8,9},{9,10},{10,11},{12,13},{... | collective-permute-start | bytes 589832 | tf_op jit(solution)/shard_map/ppermute | solution.py:14
  25.3 1.9 %collective-permute-start.2 = (f32[3,32,512]{2,1,0:T(8,128)S(1)}, f32[3,32,512]{2,1,0:T(8,128)S(1)}, u32[]{:S(2)}, u32[]{:S(2)}) collective-permute-start(f32[3,32,512]{2,1,0:T(8,128)S(1)} %pad_maximum_fusion), channel_id=1, source_target_pairs={{0,4},{4,8},{8,12},{12,16},{16,20},{20,24},{24,28},{1,5},{5,9},{9,... | collective-permute-start | bytes 589832 | tf_op jit(solution)/shard_map/ppermute | solution.py:14
  27.6 4.0 %fusion.4 = bf16[1536,1024]{1,0:T(8,128)(2,1)} fusion(bf16[768,1024]{1,0:T(8,128)(2,1)S(1)} %bitcast.85, s32[768]{0:T(1024)S(1)} %add_add_fusion), kind=kOutput, calls=%fused_computation.7 | convolution fusion | flops 2418671616 | bytes 4721664 | tf_op jit(solution)/shard_map/dot_general | solution.py:42
  32.3 4.9 %all-to-all-start.1 = ((bf16[32,48,1024]{2,1,0:T(8,128)(2,1)}), bf16[32,48,1024]{2,1,0:T(8,128)(2,1)}, u32[]{:S(2)}, u32[]{:S(2)}) async-start(bf16[32,48,1024]{2,1,0:T(8,128)(2,1)} %bitcast.82), calls=%async_computation.1 | async-start | bytes 6291456 | tf_op jit(solution)/shard_map/all_to_all | solution.py:56
  37.2 1.5 slice.138
  38.7 1.9 %slice.148 = f32[32,32,511]{2,1,0:T(8,128)} slice(f32[32,32,512]{2,1,0:T(8,128)S(1)} %copy-done.2), slice={[0:32], [0:32], [1:512]} | slice | bytes 4186112 | tf_op jit(solution)/shard_map/slice | solution.py:124
  40.6 1.7 %slice.143 = f32[32,31,512]{2,1,0:T(8,128)} slice(f32[32,32,512]{2,1,0:T(8,128)S(1)} %copy-done.2), slice={[0:32], [1:32], [0:512]} | slice | bytes 4063232 | tf_op jit(solution)/shard_map/slice | solution.py:123
  43.0 6.4 %multiply_subtract_fusion.1 = (f32[32,32,512]{2,1,0:T(8,128)S(1)}, f32[32,32,512]{2,1,0:T(8,128)S(1)}, f32[32,32,512]{2,1,0:T(8,128)S(1)}) fusion(f32[32,32,512]{2,1,0:T(8,128)} %param.15, f32[32,32,512]{2,1,0:T(8,128)S(1)} %copy-done.2, f32[32,32,511]{2,1,0:T(8,128)} %slice.148, f32[32,32,512]{2,1,0:T(8,128)} %param.16, f32[32,32,512]{2,1,0:T(8,128)} %param.14, ...), kind=kLoop, calls=%fused_computation.38 | loop fusion | flops 8388608 | bytes 23064576 | tf_op jit(solution)/shard_map/sub | solution.py:127
  52.1 3.1 %fusion.13 = f32[32,32,512]{2,1,0:T(8,128)} fusion(f32[32,32,512]{2,1,0:T(8,128)S(1)} %get-tuple-element.39, f32[31,32,512]{2,1,0:T(8,128)S(1)} %slice.165, f32[1,32,512]{2,1,0:T(8,128)S(1)} %get-tuple-element.32, f32[32,32,512]{2,1,0:T(8,128)S(1)} %get-tuple-element.38, f32[32,31,512]{2,1,0:T(8,128)S(1)} %bitcast.79, f32[32,1,512]{2,1,0:T(1,128)S(1)} %copy.45, ...), kind=kLoop, calls=%fused_computation.20 | loop fusion | flops 3670016 | bytes 14675968 | tf_op jit(solution)/shard_map/add | solution.py:135
  55.2 50.3 %all-to-all-done.1 = bf16[32,48,1024]{2,1,0:T(8,128)(2,1)} async-done(((bf16[32,48,1024]{2,1,0:T(8,128)(2,1)}), bf16[32,48,1024]{2,1,0:T(8,128)(2,1)}, u32[]{:S(2)}, u32[]{:S(2)}) %all-to-all-start.1) | async-done | bytes 3145760 | tf_op jit(solution)/shard_map/all_to_all | solution.py:56
  106.8 7.1 %all-to-all-start.2 = ((bf16[8,32,512]{2,1,0:T(8,128)(2,1)}), bf16[8,32,512]{2,1,0:T(8,128)(2,1)S(1)}, u32[]{:S(2)}, u32[]{:S(2)}) async-start(bf16[8,32,512]{2,1,0:T(8,128)(2,1)} %broadcast_select_fusion), calls=%async_computation.2 | async-start | bytes 524288 | tf_op jit(solution)/shard_map/all_to_all | solution.py:81
  113.9 4.7 %copy.42 = bf16[1536,1024]{0,1:T(8,128)(2,1)} copy(bf16[1536,1024]{1,0:T(8,128)(2,1)} %bitcast.11) | data formatting | bytes 6291456 | tf_op jit(solution)/shard_map/reshape | solution.py:67
  118.5 5.5 %fusion = f32[32,32,2,512]{3,1,2,0:T(8,128)S(1)} fusion(bf16[2,512,1536,1]{2,1,0,3:T(8,128)(2,1)} %bitcast.83, s32[1536]{0:T(1024)S(1)} %eq.76, s32[32,32]{1,0:T(8,128)S(1)} %multiply_add_fusion.2), kind=kOutput, calls=%fused_computation.1 | convolution fusion | flops 3222798336 | bytes 7350272 | tf_op jit(solution)/shard_map/dot_general | solution.py:66
  124.0 1.9 %copy-done.14 = f32[32,32,2,512]{3,1,2,0:T(8,128)} copy-done((f32[32,32,2,512]{3,1,2,0:T(8,128)}, f32[32,32,2,512]{3,1,2,0:T(8,128)S(1)}, u32[]{:S(2)}) %copy-start.14) | copy-done | bytes 4194328
  126.0 1.8 %fusion.9 = f32[32,32,512]{2,1,0:T(8,128)} fusion(f32[32,32,512]{2,1,0:T(8,128)S(1)} %copy-done.13, f32[32,32,2,512]{3,1,2,0:T(8,128)S(1)} %fusion), kind=kLoop, calls=%fused_computation.14 | loop fusion | flops 524288 | bytes 6291456 | tf_op jit(solution)/shard_map/sub | solution.py:139
  127.9 1.5 fusion.26
  129.4 3.0 %multiply_add_fusion.1 = f32[32,32,512]{2,1,0:T(8,128)S(1)} fusion(f32[32,32,512]{2,1,0:T(8,128)S(1)} %copy-done.2, f32[32,32,512]{2,1,0:T(8,128)} %fusion.26, f32[32,32,512]{2,1,0:T(8,128)} %param.16), kind=kLoop, calls=%fused_computation.37 | loop fusion | flops 3670016 | bytes 8388608 | tf_op jit(solution)/shard_map/add | solution.py:138
  132.5 2.9 %collective-permute-start.7 = (f32[32,512]{1,0:T(8,128)S(1)}, f32[32,512]{1,0:T(8,128)S(1)}, u32[]{:S(2)}, u32[]{:S(2)}) collective-permute-start(f32[32,512]{1,0:T(8,128)S(1)} %bitcast.94), channel_id=1, source_target_pairs={{0,1},{1,2},{2,3},{4,5},{5,6},{6,7},{8,9},{9,10},{10,11},{12,13},{... | collective-permute-start | bytes 196616 | tf_op jit(solution)/shard_map/ppermute | solution.py:14
  135.5 1.9 %collective-permute-start.5 = (f32[1,32,512]{2,1,0:T(8,128)S(1)}, f32[1,32,512]{2,1,0:T(8,128)S(1)}, u32[]{:S(2)}, u32[]{:S(2)}) collective-permute-start(f32[1,32,512]{2,1,0:T(8,128)S(1)} %slice.171), channel_id=1, source_target_pairs={{0,4},{4,8},{8,12},{12,16},{16,20},{20,24},{24,28},{1,5},{5,9},{9,... | collective-permute-start | bytes 196616 | tf_op jit(solution)/shard_map/ppermute | solution.py:14
  137.4 1.3 collective-permute-done.7
  138.7 1.9 %collective-permute-start.6 = (f32[32,512]{1,0:T(8,128)S(1)}, f32[32,512]{1,0:T(8,128)S(1)}, u32[]{:S(2)}, u32[]{:S(2)}) collective-permute-start(f32[32,512]{1,0:T(8,128)S(1)} %get-tuple-element.49), channel_id=1, source_target_pairs={{1,0},{2,1},{3,2},{5,4},{6,5},{7,6},{9,8},{10,9},{11,10},{13,12},{... | collective-permute-start | bytes 196616 | tf_op jit(solution)/shard_map/ppermute | solution.py:14
  141.1 2.7 %collective-permute-start.4 = (f32[1,32,512]{2,1,0:T(8,128)S(1)}, f32[1,32,512]{2,1,0:T(8,128)S(1)}, u32[]{:S(2)}, u32[]{:S(2)}) collective-permute-start(f32[1,32,512]{2,1,0:T(8,128)S(1)} %get-tuple-element.43), channel_id=1, source_target_pairs={{4,0},{8,4},{12,8},{16,12},{20,16},{24,20},{28,24},{5,1},{9,5},{13... | collective-permute-start | bytes 196616 | tf_op jit(solution)/shard_map/ppermute | solution.py:14
  147.6 2.3 %multiply_subtract_fusion = (f32[32,32,512]{2,1,0:T(8,128)S(1)}, f32[32,32,512]{2,1,0:T(8,128)S(1)}, f32[32,32,512]{2,1,0:T(8,128)S(1)}) fusion(f32[32,32,512]{2,1,0:T(8,128)S(1)} %copy-done.5, f32[32,32,512]{2,1,0:T(8,128)S(1)} %multiply_add_fusion.1, f32[32,32,511]{2,1,0:T(8,128)S(1)} %slice.177, f32[32,32,512]{2,1,0:T(8,128)S(1)} %copy-done.3, ...), kind=kLoop, calls=%fused_computation.36 | loop fusion | flops 8388608 | bytes 23064576 | tf_op jit(solution)/shard_map/sub | solution.py:127
  150.2 2.2 %fusion.8 = f32[32,32,512]{2,1,0:T(8,128)S(1)} fusion(f32[32,32,2,512]{3,1,2,0:T(8,128)S(1)} %copy-done.15, f32[32,32,512]{2,1,0:T(8,128)S(1)} %get-tuple-element.36, f32[31,32,512]{2,1,0:T(8,128)S(1)} %slice.172, f32[1,32,512]{2,1,0:T(8,128)S(1)} %get-tuple-element.42, f32[32,32,512]{2,1,0:T(8,128)S(1)} %get-tuple-element.35, ...), kind=kLoop, calls=%fused_computation.12 | loop fusion | flops 4194304 | bytes 16773120 | tf_op jit(solution)/shard_map/sub | solution.py:139
  153.3 2.1 %multiply_add_fusion = f32[32,32,512]{2,1,0:T(8,128)} fusion(f32[32,32,512]{2,1,0:T(8,128)S(1)} %multiply_add_fusion.1, f32[32,32,512]{2,1,0:T(8,128)S(1)} %fusion.25, f32[32,32,512]{2,1,0:T(8,128)S(1)} %copy-done.3), kind=kLoop, calls=%fused_computation.35 | loop fusion | flops 3670016 | bytes 8388608 | tf_op jit(solution)/shard_map/add | solution.py:138
  (92 shorter events, 15.6 us)
Async XLA Ops:
  0.6 104.8 %copy-start = (bf16[16,32,512]{2,1,0:T(8,128)(2,1)S(1)}, bf16[16,32,512]{2,1,0:T(8,128)(2,1)}, u32[]{:S(2)}) copy-start(bf16[16,32,512]{2,1,0:T(8,128)(2,1)} %param.20) | copy-start | bytes 1572868
  0.6 24.6 %slice-start = ((f32[32,32,512]{2,1,0:T(8,128)}), f32[1,32,512]{2,1,0:T(8,128)S(1)}, s32[]{:S(2)}) async-start(f32[32,32,512]{2,1,0:T(8,128)} %param.16), calls=%async_computation.3 | async-start | bytes 131072 | tf_op jit(solution)/shard_map/slice | solution.py:99
  0.7 24.6 %slice-start.1 = ((f32[32,32,512]{2,1,0:T(8,128)}), f32[1,32,512]{2,1,0:T(8,128)S(1)}, s32[]{:S(2)}) async-start(f32[32,32,512]{2,1,0:T(8,128)} %param.13), calls=%async_computation.4 | async-start | bytes 131072 | tf_op jit(solution)/shard_map/slice | solution.py:99
  0.7 26.5 %copy-start.16 = (bf16[768,2,512]{2,1,0:T(2,128)(2,1)S(1)}, bf16[768,2,512]{2,1,0:T(2,128)(2,1)}, u32[]{:S(2)}) copy-start(bf16[768,2,512]{2,1,0:T(2,128)(2,1)} %param.17) | copy-start | bytes 4718596
  5.8 25.9 %all-to-all-start = ((s32[32,1,48]{2,1,0:T(1,128)}), s32[32,1,48]{2,1,0:T(1,128)S(1)}, u32[]{:S(2)}, u32[]{:S(2)}) async-start(s32[32,1,48]{2,1,0:T(1,128)} %sub.127), calls=%async_computation | async-start | bytes 32768 | tf_op jit(solution)/shard_map/all_to_all | solution.py:48
  12.6 19.1 %collective-permute-start = (f32[1,32,512]{2,1,0:T(8,128)S(1)}, f32[1,32,512]{2,1,0:T(8,128)S(1)}, u32[]{:S(2)}, u32[]{:S(2)}) collective-permute-start(f32[1,32,512]{2,1,0:T(8,128)S(1)} %get-tuple-element.47), channel_id=1, source_target_pairs={{4,0},{8,4},{12,8},{16,12},{20,16},{24,20},{28,24},{5,1},{9,5},{13... | collective-permute-start | bytes 196616 | tf_op jit(solution)/shard_map/ppermute | solution.py:14
  16.2 15.5 %collective-permute-start.1 = (f32[32,512]{1,0:T(8,128)S(1)}, f32[32,512]{1,0:T(8,128)S(1)}, u32[]{:S(2)}, u32[]{:S(2)}) collective-permute-start(f32[32,512]{1,0:T(8,128)S(1)} %bitcast.93), channel_id=1, source_target_pairs={{1,0},{2,1},{3,2},{5,4},{6,5},{7,6},{9,8},{10,9},{11,10},{13,12},{... | collective-permute-start | bytes 196616 | tf_op jit(solution)/shard_map/ppermute | solution.py:14
  20.9 10.7 %collective-permute-start.3 = (f32[3,32,512]{2,1,0:T(8,128)S(1)}, f32[3,32,512]{2,1,0:T(8,128)S(1)}, u32[]{:S(2)}, u32[]{:S(2)}) collective-permute-start(f32[3,32,512]{2,1,0:T(8,128)S(1)} %pad_maximum_fusion.1), channel_id=1, source_target_pairs={{0,1},{1,2},{2,3},{4,5},{5,6},{6,7},{8,9},{9,10},{10,11},{12,13},{... | collective-permute-start | bytes 589832 | tf_op jit(solution)/shard_map/ppermute | solution.py:14
  25.3 7.0 %collective-permute-start.2 = (f32[3,32,512]{2,1,0:T(8,128)S(1)}, f32[3,32,512]{2,1,0:T(8,128)S(1)}, u32[]{:S(2)}, u32[]{:S(2)}) collective-permute-start(f32[3,32,512]{2,1,0:T(8,128)S(1)} %pad_maximum_fusion), channel_id=1, source_target_pairs={{0,4},{4,8},{8,12},{12,16},{16,20},{20,24},{24,28},{1,5},{5,9},{9,... | collective-permute-start | bytes 589832 | tf_op jit(solution)/shard_map/ppermute | solution.py:14
  32.3 4.9 %copy-start.2 = (f32[32,32,512]{2,1,0:T(8,128)S(1)}, f32[32,32,512]{2,1,0:T(8,128)}, u32[]{:S(2)}) copy-start(f32[32,32,512]{2,1,0:T(8,128)} %param.12) | copy-start | bytes 6291460
  32.3 73.2 %all-to-all-start.1 = ((bf16[32,48,1024]{2,1,0:T(8,128)(2,1)}), bf16[32,48,1024]{2,1,0:T(8,128)(2,1)}, u32[]{:S(2)}, u32[]{:S(2)}) async-start(bf16[32,48,1024]{2,1,0:T(8,128)(2,1)} %bitcast.82), calls=%async_computation.1 | async-start | bytes 6291456 | tf_op jit(solution)/shard_map/all_to_all | solution.py:56
  40.6 1.7 %copy-start.17 = (s32[8,8]{1,0:T(8,128)S(1)}, s32[8,8]{1,0:T(8,128)}, u32[]{:S(2)}) copy-start(s32[8,8]{1,0:T(8,128)} %param.21) | copy-start | bytes 772
  49.4 1.3 copy-start.4
  49.4 2.0 %copy-start.6 = (f32[32,32,512]{2,1,0:T(8,128)}, f32[32,32,512]{2,1,0:T(8,128)S(1)}, u32[]{:S(2)}) copy-start(f32[32,32,512]{2,1,0:T(8,128)S(1)} %get-tuple-element.38) | copy-start | bytes 6291460
  49.4 2.7 %copy-start.8 = (f32[32,32,512]{2,1,0:T(8,128)}, f32[32,32,512]{2,1,0:T(8,128)S(1)}, u32[]{:S(2)}) copy-start(f32[32,32,512]{2,1,0:T(8,128)S(1)} %get-tuple-element.39) | copy-start | bytes 6291460
  106.8 21.0 %all-to-all-start.2 = ((bf16[8,32,512]{2,1,0:T(8,128)(2,1)}), bf16[8,32,512]{2,1,0:T(8,128)(2,1)S(1)}, u32[]{:S(2)}, u32[]{:S(2)}) async-start(bf16[8,32,512]{2,1,0:T(8,128)(2,1)} %broadcast_select_fusion), calls=%async_computation.2 | async-start | bytes 524288 | tf_op jit(solution)/shard_map/all_to_all | solution.py:81
  118.5 7.5 %copy-start.13 = (f32[32,32,512]{2,1,0:T(8,128)S(1)}, f32[32,32,512]{2,1,0:T(8,128)}, u32[]{:S(2)}) copy-start(f32[32,32,512]{2,1,0:T(8,128)} %fusion.13) | copy-start | bytes 6291460
  124.0 2.0 %copy-start.14 = (f32[32,32,2,512]{3,1,2,0:T(8,128)}, f32[32,32,2,512]{3,1,2,0:T(8,128)S(1)}, u32[]{:S(2)}) copy-start(f32[32,32,2,512]{3,1,2,0:T(8,128)S(1)} %fusion) | copy-start | bytes 12582916
  132.5 6.2 %collective-permute-start.7 = (f32[32,512]{1,0:T(8,128)S(1)}, f32[32,512]{1,0:T(8,128)S(1)}, u32[]{:S(2)}, u32[]{:S(2)}) collective-permute-start(f32[32,512]{1,0:T(8,128)S(1)} %bitcast.94), channel_id=1, source_target_pairs={{0,1},{1,2},{2,3},{4,5},{5,6},{6,7},{8,9},{9,10},{10,11},{12,13},{... | collective-permute-start | bytes 196616 | tf_op jit(solution)/shard_map/ppermute | solution.py:14
  135.5 5.6 %collective-permute-start.5 = (f32[1,32,512]{2,1,0:T(8,128)S(1)}, f32[1,32,512]{2,1,0:T(8,128)S(1)}, u32[]{:S(2)}, u32[]{:S(2)}) collective-permute-start(f32[1,32,512]{2,1,0:T(8,128)S(1)} %slice.171), channel_id=1, source_target_pairs={{0,4},{4,8},{8,12},{12,16},{16,20},{20,24},{24,28},{1,5},{5,9},{9,... | collective-permute-start | bytes 196616 | tf_op jit(solution)/shard_map/ppermute | solution.py:14
  138.7 7.1 %collective-permute-start.6 = (f32[32,512]{1,0:T(8,128)S(1)}, f32[32,512]{1,0:T(8,128)S(1)}, u32[]{:S(2)}, u32[]{:S(2)}) collective-permute-start(f32[32,512]{1,0:T(8,128)S(1)} %get-tuple-element.49), channel_id=1, source_target_pairs={{1,0},{2,1},{3,2},{5,4},{6,5},{7,6},{9,8},{10,9},{11,10},{13,12},{... | collective-permute-start | bytes 196616 | tf_op jit(solution)/shard_map/ppermute | solution.py:14
  141.1 4.8 %collective-permute-start.4 = (f32[1,32,512]{2,1,0:T(8,128)S(1)}, f32[1,32,512]{2,1,0:T(8,128)S(1)}, u32[]{:S(2)}, u32[]{:S(2)}) collective-permute-start(f32[1,32,512]{2,1,0:T(8,128)S(1)} %get-tuple-element.43), channel_id=1, source_target_pairs={{4,0},{8,4},{12,8},{16,12},{20,16},{24,20},{28,24},{5,1},{9,5},{13... | collective-permute-start | bytes 196616 | tf_op jit(solution)/shard_map/ppermute | solution.py:14
  144.0 1.9 %copy-start.7 = (f32[32,32,512]{2,1,0:T(8,128)S(1)}, f32[32,32,512]{2,1,0:T(8,128)}, u32[]{:S(2)}) copy-start(f32[32,32,512]{2,1,0:T(8,128)} %copy-done.6) | copy-start | bytes 6291460
  144.0 2.2 %copy-start.9 = (f32[32,32,512]{2,1,0:T(8,128)S(1)}, f32[32,32,512]{2,1,0:T(8,128)}, u32[]{:S(2)}) copy-start(f32[32,32,512]{2,1,0:T(8,128)} %copy-done.8) | copy-start | bytes 6291460
  144.4 2.6 %copy-start.3 = (f32[32,32,512]{2,1,0:T(8,128)S(1)}, f32[32,32,512]{2,1,0:T(8,128)}, u32[]{:S(2)}) copy-start(f32[32,32,512]{2,1,0:T(8,128)} %param.16) | copy-start | bytes 6291460
  144.4 3.2 %copy-start.5 = (f32[32,32,512]{2,1,0:T(8,128)S(1)}, f32[32,32,512]{2,1,0:T(8,128)}, u32[]{:S(2)}) copy-start(f32[32,32,512]{2,1,0:T(8,128)} %copy-done.4) | copy-start | bytes 6291460
  147.6 2.6 %copy-start.15 = (f32[32,32,2,512]{3,1,2,0:T(8,128)S(1)}, f32[32,32,2,512]{3,1,2,0:T(8,128)}, u32[]{:S(2)}) copy-start(f32[32,32,2,512]{3,1,2,0:T(8,128)} %copy-done.14) | copy-start | bytes 12582916
  149.9 2.5 %copy-start.10 = (f32[32,32,512]{2,1,0:T(8,128)}, f32[32,32,512]{2,1,0:T(8,128)S(1)}, u32[]{:S(2)}) copy-start(f32[32,32,512]{2,1,0:T(8,128)S(1)} %get-tuple-element.34) | copy-start | bytes 6291460
  149.9 2.7 %copy-start.11 = (f32[32,32,512]{2,1,0:T(8,128)}, f32[32,32,512]{2,1,0:T(8,128)S(1)}, u32[]{:S(2)}) copy-start(f32[32,32,512]{2,1,0:T(8,128)S(1)} %get-tuple-element.35) | copy-start | bytes 6291460
  149.9 3.4 %copy-start.12 = (f32[32,32,512]{2,1,0:T(8,128)}, f32[32,32,512]{2,1,0:T(8,128)S(1)}, u32[]{:S(2)}) copy-start(f32[32,32,512]{2,1,0:T(8,128)S(1)} %get-tuple-element.36) | copy-start | bytes 6291460
  153.3 2.1 %copy-start.1 = (bf16[16,32,512]{2,1,0:T(8,128)(2,1)S(1)}, bf16[16,32,512]{2,1,0:T(8,128)(2,1)}, u32[]{:S(2)}) copy-start(bf16[16,32,512]{2,1,0:T(8,128)(2,1)} %param.20) | copy-start | bytes 1572868

commit v13 on v12

--- a/solution.py
+++ b/solution.py
@@ -45,16 +45,17 @@
         preferred_element_type=jnp.float32,
     ).astype(jnp.bfloat16)
     out_cols = jnp.max(jnp.where(placed, bubble_column[None, :] + 1, 0), axis=1) - 1
-    in_cols = lax.all_to_all(
-        out_cols.reshape(devices, capacity),
+    outgoing, ready = lax.optimization_barrier((outgoing, ready))
+    incoming = lax.all_to_all(
+        outgoing.reshape(devices, capacity, steps * depth),
         ("gx", "gy"),
         split_axis=0,
         concat_axis=0,
         tiled=True,
     )
-    in_cols, outgoing, ready = lax.optimization_barrier((in_cols, outgoing, ready))
-    incoming = lax.all_to_all(
-        outgoing.reshape(devices, capacity, steps * depth),
+    out_cols, incoming = lax.optimization_barrier((out_cols, incoming))
+    in_cols = lax.all_to_all(
+        out_cols.reshape(devices, capacity),
         ("gx", "gy"),
         split_axis=0,
         concat_axis=0,
@@ -69,7 +70,7 @@
     return source, incoming, ready
 
 
-def incident_plane(history, delays, size_y, depth):
+def incident_plane(history, delays, after):
     tiles_x = lax.axis_size("gx")
     my_tile = lax.axis_index("gx")
     cycle = jnp.arange(tiles_x, dtype=jnp.int32)
@@ -78,6 +79,7 @@
     weight = 1.0 / (1.0 + 2.0 * dist.astype(jnp.float32) / tiles_x)
     wanted = lax.dynamic_index_in_dim(delays, my_tile, 1, keepdims=False)
     chosen = jnp.take(history, wanted, axis=0)
+    chosen, _ = lax.optimization_barrier((chosen, after))
     rows = lax.all_to_all(chosen, "gx", split_axis=0, concat_axis=0, tiled=True)
     return jnp.sum(weight[:, None, None] * rows.astype(jnp.float32), axis=0)
 
@@ -108,8 +110,7 @@
         waves, bubble_dest, bubble_column, size_x * size_y, ready
     )
     above_x, above_y, below_x, below_y = ready
-    history, _ = lax.optimization_barrier((history, incoming))
-    incident = incident_plane(history, delays, size_y, depth)
+    incident = incident_plane(history, delays, incoming)
     source = source.reshape(size_x, size_y, steps, depth)
     p_bx, vx_bx, void_bx = below_x[0:1], below_x[1:2], below_x[2:3]
     p_by, vy_by, void_by = below_y[:, 0:1], below_y[:, 1:2], below_y[:, 2:3]

time: 157 us -> 164 us (1.045)
  other arithmetic: 28 us -> 33 us
  local copies, waits for them, and re-layouts: 25.3 us -> 27.5 us
    add x1, other arithmetic: 3.09 us -> 7.57 us  [body(): divergence = vel_x - prev_x + (vel_y - prev_y) + (vel_z - prev_z)]
    all_to_all x1, starting transfers between devices: 5.91 us -> 8.25 us  [bubble_source(): lax.all_to_all(out_cols.reshape(devices, capacity), ('gx', 'gy'), split_a...]
    all_to_all x1, starting transfers between devices: 7.06 us -> 5.16 us  [incident_plane(): rows = lax.all_to_all(chosen, 'gx', split_axis=0, concat_axis=0, tiled=True)]
  transfers between devices with their start and end apart: 11 -> 11, of which waited for: 5 -> 4; matrix products, arithmetic and copies ran while one was open for 24% -> 32% of each run, Pallas kernels for 0% -> 0%
where the time goes in v13:
time: 164 us; the launch traced here: 162 us
  waiting for transfers between devices  52.6 us (32%)
  starting transfers between devices  38.7 us (24%)
  other arithmetic  33 us (20%)
  local copies, waits for them, and re-layouts  27.5 us (17%)
  matrix products  9.49 us (6%)
    all_to_all x1, waiting for transfers between devices, bubble_source(): lax.all_to_all(outgoing.reshape(devices, capacity, steps * depth), ('gx',...  49.7 us
    ppermute x8, starting transfers between devices, from_behind(): return lax.ppermute(block, axis, route)  20 us
    sub x2, other arithmetic, body(): vel_z = vel_z - step_ratio * buoyancy * (next_z - pressure)  9.96 us
    all_to_all x1, starting transfers between devices, bubble_source(): lax.all_to_all(out_cols.reshape(devices, capacity), ('gx', 'gy'), split_a...  8.25 us
    add x1, other arithmetic, body(): divergence = vel_x - prev_x + (vel_y - prev_y) + (vel_z - prev_z)  7.57 us
    unnamed x42, local copies, waits for them, and re-layouts  5.9 us
    dot_general x1, matrix products, bubble_source(): jnp.dot(hits, incoming.reshape(slots, steps * depth), preferred_element_t...  5.49 us
    all_to_all x1, starting transfers between devices, bubble_source(): lax.all_to_all(outgoing.reshape(devices, capacity, steps * depth), ('gx',...  5.28 us
  transfers between devices with their start and end apart: 11, of which 4 were waited for; matrix products, arithmetic and copies ran while one was open for 32% of the time, Pallas kernels for 0%

profile of v13, /device:TPU:18, one launch (start us, length us, event | category | flops | bytes accessed | tf_op | source)
XLA Modules:
  0.0 162.4 jit_solution(18204554992834608593)
XLA Ops:
  1.7 1.9 %collective-permute-start = (f32[1,32,512]{2,1,0:T(8,128)S(1)}, f32[1,32,512]{2,1,0:T(8,128)S(1)}, u32[]{:S(2)}, u32[]{:S(2)}) collective-permute-start(f32[1,32,512]{2,1,0:T(8,128)S(1)} %get-tuple-element.49), channel_id=1, source_target_pairs={{4,0},{8,4},{12,8},{16,12},{20,16},{24,20},{28,24},{5,1},{9,5},{13... | collective-permute-start | bytes 196616 | tf_op jit(solution)/shard_map/ppermute | solution.py:14
  3.6 1.3 fusion.36
  5.0 2.4 %collective-permute-start.1 = (f32[32,512]{1,0:T(8,128)S(1)}, f32[32,512]{1,0:T(8,128)S(1)}, u32[]{:S(2)}, u32[]{:S(2)}) collective-permute-start(f32[32,512]{1,0:T(8,128)S(1)} %bitcast.92), channel_id=1, source_target_pairs={{1,0},{2,1},{3,2},{5,4},{6,5},{7,6},{9,8},{10,9},{11,10},{13,12},{... | collective-permute-start | bytes 196616 | tf_op jit(solution)/shard_map/ppermute | solution.py:14
  9.7 4.3 %collective-permute-start.3 = (f32[3,32,512]{2,1,0:T(8,128)S(1)}, f32[3,32,512]{2,1,0:T(8,128)S(1)}, u32[]{:S(2)}, u32[]{:S(2)}) collective-permute-start(f32[3,32,512]{2,1,0:T(8,128)S(1)} %pad_maximum_fusion.1), channel_id=1, source_target_pairs={{0,1},{1,2},{2,3},{4,5},{5,6},{6,7},{8,9},{9,10},{10,11},{12,13},{... | collective-permute-start | bytes 589832 | tf_op jit(solution)/shard_map/ppermute | solution.py:14
  15.7 1.9 %collective-permute-start.2 = (f32[3,32,512]{2,1,0:T(8,128)S(1)}, f32[3,32,512]{2,1,0:T(8,128)S(1)}, u32[]{:S(2)}, u32[]{:S(2)}) collective-permute-start(f32[3,32,512]{2,1,0:T(8,128)S(1)} %pad_maximum_fusion), channel_id=1, source_target_pairs={{0,4},{4,8},{8,12},{12,16},{16,20},{20,24},{24,28},{1,5},{5,9},{9,... | collective-permute-start | bytes 589832 | tf_op jit(solution)/shard_map/ppermute | solution.py:14
  17.7 1.7 %reduce-window.6 = s32[32,6,128]{2,0,1:T(8,128)S(1)} reduce-window(s32[32,6,128]{2,0,1:T(8,128)S(1)} %fusion.24, s32[]{:T(128)} %constant.85.clone.1), window={size=1x1x128 pad=0_0x0_0x127_0}, to_apply=%region_0.0 | reduce-window | flops 3121152 | bytes 196612 | tf_op jit(solution)/shard_map/reduce-window
  20.3 4.0 %fusion.4 = bf16[1536,1024]{1,0:T(8,128)(2,1)} fusion(bf16[768,1024]{1,0:T(8,128)(2,1)S(1)} %bitcast.84, s32[768]{0:T(1024)S(1)} %add_add_fusion), kind=kOutput, calls=%fused_computation.7 | convolution fusion | flops 2418671616 | bytes 4721664 | tf_op jit(solution)/shard_map/dot_general | solution.py:42
  24.3 5.3 %all-to-all-start = ((bf16[32,48,1024]{2,1,0:T(8,128)(2,1)}), bf16[32,48,1024]{2,1,0:T(8,128)(2,1)}, u32[]{:S(2)}, u32[]{:S(2)}) async-start(bf16[32,48,1024]{2,1,0:T(8,128)(2,1)} %bitcast.81), calls=%async_computation | async-start | bytes 6291456 | tf_op jit(solution)/shard_map/all_to_all | solution.py:49
  29.6 1.6 slice.138
  31.2 1.9 %slice.148 = f32[32,32,511]{2,1,0:T(8,128)} slice(f32[32,32,512]{2,1,0:T(8,128)S(1)} %copy-done.2), slice={[0:32], [0:32], [1:512]} | slice | bytes 4186112 | tf_op jit(solution)/shard_map/slice | solution.py:125
  33.1 1.7 %slice.143 = f32[32,31,512]{2,1,0:T(8,128)} slice(f32[32,32,512]{2,1,0:T(8,128)S(1)} %copy-done.2), slice={[0:32], [1:32], [0:512]} | slice | bytes 4063232 | tf_op jit(solution)/shard_map/slice | solution.py:124
  37.6 7.7 %multiply_subtract_fusion.1 = (f32[32,32,512]{2,1,0:T(8,128)}, f32[32,32,512]{2,1,0:T(8,128)}, f32[32,32,512]{2,1,0:T(8,128)S(1)}) fusion(f32[32,32,512]{2,1,0:T(8,128)} %param.15, f32[32,32,512]{2,1,0:T(8,128)S(1)} %copy-done.2, f32[32,32,511]{2,1,0:T(8,128)} %slice.148, f32[32,32,512]{2,1,0:T(8,128)} %param.16, f32[32,32,512]{2,1,0:T(8,128)} %param.14, ...), kind=kLoop, calls=%fused_computation.38 | loop fusion | flops 8388608 | bytes 23064576 | tf_op jit(solution)/shard_map/sub | solution.py:128
  45.3 1.3 copy-done.6
  46.6 1.5 slice.165
  48.1 49.7 %all-to-all-done = bf16[32,48,1024]{2,1,0:T(8,128)(2,1)} async-done(((bf16[32,48,1024]{2,1,0:T(8,128)(2,1)}), bf16[32,48,1024]{2,1,0:T(8,128)(2,1)}, u32[]{:S(2)}, u32[]{:S(2)}) %all-to-all-start) | async-done | bytes 3145760 | tf_op jit(solution)/shard_map/all_to_all | solution.py:49
  98.6 8.2 %all-to-all-start.1 = ((s32[32,1,48]{2,1,0:T(1,128)}), s32[32,1,48]{2,1,0:T(1,128)S(1)}, u32[]{:S(2)}, u32[]{:S(2)}) async-start(s32[32,1,48]{2,1,0:T(1,128)} %all_to_all.13), calls=%async_computation.1 | async-start | bytes 32768 | tf_op jit(solution)/shard_map/all_to_all | solution.py:57
  106.8 7.6 %fusion.13 = f32[32,32,512]{2,1,0:T(8,128)} fusion(f32[32,32,512]{2,1,0:T(8,128)} %copy-done.6, f32[31,32,512]{2,1,0:T(8,128)} %slice.165, f32[1,32,512]{2,1,0:T(8,128)S(1)} %get-tuple-element.34, f32[32,32,512]{2,1,0:T(8,128)} %get-tuple-element.40, f32[32,31,512]{2,1,0:T(8,128)} %bitcast.78, f32[32,1,512]{2,1,0:T(1,128)S(1)} %copy.45, ...), kind=kLoop, calls=%fused_computation.20 | loop fusion | flops 3670016 | bytes 14675968 | tf_op jit(solution)/shard_map/add | solution.py:136
  114.4 4.7 %copy.42 = bf16[1536,1024]{0,1:T(8,128)(2,1)} copy(bf16[1536,1024]{1,0:T(8,128)(2,1)} %bitcast.10) | data formatting | bytes 6291456 | tf_op jit(solution)/shard_map/reshape | solution.py:68
  119.0 5.2 %all-to-all-start.2 = ((bf16[8,32,512]{2,1,0:T(8,128)(2,1)}), bf16[8,32,512]{2,1,0:T(8,128)(2,1)S(1)}, u32[]{:S(2)}, u32[]{:S(2)}) async-start(bf16[8,32,512]{2,1,0:T(8,128)(2,1)} %broadcast_select_fusion), calls=%async_computation.2 | async-start | bytes 524288 | tf_op jit(solution)/shard_map/all_to_all | solution.py:83
  125.5 5.5 %fusion = f32[32,32,2,512]{3,1,2,0:T(8,128)S(1)} fusion(bf16[2,512,1536,1]{2,1,0,3:T(8,128)(2,1)} %bitcast.82, s32[1536]{0:T(1024)S(1)} %eq.76, s32[32,32]{1,0:T(8,128)S(1)} %multiply_add_fusion.2), kind=kOutput, calls=%fused_computation.1 | convolution fusion | flops 3222798336 | bytes 7350272 | tf_op jit(solution)/shard_map/dot_general | solution.py:67
  131.0 1.9 %copy-done.12 = f32[32,32,2,512]{3,1,2,0:T(8,128)} copy-done((f32[32,32,2,512]{3,1,2,0:T(8,128)}, f32[32,32,2,512]{3,1,2,0:T(8,128)S(1)}, u32[]{:S(2)}) %copy-start.12) | copy-done | bytes 4194328
  133.0 1.8 %fusion.9 = f32[32,32,512]{2,1,0:T(8,128)} fusion(f32[32,32,512]{2,1,0:T(8,128)S(1)} %copy-done.11, f32[32,32,2,512]{3,1,2,0:T(8,128)S(1)} %fusion), kind=kLoop, calls=%fused_computation.14 | loop fusion | flops 524288 | bytes 6291456 | tf_op jit(solution)/shard_map/sub | solution.py:140
  134.9 1.5 fusion.26
  136.4 3.0 %multiply_add_fusion.1 = f32[32,32,512]{2,1,0:T(8,128)S(1)} fusion(f32[32,32,512]{2,1,0:T(8,128)S(1)} %copy-done.2, f32[32,32,512]{2,1,0:T(8,128)} %fusion.26, f32[32,32,512]{2,1,0:T(8,128)} %param.16), kind=kLoop, calls=%fused_computation.37 | loop fusion | flops 3670016 | bytes 8388608 | tf_op jit(solution)/shard_map/add | solution.py:139
  139.6 3.4 %collective-permute-start.7 = (f32[32,512]{1,0:T(8,128)S(1)}, f32[32,512]{1,0:T(8,128)S(1)}, u32[]{:S(2)}, u32[]{:S(2)}) collective-permute-start(f32[32,512]{1,0:T(8,128)S(1)} %bitcast.93), channel_id=1, source_target_pairs={{0,1},{1,2},{2,3},{4,5},{5,6},{6,7},{8,9},{9,10},{10,11},{12,13},{... | collective-permute-start | bytes 196616 | tf_op jit(solution)/shard_map/ppermute | solution.py:14
  143.0 1.9 %collective-permute-start.5 = (f32[1,32,512]{2,1,0:T(8,128)S(1)}, f32[1,32,512]{2,1,0:T(8,128)S(1)}, u32[]{:S(2)}, u32[]{:S(2)}) collective-permute-start(f32[1,32,512]{2,1,0:T(8,128)S(1)} %slice.171), channel_id=1, source_target_pairs={{0,4},{4,8},{8,12},{12,16},{16,20},{20,24},{24,28},{1,5},{5,9},{9,... | collective-permute-start | bytes 196616 | tf_op jit(solution)/shard_map/ppermute | solution.py:14
  145.8 1.9 %collective-permute-start.6 = (f32[32,512]{1,0:T(8,128)S(1)}, f32[32,512]{1,0:T(8,128)S(1)}, u32[]{:S(2)}, u32[]{:S(2)}) collective-permute-start(f32[32,512]{1,0:T(8,128)S(1)} %get-tuple-element.51), channel_id=1, source_target_pairs={{1,0},{2,1},{3,2},{5,4},{6,5},{7,6},{9,8},{10,9},{11,10},{13,12},{... | collective-permute-start | bytes 196616 | tf_op jit(solution)/shard_map/ppermute | solution.py:14
  148.6 2.2 %collective-permute-start.4 = (f32[1,32,512]{2,1,0:T(8,128)S(1)}, f32[1,32,512]{2,1,0:T(8,128)S(1)}, u32[]{:S(2)}, u32[]{:S(2)}) collective-permute-start(f32[1,32,512]{2,1,0:T(8,128)S(1)} %get-tuple-element.45), channel_id=1, source_target_pairs={{4,0},{8,4},{12,8},{16,12},{20,16},{24,20},{28,24},{5,1},{9,5},{13... | collective-permute-start | bytes 196616 | tf_op jit(solution)/shard_map/ppermute | solution.py:14
  152.2 1.1 collective-permute-done.6
  154.6 2.3 %multiply_subtract_fusion = (f32[32,32,512]{2,1,0:T(8,128)S(1)}, f32[32,32,512]{2,1,0:T(8,128)S(1)}, f32[32,32,512]{2,1,0:T(8,128)S(1)}) fusion(f32[32,32,512]{2,1,0:T(8,128)S(1)} %copy-done.4, f32[32,32,512]{2,1,0:T(8,128)S(1)} %multiply_add_fusion.1, f32[32,32,511]{2,1,0:T(8,128)S(1)} %slice.177, f32[32,32,512]{2,1,0:T(8,128)S(1)} %copy-done.3, ...), kind=kLoop, calls=%fused_computation.36 | loop fusion | flops 8388608 | bytes 23064576 | tf_op jit(solution)/shard_map/sub | solution.py:128
  157.2 2.2 %fusion.8 = f32[32,32,512]{2,1,0:T(8,128)S(1)} fusion(f32[32,32,2,512]{3,1,2,0:T(8,128)S(1)} %copy-done.13, f32[32,32,512]{2,1,0:T(8,128)S(1)} %get-tuple-element.38, f32[31,32,512]{2,1,0:T(8,128)S(1)} %slice.172, f32[1,32,512]{2,1,0:T(8,128)S(1)} %get-tuple-element.44, f32[32,32,512]{2,1,0:T(8,128)S(1)} %get-tuple-element.37, ...), kind=kLoop, calls=%fused_computation.12 | loop fusion | flops 4194304 | bytes 16773120 | tf_op jit(solution)/shard_map/sub | solution.py:140
  160.3 2.1 %multiply_add_fusion = f32[32,32,512]{2,1,0:T(8,128)} fusion(f32[32,32,512]{2,1,0:T(8,128)S(1)} %multiply_add_fusion.1, f32[32,32,512]{2,1,0:T(8,128)S(1)} %fusion.25, f32[32,32,512]{2,1,0:T(8,128)S(1)} %copy-done.3), kind=kLoop, calls=%fused_computation.35 | loop fusion | flops 3670016 | bytes 8388608 | tf_op jit(solution)/shard_map/add | solution.py:139
  (92 shorter events, 16.3 us)
Async XLA Ops:
  0.6 34.4 %copy-start = (bf16[16,32,512]{2,1,0:T(8,128)(2,1)S(1)}, bf16[16,32,512]{2,1,0:T(8,128)(2,1)}, u32[]{:S(2)}) copy-start(bf16[16,32,512]{2,1,0:T(8,128)(2,1)} %param.20) | copy-start | bytes 1572868
  0.6 17.0 %copy-start.17 = (s32[768,1]{0,1:T(1,128)S(1)}, s32[768,1]{0,1:T(1,128)}, u32[]{:S(2)}) copy-start(s32[768,1]{0,1:T(1,128)} %param.18) | copy-start | bytes 9220
  0.7 19.2 %copy-start.14 = (bf16[768,2,512]{2,1,0:T(2,128)(2,1)S(1)}, bf16[768,2,512]{2,1,0:T(2,128)(2,1)}, u32[]{:S(2)}) copy-start(bf16[768,2,512]{2,1,0:T(2,128)(2,1)} %param.17) | copy-start | bytes 4718596
  1.7 22.6 %collective-permute-start = (f32[1,32,512]{2,1,0:T(8,128)S(1)}, f32[1,32,512]{2,1,0:T(8,128)S(1)}, u32[]{:S(2)}, u32[]{:S(2)}) collective-permute-start(f32[1,32,512]{2,1,0:T(8,128)S(1)} %get-tuple-element.49), channel_id=1, source_target_pairs={{4,0},{8,4},{12,8},{16,12},{20,16},{24,20},{28,24},{5,1},{9,5},{13... | collective-permute-start | bytes 196616 | tf_op jit(solution)/shard_map/ppermute | solution.py:14
  5.0 19.3 %collective-permute-start.1 = (f32[32,512]{1,0:T(8,128)S(1)}, f32[32,512]{1,0:T(8,128)S(1)}, u32[]{:S(2)}, u32[]{:S(2)}) collective-permute-start(f32[32,512]{1,0:T(8,128)S(1)} %bitcast.92), channel_id=1, source_target_pairs={{1,0},{2,1},{3,2},{5,4},{6,5},{7,6},{9,8},{10,9},{11,10},{13,12},{... | collective-permute-start | bytes 196616 | tf_op jit(solution)/shard_map/ppermute | solution.py:14
  9.7 14.6 %collective-permute-start.3 = (f32[3,32,512]{2,1,0:T(8,128)S(1)}, f32[3,32,512]{2,1,0:T(8,128)S(1)}, u32[]{:S(2)}, u32[]{:S(2)}) collective-permute-start(f32[3,32,512]{2,1,0:T(8,128)S(1)} %pad_maximum_fusion.1), channel_id=1, source_target_pairs={{0,1},{1,2},{2,3},{4,5},{5,6},{6,7},{8,9},{9,10},{10,11},{12,13},{... | collective-permute-start | bytes 589832 | tf_op jit(solution)/shard_map/ppermute | solution.py:14
  15.7 8.6 %collective-permute-start.2 = (f32[3,32,512]{2,1,0:T(8,128)S(1)}, f32[3,32,512]{2,1,0:T(8,128)S(1)}, u32[]{:S(2)}, u32[]{:S(2)}) collective-permute-start(f32[3,32,512]{2,1,0:T(8,128)S(1)} %pad_maximum_fusion), channel_id=1, source_target_pairs={{0,4},{4,8},{8,12},{12,16},{16,20},{20,24},{24,28},{1,5},{5,9},{9,... | collective-permute-start | bytes 589832 | tf_op jit(solution)/shard_map/ppermute | solution.py:14
  24.3 5.3 %copy-start.2 = (f32[32,32,512]{2,1,0:T(8,128)S(1)}, f32[32,32,512]{2,1,0:T(8,128)}, u32[]{:S(2)}) copy-start(f32[32,32,512]{2,1,0:T(8,128)} %param.12) | copy-start | bytes 6291460
  24.3 73.5 %all-to-all-start = ((bf16[32,48,1024]{2,1,0:T(8,128)(2,1)}), bf16[32,48,1024]{2,1,0:T(8,128)(2,1)}, u32[]{:S(2)}, u32[]{:S(2)}) async-start(bf16[32,48,1024]{2,1,0:T(8,128)(2,1)} %bitcast.81), calls=%async_computation | async-start | bytes 6291456 | tf_op jit(solution)/shard_map/all_to_all | solution.py:49
  33.1 1.7 %copy-start.15 = (s32[8,8]{1,0:T(8,128)S(1)}, s32[8,8]{1,0:T(8,128)}, u32[]{:S(2)}) copy-start(s32[8,8]{1,0:T(8,128)} %param.21) | copy-start | bytes 772
  33.1 2.7 %copy-start.16 = (s32[768]{0:T(1024)S(1)}, s32[768]{0:T(1024)}, u32[]{:S(2)}) copy-start(s32[768]{0:T(1024)} %param.19) | copy-start | bytes 9220
  45.3 1.3 copy-start.6
  98.6 20.5 %all-to-all-start.1 = ((s32[32,1,48]{2,1,0:T(1,128)}), s32[32,1,48]{2,1,0:T(1,128)S(1)}, u32[]{:S(2)}, u32[]{:S(2)}) async-start(s32[32,1,48]{2,1,0:T(1,128)} %all_to_all.13), calls=%async_computation.1 | async-start | bytes 32768 | tf_op jit(solution)/shard_map/all_to_all | solution.py:57
  119.0 15.8 %all-to-all-start.2 = ((bf16[8,32,512]{2,1,0:T(8,128)(2,1)}), bf16[8,32,512]{2,1,0:T(8,128)(2,1)S(1)}, u32[]{:S(2)}, u32[]{:S(2)}) async-start(bf16[8,32,512]{2,1,0:T(8,128)(2,1)} %broadcast_select_fusion), calls=%async_computation.2 | async-start | bytes 524288 | tf_op jit(solution)/shard_map/all_to_all | solution.py:83
  125.5 7.5 %copy-start.11 = (f32[32,32,512]{2,1,0:T(8,128)S(1)}, f32[32,32,512]{2,1,0:T(8,128)}, u32[]{:S(2)}) copy-start(f32[32,32,512]{2,1,0:T(8,128)} %fusion.13) | copy-start | bytes 6291460
  131.0 2.0 %copy-start.12 = (f32[32,32,2,512]{3,1,2,0:T(8,128)}, f32[32,32,2,512]{3,1,2,0:T(8,128)S(1)}, u32[]{:S(2)}) copy-start(f32[32,32,2,512]{3,1,2,0:T(8,128)S(1)} %fusion) | copy-start | bytes 12582916
  139.6 6.2 %collective-permute-start.7 = (f32[32,512]{1,0:T(8,128)S(1)}, f32[32,512]{1,0:T(8,128)S(1)}, u32[]{:S(2)}, u32[]{:S(2)}) collective-permute-start(f32[32,512]{1,0:T(8,128)S(1)} %bitcast.93), channel_id=1, source_target_pairs={{0,1},{1,2},{2,3},{4,5},{5,6},{6,7},{8,9},{9,10},{10,11},{12,13},{... | collective-permute-start | bytes 196616 | tf_op jit(solution)/shard_map/ppermute | solution.py:14
  143.0 5.6 %collective-permute-start.5 = (f32[1,32,512]{2,1,0:T(8,128)S(1)}, f32[1,32,512]{2,1,0:T(8,128)S(1)}, u32[]{:S(2)}, u32[]{:S(2)}) collective-permute-start(f32[1,32,512]{2,1,0:T(8,128)S(1)} %slice.171), channel_id=1, source_target_pairs={{0,4},{4,8},{8,12},{12,16},{16,20},{20,24},{24,28},{1,5},{5,9},{9,... | collective-permute-start | bytes 196616 | tf_op jit(solution)/shard_map/ppermute | solution.py:14
  145.8 7.6 %collective-permute-start.6 = (f32[32,512]{1,0:T(8,128)S(1)}, f32[32,512]{1,0:T(8,128)S(1)}, u32[]{:S(2)}, u32[]{:S(2)}) collective-permute-start(f32[32,512]{1,0:T(8,128)S(1)} %get-tuple-element.51), channel_id=1, source_target_pairs={{1,0},{2,1},{3,2},{5,4},{6,5},{7,6},{9,8},{10,9},{11,10},{13,12},{... | collective-permute-start | bytes 196616 | tf_op jit(solution)/shard_map/ppermute | solution.py:14
  148.6 4.8 %collective-permute-start.4 = (f32[1,32,512]{2,1,0:T(8,128)S(1)}, f32[1,32,512]{2,1,0:T(8,128)S(1)}, u32[]{:S(2)}, u32[]{:S(2)}) collective-permute-start(f32[1,32,512]{2,1,0:T(8,128)S(1)} %get-tuple-element.45), channel_id=1, source_target_pairs={{4,0},{8,4},{12,8},{16,12},{20,16},{24,20},{28,24},{5,1},{9,5},{13... | collective-permute-start | bytes 196616 | tf_op jit(solution)/shard_map/ppermute | solution.py:14
  151.0 2.3 %copy-start.5 = (f32[32,32,512]{2,1,0:T(8,128)S(1)}, f32[32,32,512]{2,1,0:T(8,128)}, u32[]{:S(2)}) copy-start(f32[32,32,512]{2,1,0:T(8,128)} %get-tuple-element.40) | copy-start | bytes 6291460
  151.1 2.3 %copy-start.7 = (f32[32,32,512]{2,1,0:T(8,128)S(1)}, f32[32,32,512]{2,1,0:T(8,128)}, u32[]{:S(2)}) copy-start(f32[32,32,512]{2,1,0:T(8,128)} %copy-done.6) | copy-start | bytes 6291460
  151.5 2.6 %copy-start.3 = (f32[32,32,512]{2,1,0:T(8,128)S(1)}, f32[32,32,512]{2,1,0:T(8,128)}, u32[]{:S(2)}) copy-start(f32[32,32,512]{2,1,0:T(8,128)} %param.16) | copy-start | bytes 6291460
  151.5 3.2 %copy-start.4 = (f32[32,32,512]{2,1,0:T(8,128)S(1)}, f32[32,32,512]{2,1,0:T(8,128)}, u32[]{:S(2)}) copy-start(f32[32,32,512]{2,1,0:T(8,128)} %get-tuple-element.39) | copy-start | bytes 6291460
  154.6 2.6 %copy-start.13 = (f32[32,32,2,512]{3,1,2,0:T(8,128)S(1)}, f32[32,32,2,512]{3,1,2,0:T(8,128)}, u32[]{:S(2)}) copy-start(f32[32,32,2,512]{3,1,2,0:T(8,128)} %copy-done.12) | copy-start | bytes 12582916
  156.9 2.5 %copy-start.8 = (f32[32,32,512]{2,1,0:T(8,128)}, f32[32,32,512]{2,1,0:T(8,128)S(1)}, u32[]{:S(2)}) copy-start(f32[32,32,512]{2,1,0:T(8,128)S(1)} %get-tuple-element.36) | copy-start | bytes 6291460
  156.9 2.7 %copy-start.9 = (f32[32,32,512]{2,1,0:T(8,128)}, f32[32,32,512]{2,1,0:T(8,128)S(1)}, u32[]{:S(2)}) copy-start(f32[32,32,512]{2,1,0:T(8,128)S(1)} %get-tuple-element.37) | copy-start | bytes 6291460
  156.9 3.4 %copy-start.10 = (f32[32,32,512]{2,1,0:T(8,128)}, f32[32,32,512]{2,1,0:T(8,128)S(1)}, u32[]{:S(2)}) copy-start(f32[32,32,512]{2,1,0:T(8,128)S(1)} %get-tuple-element.38) | copy-start | bytes 6291460
  160.3 2.1 %copy-start.1 = (bf16[16,32,512]{2,1,0:T(8,128)(2,1)S(1)}, bf16[16,32,512]{2,1,0:T(8,128)(2,1)}, u32[]{:S(2)}) copy-start(bf16[16,32,512]{2,1,0:T(8,128)(2,1)} %param.20) | copy-start | bytes 1572868

commit v14 on v12

--- a/solution.py
+++ b/solution.py
@@ -69,7 +69,7 @@
     return source, incoming, ready
 
 
-def incident_plane(history, delays, size_y, depth):
+def incident_plane(history, delays, after):
     tiles_x = lax.axis_size("gx")
     my_tile = lax.axis_index("gx")
     cycle = jnp.arange(tiles_x, dtype=jnp.int32)
@@ -78,6 +78,7 @@
     weight = 1.0 / (1.0 + 2.0 * dist.astype(jnp.float32) / tiles_x)
     wanted = lax.dynamic_index_in_dim(delays, my_tile, 1, keepdims=False)
     chosen = jnp.take(history, wanted, axis=0)
+    chosen, _ = lax.optimization_barrier((chosen, after))
     rows = lax.all_to_all(chosen, "gx", split_axis=0, concat_axis=0, tiled=True)
     return jnp.sum(weight[:, None, None] * rows.astype(jnp.float32), axis=0)
 
@@ -108,8 +109,7 @@
         waves, bubble_dest, bubble_column, size_x * size_y, ready
     )
     above_x, above_y, below_x, below_y = ready
-    history, _ = lax.optimization_barrier((history, incoming))
-    incident = incident_plane(history, delays, size_y, depth)
+    incident = incident_plane(history, delays, incoming)
     source = source.reshape(size_x, size_y, steps, depth)
     p_bx, vx_bx, void_bx = below_x[0:1], below_x[1:2], below_x[2:3]
     p_by, vy_by, void_by = below_y[:, 0:1], below_y[:, 1:2], below_y[:, 2:3]

time: 157 us -> 157 us (level)
    unnamed x42 -> x46, local copies, waits for them, and re-layouts: 7.41 us -> 7.98 us
  transfers between devices with their start and end apart: 11 -> 11, of which waited for: 5 -> 5; matrix products, arithmetic and copies ran while one was open for 24% -> 26% of each run, Pallas kernels for 0% -> 0%
where the time goes in v14:
time: 157 us; the launch traced here: 155 us
  waiting for transfers between devices  51.9 us (33%)
  starting transfers between devices  38.2 us (24%)
  other arithmetic  28 us (18%)
  local copies, waits for them, and re-layouts  26.5 us (17%)
  matrix products  9.51 us (6%)
    all_to_all x1, waiting for transfers between devices, bubble_source(): lax.all_to_all(outgoing.reshape(devices, capacity, steps * depth), ('gx',...  48.9 us
    ppermute x8, starting transfers between devices, from_behind(): return lax.ppermute(block, axis, route)  20.3 us
    sub x2, other arithmetic, body(): vel_z = vel_z - step_ratio * buoyancy * (next_z - pressure)  8.61 us
    unnamed x46, local copies, waits for them, and re-layouts  7.98 us
    all_to_all x1, starting transfers between devices, incident_plane(): rows = lax.all_to_all(chosen, 'gx', split_axis=0, concat_axis=0, tiled=True)  7.06 us
    all_to_all x1, starting transfers between devices, bubble_source(): lax.all_to_all(out_cols.reshape(devices, capacity), ('gx', 'gy'), split_a...  5.91 us
    dot_general x1, matrix products, bubble_source(): jnp.dot(hits, incoming.reshape(slots, steps * depth), preferred_element_t...  5.48 us
    add x2, other arithmetic, body(): pressure + step_ratio * stiffness * (source[:, :, step, :] - divergence +...  5.09 us
  transfers between devices with their start and end apart: 11, of which 5 were waited for; matrix products, arithmetic and copies ran while one was open for 26% of the time, Pallas kernels for 0%

profile of v14, /device:TPU:18, one launch (start us, length us, event | category | flops | bytes accessed | tf_op | source)
XLA Modules:
  0.0 155.3 jit_solution(15862084371971049725)
XLA Ops:
  2.2 1.7 %reduce-window.6 = s32[32,6,128]{2,0,1:T(8,128)S(1)} reduce-window(s32[32,6,128]{2,0,1:T(8,128)S(1)} %fusion.24, s32[]{:T(128)} %constant.85.clone.1), window={size=1x1x128 pad=0_0x0_0x127_0}, to_apply=%region_0.0 | reduce-window | flops 3121152 | bytes 196612 | tf_op jit(solution)/shard_map/reduce-window
  6.4 5.9 %all-to-all-start = ((s32[32,1,48]{2,1,0:T(1,128)}), s32[32,1,48]{2,1,0:T(1,128)S(1)}, u32[]{:S(2)}, u32[]{:S(2)}) async-start(s32[32,1,48]{2,1,0:T(1,128)} %sub.127), calls=%async_computation | async-start | bytes 32768 | tf_op jit(solution)/shard_map/all_to_all | solution.py:48
  12.3 1.5 fusion.37
  13.8 2.2 %collective-permute-start = (f32[1,32,512]{2,1,0:T(8,128)}, f32[1,32,512]{2,1,0:T(8,128)S(1)}, u32[]{:S(2)}, u32[]{:S(2)}) collective-permute-start(f32[1,32,512]{2,1,0:T(8,128)} %get-tuple-element.47), channel_id=1, source_target_pairs={{4,0},{8,4},{12,8},{16,12},{20,16},{24,20},{28,24},{5,1},{9,5},{13... | collective-permute-start | bytes 196616 | tf_op jit(solution)/shard_map/ppermute | solution.py:14
  16.1 1.3 fusion.36
  17.4 2.5 %collective-permute-start.1 = (f32[32,512]{1,0:T(8,128)S(1)}, f32[32,512]{1,0:T(8,128)S(1)}, u32[]{:S(2)}, u32[]{:S(2)}) collective-permute-start(f32[32,512]{1,0:T(8,128)S(1)} %bitcast.93), channel_id=1, source_target_pairs={{1,0},{2,1},{3,2},{5,4},{6,5},{7,6},{9,8},{10,9},{11,10},{13,12},{... | collective-permute-start | bytes 196616 | tf_op jit(solution)/shard_map/ppermute | solution.py:14
  19.9 1.1 slice.135
  22.2 4.3 %collective-permute-start.3 = (f32[3,32,512]{2,1,0:T(8,128)S(1)}, f32[3,32,512]{2,1,0:T(8,128)S(1)}, u32[]{:S(2)}, u32[]{:S(2)}) collective-permute-start(f32[3,32,512]{2,1,0:T(8,128)S(1)} %pad_maximum_fusion.1), channel_id=1, source_target_pairs={{0,1},{1,2},{2,3},{4,5},{5,6},{6,7},{8,9},{9,10},{10,11},{12,13},{... | collective-permute-start | bytes 589832 | tf_op jit(solution)/shard_map/ppermute | solution.py:14
  26.5 1.9 %collective-permute-start.2 = (f32[3,32,512]{2,1,0:T(8,128)S(1)}, f32[3,32,512]{2,1,0:T(8,128)S(1)}, u32[]{:S(2)}, u32[]{:S(2)}) collective-permute-start(f32[3,32,512]{2,1,0:T(8,128)S(1)} %pad_maximum_fusion), channel_id=1, source_target_pairs={{0,4},{4,8},{8,12},{12,16},{16,20},{20,24},{24,28},{1,5},{5,9},{9,... | collective-permute-start | bytes 589832 | tf_op jit(solution)/shard_map/ppermute | solution.py:14
  28.9 4.0 %fusion.4 = bf16[1536,1024]{1,0:T(8,128)(2,1)} fusion(bf16[768,1024]{1,0:T(8,128)(2,1)S(1)} %bitcast.85, s32[768]{0:T(1024)S(1)} %copy-done.19), kind=kOutput, calls=%fused_computation.7 | convolution fusion | flops 2418671616 | bytes 4721664 | tf_op jit(solution)/shard_map/dot_general | solution.py:42
  33.5 4.9 %all-to-all-start.1 = ((bf16[32,48,1024]{2,1,0:T(8,128)(2,1)}), bf16[32,48,1024]{2,1,0:T(8,128)(2,1)}, u32[]{:S(2)}, u32[]{:S(2)}) async-start(bf16[32,48,1024]{2,1,0:T(8,128)(2,1)} %bitcast.82), calls=%async_computation.1 | async-start | bytes 6291456 | tf_op jit(solution)/shard_map/all_to_all | solution.py:56
  38.4 1.5 slice.138
  39.9 1.9 %slice.148 = f32[32,32,511]{2,1,0:T(8,128)} slice(f32[32,32,512]{2,1,0:T(8,128)S(1)} %copy-done.2), slice={[0:32], [0:32], [1:512]} | slice | bytes 4186112 | tf_op jit(solution)/shard_map/slice | solution.py:124
  41.8 1.7 %slice.143 = f32[32,31,512]{2,1,0:T(8,128)} slice(f32[32,32,512]{2,1,0:T(8,128)S(1)} %copy-done.2), slice={[0:32], [1:32], [0:512]} | slice | bytes 4063232 | tf_op jit(solution)/shard_map/slice | solution.py:123
  45.6 6.4 %multiply_subtract_fusion.1 = (f32[32,32,512]{2,1,0:T(8,128)S(1)}, f32[32,32,512]{2,1,0:T(8,128)S(1)}, f32[32,32,512]{2,1,0:T(8,128)S(1)}) fusion(f32[32,32,512]{2,1,0:T(8,128)} %param.15, f32[32,32,512]{2,1,0:T(8,128)S(1)} %copy-done.2, f32[32,32,511]{2,1,0:T(8,128)} %slice.148, f32[32,32,512]{2,1,0:T(8,128)} %param.16, f32[32,32,512]{2,1,0:T(8,128)} %param.14, ...), kind=kLoop, calls=%fused_computation.38 | loop fusion | flops 8388608 | bytes 23064576 | tf_op jit(solution)/shard_map/sub | solution.py:127
  54.7 3.1 %fusion.13 = f32[32,32,512]{2,1,0:T(8,128)} fusion(f32[32,32,512]{2,1,0:T(8,128)S(1)} %get-tuple-element.39, f32[31,32,512]{2,1,0:T(8,128)S(1)} %slice.165, f32[1,32,512]{2,1,0:T(8,128)S(1)} %get-tuple-element.32, f32[32,32,512]{2,1,0:T(8,128)S(1)} %get-tuple-element.38, f32[32,31,512]{2,1,0:T(8,128)S(1)} %bitcast.79, f32[32,1,512]{2,1,0:T(1,128)S(1)} %copy.45, ...), kind=kLoop, calls=%fused_computation.20 | loop fusion | flops 3670016 | bytes 14675968 | tf_op jit(solution)/shard_map/add | solution.py:135
  57.8 48.9 %all-to-all-done.1 = bf16[32,48,1024]{2,1,0:T(8,128)(2,1)} async-done(((bf16[32,48,1024]{2,1,0:T(8,128)(2,1)}), bf16[32,48,1024]{2,1,0:T(8,128)(2,1)}, u32[]{:S(2)}, u32[]{:S(2)}) %all-to-all-start.1) | async-done | bytes 3145760 | tf_op jit(solution)/shard_map/all_to_all | solution.py:56
  106.6 7.1 %all-to-all-start.2 = ((bf16[8,32,512]{2,1,0:T(8,128)(2,1)}), bf16[8,32,512]{2,1,0:T(8,128)(2,1)S(1)}, u32[]{:S(2)}, u32[]{:S(2)}) async-start(bf16[8,32,512]{2,1,0:T(8,128)(2,1)} %broadcast_select_fusion), calls=%async_computation.2 | async-start | bytes 524288 | tf_op jit(solution)/shard_map/all_to_all | solution.py:82
  113.7 4.7 %copy.42 = bf16[1536,1024]{0,1:T(8,128)(2,1)} copy(bf16[1536,1024]{1,0:T(8,128)(2,1)} %bitcast.11) | data formatting | bytes 6291456 | tf_op jit(solution)/shard_map/reshape | solution.py:67
  118.4 5.5 %fusion = f32[32,32,2,512]{3,1,2,0:T(8,128)S(1)} fusion(bf16[2,512,1536,1]{2,1,0,3:T(8,128)(2,1)} %bitcast.83, s32[1536]{0:T(1024)S(1)} %eq.76, s32[32,32]{1,0:T(8,128)S(1)} %multiply_add_fusion.2), kind=kOutput, calls=%fused_computation.1 | convolution fusion | flops 3222798336 | bytes 7350272 | tf_op jit(solution)/shard_map/dot_general | solution.py:66
  123.9 1.9 %copy-done.14 = f32[32,32,2,512]{3,1,2,0:T(8,128)} copy-done((f32[32,32,2,512]{3,1,2,0:T(8,128)}, f32[32,32,2,512]{3,1,2,0:T(8,128)S(1)}, u32[]{:S(2)}) %copy-start.14) | copy-done | bytes 4194328
  125.8 1.8 %fusion.9 = f32[32,32,512]{2,1,0:T(8,128)} fusion(f32[32,32,512]{2,1,0:T(8,128)S(1)} %copy-done.13, f32[32,32,2,512]{3,1,2,0:T(8,128)S(1)} %fusion), kind=kLoop, calls=%fused_computation.14 | loop fusion | flops 524288 | bytes 6291456 | tf_op jit(solution)/shard_map/sub | solution.py:139
  127.8 1.5 fusion.26
  129.2 3.0 %multiply_add_fusion.1 = f32[32,32,512]{2,1,0:T(8,128)S(1)} fusion(f32[32,32,512]{2,1,0:T(8,128)S(1)} %copy-done.2, f32[32,32,512]{2,1,0:T(8,128)} %fusion.26, f32[32,32,512]{2,1,0:T(8,128)} %param.16), kind=kLoop, calls=%fused_computation.37 | loop fusion | flops 3670016 | bytes 8388608 | tf_op jit(solution)/shard_map/add | solution.py:138
  132.4 2.9 %collective-permute-start.7 = (f32[32,512]{1,0:T(8,128)S(1)}, f32[32,512]{1,0:T(8,128)S(1)}, u32[]{:S(2)}, u32[]{:S(2)}) collective-permute-start(f32[32,512]{1,0:T(8,128)S(1)} %bitcast.94), channel_id=1, source_target_pairs={{0,1},{1,2},{2,3},{4,5},{5,6},{6,7},{8,9},{9,10},{10,11},{12,13},{... | collective-permute-start | bytes 196616 | tf_op jit(solution)/shard_map/ppermute | solution.py:14
  135.3 1.9 %collective-permute-start.5 = (f32[1,32,512]{2,1,0:T(8,128)S(1)}, f32[1,32,512]{2,1,0:T(8,128)S(1)}, u32[]{:S(2)}, u32[]{:S(2)}) collective-permute-start(f32[1,32,512]{2,1,0:T(8,128)S(1)} %slice.171), channel_id=1, source_target_pairs={{0,4},{4,8},{8,12},{12,16},{16,20},{20,24},{24,28},{1,5},{5,9},{9,... | collective-permute-start | bytes 196616 | tf_op jit(solution)/shard_map/ppermute | solution.py:14
  137.3 1.3 collective-permute-done.7
  138.6 1.9 %collective-permute-start.6 = (f32[32,512]{1,0:T(8,128)S(1)}, f32[32,512]{1,0:T(8,128)S(1)}, u32[]{:S(2)}, u32[]{:S(2)}) collective-permute-start(f32[32,512]{1,0:T(8,128)S(1)} %get-tuple-element.49), channel_id=1, source_target_pairs={{1,0},{2,1},{3,2},{5,4},{6,5},{7,6},{9,8},{10,9},{11,10},{13,12},{... | collective-permute-start | bytes 196616 | tf_op jit(solution)/shard_map/ppermute | solution.py:14
  140.9 2.7 %collective-permute-start.4 = (f32[1,32,512]{2,1,0:T(8,128)S(1)}, f32[1,32,512]{2,1,0:T(8,128)S(1)}, u32[]{:S(2)}, u32[]{:S(2)}) collective-permute-start(f32[1,32,512]{2,1,0:T(8,128)S(1)} %get-tuple-element.43), channel_id=1, source_target_pairs={{4,0},{8,4},{12,8},{16,12},{20,16},{24,20},{28,24},{5,1},{9,5},{13... | collective-permute-start | bytes 196616 | tf_op jit(solution)/shard_map/ppermute | solution.py:14
  147.4 2.3 %multiply_subtract_fusion = (f32[32,32,512]{2,1,0:T(8,128)S(1)}, f32[32,32,512]{2,1,0:T(8,128)S(1)}, f32[32,32,512]{2,1,0:T(8,128)S(1)}) fusion(f32[32,32,512]{2,1,0:T(8,128)S(1)} %copy-done.5, f32[32,32,512]{2,1,0:T(8,128)S(1)} %multiply_add_fusion.1, f32[32,32,511]{2,1,0:T(8,128)S(1)} %slice.177, f32[32,32,512]{2,1,0:T(8,128)S(1)} %copy-done.3, ...), kind=kLoop, calls=%fused_computation.36 | loop fusion | flops 8388608 | bytes 23064576 | tf_op jit(solution)/shard_map/sub | solution.py:127
  150.0 2.2 %fusion.8 = f32[32,32,512]{2,1,0:T(8,128)S(1)} fusion(f32[32,32,2,512]{3,1,2,0:T(8,128)S(1)} %copy-done.15, f32[32,32,512]{2,1,0:T(8,128)S(1)} %get-tuple-element.36, f32[31,32,512]{2,1,0:T(8,128)S(1)} %slice.172, f32[1,32,512]{2,1,0:T(8,128)S(1)} %get-tuple-element.42, f32[32,32,512]{2,1,0:T(8,128)S(1)} %get-tuple-element.35, ...), kind=kLoop, calls=%fused_computation.12 | loop fusion | flops 4194304 | bytes 16773120 | tf_op jit(solution)/shard_map/sub | solution.py:139
  153.1 2.1 %multiply_add_fusion = f32[32,32,512]{2,1,0:T(8,128)} fusion(f32[32,32,512]{2,1,0:T(8,128)S(1)} %multiply_add_fusion.1, f32[32,32,512]{2,1,0:T(8,128)S(1)} %fusion.25, f32[32,32,512]{2,1,0:T(8,128)S(1)} %copy-done.3), kind=kLoop, calls=%fused_computation.35 | loop fusion | flops 3670016 | bytes 8388608 | tf_op jit(solution)/shard_map/add | solution.py:138
  (96 shorter events, 16.4 us)
Async XLA Ops:
  0.6 43.1 %copy-start = (bf16[16,32,512]{2,1,0:T(8,128)(2,1)S(1)}, bf16[16,32,512]{2,1,0:T(8,128)(2,1)}, u32[]{:S(2)}) copy-start(bf16[16,32,512]{2,1,0:T(8,128)(2,1)} %param.20) | copy-start | bytes 1572868
  0.6 25.8 %slice-start = ((f32[32,32,512]{2,1,0:T(8,128)}), f32[1,32,512]{2,1,0:T(8,128)S(1)}, s32[]{:S(2)}) async-start(f32[32,32,512]{2,1,0:T(8,128)} %param.16), calls=%async_computation.3 | async-start | bytes 131072 | tf_op jit(solution)/shard_map/slice | solution.py:100
  0.7 25.8 %slice-start.1 = ((f32[32,32,512]{2,1,0:T(8,128)}), f32[1,32,512]{2,1,0:T(8,128)S(1)}, s32[]{:S(2)}) async-start(f32[32,32,512]{2,1,0:T(8,128)} %param.13), calls=%async_computation.4 | async-start | bytes 131072 | tf_op jit(solution)/shard_map/slice | solution.py:100
  0.7 27.7 %copy-start.16 = (bf16[768,2,512]{2,1,0:T(2,128)(2,1)S(1)}, bf16[768,2,512]{2,1,0:T(2,128)(2,1)}, u32[]{:S(2)}) copy-start(bf16[768,2,512]{2,1,0:T(2,128)(2,1)} %param.17) | copy-start | bytes 4718596
  6.4 26.5 %all-to-all-start = ((s32[32,1,48]{2,1,0:T(1,128)}), s32[32,1,48]{2,1,0:T(1,128)S(1)}, u32[]{:S(2)}, u32[]{:S(2)}) async-start(s32[32,1,48]{2,1,0:T(1,128)} %sub.127), calls=%async_computation | async-start | bytes 32768 | tf_op jit(solution)/shard_map/all_to_all | solution.py:48
  13.8 19.1 %collective-permute-start = (f32[1,32,512]{2,1,0:T(8,128)}, f32[1,32,512]{2,1,0:T(8,128)S(1)}, u32[]{:S(2)}, u32[]{:S(2)}) collective-permute-start(f32[1,32,512]{2,1,0:T(8,128)} %get-tuple-element.47), channel_id=1, source_target_pairs={{4,0},{8,4},{12,8},{16,12},{20,16},{24,20},{28,24},{5,1},{9,5},{13... | collective-permute-start | bytes 196616 | tf_op jit(solution)/shard_map/ppermute | solution.py:14
  17.4 15.5 %collective-permute-start.1 = (f32[32,512]{1,0:T(8,128)S(1)}, f32[32,512]{1,0:T(8,128)S(1)}, u32[]{:S(2)}, u32[]{:S(2)}) collective-permute-start(f32[32,512]{1,0:T(8,128)S(1)} %bitcast.93), channel_id=1, source_target_pairs={{1,0},{2,1},{3,2},{5,4},{6,5},{7,6},{9,8},{10,9},{11,10},{13,12},{... | collective-permute-start | bytes 196616 | tf_op jit(solution)/shard_map/ppermute | solution.py:14
  22.1 6.7 %copy-start.19 = (s32[768]{0:T(1024)S(1)}, s32[768]{0:T(1024)}, u32[]{:S(2)}) copy-start(s32[768]{0:T(1024)} %copy-done.18) | copy-start | bytes 9220
  22.2 10.7 %collective-permute-start.3 = (f32[3,32,512]{2,1,0:T(8,128)S(1)}, f32[3,32,512]{2,1,0:T(8,128)S(1)}, u32[]{:S(2)}, u32[]{:S(2)}) collective-permute-start(f32[3,32,512]{2,1,0:T(8,128)S(1)} %pad_maximum_fusion.1), channel_id=1, source_target_pairs={{0,1},{1,2},{2,3},{4,5},{5,6},{6,7},{8,9},{9,10},{10,11},{12,13},{... | collective-permute-start | bytes 589832 | tf_op jit(solution)/shard_map/ppermute | solution.py:14
  26.5 7.0 %collective-permute-start.2 = (f32[3,32,512]{2,1,0:T(8,128)S(1)}, f32[3,32,512]{2,1,0:T(8,128)S(1)}, u32[]{:S(2)}, u32[]{:S(2)}) collective-permute-start(f32[3,32,512]{2,1,0:T(8,128)S(1)} %pad_maximum_fusion), channel_id=1, source_target_pairs={{0,4},{4,8},{8,12},{12,16},{16,20},{20,24},{24,28},{1,5},{5,9},{9,... | collective-permute-start | bytes 589832 | tf_op jit(solution)/shard_map/ppermute | solution.py:14
  33.5 4.9 %copy-start.2 = (f32[32,32,512]{2,1,0:T(8,128)S(1)}, f32[32,32,512]{2,1,0:T(8,128)}, u32[]{:S(2)}) copy-start(f32[32,32,512]{2,1,0:T(8,128)} %param.12) | copy-start | bytes 6291460
  33.5 73.2 %all-to-all-start.1 = ((bf16[32,48,1024]{2,1,0:T(8,128)(2,1)}), bf16[32,48,1024]{2,1,0:T(8,128)(2,1)}, u32[]{:S(2)}, u32[]{:S(2)}) async-start(bf16[32,48,1024]{2,1,0:T(8,128)(2,1)} %bitcast.82), calls=%async_computation.1 | async-start | bytes 6291456 | tf_op jit(solution)/shard_map/all_to_all | solution.py:56
  41.8 1.7 %copy-start.17 = (s32[8,8]{1,0:T(8,128)S(1)}, s32[8,8]{1,0:T(8,128)}, u32[]{:S(2)}) copy-start(s32[8,8]{1,0:T(8,128)} %param.21) | copy-start | bytes 772
  52.0 1.3 copy-start.4
  52.0 2.0 %copy-start.6 = (f32[32,32,512]{2,1,0:T(8,128)}, f32[32,32,512]{2,1,0:T(8,128)S(1)}, u32[]{:S(2)}) copy-start(f32[32,32,512]{2,1,0:T(8,128)S(1)} %get-tuple-element.38) | copy-start | bytes 6291460
  52.0 2.7 %copy-start.8 = (f32[32,32,512]{2,1,0:T(8,128)}, f32[32,32,512]{2,1,0:T(8,128)S(1)}, u32[]{:S(2)}) copy-start(f32[32,32,512]{2,1,0:T(8,128)S(1)} %get-tuple-element.39) | copy-start | bytes 6291460
  106.6 21.0 %all-to-all-start.2 = ((bf16[8,32,512]{2,1,0:T(8,128)(2,1)}), bf16[8,32,512]{2,1,0:T(8,128)(2,1)S(1)}, u32[]{:S(2)}, u32[]{:S(2)}) async-start(bf16[8,32,512]{2,1,0:T(8,128)(2,1)} %broadcast_select_fusion), calls=%async_computation.2 | async-start | bytes 524288 | tf_op jit(solution)/shard_map/all_to_all | solution.py:82
  118.4 7.4 %copy-start.13 = (f32[32,32,512]{2,1,0:T(8,128)S(1)}, f32[32,32,512]{2,1,0:T(8,128)}, u32[]{:S(2)}) copy-start(f32[32,32,512]{2,1,0:T(8,128)} %fusion.13) | copy-start | bytes 6291460
  123.9 1.9 %copy-start.14 = (f32[32,32,2,512]{3,1,2,0:T(8,128)}, f32[32,32,2,512]{3,1,2,0:T(8,128)S(1)}, u32[]{:S(2)}) copy-start(f32[32,32,2,512]{3,1,2,0:T(8,128)S(1)} %fusion) | copy-start | bytes 12582916
  132.4 6.2 %collective-permute-start.7 = (f32[32,512]{1,0:T(8,128)S(1)}, f32[32,512]{1,0:T(8,128)S(1)}, u32[]{:S(2)}, u32[]{:S(2)}) collective-permute-start(f32[32,512]{1,0:T(8,128)S(1)} %bitcast.94), channel_id=1, source_target_pairs={{0,1},{1,2},{2,3},{4,5},{5,6},{6,7},{8,9},{9,10},{10,11},{12,13},{... | collective-permute-start | bytes 196616 | tf_op jit(solution)/shard_map/ppermute | solution.py:14
  135.3 5.6 %collective-permute-start.5 = (f32[1,32,512]{2,1,0:T(8,128)S(1)}, f32[1,32,512]{2,1,0:T(8,128)S(1)}, u32[]{:S(2)}, u32[]{:S(2)}) collective-permute-start(f32[1,32,512]{2,1,0:T(8,128)S(1)} %slice.171), channel_id=1, source_target_pairs={{0,4},{4,8},{8,12},{12,16},{16,20},{20,24},{24,28},{1,5},{5,9},{9,... | collective-permute-start | bytes 196616 | tf_op jit(solution)/shard_map/ppermute | solution.py:14
  138.6 7.1 %collective-permute-start.6 = (f32[32,512]{1,0:T(8,128)S(1)}, f32[32,512]{1,0:T(8,128)S(1)}, u32[]{:S(2)}, u32[]{:S(2)}) collective-permute-start(f32[32,512]{1,0:T(8,128)S(1)} %get-tuple-element.49), channel_id=1, source_target_pairs={{1,0},{2,1},{3,2},{5,4},{6,5},{7,6},{9,8},{10,9},{11,10},{13,12},{... | collective-permute-start | bytes 196616 | tf_op jit(solution)/shard_map/ppermute | solution.py:14
  140.9 4.8 %collective-permute-start.4 = (f32[1,32,512]{2,1,0:T(8,128)S(1)}, f32[1,32,512]{2,1,0:T(8,128)S(1)}, u32[]{:S(2)}, u32[]{:S(2)}) collective-permute-start(f32[1,32,512]{2,1,0:T(8,128)S(1)} %get-tuple-element.43), channel_id=1, source_target_pairs={{4,0},{8,4},{12,8},{16,12},{20,16},{24,20},{28,24},{5,1},{9,5},{13... | collective-permute-start | bytes 196616 | tf_op jit(solution)/shard_map/ppermute | solution.py:14
  143.9 1.9 %copy-start.7 = (f32[32,32,512]{2,1,0:T(8,128)S(1)}, f32[32,32,512]{2,1,0:T(8,128)}, u32[]{:S(2)}) copy-start(f32[32,32,512]{2,1,0:T(8,128)} %copy-done.6) | copy-start | bytes 6291460
  143.9 2.2 %copy-start.9 = (f32[32,32,512]{2,1,0:T(8,128)S(1)}, f32[32,32,512]{2,1,0:T(8,128)}, u32[]{:S(2)}) copy-start(f32[32,32,512]{2,1,0:T(8,128)} %copy-done.8) | copy-start | bytes 6291460
  144.3 2.6 %copy-start.3 = (f32[32,32,512]{2,1,0:T(8,128)S(1)}, f32[32,32,512]{2,1,0:T(8,128)}, u32[]{:S(2)}) copy-start(f32[32,32,512]{2,1,0:T(8,128)} %param.16) | copy-start | bytes 6291460
  144.3 3.2 %copy-start.5 = (f32[32,32,512]{2,1,0:T(8,128)S(1)}, f32[32,32,512]{2,1,0:T(8,128)}, u32[]{:S(2)}) copy-start(f32[32,32,512]{2,1,0:T(8,128)} %copy-done.4) | copy-start | bytes 6291460
  147.4 2.6 %copy-start.15 = (f32[32,32,2,512]{3,1,2,0:T(8,128)S(1)}, f32[32,32,2,512]{3,1,2,0:T(8,128)}, u32[]{:S(2)}) copy-start(f32[32,32,2,512]{3,1,2,0:T(8,128)} %copy-done.14) | copy-start | bytes 12582916
  149.7 2.5 %copy-start.10 = (f32[32,32,512]{2,1,0:T(8,128)}, f32[32,32,512]{2,1,0:T(8,128)S(1)}, u32[]{:S(2)}) copy-start(f32[32,32,512]{2,1,0:T(8,128)S(1)} %get-tuple-element.34) | copy-start | bytes 6291460
  149.7 2.7 %copy-start.11 = (f32[32,32,512]{2,1,0:T(8,128)}, f32[32,32,512]{2,1,0:T(8,128)S(1)}, u32[]{:S(2)}) copy-start(f32[32,32,512]{2,1,0:T(8,128)S(1)} %get-tuple-element.35) | copy-start | bytes 6291460
  149.7 3.4 %copy-start.12 = (f32[32,32,512]{2,1,0:T(8,128)}, f32[32,32,512]{2,1,0:T(8,128)S(1)}, u32[]{:S(2)}) copy-start(f32[32,32,512]{2,1,0:T(8,128)S(1)} %get-tuple-element.36) | copy-start | bytes 6291460
  153.1 2.1 %copy-start.1 = (bf16[16,32,512]{2,1,0:T(8,128)(2,1)S(1)}, bf16[16,32,512]{2,1,0:T(8,128)(2,1)}, u32[]{:S(2)}) copy-start(bf16[16,32,512]{2,1,0:T(8,128)(2,1)} %param.20) | copy-start | bytes 1572868
  (1 other events, 0.6 us)

commit v15 on v14

--- a/solution.py
+++ b/solution.py
@@ -35,8 +35,11 @@
     capacity = 2 * bubbles // devices
     slots = devices * capacity
     dest = bubble_dest[:, 0]
-    owners = (dest[:, None] == jnp.arange(devices, dtype=jnp.int32)[None, :]).astype(jnp.int32)
-    rank = jnp.sum(jnp.cumsum(owners, axis=0) * owners, axis=1) - 1
+    owners = (dest[:, None] == jnp.arange(devices, dtype=jnp.int32)[None, :]).astype(jnp.bfloat16)
+    listed = jnp.arange(bubbles, dtype=jnp.int32)
+    earlier = (listed[:, None] > listed[None, :]).astype(jnp.bfloat16)
+    before = jnp.dot(earlier, owners, preferred_element_type=jnp.float32)
+    rank = jnp.sum(before * owners.astype(jnp.float32), axis=1).astype(jnp.int32)
     slot_ids = dest * capacity + rank
     placed = slot_ids[None, :] == jnp.arange(slots, dtype=jnp.int32)[:, None]
     outgoing = jnp.dot(

time: 157 us -> 155 us (0.987)
  other arithmetic: 28 us -> 26.1 us
    another operation x2 -> x0, other arithmetic: 1.77 us -> none
where the time goes in v15:
time: 155 us; the launch traced here: 153 us
  waiting for transfers between devices  51.9 us (33%)
  starting transfers between devices  38.2 us (25%)
  other arithmetic  26.1 us (17%)
  local copies, waits for them, and re-layouts  25.7 us (17%)
  matrix products  9.87 us (6%)
    all_to_all x1, waiting for transfers between devices, bubble_source(): lax.all_to_all(outgoing.reshape(devices, capacity, steps * depth), ('gx',...  48.9 us
    ppermute x8, starting transfers between devices, from_behind(): return lax.ppermute(block, axis, route)  20.3 us
    sub x2, other arithmetic, body(): vel_z = vel_z - step_ratio * buoyancy * (next_z - pressure)  8.61 us
    unnamed x46, local copies, waits for them, and re-layouts  7.41 us
    all_to_all x1, starting transfers between devices, incident_plane(): rows = lax.all_to_all(chosen, 'gx', split_axis=0, concat_axis=0, tiled=True)  7.06 us
    all_to_all x1, starting transfers between devices, bubble_source(): lax.all_to_all(out_cols.reshape(devices, capacity), ('gx', 'gy'), split_a...  5.91 us
    dot_general x1, matrix products, bubble_source(): jnp.dot(hits, incoming.reshape(slots, steps * depth), preferred_element_t...  5.48 us
    add x2, other arithmetic, body(): pressure + step_ratio * stiffness * (source[:, :, step, :] - divergence +...  5.09 us
  transfers between devices with their start and end apart: 11, of which 5 were waited for; matrix products, arithmetic and copies ran while one was open for 26% of the time, Pallas kernels for 0%

profile of v15, /device:TPU:18, one launch (start us, length us, event | category | flops | bytes accessed | tf_op | source)
XLA Modules:
  0.0 152.9 jit_solution(10378543908260824307)
XLA Ops:
  4.0 5.9 %all-to-all-start = ((s32[32,1,48]{2,1,0:T(1,128)}), s32[32,1,48]{2,1,0:T(1,128)S(1)}, u32[]{:S(2)}, u32[]{:S(2)}) async-start(s32[32,1,48]{2,1,0:T(1,128)} %sub.122), calls=%async_computation | async-start | bytes 32768 | tf_op jit(solution)/shard_map/all_to_all | solution.py:51
  9.9 1.5 fusion.39
  11.5 2.2 %collective-permute-start = (f32[1,32,512]{2,1,0:T(8,128)}, f32[1,32,512]{2,1,0:T(8,128)S(1)}, u32[]{:S(2)}, u32[]{:S(2)}) collective-permute-start(f32[1,32,512]{2,1,0:T(8,128)} %get-tuple-element.47), channel_id=1, source_target_pairs={{4,0},{8,4},{12,8},{16,12},{20,16},{24,20},{28,24},{5,1},{9,5},{13... | collective-permute-start | bytes 196616 | tf_op jit(solution)/shard_map/ppermute | solution.py:14
  13.7 1.3 fusion.38
  15.0 2.5 %collective-permute-start.1 = (f32[32,512]{1,0:T(8,128)S(1)}, f32[32,512]{1,0:T(8,128)S(1)}, u32[]{:S(2)}, u32[]{:S(2)}) collective-permute-start(f32[32,512]{1,0:T(8,128)S(1)} %bitcast.75), channel_id=1, source_target_pairs={{1,0},{2,1},{3,2},{5,4},{6,5},{7,6},{9,8},{10,9},{11,10},{13,12},{... | collective-permute-start | bytes 196616 | tf_op jit(solution)/shard_map/ppermute | solution.py:14
  17.5 1.1 slice.127
  18.6 1.1 slice.128
  19.8 4.3 %collective-permute-start.3 = (f32[3,32,512]{2,1,0:T(8,128)S(1)}, f32[3,32,512]{2,1,0:T(8,128)S(1)}, u32[]{:S(2)}, u32[]{:S(2)}) collective-permute-start(f32[3,32,512]{2,1,0:T(8,128)S(1)} %pad_maximum_fusion.1), channel_id=1, source_target_pairs={{0,1},{1,2},{2,3},{4,5},{5,6},{6,7},{8,9},{9,10},{10,11},{12,13},{... | collective-permute-start | bytes 589832 | tf_op jit(solution)/shard_map/ppermute | solution.py:14
  24.1 1.9 %collective-permute-start.2 = (f32[3,32,512]{2,1,0:T(8,128)S(1)}, f32[3,32,512]{2,1,0:T(8,128)S(1)}, u32[]{:S(2)}, u32[]{:S(2)}) collective-permute-start(f32[3,32,512]{2,1,0:T(8,128)S(1)} %pad_maximum_fusion), channel_id=1, source_target_pairs={{0,4},{4,8},{8,12},{12,16},{16,20},{20,24},{24,28},{1,5},{5,9},{9,... | collective-permute-start | bytes 589832 | tf_op jit(solution)/shard_map/ppermute | solution.py:14
  26.5 4.0 %fusion.4 = bf16[1536,1024]{1,0:T(8,128)(2,1)} fusion(bf16[768,1024]{1,0:T(8,128)(2,1)S(1)} %bitcast.68, s32[768]{0:T(1024)S(1)} %copy-done.19), kind=kOutput, calls=%fused_computation.7 | convolution fusion | flops 2418671616 | bytes 4721664 | tf_op jit(solution)/shard_map/dot_general | solution.py:45
  31.1 4.9 %all-to-all-start.1 = ((bf16[32,48,1024]{2,1,0:T(8,128)(2,1)}), bf16[32,48,1024]{2,1,0:T(8,128)(2,1)}, u32[]{:S(2)}, u32[]{:S(2)}) async-start(bf16[32,48,1024]{2,1,0:T(8,128)(2,1)} %bitcast.65), calls=%async_computation.1 | async-start | bytes 6291456 | tf_op jit(solution)/shard_map/all_to_all | solution.py:59
  36.0 1.5 slice.130
  37.5 1.9 %slice.140 = f32[32,32,511]{2,1,0:T(8,128)} slice(f32[32,32,512]{2,1,0:T(8,128)S(1)} %copy-done.2), slice={[0:32], [0:32], [1:512]} | slice | bytes 4186112 | tf_op jit(solution)/shard_map/slice | solution.py:127
  39.4 1.7 %slice.135 = f32[32,31,512]{2,1,0:T(8,128)} slice(f32[32,32,512]{2,1,0:T(8,128)S(1)} %copy-done.2), slice={[0:32], [1:32], [0:512]} | slice | bytes 4063232 | tf_op jit(solution)/shard_map/slice | solution.py:126
  43.2 6.4 %multiply_subtract_fusion.1 = (f32[32,32,512]{2,1,0:T(8,128)S(1)}, f32[32,32,512]{2,1,0:T(8,128)S(1)}, f32[32,32,512]{2,1,0:T(8,128)S(1)}) fusion(f32[32,32,512]{2,1,0:T(8,128)} %param.15, f32[32,32,512]{2,1,0:T(8,128)S(1)} %copy-done.2, f32[32,32,511]{2,1,0:T(8,128)} %slice.140, f32[32,32,512]{2,1,0:T(8,128)} %param.16, f32[32,32,512]{2,1,0:T(8,128)} %param.14, ...), kind=kLoop, calls=%fused_computation.40 | loop fusion | flops 8388608 | bytes 23064576 | tf_op jit(solution)/shard_map/sub | solution.py:130
  52.3 3.1 %fusion.14 = f32[32,32,512]{2,1,0:T(8,128)} fusion(f32[32,32,512]{2,1,0:T(8,128)S(1)} %get-tuple-element.39, f32[31,32,512]{2,1,0:T(8,128)S(1)} %slice.156, f32[1,32,512]{2,1,0:T(8,128)S(1)} %get-tuple-element.32, f32[32,32,512]{2,1,0:T(8,128)S(1)} %get-tuple-element.38, f32[32,31,512]{2,1,0:T(8,128)S(1)} %bitcast.62, f32[32,1,512]{2,1,0:T(1,128)S(1)} %copy.32, ...), kind=kLoop, calls=%fused_computation.22 | loop fusion | flops 3670016 | bytes 14675968 | tf_op jit(solution)/shard_map/add | solution.py:138
  55.4 48.9 %all-to-all-done.1 = bf16[32,48,1024]{2,1,0:T(8,128)(2,1)} async-done(((bf16[32,48,1024]{2,1,0:T(8,128)(2,1)}), bf16[32,48,1024]{2,1,0:T(8,128)(2,1)}, u32[]{:S(2)}, u32[]{:S(2)}) %all-to-all-start.1) | async-done | bytes 3145760 | tf_op jit(solution)/shard_map/all_to_all | solution.py:59
  104.3 7.1 %all-to-all-start.2 = ((bf16[8,32,512]{2,1,0:T(8,128)(2,1)}), bf16[8,32,512]{2,1,0:T(8,128)(2,1)S(1)}, u32[]{:S(2)}, u32[]{:S(2)}) async-start(bf16[8,32,512]{2,1,0:T(8,128)(2,1)} %broadcast_select_fusion), calls=%async_computation.2 | async-start | bytes 524288 | tf_op jit(solution)/shard_map/all_to_all | solution.py:85
  111.3 4.7 %copy.29 = bf16[1536,1024]{0,1:T(8,128)(2,1)} copy(bf16[1536,1024]{1,0:T(8,128)(2,1)} %bitcast.10) | data formatting | bytes 6291456 | tf_op jit(solution)/shard_map/reshape | solution.py:70
  116.0 5.5 %fusion = f32[32,32,2,512]{3,1,2,0:T(8,128)S(1)} fusion(bf16[2,512,1536,1]{2,1,0,3:T(8,128)(2,1)} %bitcast.66, s32[1536]{0:T(1024)S(1)} %eq.62, s32[32,32]{1,0:T(8,128)S(1)} %multiply_add_fusion.2), kind=kOutput, calls=%fused_computation.1 | convolution fusion | flops 3222798336 | bytes 7350272 | tf_op jit(solution)/shard_map/dot_general | solution.py:69
  121.5 1.9 %copy-done.14 = f32[32,32,2,512]{3,1,2,0:T(8,128)} copy-done((f32[32,32,2,512]{3,1,2,0:T(8,128)}, f32[32,32,2,512]{3,1,2,0:T(8,128)S(1)}, u32[]{:S(2)}) %copy-start.14) | copy-done | bytes 4194328
  123.4 1.8 %fusion.10 = f32[32,32,512]{2,1,0:T(8,128)} fusion(f32[32,32,512]{2,1,0:T(8,128)S(1)} %copy-done.13, f32[32,32,2,512]{3,1,2,0:T(8,128)S(1)} %fusion), kind=kLoop, calls=%fused_computation.16 | loop fusion | flops 524288 | bytes 6291456 | tf_op jit(solution)/shard_map/sub | solution.py:142
  125.4 1.5 fusion.27
  126.8 3.0 %multiply_add_fusion.1 = f32[32,32,512]{2,1,0:T(8,128)S(1)} fusion(f32[32,32,512]{2,1,0:T(8,128)S(1)} %copy-done.2, f32[32,32,512]{2,1,0:T(8,128)} %fusion.27, f32[32,32,512]{2,1,0:T(8,128)} %param.16), kind=kLoop, calls=%fused_computation.39 | loop fusion | flops 3670016 | bytes 8388608 | tf_op jit(solution)/shard_map/add | solution.py:141
  130.0 2.9 %collective-permute-start.7 = (f32[32,512]{1,0:T(8,128)S(1)}, f32[32,512]{1,0:T(8,128)S(1)}, u32[]{:S(2)}, u32[]{:S(2)}) collective-permute-start(f32[32,512]{1,0:T(8,128)S(1)} %bitcast.76), channel_id=1, source_target_pairs={{0,1},{1,2},{2,3},{4,5},{5,6},{6,7},{8,9},{9,10},{10,11},{12,13},{... | collective-permute-start | bytes 196616 | tf_op jit(solution)/shard_map/ppermute | solution.py:14
  132.9 1.9 %collective-permute-start.5 = (f32[1,32,512]{2,1,0:T(8,128)S(1)}, f32[1,32,512]{2,1,0:T(8,128)S(1)}, u32[]{:S(2)}, u32[]{:S(2)}) collective-permute-start(f32[1,32,512]{2,1,0:T(8,128)S(1)} %slice.162), channel_id=1, source_target_pairs={{0,4},{4,8},{8,12},{12,16},{16,20},{20,24},{24,28},{1,5},{5,9},{9,... | collective-permute-start | bytes 196616 | tf_op jit(solution)/shard_map/ppermute | solution.py:14
  134.9 1.3 collective-permute-done.7
  136.2 1.9 %collective-permute-start.6 = (f32[32,512]{1,0:T(8,128)S(1)}, f32[32,512]{1,0:T(8,128)S(1)}, u32[]{:S(2)}, u32[]{:S(2)}) collective-permute-start(f32[32,512]{1,0:T(8,128)S(1)} %get-tuple-element.49), channel_id=1, source_target_pairs={{1,0},{2,1},{3,2},{5,4},{6,5},{7,6},{9,8},{10,9},{11,10},{13,12},{... | collective-permute-start | bytes 196616 | tf_op jit(solution)/shard_map/ppermute | solution.py:14
  138.6 2.7 %collective-permute-start.4 = (f32[1,32,512]{2,1,0:T(8,128)S(1)}, f32[1,32,512]{2,1,0:T(8,128)S(1)}, u32[]{:S(2)}, u32[]{:S(2)}) collective-permute-start(f32[1,32,512]{2,1,0:T(8,128)S(1)} %get-tuple-element.43), channel_id=1, source_target_pairs={{4,0},{8,4},{12,8},{16,12},{20,16},{24,20},{28,24},{5,1},{9,5},{13... | collective-permute-start | bytes 196616 | tf_op jit(solution)/shard_map/ppermute | solution.py:14
  145.0 2.3 %multiply_subtract_fusion = (f32[32,32,512]{2,1,0:T(8,128)S(1)}, f32[32,32,512]{2,1,0:T(8,128)S(1)}, f32[32,32,512]{2,1,0:T(8,128)S(1)}) fusion(f32[32,32,512]{2,1,0:T(8,128)S(1)} %copy-done.5, f32[32,32,512]{2,1,0:T(8,128)S(1)} %multiply_add_fusion.1, f32[32,32,511]{2,1,0:T(8,128)S(1)} %slice.168, f32[32,32,512]{2,1,0:T(8,128)S(1)} %copy-done.3, ...), kind=kLoop, calls=%fused_computation.38 | loop fusion | flops 8388608 | bytes 23064576 | tf_op jit(solution)/shard_map/sub | solution.py:130
  147.6 2.2 %fusion.9 = f32[32,32,512]{2,1,0:T(8,128)S(1)} fusion(f32[32,32,2,512]{3,1,2,0:T(8,128)S(1)} %copy-done.15, f32[32,32,512]{2,1,0:T(8,128)S(1)} %get-tuple-element.36, f32[31,32,512]{2,1,0:T(8,128)S(1)} %slice.163, f32[1,32,512]{2,1,0:T(8,128)S(1)} %get-tuple-element.42, f32[32,32,512]{2,1,0:T(8,128)S(1)} %get-tuple-element.35, ...), kind=kLoop, calls=%fused_computation.14 | loop fusion | flops 4194304 | bytes 16773120 | tf_op jit(solution)/shard_map/sub | solution.py:142
  150.8 2.1 %multiply_add_fusion = f32[32,32,512]{2,1,0:T(8,128)} fusion(f32[32,32,512]{2,1,0:T(8,128)S(1)} %multiply_add_fusion.1, f32[32,32,512]{2,1,0:T(8,128)S(1)} %fusion.26, f32[32,32,512]{2,1,0:T(8,128)S(1)} %copy-done.3), kind=kLoop, calls=%fused_computation.37 | loop fusion | flops 3670016 | bytes 8388608 | tf_op jit(solution)/shard_map/add | solution.py:141
  (92 shorter events, 14.7 us)
Async XLA Ops:
  0.6 40.7 %copy-start = (bf16[16,32,512]{2,1,0:T(8,128)(2,1)S(1)}, bf16[16,32,512]{2,1,0:T(8,128)(2,1)}, u32[]{:S(2)}) copy-start(bf16[16,32,512]{2,1,0:T(8,128)(2,1)} %param.20) | copy-start | bytes 1572868
  0.6 23.4 %slice-start = ((f32[32,32,512]{2,1,0:T(8,128)}), f32[1,32,512]{2,1,0:T(8,128)S(1)}, s32[]{:S(2)}) async-start(f32[32,32,512]{2,1,0:T(8,128)} %param.16), calls=%async_computation.3 | async-start | bytes 131072 | tf_op jit(solution)/shard_map/slice | solution.py:103
  0.7 23.4 %slice-start.1 = ((f32[32,32,512]{2,1,0:T(8,128)}), f32[1,32,512]{2,1,0:T(8,128)S(1)}, s32[]{:S(2)}) async-start(f32[32,32,512]{2,1,0:T(8,128)} %param.13), calls=%async_computation.4 | async-start | bytes 131072 | tf_op jit(solution)/shard_map/slice | solution.py:103
  0.7 25.4 %copy-start.16 = (bf16[768,2,512]{2,1,0:T(2,128)(2,1)S(1)}, bf16[768,2,512]{2,1,0:T(2,128)(2,1)}, u32[]{:S(2)}) copy-start(bf16[768,2,512]{2,1,0:T(2,128)(2,1)} %param.17) | copy-start | bytes 4718596
  4.0 26.5 %all-to-all-start = ((s32[32,1,48]{2,1,0:T(1,128)}), s32[32,1,48]{2,1,0:T(1,128)S(1)}, u32[]{:S(2)}, u32[]{:S(2)}) async-start(s32[32,1,48]{2,1,0:T(1,128)} %sub.122), calls=%async_computation | async-start | bytes 32768 | tf_op jit(solution)/shard_map/all_to_all | solution.py:51
  11.5 19.1 %collective-permute-start = (f32[1,32,512]{2,1,0:T(8,128)}, f32[1,32,512]{2,1,0:T(8,128)S(1)}, u32[]{:S(2)}, u32[]{:S(2)}) collective-permute-start(f32[1,32,512]{2,1,0:T(8,128)} %get-tuple-element.47), channel_id=1, source_target_pairs={{4,0},{8,4},{12,8},{16,12},{20,16},{24,20},{28,24},{5,1},{9,5},{13... | collective-permute-start | bytes 196616 | tf_op jit(solution)/shard_map/ppermute | solution.py:14
  15.0 15.5 %collective-permute-start.1 = (f32[32,512]{1,0:T(8,128)S(1)}, f32[32,512]{1,0:T(8,128)S(1)}, u32[]{:S(2)}, u32[]{:S(2)}) collective-permute-start(f32[32,512]{1,0:T(8,128)S(1)} %bitcast.75), channel_id=1, source_target_pairs={{1,0},{2,1},{3,2},{5,4},{6,5},{7,6},{9,8},{10,9},{11,10},{13,12},{... | collective-permute-start | bytes 196616 | tf_op jit(solution)/shard_map/ppermute | solution.py:14
  19.7 6.7 %copy-start.19 = (s32[768]{0:T(1024)S(1)}, s32[768]{0:T(1024)}, u32[]{:S(2)}) copy-start(s32[768]{0:T(1024)} %copy-done.18) | copy-start | bytes 9220
  19.8 10.7 %collective-permute-start.3 = (f32[3,32,512]{2,1,0:T(8,128)S(1)}, f32[3,32,512]{2,1,0:T(8,128)S(1)}, u32[]{:S(2)}, u32[]{:S(2)}) collective-permute-start(f32[3,32,512]{2,1,0:T(8,128)S(1)} %pad_maximum_fusion.1), channel_id=1, source_target_pairs={{0,1},{1,2},{2,3},{4,5},{5,6},{6,7},{8,9},{9,10},{10,11},{12,13},{... | collective-permute-start | bytes 589832 | tf_op jit(solution)/shard_map/ppermute | solution.py:14
  24.1 7.0 %collective-permute-start.2 = (f32[3,32,512]{2,1,0:T(8,128)S(1)}, f32[3,32,512]{2,1,0:T(8,128)S(1)}, u32[]{:S(2)}, u32[]{:S(2)}) collective-permute-start(f32[3,32,512]{2,1,0:T(8,128)S(1)} %pad_maximum_fusion), channel_id=1, source_target_pairs={{0,4},{4,8},{8,12},{12,16},{16,20},{20,24},{24,28},{1,5},{5,9},{9,... | collective-permute-start | bytes 589832 | tf_op jit(solution)/shard_map/ppermute | solution.py:14
  31.1 4.9 %copy-start.2 = (f32[32,32,512]{2,1,0:T(8,128)S(1)}, f32[32,32,512]{2,1,0:T(8,128)}, u32[]{:S(2)}) copy-start(f32[32,32,512]{2,1,0:T(8,128)} %param.12) | copy-start | bytes 6291460
  31.1 73.2 %all-to-all-start.1 = ((bf16[32,48,1024]{2,1,0:T(8,128)(2,1)}), bf16[32,48,1024]{2,1,0:T(8,128)(2,1)}, u32[]{:S(2)}, u32[]{:S(2)}) async-start(bf16[32,48,1024]{2,1,0:T(8,128)(2,1)} %bitcast.65), calls=%async_computation.1 | async-start | bytes 6291456 | tf_op jit(solution)/shard_map/all_to_all | solution.py:59
  39.4 1.7 %copy-start.17 = (s32[8,8]{1,0:T(8,128)S(1)}, s32[8,8]{1,0:T(8,128)}, u32[]{:S(2)}) copy-start(s32[8,8]{1,0:T(8,128)} %param.21) | copy-start | bytes 772
  49.6 1.3 copy-start.4
  49.6 2.0 %copy-start.6 = (f32[32,32,512]{2,1,0:T(8,128)}, f32[32,32,512]{2,1,0:T(8,128)S(1)}, u32[]{:S(2)}) copy-start(f32[32,32,512]{2,1,0:T(8,128)S(1)} %get-tuple-element.38) | copy-start | bytes 6291460
  49.6 2.7 %copy-start.8 = (f32[32,32,512]{2,1,0:T(8,128)}, f32[32,32,512]{2,1,0:T(8,128)S(1)}, u32[]{:S(2)}) copy-start(f32[32,32,512]{2,1,0:T(8,128)S(1)} %get-tuple-element.39) | copy-start | bytes 6291460
  104.3 21.0 %all-to-all-start.2 = ((bf16[8,32,512]{2,1,0:T(8,128)(2,1)}), bf16[8,32,512]{2,1,0:T(8,128)(2,1)S(1)}, u32[]{:S(2)}, u32[]{:S(2)}) async-start(bf16[8,32,512]{2,1,0:T(8,128)(2,1)} %broadcast_select_fusion), calls=%async_computation.2 | async-start | bytes 524288 | tf_op jit(solution)/shard_map/all_to_all | solution.py:85
  116.0 7.5 %copy-start.13 = (f32[32,32,512]{2,1,0:T(8,128)S(1)}, f32[32,32,512]{2,1,0:T(8,128)}, u32[]{:S(2)}) copy-start(f32[32,32,512]{2,1,0:T(8,128)} %fusion.14) | copy-start | bytes 6291460
  121.5 2.0 %copy-start.14 = (f32[32,32,2,512]{3,1,2,0:T(8,128)}, f32[32,32,2,512]{3,1,2,0:T(8,128)S(1)}, u32[]{:S(2)}) copy-start(f32[32,32,2,512]{3,1,2,0:T(8,128)S(1)} %fusion) | copy-start | bytes 12582916
  130.0 6.2 %collective-permute-start.7 = (f32[32,512]{1,0:T(8,128)S(1)}, f32[32,512]{1,0:T(8,128)S(1)}, u32[]{:S(2)}, u32[]{:S(2)}) collective-permute-start(f32[32,512]{1,0:T(8,128)S(1)} %bitcast.76), channel_id=1, source_target_pairs={{0,1},{1,2},{2,3},{4,5},{5,6},{6,7},{8,9},{9,10},{10,11},{12,13},{... | collective-permute-start | bytes 196616 | tf_op jit(solution)/shard_map/ppermute | solution.py:14
  132.9 5.6 %collective-permute-start.5 = (f32[1,32,512]{2,1,0:T(8,128)S(1)}, f32[1,32,512]{2,1,0:T(8,128)S(1)}, u32[]{:S(2)}, u32[]{:S(2)}) collective-permute-start(f32[1,32,512]{2,1,0:T(8,128)S(1)} %slice.162), channel_id=1, source_target_pairs={{0,4},{4,8},{8,12},{12,16},{16,20},{20,24},{24,28},{1,5},{5,9},{9,... | collective-permute-start | bytes 196616 | tf_op jit(solution)/shard_map/ppermute | solution.py:14
  136.2 7.1 %collective-permute-start.6 = (f32[32,512]{1,0:T(8,128)S(1)}, f32[32,512]{1,0:T(8,128)S(1)}, u32[]{:S(2)}, u32[]{:S(2)}) collective-permute-start(f32[32,512]{1,0:T(8,128)S(1)} %get-tuple-element.49), channel_id=1, source_target_pairs={{1,0},{2,1},{3,2},{5,4},{6,5},{7,6},{9,8},{10,9},{11,10},{13,12},{... | collective-permute-start | bytes 196616 | tf_op jit(solution)/shard_map/ppermute | solution.py:14
  138.6 4.8 %collective-permute-start.4 = (f32[1,32,512]{2,1,0:T(8,128)S(1)}, f32[1,32,512]{2,1,0:T(8,128)S(1)}, u32[]{:S(2)}, u32[]{:S(2)}) collective-permute-start(f32[1,32,512]{2,1,0:T(8,128)S(1)} %get-tuple-element.43), channel_id=1, source_target_pairs={{4,0},{8,4},{12,8},{16,12},{20,16},{24,20},{28,24},{5,1},{9,5},{13... | collective-permute-start | bytes 196616 | tf_op jit(solution)/shard_map/ppermute | solution.py:14
  141.5 1.9 %copy-start.7 = (f32[32,32,512]{2,1,0:T(8,128)S(1)}, f32[32,32,512]{2,1,0:T(8,128)}, u32[]{:S(2)}) copy-start(f32[32,32,512]{2,1,0:T(8,128)} %copy-done.6) | copy-start | bytes 6291460
  141.5 2.2 %copy-start.9 = (f32[32,32,512]{2,1,0:T(8,128)S(1)}, f32[32,32,512]{2,1,0:T(8,128)}, u32[]{:S(2)}) copy-start(f32[32,32,512]{2,1,0:T(8,128)} %copy-done.8) | copy-start | bytes 6291460
  141.9 2.6 %copy-start.3 = (f32[32,32,512]{2,1,0:T(8,128)S(1)}, f32[32,32,512]{2,1,0:T(8,128)}, u32[]{:S(2)}) copy-start(f32[32,32,512]{2,1,0:T(8,128)} %param.16) | copy-start | bytes 6291460
  141.9 3.2 %copy-start.5 = (f32[32,32,512]{2,1,0:T(8,128)S(1)}, f32[32,32,512]{2,1,0:T(8,128)}, u32[]{:S(2)}) copy-start(f32[32,32,512]{2,1,0:T(8,128)} %copy-done.4) | copy-start | bytes 6291460
  145.0 2.6 %copy-start.15 = (f32[32,32,2,512]{3,1,2,0:T(8,128)S(1)}, f32[32,32,2,512]{3,1,2,0:T(8,128)}, u32[]{:S(2)}) copy-start(f32[32,32,2,512]{3,1,2,0:T(8,128)} %copy-done.14) | copy-start | bytes 12582916
  147.3 2.5 %copy-start.10 = (f32[32,32,512]{2,1,0:T(8,128)}, f32[32,32,512]{2,1,0:T(8,128)S(1)}, u32[]{:S(2)}) copy-start(f32[32,32,512]{2,1,0:T(8,128)S(1)} %get-tuple-element.34) | copy-start | bytes 6291460
  147.3 2.7 %copy-start.11 = (f32[32,32,512]{2,1,0:T(8,128)}, f32[32,32,512]{2,1,0:T(8,128)S(1)}, u32[]{:S(2)}) copy-start(f32[32,32,512]{2,1,0:T(8,128)S(1)} %get-tuple-element.35) | copy-start | bytes 6291460
  147.3 3.4 %copy-start.12 = (f32[32,32,512]{2,1,0:T(8,128)}, f32[32,32,512]{2,1,0:T(8,128)S(1)}, u32[]{:S(2)}) copy-start(f32[32,32,512]{2,1,0:T(8,128)S(1)} %get-tuple-element.36) | copy-start | bytes 6291460
  150.7 2.1 %copy-start.1 = (bf16[16,32,512]{2,1,0:T(8,128)(2,1)S(1)}, bf16[16,32,512]{2,1,0:T(8,128)(2,1)}, u32[]{:S(2)}) copy-start(bf16[16,32,512]{2,1,0:T(8,128)(2,1)} %param.20) | copy-start | bytes 1572868
  (1 other events, 0.7 us)

commit v16 on v15

--- a/solution.py
+++ b/solution.py
@@ -47,7 +47,7 @@
         waves.reshape(bubbles, steps * depth),
         preferred_element_type=jnp.float32,
     ).astype(jnp.bfloat16)
-    out_cols = jnp.max(jnp.where(placed, bubble_column[None, :] + 1, 0), axis=1) - 1
+    out_cols = jnp.max(jnp.where(placed, bubble_column[None, :], -1), axis=1)
     in_cols = lax.all_to_all(
         out_cols.reshape(devices, capacity),
         ("gx", "gy"),

time: 155 us -> 155 us (level)
  no operation moved by 1% of the time
where the time goes in v16:
time: 155 us; the launch traced here: 153 us
  waiting for transfers between devices  51.9 us (33%)
  starting transfers between devices  38.2 us (25%)
  other arithmetic  26.1 us (17%)
  local copies, waits for them, and re-layouts  25.7 us (17%)
  matrix products  9.87 us (6%)
    all_to_all x1, waiting for transfers between devices, bubble_source(): lax.all_to_all(outgoing.reshape(devices, capacity, steps * depth), ('gx',...  48.9 us
    ppermute x8, starting transfers between devices, from_behind(): return lax.ppermute(block, axis, route)  20.3 us
    sub x2, other arithmetic, body(): vel_z = vel_z - step_ratio * buoyancy * (next_z - pressure)  8.61 us
    unnamed x46, local copies, waits for them, and re-layouts  7.42 us
    all_to_all x1, starting transfers between devices, incident_plane(): rows = lax.all_to_all(chosen, 'gx', split_axis=0, concat_axis=0, tiled=True)  7.06 us
    all_to_all x1, starting transfers between devices, bubble_source(): lax.all_to_all(out_cols.reshape(devices, capacity), ('gx', 'gy'), split_a...  5.91 us
    dot_general x1, matrix products, bubble_source(): jnp.dot(hits, incoming.reshape(slots, steps * depth), preferred_element_t...  5.48 us
    add x2, other arithmetic, body(): pressure + step_ratio * stiffness * (source[:, :, step, :] - divergence +...  5.09 us
  transfers between devices with their start and end apart: 11, of which 5 were waited for; matrix products, arithmetic and copies ran while one was open for 26% of the time, Pallas kernels for 0%

profile of v16, /device:TPU:18, one launch (start us, length us, event | category | flops | bytes accessed | tf_op | source)
XLA Modules:
  0.0 152.9 jit_solution(1721491971640636845)
XLA Ops:
  1.9 1.4 select_reduce_fusion
  4.0 5.9 %all-to-all-start = ((s32[32,1,48]{2,1,0:T(1,128)}), s32[32,1,48]{2,1,0:T(1,128)S(1)}, u32[]{:S(2)}, u32[]{:S(2)}) async-start(s32[32,1,48]{2,1,0:T(1,128)} %all_to_all.14), calls=%async_computation | async-start | bytes 32768 | tf_op jit(solution)/shard_map/all_to_all | solution.py:51
  9.9 1.5 fusion.39
  11.4 2.2 %collective-permute-start = (f32[1,32,512]{2,1,0:T(8,128)}, f32[1,32,512]{2,1,0:T(8,128)S(1)}, u32[]{:S(2)}, u32[]{:S(2)}) collective-permute-start(f32[1,32,512]{2,1,0:T(8,128)} %get-tuple-element.47), channel_id=1, source_target_pairs={{4,0},{8,4},{12,8},{16,12},{20,16},{24,20},{28,24},{5,1},{9,5},{13... | collective-permute-start | bytes 196616 | tf_op jit(solution)/shard_map/ppermute | solution.py:14
  13.7 1.3 fusion.38
  15.0 2.5 %collective-permute-start.1 = (f32[32,512]{1,0:T(8,128)S(1)}, f32[32,512]{1,0:T(8,128)S(1)}, u32[]{:S(2)}, u32[]{:S(2)}) collective-permute-start(f32[32,512]{1,0:T(8,128)S(1)} %bitcast.75), channel_id=1, source_target_pairs={{1,0},{2,1},{3,2},{5,4},{6,5},{7,6},{9,8},{10,9},{11,10},{13,12},{... | collective-permute-start | bytes 196616 | tf_op jit(solution)/shard_map/ppermute | solution.py:14
  17.5 1.1 slice.127
  19.8 4.3 %collective-permute-start.3 = (f32[3,32,512]{2,1,0:T(8,128)S(1)}, f32[3,32,512]{2,1,0:T(8,128)S(1)}, u32[]{:S(2)}, u32[]{:S(2)}) collective-permute-start(f32[3,32,512]{2,1,0:T(8,128)S(1)} %pad_maximum_fusion.1), channel_id=1, source_target_pairs={{0,1},{1,2},{2,3},{4,5},{5,6},{6,7},{8,9},{9,10},{10,11},{12,13},{... | collective-permute-start | bytes 589832 | tf_op jit(solution)/shard_map/ppermute | solution.py:14
  24.1 1.9 %collective-permute-start.2 = (f32[3,32,512]{2,1,0:T(8,128)S(1)}, f32[3,32,512]{2,1,0:T(8,128)S(1)}, u32[]{:S(2)}, u32[]{:S(2)}) collective-permute-start(f32[3,32,512]{2,1,0:T(8,128)S(1)} %pad_maximum_fusion), channel_id=1, source_target_pairs={{0,4},{4,8},{8,12},{12,16},{16,20},{20,24},{24,28},{1,5},{5,9},{9,... | collective-permute-start | bytes 589832 | tf_op jit(solution)/shard_map/ppermute | solution.py:14
  26.5 4.0 %fusion.4 = bf16[1536,1024]{1,0:T(8,128)(2,1)} fusion(bf16[768,1024]{1,0:T(8,128)(2,1)S(1)} %bitcast.68, s32[768]{0:T(1024)S(1)} %copy-done.19), kind=kOutput, calls=%fused_computation.7 | convolution fusion | flops 2418671616 | bytes 4721664 | tf_op jit(solution)/shard_map/dot_general | solution.py:45
  31.1 4.9 %all-to-all-start.1 = ((bf16[32,48,1024]{2,1,0:T(8,128)(2,1)}), bf16[32,48,1024]{2,1,0:T(8,128)(2,1)}, u32[]{:S(2)}, u32[]{:S(2)}) async-start(bf16[32,48,1024]{2,1,0:T(8,128)(2,1)} %bitcast.65), calls=%async_computation.1 | async-start | bytes 6291456 | tf_op jit(solution)/shard_map/all_to_all | solution.py:59
  36.0 1.5 slice.130
  37.5 1.9 %slice.140 = f32[32,32,511]{2,1,0:T(8,128)} slice(f32[32,32,512]{2,1,0:T(8,128)S(1)} %copy-done.2), slice={[0:32], [0:32], [1:512]} | slice | bytes 4186112 | tf_op jit(solution)/shard_map/slice | solution.py:127
  39.4 1.7 %slice.135 = f32[32,31,512]{2,1,0:T(8,128)} slice(f32[32,32,512]{2,1,0:T(8,128)S(1)} %copy-done.2), slice={[0:32], [1:32], [0:512]} | slice | bytes 4063232 | tf_op jit(solution)/shard_map/slice | solution.py:126
  43.2 6.4 %multiply_subtract_fusion.1 = (f32[32,32,512]{2,1,0:T(8,128)S(1)}, f32[32,32,512]{2,1,0:T(8,128)S(1)}, f32[32,32,512]{2,1,0:T(8,128)S(1)}) fusion(f32[32,32,512]{2,1,0:T(8,128)} %param.15, f32[32,32,512]{2,1,0:T(8,128)S(1)} %copy-done.2, f32[32,32,511]{2,1,0:T(8,128)} %slice.140, f32[32,32,512]{2,1,0:T(8,128)} %param.16, f32[32,32,512]{2,1,0:T(8,128)} %param.14, ...), kind=kLoop, calls=%fused_computation.40 | loop fusion | flops 8388608 | bytes 23064576 | tf_op jit(solution)/shard_map/sub | solution.py:130
  52.3 3.1 %fusion.14 = f32[32,32,512]{2,1,0:T(8,128)} fusion(f32[32,32,512]{2,1,0:T(8,128)S(1)} %get-tuple-element.39, f32[31,32,512]{2,1,0:T(8,128)S(1)} %slice.156, f32[1,32,512]{2,1,0:T(8,128)S(1)} %get-tuple-element.32, f32[32,32,512]{2,1,0:T(8,128)S(1)} %get-tuple-element.38, f32[32,31,512]{2,1,0:T(8,128)S(1)} %bitcast.62, f32[32,1,512]{2,1,0:T(1,128)S(1)} %copy.32, ...), kind=kLoop, calls=%fused_computation.22 | loop fusion | flops 3670016 | bytes 14675968 | tf_op jit(solution)/shard_map/add | solution.py:138
  55.4 48.9 %all-to-all-done.1 = bf16[32,48,1024]{2,1,0:T(8,128)(2,1)} async-done(((bf16[32,48,1024]{2,1,0:T(8,128)(2,1)}), bf16[32,48,1024]{2,1,0:T(8,128)(2,1)}, u32[]{:S(2)}, u32[]{:S(2)}) %all-to-all-start.1) | async-done | bytes 3145760 | tf_op jit(solution)/shard_map/all_to_all | solution.py:59
  104.2 7.1 %all-to-all-start.2 = ((bf16[8,32,512]{2,1,0:T(8,128)(2,1)}), bf16[8,32,512]{2,1,0:T(8,128)(2,1)S(1)}, u32[]{:S(2)}, u32[]{:S(2)}) async-start(bf16[8,32,512]{2,1,0:T(8,128)(2,1)} %broadcast_select_fusion), calls=%async_computation.2 | async-start | bytes 524288 | tf_op jit(solution)/shard_map/all_to_all | solution.py:85
  111.3 4.7 %copy.29 = bf16[1536,1024]{0,1:T(8,128)(2,1)} copy(bf16[1536,1024]{1,0:T(8,128)(2,1)} %bitcast.10) | data formatting | bytes 6291456 | tf_op jit(solution)/shard_map/reshape | solution.py:70
  116.0 5.5 %fusion = f32[32,32,2,512]{3,1,2,0:T(8,128)S(1)} fusion(bf16[2,512,1536,1]{2,1,0,3:T(8,128)(2,1)} %bitcast.66, s32[1536]{0:T(1024)S(1)} %eq.62, s32[32,32]{1,0:T(8,128)S(1)} %multiply_add_fusion.2), kind=kOutput, calls=%fused_computation.1 | convolution fusion | flops 3222798336 | bytes 7350272 | tf_op jit(solution)/shard_map/dot_general | solution.py:69
  121.5 1.9 %copy-done.14 = f32[32,32,2,512]{3,1,2,0:T(8,128)} copy-done((f32[32,32,2,512]{3,1,2,0:T(8,128)}, f32[32,32,2,512]{3,1,2,0:T(8,128)S(1)}, u32[]{:S(2)}) %copy-start.14) | copy-done | bytes 4194328
  123.4 1.8 %fusion.10 = f32[32,32,512]{2,1,0:T(8,128)} fusion(f32[32,32,512]{2,1,0:T(8,128)S(1)} %copy-done.13, f32[32,32,2,512]{3,1,2,0:T(8,128)S(1)} %fusion), kind=kLoop, calls=%fused_computation.16 | loop fusion | flops 524288 | bytes 6291456 | tf_op jit(solution)/shard_map/sub | solution.py:142
  125.4 1.5 fusion.27
  126.8 3.0 %multiply_add_fusion.1 = f32[32,32,512]{2,1,0:T(8,128)S(1)} fusion(f32[32,32,512]{2,1,0:T(8,128)S(1)} %copy-done.2, f32[32,32,512]{2,1,0:T(8,128)} %fusion.27, f32[32,32,512]{2,1,0:T(8,128)} %param.16), kind=kLoop, calls=%fused_computation.39 | loop fusion | flops 3670016 | bytes 8388608 | tf_op jit(solution)/shard_map/add | solution.py:141
  130.0 2.9 %collective-permute-start.7 = (f32[32,512]{1,0:T(8,128)S(1)}, f32[32,512]{1,0:T(8,128)S(1)}, u32[]{:S(2)}, u32[]{:S(2)}) collective-permute-start(f32[32,512]{1,0:T(8,128)S(1)} %bitcast.76), channel_id=1, source_target_pairs={{0,1},{1,2},{2,3},{4,5},{5,6},{6,7},{8,9},{9,10},{10,11},{12,13},{... | collective-permute-start | bytes 196616 | tf_op jit(solution)/shard_map/ppermute | solution.py:14
  132.9 1.9 %collective-permute-start.5 = (f32[1,32,512]{2,1,0:T(8,128)S(1)}, f32[1,32,512]{2,1,0:T(8,128)S(1)}, u32[]{:S(2)}, u32[]{:S(2)}) collective-permute-start(f32[1,32,512]{2,1,0:T(8,128)S(1)} %slice.162), channel_id=1, source_target_pairs={{0,4},{4,8},{8,12},{12,16},{16,20},{20,24},{24,28},{1,5},{5,9},{9,... | collective-permute-start | bytes 196616 | tf_op jit(solution)/shard_map/ppermute | solution.py:14
  134.9 1.3 collective-permute-done.7
  136.2 1.9 %collective-permute-start.6 = (f32[32,512]{1,0:T(8,128)S(1)}, f32[32,512]{1,0:T(8,128)S(1)}, u32[]{:S(2)}, u32[]{:S(2)}) collective-permute-start(f32[32,512]{1,0:T(8,128)S(1)} %get-tuple-element.49), channel_id=1, source_target_pairs={{1,0},{2,1},{3,2},{5,4},{6,5},{7,6},{9,8},{10,9},{11,10},{13,12},{... | collective-permute-start | bytes 196616 | tf_op jit(solution)/shard_map/ppermute | solution.py:14
  138.5 2.7 %collective-permute-start.4 = (f32[1,32,512]{2,1,0:T(8,128)S(1)}, f32[1,32,512]{2,1,0:T(8,128)S(1)}, u32[]{:S(2)}, u32[]{:S(2)}) collective-permute-start(f32[1,32,512]{2,1,0:T(8,128)S(1)} %get-tuple-element.43), channel_id=1, source_target_pairs={{4,0},{8,4},{12,8},{16,12},{20,16},{24,20},{28,24},{5,1},{9,5},{13... | collective-permute-start | bytes 196616 | tf_op jit(solution)/shard_map/ppermute | solution.py:14
  145.0 2.3 %multiply_subtract_fusion = (f32[32,32,512]{2,1,0:T(8,128)S(1)}, f32[32,32,512]{2,1,0:T(8,128)S(1)}, f32[32,32,512]{2,1,0:T(8,128)S(1)}) fusion(f32[32,32,512]{2,1,0:T(8,128)S(1)} %copy-done.5, f32[32,32,512]{2,1,0:T(8,128)S(1)} %multiply_add_fusion.1, f32[32,32,511]{2,1,0:T(8,128)S(1)} %slice.168, f32[32,32,512]{2,1,0:T(8,128)S(1)} %copy-done.3, ...), kind=kLoop, calls=%fused_computation.38 | loop fusion | flops 8388608 | bytes 23064576 | tf_op jit(solution)/shard_map/sub | solution.py:130
  147.6 2.2 %fusion.9 = f32[32,32,512]{2,1,0:T(8,128)S(1)} fusion(f32[32,32,2,512]{3,1,2,0:T(8,128)S(1)} %copy-done.15, f32[32,32,512]{2,1,0:T(8,128)S(1)} %get-tuple-element.36, f32[31,32,512]{2,1,0:T(8,128)S(1)} %slice.163, f32[1,32,512]{2,1,0:T(8,128)S(1)} %get-tuple-element.42, f32[32,32,512]{2,1,0:T(8,128)S(1)} %get-tuple-element.35, ...), kind=kLoop, calls=%fused_computation.14 | loop fusion | flops 4194304 | bytes 16773120 | tf_op jit(solution)/shard_map/sub | solution.py:142
  150.7 2.1 %multiply_add_fusion = f32[32,32,512]{2,1,0:T(8,128)} fusion(f32[32,32,512]{2,1,0:T(8,128)S(1)} %multiply_add_fusion.1, f32[32,32,512]{2,1,0:T(8,128)S(1)} %fusion.26, f32[32,32,512]{2,1,0:T(8,128)S(1)} %copy-done.3), kind=kLoop, calls=%fused_computation.37 | loop fusion | flops 3670016 | bytes 8388608 | tf_op jit(solution)/shard_map/add | solution.py:141
  (90 shorter events, 14.4 us)
Async XLA Ops:
  0.6 40.7 %copy-start = (bf16[16,32,512]{2,1,0:T(8,128)(2,1)S(1)}, bf16[16,32,512]{2,1,0:T(8,128)(2,1)}, u32[]{:S(2)}) copy-start(bf16[16,32,512]{2,1,0:T(8,128)(2,1)} %param.20) | copy-start | bytes 1572868
  0.6 23.4 %slice-start = ((f32[32,32,512]{2,1,0:T(8,128)}), f32[1,32,512]{2,1,0:T(8,128)S(1)}, s32[]{:S(2)}) async-start(f32[32,32,512]{2,1,0:T(8,128)} %param.16), calls=%async_computation.3 | async-start | bytes 131072 | tf_op jit(solution)/shard_map/slice | solution.py:103
  0.7 23.4 %slice-start.1 = ((f32[32,32,512]{2,1,0:T(8,128)}), f32[1,32,512]{2,1,0:T(8,128)S(1)}, s32[]{:S(2)}) async-start(f32[32,32,512]{2,1,0:T(8,128)} %param.13), calls=%async_computation.4 | async-start | bytes 131072 | tf_op jit(solution)/shard_map/slice | solution.py:103
  0.7 25.4 %copy-start.16 = (bf16[768,2,512]{2,1,0:T(2,128)(2,1)S(1)}, bf16[768,2,512]{2,1,0:T(2,128)(2,1)}, u32[]{:S(2)}) copy-start(bf16[768,2,512]{2,1,0:T(2,128)(2,1)} %param.17) | copy-start | bytes 4718596
  1.9 15.6 %copy-start.18 = (s32[768]{0:T(1024)}, s32[768]{0:T(1024)S(1)}, u32[]{:S(2)}) copy-start(s32[768]{0:T(1024)S(1)} %convert_add_fusion) | copy-start | bytes 9220
  4.0 26.5 %all-to-all-start = ((s32[32,1,48]{2,1,0:T(1,128)}), s32[32,1,48]{2,1,0:T(1,128)S(1)}, u32[]{:S(2)}, u32[]{:S(2)}) async-start(s32[32,1,48]{2,1,0:T(1,128)} %all_to_all.14), calls=%async_computation | async-start | bytes 32768 | tf_op jit(solution)/shard_map/all_to_all | solution.py:51
  11.4 19.1 %collective-permute-start = (f32[1,32,512]{2,1,0:T(8,128)}, f32[1,32,512]{2,1,0:T(8,128)S(1)}, u32[]{:S(2)}, u32[]{:S(2)}) collective-permute-start(f32[1,32,512]{2,1,0:T(8,128)} %get-tuple-element.47), channel_id=1, source_target_pairs={{4,0},{8,4},{12,8},{16,12},{20,16},{24,20},{28,24},{5,1},{9,5},{13... | collective-permute-start | bytes 196616 | tf_op jit(solution)/shard_map/ppermute | solution.py:14
  15.0 15.5 %collective-permute-start.1 = (f32[32,512]{1,0:T(8,128)S(1)}, f32[32,512]{1,0:T(8,128)S(1)}, u32[]{:S(2)}, u32[]{:S(2)}) collective-permute-start(f32[32,512]{1,0:T(8,128)S(1)} %bitcast.75), channel_id=1, source_target_pairs={{1,0},{2,1},{3,2},{5,4},{6,5},{7,6},{9,8},{10,9},{11,10},{13,12},{... | collective-permute-start | bytes 196616 | tf_op jit(solution)/shard_map/ppermute | solution.py:14
  19.7 6.7 %copy-start.19 = (s32[768]{0:T(1024)S(1)}, s32[768]{0:T(1024)}, u32[]{:S(2)}) copy-start(s32[768]{0:T(1024)} %copy-done.18) | copy-start | bytes 9220
  19.8 10.7 %collective-permute-start.3 = (f32[3,32,512]{2,1,0:T(8,128)S(1)}, f32[3,32,512]{2,1,0:T(8,128)S(1)}, u32[]{:S(2)}, u32[]{:S(2)}) collective-permute-start(f32[3,32,512]{2,1,0:T(8,128)S(1)} %pad_maximum_fusion.1), channel_id=1, source_target_pairs={{0,1},{1,2},{2,3},{4,5},{5,6},{6,7},{8,9},{9,10},{10,11},{12,13},{... | collective-permute-start | bytes 589832 | tf_op jit(solution)/shard_map/ppermute | solution.py:14
  24.1 7.0 %collective-permute-start.2 = (f32[3,32,512]{2,1,0:T(8,128)S(1)}, f32[3,32,512]{2,1,0:T(8,128)S(1)}, u32[]{:S(2)}, u32[]{:S(2)}) collective-permute-start(f32[3,32,512]{2,1,0:T(8,128)S(1)} %pad_maximum_fusion), channel_id=1, source_target_pairs={{0,4},{4,8},{8,12},{12,16},{16,20},{20,24},{24,28},{1,5},{5,9},{9,... | collective-permute-start | bytes 589832 | tf_op jit(solution)/shard_map/ppermute | solution.py:14
  31.1 4.9 %copy-start.2 = (f32[32,32,512]{2,1,0:T(8,128)S(1)}, f32[32,32,512]{2,1,0:T(8,128)}, u32[]{:S(2)}) copy-start(f32[32,32,512]{2,1,0:T(8,128)} %param.12) | copy-start | bytes 6291460
  31.1 73.2 %all-to-all-start.1 = ((bf16[32,48,1024]{2,1,0:T(8,128)(2,1)}), bf16[32,48,1024]{2,1,0:T(8,128)(2,1)}, u32[]{:S(2)}, u32[]{:S(2)}) async-start(bf16[32,48,1024]{2,1,0:T(8,128)(2,1)} %bitcast.65), calls=%async_computation.1 | async-start | bytes 6291456 | tf_op jit(solution)/shard_map/all_to_all | solution.py:59
  39.4 1.7 %copy-start.17 = (s32[8,8]{1,0:T(8,128)S(1)}, s32[8,8]{1,0:T(8,128)}, u32[]{:S(2)}) copy-start(s32[8,8]{1,0:T(8,128)} %param.21) | copy-start | bytes 772
  49.6 2.0 %copy-start.6 = (f32[32,32,512]{2,1,0:T(8,128)}, f32[32,32,512]{2,1,0:T(8,128)S(1)}, u32[]{:S(2)}) copy-start(f32[32,32,512]{2,1,0:T(8,128)S(1)} %get-tuple-element.38) | copy-start | bytes 6291460
  49.6 2.7 %copy-start.8 = (f32[32,32,512]{2,1,0:T(8,128)}, f32[32,32,512]{2,1,0:T(8,128)S(1)}, u32[]{:S(2)}) copy-start(f32[32,32,512]{2,1,0:T(8,128)S(1)} %get-tuple-element.39) | copy-start | bytes 6291460
  104.2 21.0 %all-to-all-start.2 = ((bf16[8,32,512]{2,1,0:T(8,128)(2,1)}), bf16[8,32,512]{2,1,0:T(8,128)(2,1)S(1)}, u32[]{:S(2)}, u32[]{:S(2)}) async-start(bf16[8,32,512]{2,1,0:T(8,128)(2,1)} %broadcast_select_fusion), calls=%async_computation.2 | async-start | bytes 524288 | tf_op jit(solution)/shard_map/all_to_all | solution.py:85
  116.0 7.5 %copy-start.13 = (f32[32,32,512]{2,1,0:T(8,128)S(1)}, f32[32,32,512]{2,1,0:T(8,128)}, u32[]{:S(2)}) copy-start(f32[32,32,512]{2,1,0:T(8,128)} %fusion.14) | copy-start | bytes 6291460
  121.4 2.0 %copy-start.14 = (f32[32,32,2,512]{3,1,2,0:T(8,128)}, f32[32,32,2,512]{3,1,2,0:T(8,128)S(1)}, u32[]{:S(2)}) copy-start(f32[32,32,2,512]{3,1,2,0:T(8,128)S(1)} %fusion) | copy-start | bytes 12582916
  130.0 6.2 %collective-permute-start.7 = (f32[32,512]{1,0:T(8,128)S(1)}, f32[32,512]{1,0:T(8,128)S(1)}, u32[]{:S(2)}, u32[]{:S(2)}) collective-permute-start(f32[32,512]{1,0:T(8,128)S(1)} %bitcast.76), channel_id=1, source_target_pairs={{0,1},{1,2},{2,3},{4,5},{5,6},{6,7},{8,9},{9,10},{10,11},{12,13},{... | collective-permute-start | bytes 196616 | tf_op jit(solution)/shard_map/ppermute | solution.py:14
  132.9 5.6 %collective-permute-start.5 = (f32[1,32,512]{2,1,0:T(8,128)S(1)}, f32[1,32,512]{2,1,0:T(8,128)S(1)}, u32[]{:S(2)}, u32[]{:S(2)}) collective-permute-start(f32[1,32,512]{2,1,0:T(8,128)S(1)} %slice.162), channel_id=1, source_target_pairs={{0,4},{4,8},{8,12},{12,16},{16,20},{20,24},{24,28},{1,5},{5,9},{9,... | collective-permute-start | bytes 196616 | tf_op jit(solution)/shard_map/ppermute | solution.py:14
  136.2 7.1 %collective-permute-start.6 = (f32[32,512]{1,0:T(8,128)S(1)}, f32[32,512]{1,0:T(8,128)S(1)}, u32[]{:S(2)}, u32[]{:S(2)}) collective-permute-start(f32[32,512]{1,0:T(8,128)S(1)} %get-tuple-element.49), channel_id=1, source_target_pairs={{1,0},{2,1},{3,2},{5,4},{6,5},{7,6},{9,8},{10,9},{11,10},{13,12},{... | collective-permute-start | bytes 196616 | tf_op jit(solution)/shard_map/ppermute | solution.py:14
  138.5 4.8 %collective-permute-start.4 = (f32[1,32,512]{2,1,0:T(8,128)S(1)}, f32[1,32,512]{2,1,0:T(8,128)S(1)}, u32[]{:S(2)}, u32[]{:S(2)}) collective-permute-start(f32[1,32,512]{2,1,0:T(8,128)S(1)} %get-tuple-element.43), channel_id=1, source_target_pairs={{4,0},{8,4},{12,8},{16,12},{20,16},{24,20},{28,24},{5,1},{9,5},{13... | collective-permute-start | bytes 196616 | tf_op jit(solution)/shard_map/ppermute | solution.py:14
  141.5 1.9 %copy-start.7 = (f32[32,32,512]{2,1,0:T(8,128)S(1)}, f32[32,32,512]{2,1,0:T(8,128)}, u32[]{:S(2)}) copy-start(f32[32,32,512]{2,1,0:T(8,128)} %copy-done.6) | copy-start | bytes 6291460
  141.5 2.2 %copy-start.9 = (f32[32,32,512]{2,1,0:T(8,128)S(1)}, f32[32,32,512]{2,1,0:T(8,128)}, u32[]{:S(2)}) copy-start(f32[32,32,512]{2,1,0:T(8,128)} %copy-done.8) | copy-start | bytes 6291460
  141.9 2.6 %copy-start.3 = (f32[32,32,512]{2,1,0:T(8,128)S(1)}, f32[32,32,512]{2,1,0:T(8,128)}, u32[]{:S(2)}) copy-start(f32[32,32,512]{2,1,0:T(8,128)} %param.16) | copy-start | bytes 6291460
  141.9 3.2 %copy-start.5 = (f32[32,32,512]{2,1,0:T(8,128)S(1)}, f32[32,32,512]{2,1,0:T(8,128)}, u32[]{:S(2)}) copy-start(f32[32,32,512]{2,1,0:T(8,128)} %copy-done.4) | copy-start | bytes 6291460
  145.0 2.6 %copy-start.15 = (f32[32,32,2,512]{3,1,2,0:T(8,128)S(1)}, f32[32,32,2,512]{3,1,2,0:T(8,128)}, u32[]{:S(2)}) copy-start(f32[32,32,2,512]{3,1,2,0:T(8,128)} %copy-done.14) | copy-start | bytes 12582916
  147.3 2.5 %copy-start.10 = (f32[32,32,512]{2,1,0:T(8,128)}, f32[32,32,512]{2,1,0:T(8,128)S(1)}, u32[]{:S(2)}) copy-start(f32[32,32,512]{2,1,0:T(8,128)S(1)} %get-tuple-element.34) | copy-start | bytes 6291460
  147.3 2.7 %copy-start.11 = (f32[32,32,512]{2,1,0:T(8,128)}, f32[32,32,512]{2,1,0:T(8,128)S(1)}, u32[]{:S(2)}) copy-start(f32[32,32,512]{2,1,0:T(8,128)S(1)} %get-tuple-element.35) | copy-start | bytes 6291460
  147.3 3.4 %copy-start.12 = (f32[32,32,512]{2,1,0:T(8,128)}, f32[32,32,512]{2,1,0:T(8,128)S(1)}, u32[]{:S(2)}) copy-start(f32[32,32,512]{2,1,0:T(8,128)S(1)} %get-tuple-element.36) | copy-start | bytes 6291460
  150.7 2.1 %copy-start.1 = (bf16[16,32,512]{2,1,0:T(8,128)(2,1)S(1)}, bf16[16,32,512]{2,1,0:T(8,128)(2,1)}, u32[]{:S(2)}) copy-start(bf16[16,32,512]{2,1,0:T(8,128)(2,1)} %param.20) | copy-start | bytes 1572868
  (1 other events, 1.3 us)

commit v17 on v15

--- a/solution.py
+++ b/solution.py
@@ -99,11 +99,13 @@
 
     above_x = from_behind(pressure[0:1], "gx", -1)
     above_y = y_plane_from_behind(pressure[:, 0], "gy", -1)
+    kick_x = step_ratio * buoyancy[-1:]
+    kick_y = step_ratio * buoyancy[:, -1]
     below_x = from_behind(
-        jnp.concatenate([pressure[-1:], vel_x[-1:], void_frac[-1:]], 0), "gx", 1
+        jnp.concatenate([vel_x[-1:] + kick_x * pressure[-1:], kick_x], 0), "gx", 1
     )
     below_y = from_behind(
-        jnp.stack([pressure[:, -1], vel_y[:, -1], void_frac[:, -1]], 0), "gy", 1
+        jnp.stack([vel_y[:, -1] + kick_y * pressure[:, -1], kick_y], 0), "gy", 1
     )
     below_y = jnp.moveaxis(below_y, 0, 1)
 
@@ -114,10 +116,8 @@
     above_x, above_y, below_x, below_y = ready
     incident = incident_plane(history, delays, incoming)
     source = source.reshape(size_x, size_y, steps, depth)
-    p_bx, vx_bx, void_bx = below_x[0:1], below_x[1:2], below_x[2:3]
-    p_by, vy_by, void_by = below_y[:, 0:1], below_y[:, 1:2], below_y[:, 2:3]
-    b_bx, _ = material(void_bx)
-    b_by, _ = material(void_by)
+    lead_x, kick_bx = below_x[0:1], below_x[1:2]
+    lead_y, kick_by = below_y[:, 0:1], below_y[:, 1:2]
     forcing = jnp.zeros_like(pressure).at[0].set(incident)
     z_edge = jnp.zeros((size_x, size_y, 1), jnp.float32)
 
@@ -128,8 +128,12 @@
         vel_x = vel_x - step_ratio * buoyancy * (next_x - pressure)
         vel_y = vel_y - step_ratio * buoyancy * (next_y - pressure)
         vel_z = vel_z - step_ratio * buoyancy * (next_z - pressure)
-        vx_bx = vx_bx - step_ratio * b_bx * (pressure[0:1] - p_bx)
-        vy_by = vy_by - step_ratio * b_by * (pressure[:, 0:1] - p_by)
+        if step == 0:
+            vx_bx = lead_x - kick_bx * pressure[0:1]
+            vy_by = lead_y - kick_by * pressure[:, 0:1]
+        else:
+            vx_bx = vx_bx - kick_bx * (pressure[0:1] - p_bx)
+            vy_by = vy_by - kick_by * (pressure[:, 0:1] - p_by)
         lower_x = jnp.where(has_below_x, vx_bx, 0.0)
         lower_y = jnp.where(has_below_y, vy_by, 0.0)
         prev_x = jnp.concatenate([lower_x, vel_x[:-1]], 0)

time: 155 us -> 160 us (1.032)
  other arithmetic: 26.1 us -> 34.2 us
  local copies, waits for them, and re-layouts: 25.7 us -> 23.6 us
    div x0 -> x1, other arithmetic: none -> 4.4 us  [material(): stiffness = 1.0 / (liquid + void_frac / gas_stiffness)]
    slice x7 -> x2, local copies, waits for them, and re-layouts: 3.74 us -> 1.17 us  [the longest x1 1.11 us: body(): vel_y[:, -1] + kick_y * pressure[:, -1]]
    add x2, other arithmetic: 5.09 us -> 6.78 us  [body(): pressure + step_ratio * stiffness * (source[:, :, step, :] - divergence +...]
    unnamed x46 -> x43, local copies, waits for them, and re-layouts: 7.41 us -> 7.85 us
  transfers between devices with their start and end apart: 11 -> 11, of which waited for: 5 -> 4; matrix products, arithmetic and copies ran while one was open for 26% -> 27% of each run, Pallas kernels for 0% -> 0%
where the time goes in v17:
time: 160 us; the launch traced here: 158 us
  waiting for transfers between devices  50.7 us (32%)
  starting transfers between devices  39 us (24%)
  other arithmetic  34.2 us (21%)
  local copies, waits for them, and re-layouts  23.6 us (15%)
  matrix products  9.85 us (6%)
    all_to_all x1, waiting for transfers between devices, bubble_source(): lax.all_to_all(outgoing.reshape(devices, capacity, steps * depth), ('gx',...  48.5 us
    ppermute x8, starting transfers between devices, from_behind(): return lax.ppermute(block, axis, route)  20.9 us
    sub x2, other arithmetic, body(): vel_z = vel_z - step_ratio * buoyancy * (next_z - pressure)  9.65 us
    unnamed x43, local copies, waits for them, and re-layouts  7.85 us
    all_to_all x1, starting transfers between devices, incident_plane(): rows = lax.all_to_all(chosen, 'gx', split_axis=0, concat_axis=0, tiled=True)  7.06 us
    add x2, other arithmetic, body(): pressure + step_ratio * stiffness * (source[:, :, step, :] - divergence +...  6.78 us
    all_to_all x1, starting transfers between devices, bubble_source(): lax.all_to_all(out_cols.reshape(devices, capacity), ('gx', 'gy'), split_a...  5.91 us
    dot_general x1, matrix products, bubble_source(): jnp.dot(hits, incoming.reshape(slots, steps * depth), preferred_element_t...  5.48 us
  transfers between devices with their start and end apart: 11, of which 4 were waited for; matrix products, arithmetic and copies ran while one was open for 27% of the time, Pallas kernels for 0%

profile of v17, /device:TPU:18, one launch (start us, length us, event | category | flops | bytes accessed | tf_op | source)
XLA Modules:
  0.0 158.5 jit_solution(3398317955934885091)
XLA Ops:
  3.9 5.9 %all-to-all-start = ((s32[32,1,48]{2,1,0:T(1,128)}), s32[32,1,48]{2,1,0:T(1,128)S(1)}, u32[]{:S(2)}, u32[]{:S(2)}) async-start(s32[32,1,48]{2,1,0:T(1,128)} %sub.110), calls=%async_computation | async-start | bytes 32768 | tf_op jit(solution)/shard_map/all_to_all | solution.py:51
  9.8 1.3 fusion.41
  11.1 2.6 %collective-permute-start.1 = (f32[32,512]{1,0:T(8,128)S(1)}, f32[32,512]{1,0:T(8,128)S(1)}, u32[]{:S(2)}, u32[]{:S(2)}) collective-permute-start(f32[32,512]{1,0:T(8,128)S(1)} %bitcast.75), channel_id=1, source_target_pairs={{1,0},{2,1},{3,2},{5,4},{6,5},{7,6},{9,8},{10,9},{11,10},{13,12},{... | collective-permute-start | bytes 196616 | tf_op jit(solution)/shard_map/ppermute | solution.py:14
  13.8 4.4 %add_divide_fusion.1 = (f32[32,32,512]{2,0,1:T(8,128)}, f32[32,32,512]{2,0,1:T(8,128)S(1)}) fusion(f32[32,32,512]{2,1,0:T(8,128)} %param.16), kind=kLoop, calls=%fused_computation.44 | loop fusion | flops 3670016 | bytes 6291456 | tf_op jit(solution)/shard_map/div | solution.py:24
  18.2 1.3 multiply_add_fusion.2
  19.5 1.9 %collective-permute-start = (f32[1,32,512]{2,1,0:T(8,128)S(1)}, f32[1,32,512]{2,1,0:T(8,128)S(1)}, u32[]{:S(2)}, u32[]{:S(2)}) collective-permute-start(f32[1,32,512]{2,1,0:T(8,128)S(1)} %get-tuple-element.53), channel_id=1, source_target_pairs={{4,0},{8,4},{12,8},{16,12},{20,16},{24,20},{28,24},{5,1},{9,5},{13... | collective-permute-start | bytes 196616 | tf_op jit(solution)/shard_map/ppermute | solution.py:14
  21.5 2.4 %collective-permute-start.2 = (f32[2,32,512]{2,1,0:T(8,128)S(1)}, f32[2,32,512]{2,1,0:T(8,128)S(1)}, u32[]{:S(2)}, u32[]{:S(2)}) collective-permute-start(f32[2,32,512]{2,1,0:T(8,128)S(1)} %pad_maximum_fusion), channel_id=1, source_target_pairs={{0,4},{4,8},{8,12},{12,16},{16,20},{20,24},{24,28},{1,5},{5,9},{9,... | collective-permute-start | bytes 393224 | tf_op jit(solution)/shard_map/ppermute | solution.py:14
  23.9 1.1 slice.120
  25.0 4.3 %collective-permute-start.3 = (f32[2,32,512]{2,1,0:T(8,128)S(1)}, f32[2,32,512]{2,1,0:T(8,128)S(1)}, u32[]{:S(2)}, u32[]{:S(2)}) collective-permute-start(f32[2,32,512]{2,1,0:T(8,128)S(1)} %pad_maximum_fusion.1), channel_id=1, source_target_pairs={{0,1},{1,2},{2,3},{4,5},{5,6},{6,7},{8,9},{9,10},{10,11},{12,13},{... | collective-permute-start | bytes 393224 | tf_op jit(solution)/shard_map/ppermute | solution.py:14
  29.8 4.0 %fusion.4 = bf16[1536,1024]{1,0:T(8,128)(2,1)} fusion(bf16[768,1024]{1,0:T(8,128)(2,1)S(1)} %bitcast.71, s32[768]{0:T(1024)S(1)} %convert_add_fusion), kind=kOutput, calls=%fused_computation.7 | convolution fusion | flops 2418671616 | bytes 4721664 | tf_op jit(solution)/shard_map/dot_general | solution.py:45
  33.8 5.1 %all-to-all-start.1 = ((bf16[32,48,1024]{2,1,0:T(8,128)(2,1)}), bf16[32,48,1024]{2,1,0:T(8,128)(2,1)}, u32[]{:S(2)}, u32[]{:S(2)}) async-start(bf16[32,48,1024]{2,1,0:T(8,128)(2,1)} %bitcast.68), calls=%async_computation.1 | async-start | bytes 6291456 | tf_op jit(solution)/shard_map/all_to_all | solution.py:59
  38.9 1.6 %slice.124 = f32[31,32,512]{2,1,0:T(8,128)} slice(f32[32,32,512]{2,1,0:T(8,128)S(1)} %copy-done.2), slice={[1:32], [0:32], [0:512]} | slice | bytes 4063232 | tf_op jit(solution)/shard_map/slice | solution.py:125
  40.5 1.7 %slice.128 = f32[32,31,512]{2,1,0:T(8,128)} slice(f32[32,32,512]{2,1,0:T(8,128)S(1)} %copy-done.2), slice={[0:32], [1:32], [0:512]} | slice | bytes 4063232 | tf_op jit(solution)/shard_map/slice | solution.py:126
  42.2 1.9 %slice.132 = f32[32,32,511]{2,1,0:T(8,128)} slice(f32[32,32,512]{2,1,0:T(8,128)S(1)} %copy-done.2), slice={[0:32], [0:32], [1:512]} | slice | bytes 4186112 | tf_op jit(solution)/shard_map/slice | solution.py:127
  46.2 6.6 %multiply_subtract_fusion.1 = (f32[32,32,512]{2,1,0:T(8,128)S(1)}, f32[32,32,512]{2,1,0:T(8,128)S(1)}, f32[32,32,512]{2,1,0:T(8,128)S(1)}) fusion(f32[32,32,512]{2,1,0:T(8,128)} %param.15, f32[32,32,512]{2,1,0:T(8,128)S(1)} %copy-done.2, f32[32,32,511]{2,1,0:T(8,128)} %slice.132, f32[32,32,512]{2,0,1:T(8,128)} %copy-done.9, f32[32,32,512]{2,1,0:T(8,128)} %param.14, ...), kind=kLoop, calls=%fused_computation.42 | loop fusion | flops 6291456 | bytes 23064576 | tf_op jit(solution)/shard_map/sub | solution.py:130
  55.6 3.1 %fusion.14 = f32[32,32,512]{2,1,0:T(8,128)} fusion(f32[32,32,512]{2,1,0:T(8,128)S(1)} %get-tuple-element.43, f32[31,32,512]{2,1,0:T(8,128)S(1)} %slice.150, f32[1,32,512]{2,1,0:T(8,128)S(1)} %broadcast_select_fusion.2, f32[32,32,512]{2,1,0:T(8,128)S(1)} %get-tuple-element.42, f32[32,31,512]{2,1,0:T(8,128)S(1)} %bitcast.65, f32[32,1,512]{2,1,0:T(1,128)S(1)} %copy.100, ...), kind=kLoop, calls=%fused_computation.22 | loop fusion | flops 3670016 | bytes 14675968 | tf_op jit(solution)/shard_map/add | solution.py:142
  58.7 48.5 %all-to-all-done.1 = bf16[32,48,1024]{2,1,0:T(8,128)(2,1)} async-done(((bf16[32,48,1024]{2,1,0:T(8,128)(2,1)}), bf16[32,48,1024]{2,1,0:T(8,128)(2,1)}, u32[]{:S(2)}, u32[]{:S(2)}) %all-to-all-start.1) | async-done | bytes 3145760 | tf_op jit(solution)/shard_map/all_to_all | solution.py:59
  107.2 7.1 %all-to-all-start.2 = ((bf16[8,32,512]{2,1,0:T(8,128)(2,1)}), bf16[8,32,512]{2,1,0:T(8,128)(2,1)S(1)}, u32[]{:S(2)}, u32[]{:S(2)}) async-start(bf16[8,32,512]{2,1,0:T(8,128)(2,1)} %broadcast_select_fusion), calls=%async_computation.2 | async-start | bytes 524288 | tf_op jit(solution)/shard_map/all_to_all | solution.py:85
  114.2 4.6 %copy.96 = bf16[1536,1024]{0,1:T(8,128)(2,1)} copy(bf16[1536,1024]{1,0:T(8,128)(2,1)} %bitcast.9) | data formatting | bytes 6291456 | tf_op jit(solution)/shard_map/reshape | solution.py:70
  118.9 5.5 %fusion = f32[32,32,2,512]{3,1,0,2:T(8,128)S(1)} fusion(bf16[2,512,1536,1]{2,1,3,0:T(8,128)(2,1)} %bitcast.69, s32[1536]{0:T(1024)S(1)} %eq.62, s32[32,32]{1,0:T(8,128)S(1)} %multiply_add_fusion.3), kind=kOutput, calls=%fused_computation.1 | convolution fusion | flops 3222798336 | bytes 7350272 | tf_op jit(solution)/shard_map/dot_general | solution.py:69
  124.4 1.9 %copy-done.16 = f32[32,32,2,512]{3,1,0,2:T(8,128)} copy-done((f32[32,32,2,512]{3,1,0,2:T(8,128)}, f32[32,32,2,512]{3,1,0,2:T(8,128)S(1)}, u32[]{:S(2)}) %copy-start.16) | copy-done | bytes 4194328
  126.3 1.8 %fusion.10 = f32[32,32,512]{2,1,0:T(8,128)} fusion(f32[32,32,512]{2,1,0:T(8,128)S(1)} %copy-done.15, f32[32,32,2,512]{3,1,0,2:T(8,128)S(1)} %fusion), kind=kLoop, calls=%fused_computation.16 | loop fusion | flops 524288 | bytes 6291456 | tf_op jit(solution)/shard_map/sub | solution.py:146
  128.3 1.5 fusion.27
  129.8 3.8 %multiply_add_fusion.1 = f32[32,32,512]{2,1,0:T(8,128)S(1)} fusion(f32[32,32,512]{2,1,0:T(8,128)S(1)} %copy-done.2, f32[32,32,512]{2,1,0:T(8,128)} %fusion.27, f32[32,32,512]{2,0,1:T(8,128)} %get-tuple-element.48), kind=kLoop, calls=%fused_computation.41 | loop fusion | flops 1572864 | bytes 8388608 | tf_op jit(solution)/shard_map/add | solution.py:145
  133.7 2.9 %collective-permute-start.7 = (f32[32,512]{1,0:T(8,128)S(1)}, f32[32,512]{1,0:T(8,128)S(1)}, u32[]{:S(2)}, u32[]{:S(2)}) collective-permute-start(f32[32,512]{1,0:T(8,128)S(1)} %bitcast.76), channel_id=1, source_target_pairs={{0,1},{1,2},{2,3},{4,5},{5,6},{6,7},{8,9},{9,10},{10,11},{12,13},{... | collective-permute-start | bytes 196616 | tf_op jit(solution)/shard_map/ppermute | solution.py:14
  136.7 1.9 %collective-permute-start.5 = (f32[1,32,512]{2,1,0:T(8,128)S(1)}, f32[1,32,512]{2,1,0:T(8,128)S(1)}, u32[]{:S(2)}, u32[]{:S(2)}) collective-permute-start(f32[1,32,512]{2,1,0:T(8,128)S(1)} %slice.156), channel_id=1, source_target_pairs={{0,4},{4,8},{8,12},{12,16},{16,20},{20,24},{24,28},{1,5},{5,9},{9,... | collective-permute-start | bytes 196616 | tf_op jit(solution)/shard_map/ppermute | solution.py:14
  138.6 1.3 collective-permute-done.7
  139.9 1.9 %collective-permute-start.6 = (f32[32,512]{1,0:T(8,128)S(1)}, f32[32,512]{1,0:T(8,128)S(1)}, u32[]{:S(2)}, u32[]{:S(2)}) collective-permute-start(f32[32,512]{1,0:T(8,128)S(1)} %get-tuple-element.55), channel_id=1, source_target_pairs={{1,0},{2,1},{3,2},{5,4},{6,5},{7,6},{9,8},{10,9},{11,10},{13,12},{... | collective-permute-start | bytes 196616 | tf_op jit(solution)/shard_map/ppermute | solution.py:14
  142.3 2.9 %collective-permute-start.4 = (f32[1,32,512]{2,1,0:T(8,128)S(1)}, f32[1,32,512]{2,1,0:T(8,128)S(1)}, u32[]{:S(2)}, u32[]{:S(2)}) collective-permute-start(f32[1,32,512]{2,1,0:T(8,128)S(1)} %get-tuple-element.47), channel_id=1, source_target_pairs={{4,0},{8,4},{12,8},{16,12},{20,16},{24,20},{28,24},{5,1},{9,5},{13... | collective-permute-start | bytes 196616 | tf_op jit(solution)/shard_map/ppermute | solution.py:14
  149.1 3.0 %multiply_subtract_fusion = (f32[32,32,512]{2,1,0:T(8,128)S(1)}, f32[32,32,512]{2,1,0:T(8,128)S(1)}, f32[32,32,512]{2,1,0:T(8,128)S(1)}) fusion(f32[32,32,512]{2,1,0:T(8,128)S(1)} %copy-done.4, f32[32,32,512]{2,1,0:T(8,128)S(1)} %multiply_add_fusion.1, f32[32,32,511]{2,1,0:T(8,128)S(1)} %slice.162, f32[32,32,512]{2,0,1:T(8,128)S(1)} %copy-done.10, ...), kind=kLoop, calls=%fused_computation.40 | loop fusion | flops 6291456 | bytes 23064576 | tf_op jit(solution)/shard_map/sub | solution.py:130
  152.4 2.1 %fusion.9 = f32[32,32,512]{2,1,0:T(8,128)S(1)} fusion(f32[32,32,2,512]{3,1,0,2:T(8,128)S(1)} %copy-done.17, f32[32,32,512]{2,1,0:T(8,128)S(1)} %get-tuple-element.40, f32[31,32,512]{2,1,0:T(8,128)S(1)} %slice.157, f32[1,32,512]{2,1,0:T(8,128)S(1)} %get-tuple-element.46, f32[32,32,512]{2,1,0:T(8,128)S(1)} %get-tuple-element.39, ...), kind=kLoop, calls=%fused_computation.14 | loop fusion | flops 4194304 | bytes 16773120 | tf_op jit(solution)/shard_map/sub | solution.py:146
  155.5 2.9 %multiply_add_fusion = f32[32,32,512]{2,1,0:T(8,128)} fusion(f32[32,32,512]{2,1,0:T(8,128)S(1)} %multiply_add_fusion.1, f32[32,32,512]{2,1,0:T(8,128)S(1)} %fusion.26, f32[32,32,512]{2,0,1:T(8,128)S(1)} %copy-done.11), kind=kLoop, calls=%fused_computation.39 | loop fusion | flops 1572864 | bytes 8388608 | tf_op jit(solution)/shard_map/add | solution.py:145
  (88 shorter events, 14.3 us)
Async XLA Ops:
  0.6 43.7 %copy-start = (bf16[16,32,512]{2,1,0:T(8,128)(2,1)S(1)}, bf16[16,32,512]{2,1,0:T(8,128)(2,1)}, u32[]{:S(2)}) copy-start(bf16[16,32,512]{2,1,0:T(8,128)(2,1)} %param.20) | copy-start | bytes 1572868
  3.9 29.9 %all-to-all-start = ((s32[32,1,48]{2,1,0:T(1,128)}), s32[32,1,48]{2,1,0:T(1,128)S(1)}, u32[]{:S(2)}, u32[]{:S(2)}) async-start(s32[32,1,48]{2,1,0:T(1,128)} %sub.110), calls=%async_computation | async-start | bytes 32768 | tf_op jit(solution)/shard_map/all_to_all | solution.py:51
  11.1 7.1 %copy-start.2 = (f32[32,32,512]{2,1,0:T(8,128)S(1)}, f32[32,32,512]{2,1,0:T(8,128)}, u32[]{:S(2)}) copy-start(f32[32,32,512]{2,1,0:T(8,128)} %param.12) | copy-start | bytes 6291460
  11.1 22.6 %collective-permute-start.1 = (f32[32,512]{1,0:T(8,128)S(1)}, f32[32,512]{1,0:T(8,128)S(1)}, u32[]{:S(2)}, u32[]{:S(2)}) collective-permute-start(f32[32,512]{1,0:T(8,128)S(1)} %bitcast.75), channel_id=1, source_target_pairs={{1,0},{2,1},{3,2},{5,4},{6,5},{7,6},{9,8},{10,9},{11,10},{13,12},{... | collective-permute-start | bytes 196616 | tf_op jit(solution)/shard_map/ppermute | solution.py:14
  18.2 11.6 %copy-start.9 = (f32[32,32,512]{2,0,1:T(8,128)}, f32[32,32,512]{2,0,1:T(8,128)S(1)}, u32[]{:S(2)}) copy-start(f32[32,32,512]{2,0,1:T(8,128)S(1)} %get-tuple-element.49) | copy-start | bytes 6291460
  18.2 11.2 %copy-start.18 = (bf16[768,2,512]{2,1,0:T(2,128)(2,1)S(1)}, bf16[768,2,512]{2,1,0:T(2,128)(2,1)}, u32[]{:S(2)}) copy-start(bf16[768,2,512]{2,1,0:T(2,128)(2,1)} %param.17) | copy-start | bytes 4718596
  19.5 14.3 %collective-permute-start = (f32[1,32,512]{2,1,0:T(8,128)S(1)}, f32[1,32,512]{2,1,0:T(8,128)S(1)}, u32[]{:S(2)}, u32[]{:S(2)}) collective-permute-start(f32[1,32,512]{2,1,0:T(8,128)S(1)} %get-tuple-element.53), channel_id=1, source_target_pairs={{4,0},{8,4},{12,8},{16,12},{20,16},{24,20},{28,24},{5,1},{9,5},{13... | collective-permute-start | bytes 196616 | tf_op jit(solution)/shard_map/ppermute | solution.py:14
  21.5 12.3 %collective-permute-start.2 = (f32[2,32,512]{2,1,0:T(8,128)S(1)}, f32[2,32,512]{2,1,0:T(8,128)S(1)}, u32[]{:S(2)}, u32[]{:S(2)}) collective-permute-start(f32[2,32,512]{2,1,0:T(8,128)S(1)} %pad_maximum_fusion), channel_id=1, source_target_pairs={{0,4},{4,8},{8,12},{12,16},{16,20},{20,24},{24,28},{1,5},{5,9},{9,... | collective-permute-start | bytes 393224 | tf_op jit(solution)/shard_map/ppermute | solution.py:14
  25.0 8.8 %collective-permute-start.3 = (f32[2,32,512]{2,1,0:T(8,128)S(1)}, f32[2,32,512]{2,1,0:T(8,128)S(1)}, u32[]{:S(2)}, u32[]{:S(2)}) collective-permute-start(f32[2,32,512]{2,1,0:T(8,128)S(1)} %pad_maximum_fusion.1), channel_id=1, source_target_pairs={{0,1},{1,2},{2,3},{4,5},{5,6},{6,7},{8,9},{9,10},{10,11},{12,13},{... | collective-permute-start | bytes 393224 | tf_op jit(solution)/shard_map/ppermute | solution.py:14
  33.8 73.4 %all-to-all-start.1 = ((bf16[32,48,1024]{2,1,0:T(8,128)(2,1)}), bf16[32,48,1024]{2,1,0:T(8,128)(2,1)}, u32[]{:S(2)}, u32[]{:S(2)}) async-start(bf16[32,48,1024]{2,1,0:T(8,128)(2,1)} %bitcast.68), calls=%async_computation.1 | async-start | bytes 6291456 | tf_op jit(solution)/shard_map/all_to_all | solution.py:59
  42.2 1.9 %copy-start.19 = (s32[8,8]{1,0:T(8,128)S(1)}, s32[8,8]{1,0:T(8,128)}, u32[]{:S(2)}) copy-start(s32[8,8]{1,0:T(8,128)} %param.21) | copy-start | bytes 772
  52.8 1.3 copy-start.3
  52.8 2.1 %copy-start.5 = (f32[32,32,512]{2,1,0:T(8,128)}, f32[32,32,512]{2,1,0:T(8,128)S(1)}, u32[]{:S(2)}) copy-start(f32[32,32,512]{2,1,0:T(8,128)S(1)} %get-tuple-element.42) | copy-start | bytes 6291460
  52.9 2.8 %copy-start.7 = (f32[32,32,512]{2,1,0:T(8,128)}, f32[32,32,512]{2,1,0:T(8,128)S(1)}, u32[]{:S(2)}) copy-start(f32[32,32,512]{2,1,0:T(8,128)S(1)} %get-tuple-element.43) | copy-start | bytes 6291460
  107.2 21.0 %all-to-all-start.2 = ((bf16[8,32,512]{2,1,0:T(8,128)(2,1)}), bf16[8,32,512]{2,1,0:T(8,128)(2,1)S(1)}, u32[]{:S(2)}, u32[]{:S(2)}) async-start(bf16[8,32,512]{2,1,0:T(8,128)(2,1)} %broadcast_select_fusion), calls=%async_computation.2 | async-start | bytes 524288 | tf_op jit(solution)/shard_map/all_to_all | solution.py:85
  118.9 7.4 %copy-start.15 = (f32[32,32,512]{2,1,0:T(8,128)S(1)}, f32[32,32,512]{2,1,0:T(8,128)}, u32[]{:S(2)}) copy-start(f32[32,32,512]{2,1,0:T(8,128)} %fusion.14) | copy-start | bytes 6291460
  124.4 1.9 %copy-start.16 = (f32[32,32,2,512]{3,1,0,2:T(8,128)}, f32[32,32,2,512]{3,1,0,2:T(8,128)S(1)}, u32[]{:S(2)}) copy-start(f32[32,32,2,512]{3,1,0,2:T(8,128)S(1)} %fusion) | copy-start | bytes 12582916
  133.7 6.2 %collective-permute-start.7 = (f32[32,512]{1,0:T(8,128)S(1)}, f32[32,512]{1,0:T(8,128)S(1)}, u32[]{:S(2)}, u32[]{:S(2)}) collective-permute-start(f32[32,512]{1,0:T(8,128)S(1)} %bitcast.76), channel_id=1, source_target_pairs={{0,1},{1,2},{2,3},{4,5},{5,6},{6,7},{8,9},{9,10},{10,11},{12,13},{... | collective-permute-start | bytes 196616 | tf_op jit(solution)/shard_map/ppermute | solution.py:14
  136.7 5.6 %collective-permute-start.5 = (f32[1,32,512]{2,1,0:T(8,128)S(1)}, f32[1,32,512]{2,1,0:T(8,128)S(1)}, u32[]{:S(2)}, u32[]{:S(2)}) collective-permute-start(f32[1,32,512]{2,1,0:T(8,128)S(1)} %slice.156), channel_id=1, source_target_pairs={{0,4},{4,8},{8,12},{12,16},{16,20},{20,24},{24,28},{1,5},{5,9},{9,... | collective-permute-start | bytes 196616 | tf_op jit(solution)/shard_map/ppermute | solution.py:14
  139.9 7.1 %collective-permute-start.6 = (f32[32,512]{1,0:T(8,128)S(1)}, f32[32,512]{1,0:T(8,128)S(1)}, u32[]{:S(2)}, u32[]{:S(2)}) collective-permute-start(f32[32,512]{1,0:T(8,128)S(1)} %get-tuple-element.55), channel_id=1, source_target_pairs={{1,0},{2,1},{3,2},{5,4},{6,5},{7,6},{9,8},{10,9},{11,10},{13,12},{... | collective-permute-start | bytes 196616 | tf_op jit(solution)/shard_map/ppermute | solution.py:14
  142.3 4.8 %collective-permute-start.4 = (f32[1,32,512]{2,1,0:T(8,128)S(1)}, f32[1,32,512]{2,1,0:T(8,128)S(1)}, u32[]{:S(2)}, u32[]{:S(2)}) collective-permute-start(f32[1,32,512]{2,1,0:T(8,128)S(1)} %get-tuple-element.47), channel_id=1, source_target_pairs={{4,0},{8,4},{12,8},{16,12},{20,16},{24,20},{28,24},{5,1},{9,5},{13... | collective-permute-start | bytes 196616 | tf_op jit(solution)/shard_map/ppermute | solution.py:14
  145.5 1.6 %copy-start.8 = (f32[32,32,512]{2,1,0:T(8,128)S(1)}, f32[32,32,512]{2,1,0:T(8,128)}, u32[]{:S(2)}) copy-start(f32[32,32,512]{2,1,0:T(8,128)} %copy-done.7) | copy-start | bytes 6291460
  145.5 2.2 %copy-start.10 = (f32[32,32,512]{2,0,1:T(8,128)S(1)}, f32[32,32,512]{2,0,1:T(8,128)}, u32[]{:S(2)}) copy-start(f32[32,32,512]{2,0,1:T(8,128)} %copy-done.9) | copy-start | bytes 6291460
  145.9 2.6 %copy-start.4 = (f32[32,32,512]{2,1,0:T(8,128)S(1)}, f32[32,32,512]{2,1,0:T(8,128)}, u32[]{:S(2)}) copy-start(f32[32,32,512]{2,1,0:T(8,128)} %copy-done.3) | copy-start | bytes 6291460
  145.9 3.2 %copy-start.6 = (f32[32,32,512]{2,1,0:T(8,128)S(1)}, f32[32,32,512]{2,1,0:T(8,128)}, u32[]{:S(2)}) copy-start(f32[32,32,512]{2,1,0:T(8,128)} %copy-done.5) | copy-start | bytes 6291460
  149.1 3.3 %copy-start.17 = (f32[32,32,2,512]{3,1,0,2:T(8,128)S(1)}, f32[32,32,2,512]{3,1,0,2:T(8,128)}, u32[]{:S(2)}) copy-start(f32[32,32,2,512]{3,1,0,2:T(8,128)} %copy-done.16) | copy-start | bytes 12582916
  152.1 2.4 %copy-start.12 = (f32[32,32,512]{2,1,0:T(8,128)}, f32[32,32,512]{2,1,0:T(8,128)S(1)}, u32[]{:S(2)}) copy-start(f32[32,32,512]{2,1,0:T(8,128)S(1)} %get-tuple-element.38) | copy-start | bytes 6291460
  152.1 2.4 %copy-start.13 = (f32[32,32,512]{2,1,0:T(8,128)}, f32[32,32,512]{2,1,0:T(8,128)S(1)}, u32[]{:S(2)}) copy-start(f32[32,32,512]{2,1,0:T(8,128)S(1)} %get-tuple-element.39) | copy-start | bytes 6291460
  152.1 2.8 %copy-start.14 = (f32[32,32,512]{2,1,0:T(8,128)}, f32[32,32,512]{2,1,0:T(8,128)S(1)}, u32[]{:S(2)}) copy-start(f32[32,32,512]{2,1,0:T(8,128)S(1)} %get-tuple-element.40) | copy-start | bytes 6291460
  152.4 3.2 %copy-start.11 = (f32[32,32,512]{2,0,1:T(8,128)S(1)}, f32[32,32,512]{2,0,1:T(8,128)}, u32[]{:S(2)}) copy-start(f32[32,32,512]{2,0,1:T(8,128)} %get-tuple-element.48) | copy-start | bytes 6291460
  155.5 2.9 %copy-start.1 = (bf16[16,32,512]{2,1,0:T(8,128)(2,1)S(1)}, bf16[16,32,512]{2,1,0:T(8,128)(2,1)}, u32[]{:S(2)}) copy-start(bf16[16,32,512]{2,1,0:T(8,128)(2,1)} %param.20) | copy-start | bytes 1572868

commit v18 on v15

--- a/solution.py
+++ b/solution.py
@@ -48,6 +48,7 @@
         preferred_element_type=jnp.float32,
     ).astype(jnp.bfloat16)
     out_cols = jnp.max(jnp.where(placed, bubble_column[None, :] + 1, 0), axis=1) - 1
+    out_cols, ready = lax.optimization_barrier((out_cols, ready))
     in_cols = lax.all_to_all(
         out_cols.reshape(devices, capacity),
         ("gx", "gy"),

time: 155 us -> 158 us (1.019)
  local copies, waits for them, and re-layouts: 25.7 us -> 28 us
  waiting for transfers between devices: 51.9 us -> 53.6 us
    ppermute x8, waiting for transfers between devices: 2.97 us -> 4.73 us  [from_behind(): return lax.ppermute(block, axis, route)]
  transfers between devices with their start and end apart: 11 -> 11, of which waited for: 5 -> 5; matrix products, arithmetic and copies ran while one was open for 26% -> 28% of each run, Pallas kernels for 0% -> 0%
where the time goes in v18:
time: 158 us; the launch traced here: 157 us
  waiting for transfers between devices  53.6 us (34%)
  starting transfers between devices  37.9 us (24%)
  local copies, waits for them, and re-layouts  28 us (18%)
  other arithmetic  24.6 us (16%)
  matrix products  11.2 us (7%)
    all_to_all x1, waiting for transfers between devices, bubble_source(): lax.all_to_all(outgoing.reshape(devices, capacity, steps * depth), ('gx',...  48.9 us
    ppermute x8, starting transfers between devices, from_behind(): return lax.ppermute(block, axis, route)  20 us
    sub x2, other arithmetic, body(): vel_z = vel_z - step_ratio * buoyancy * (next_z - pressure)  8.61 us
    unnamed x46, local copies, waits for them, and re-layouts  8.56 us
    all_to_all x1, starting transfers between devices, incident_plane(): rows = lax.all_to_all(chosen, 'gx', split_axis=0, concat_axis=0, tiled=True)  7.06 us
    all_to_all x1, starting transfers between devices, bubble_source(): lax.all_to_all(outgoing.reshape(devices, capacity, steps * depth), ('gx',...  5.88 us
    dot_general x1, matrix products, bubble_source(): jnp.dot(hits, incoming.reshape(slots, steps * depth), preferred_element_t...  5.49 us
    dot_general x1, matrix products, bubble_source(): jnp.dot(placed.astype(jnp.bfloat16), waves.reshape(bubbles, steps * depth...  5.41 us
  transfers between devices with their start and end apart: 11, of which 5 were waited for; matrix products, arithmetic and copies ran while one was open for 28% of the time, Pallas kernels for 0%

profile of v18, /device:TPU:18, one launch (start us, length us, event | category | flops | bytes accessed | tf_op | source)
XLA Modules:
  0.0 156.5 jit_solution(4254607363766401843)
XLA Ops:
  1.7 1.9 %collective-permute-start = (f32[1,32,512]{2,1,0:T(8,128)S(1)}, f32[1,32,512]{2,1,0:T(8,128)S(1)}, u32[]{:S(2)}, u32[]{:S(2)}) collective-permute-start(f32[1,32,512]{2,1,0:T(8,128)S(1)} %get-tuple-element.57), channel_id=1, source_target_pairs={{4,0},{8,4},{12,8},{16,12},{20,16},{24,20},{28,24},{5,1},{9,5},{13... | collective-permute-start | bytes 196616 | tf_op jit(solution)/shard_map/ppermute | solution.py:14
  3.6 1.3 fusion.38
  5.0 2.4 %collective-permute-start.1 = (f32[32,512]{1,0:T(8,128)S(1)}, f32[32,512]{1,0:T(8,128)S(1)}, u32[]{:S(2)}, u32[]{:S(2)}) collective-permute-start(f32[32,512]{1,0:T(8,128)S(1)} %bitcast.75), channel_id=1, source_target_pairs={{1,0},{2,1},{3,2},{5,4},{6,5},{7,6},{9,8},{10,9},{11,10},{13,12},{... | collective-permute-start | bytes 196616 | tf_op jit(solution)/shard_map/ppermute | solution.py:14
  7.4 1.1 slice.127
  9.7 4.3 %collective-permute-start.3 = (f32[3,32,512]{2,1,0:T(8,128)S(1)}, f32[3,32,512]{2,1,0:T(8,128)S(1)}, u32[]{:S(2)}, u32[]{:S(2)}) collective-permute-start(f32[3,32,512]{2,1,0:T(8,128)S(1)} %pad_maximum_fusion.1), channel_id=1, source_target_pairs={{0,1},{1,2},{2,3},{4,5},{5,6},{6,7},{8,9},{9,10},{10,11},{12,13},{... | collective-permute-start | bytes 589832 | tf_op jit(solution)/shard_map/ppermute | solution.py:14
  15.7 1.9 %collective-permute-start.2 = (f32[3,32,512]{2,1,0:T(8,128)S(1)}, f32[3,32,512]{2,1,0:T(8,128)S(1)}, u32[]{:S(2)}, u32[]{:S(2)}) collective-permute-start(f32[3,32,512]{2,1,0:T(8,128)S(1)} %pad_maximum_fusion), channel_id=1, source_target_pairs={{0,4},{4,8},{8,12},{12,16},{16,20},{20,24},{24,28},{1,5},{5,9},{9,... | collective-permute-start | bytes 589832 | tf_op jit(solution)/shard_map/ppermute | solution.py:14
  18.8 1.6 %copy.44 = bf16[96,8,2,512]{3,1,2,0:T(8,128)(2,1)} copy(bf16[96,8,2,512]{3,2,1,0:T(2,128)(2,1)S(1)} %bitcast.67) | data formatting | bytes 3145728
  20.4 2.3 %collective-permute-done.2 = f32[3,32,512]{2,1,0:T(8,128)S(1)} collective-permute-done((f32[3,32,512]{2,1,0:T(8,128)S(1)}, f32[3,32,512]{2,1,0:T(8,128)S(1)}, u32[]{:S(2)}, u32[]{:S(2)}) %collective-permute-start.2) | collective-permute-done | bytes 196640 | tf_op jit(solution)/shard_map/ppermute | solution.py:14
  23.4 5.0 %all-to-all-start = ((s32[32,1,48]{2,1,0:T(1,128)}), s32[32,1,48]{2,1,0:T(1,128)S(1)}, u32[]{:S(2)}, u32[]{:S(2)}) async-start(s32[32,1,48]{2,1,0:T(1,128)} %all_to_all.14), calls=%async_computation | async-start | bytes 32768 | tf_op jit(solution)/shard_map/all_to_all | solution.py:52
  28.4 5.4 %fusion.4 = bf16[1536,1024]{1,0:T(8,128)(2,1)} fusion(bf16[768,1024]{1,0:T(8,128)(2,1)} %bitcast.68, s32[768]{0:T(1024)S(1)} %convert_add_fusion), kind=kOutput, calls=%fused_computation.7 | convolution fusion | flops 2418671616 | bytes 4721664 | tf_op jit(solution)/shard_map/dot_general | solution.py:45
  33.8 5.9 %all-to-all-start.1 = ((bf16[32,48,1024]{2,1,0:T(8,128)(2,1)}), bf16[32,48,1024]{2,1,0:T(8,128)(2,1)}, u32[]{:S(2)}, u32[]{:S(2)}) async-start(bf16[32,48,1024]{2,1,0:T(8,128)(2,1)} %bitcast.65), calls=%async_computation.1 | async-start | bytes 6291456 | tf_op jit(solution)/shard_map/all_to_all | solution.py:60
  39.7 1.5 slice.130
  41.2 1.9 %slice.140 = f32[32,32,511]{2,1,0:T(8,128)} slice(f32[32,32,512]{2,1,0:T(8,128)S(1)} %copy-done.2), slice={[0:32], [0:32], [1:512]} | slice | bytes 4186112 | tf_op jit(solution)/shard_map/slice | solution.py:128
  43.1 1.7 %slice.135 = f32[32,31,512]{2,1,0:T(8,128)} slice(f32[32,32,512]{2,1,0:T(8,128)S(1)} %copy-done.2), slice={[0:32], [1:32], [0:512]} | slice | bytes 4063232 | tf_op jit(solution)/shard_map/slice | solution.py:127
  46.9 6.4 %multiply_subtract_fusion.1 = (f32[32,32,512]{2,1,0:T(8,128)S(1)}, f32[32,32,512]{2,1,0:T(8,128)S(1)}, f32[32,32,512]{2,1,0:T(8,128)S(1)}) fusion(f32[32,32,512]{2,1,0:T(8,128)} %param.15, f32[32,32,512]{2,1,0:T(8,128)S(1)} %copy-done.2, f32[32,32,511]{2,1,0:T(8,128)} %slice.140, f32[32,32,512]{2,1,0:T(8,128)} %param.16, f32[32,32,512]{2,1,0:T(8,128)} %param.14, ...), kind=kLoop, calls=%fused_computation.40 | loop fusion | flops 8388608 | bytes 23064576 | tf_op jit(solution)/shard_map/sub | solution.py:131
  56.0 3.1 %fusion.14 = f32[32,32,512]{2,1,0:T(8,128)} fusion(f32[32,32,512]{2,1,0:T(8,128)S(1)} %get-tuple-element.49, f32[31,32,512]{2,1,0:T(8,128)S(1)} %slice.156, f32[1,32,512]{2,1,0:T(8,128)S(1)} %get-tuple-element.42, f32[32,32,512]{2,1,0:T(8,128)S(1)} %get-tuple-element.48, f32[32,31,512]{2,1,0:T(8,128)S(1)} %bitcast.62, f32[32,1,512]{2,1,0:T(1,128)S(1)} %copy.32, ...), kind=kLoop, calls=%fused_computation.22 | loop fusion | flops 3670016 | bytes 14675968 | tf_op jit(solution)/shard_map/add | solution.py:139
  59.1 48.9 %all-to-all-done.1 = bf16[32,48,1024]{2,1,0:T(8,128)(2,1)} async-done(((bf16[32,48,1024]{2,1,0:T(8,128)(2,1)}), bf16[32,48,1024]{2,1,0:T(8,128)(2,1)}, u32[]{:S(2)}, u32[]{:S(2)}) %all-to-all-start.1) | async-done | bytes 3145760 | tf_op jit(solution)/shard_map/all_to_all | solution.py:60
  107.9 7.1 %all-to-all-start.2 = ((bf16[8,32,512]{2,1,0:T(8,128)(2,1)}), bf16[8,32,512]{2,1,0:T(8,128)(2,1)S(1)}, u32[]{:S(2)}, u32[]{:S(2)}) async-start(bf16[8,32,512]{2,1,0:T(8,128)(2,1)} %broadcast_select_fusion), calls=%async_computation.2 | async-start | bytes 524288 | tf_op jit(solution)/shard_map/all_to_all | solution.py:86
  115.0 4.7 %copy.29 = bf16[1536,1024]{0,1:T(8,128)(2,1)} copy(bf16[1536,1024]{1,0:T(8,128)(2,1)} %bitcast.10) | data formatting | bytes 6291456 | tf_op jit(solution)/shard_map/reshape | solution.py:71
  119.6 5.5 %fusion = f32[32,32,2,512]{3,1,2,0:T(8,128)S(1)} fusion(bf16[2,512,1536,1]{2,1,0,3:T(8,128)(2,1)} %bitcast.66, s32[1536]{0:T(1024)S(1)} %eq.62, s32[32,32]{1,0:T(8,128)S(1)} %multiply_add_fusion.2), kind=kOutput, calls=%fused_computation.1 | convolution fusion | flops 3222798336 | bytes 7350272 | tf_op jit(solution)/shard_map/dot_general | solution.py:70
  125.1 1.9 %copy-done.14 = f32[32,32,2,512]{3,1,2,0:T(8,128)} copy-done((f32[32,32,2,512]{3,1,2,0:T(8,128)}, f32[32,32,2,512]{3,1,2,0:T(8,128)S(1)}, u32[]{:S(2)}) %copy-start.14) | copy-done | bytes 4194328
  127.1 1.8 %fusion.10 = f32[32,32,512]{2,1,0:T(8,128)} fusion(f32[32,32,512]{2,1,0:T(8,128)S(1)} %copy-done.13, f32[32,32,2,512]{3,1,2,0:T(8,128)S(1)} %fusion), kind=kLoop, calls=%fused_computation.16 | loop fusion | flops 524288 | bytes 6291456 | tf_op jit(solution)/shard_map/sub | solution.py:143
  129.0 1.5 fusion.27
  130.5 3.0 %multiply_add_fusion.1 = f32[32,32,512]{2,1,0:T(8,128)S(1)} fusion(f32[32,32,512]{2,1,0:T(8,128)S(1)} %copy-done.2, f32[32,32,512]{2,1,0:T(8,128)} %fusion.27, f32[32,32,512]{2,1,0:T(8,128)} %param.16), kind=kLoop, calls=%fused_computation.39 | loop fusion | flops 3670016 | bytes 8388608 | tf_op jit(solution)/shard_map/add | solution.py:142
  133.6 2.9 %collective-permute-start.7 = (f32[32,512]{1,0:T(8,128)S(1)}, f32[32,512]{1,0:T(8,128)S(1)}, u32[]{:S(2)}, u32[]{:S(2)}) collective-permute-start(f32[32,512]{1,0:T(8,128)S(1)} %bitcast.76), channel_id=1, source_target_pairs={{0,1},{1,2},{2,3},{4,5},{5,6},{6,7},{8,9},{9,10},{10,11},{12,13},{... | collective-permute-start | bytes 196616 | tf_op jit(solution)/shard_map/ppermute | solution.py:14
  136.6 1.9 %collective-permute-start.5 = (f32[1,32,512]{2,1,0:T(8,128)S(1)}, f32[1,32,512]{2,1,0:T(8,128)S(1)}, u32[]{:S(2)}, u32[]{:S(2)}) collective-permute-start(f32[1,32,512]{2,1,0:T(8,128)S(1)} %slice.162), channel_id=1, source_target_pairs={{0,4},{4,8},{8,12},{12,16},{16,20},{20,24},{24,28},{1,5},{5,9},{9,... | collective-permute-start | bytes 196616 | tf_op jit(solution)/shard_map/ppermute | solution.py:14
  138.5 1.3 collective-permute-done.7
  139.8 1.9 %collective-permute-start.6 = (f32[32,512]{1,0:T(8,128)S(1)}, f32[32,512]{1,0:T(8,128)S(1)}, u32[]{:S(2)}, u32[]{:S(2)}) collective-permute-start(f32[32,512]{1,0:T(8,128)S(1)} %get-tuple-element.59), channel_id=1, source_target_pairs={{1,0},{2,1},{3,2},{5,4},{6,5},{7,6},{9,8},{10,9},{11,10},{13,12},{... | collective-permute-start | bytes 196616 | tf_op jit(solution)/shard_map/ppermute | solution.py:14
  142.2 2.7 %collective-permute-start.4 = (f32[1,32,512]{2,1,0:T(8,128)S(1)}, f32[1,32,512]{2,1,0:T(8,128)S(1)}, u32[]{:S(2)}, u32[]{:S(2)}) collective-permute-start(f32[1,32,512]{2,1,0:T(8,128)S(1)} %get-tuple-element.53), channel_id=1, source_target_pairs={{4,0},{8,4},{12,8},{16,12},{20,16},{24,20},{28,24},{5,1},{9,5},{13... | collective-permute-start | bytes 196616 | tf_op jit(solution)/shard_map/ppermute | solution.py:14
  148.7 2.3 %multiply_subtract_fusion = (f32[32,32,512]{2,1,0:T(8,128)S(1)}, f32[32,32,512]{2,1,0:T(8,128)S(1)}, f32[32,32,512]{2,1,0:T(8,128)S(1)}) fusion(f32[32,32,512]{2,1,0:T(8,128)S(1)} %copy-done.5, f32[32,32,512]{2,1,0:T(8,128)S(1)} %multiply_add_fusion.1, f32[32,32,511]{2,1,0:T(8,128)S(1)} %slice.168, f32[32,32,512]{2,1,0:T(8,128)S(1)} %copy-done.3, ...), kind=kLoop, calls=%fused_computation.38 | loop fusion | flops 8388608 | bytes 23064576 | tf_op jit(solution)/shard_map/sub | solution.py:131
  151.3 2.2 %fusion.9 = f32[32,32,512]{2,1,0:T(8,128)S(1)} fusion(f32[32,32,2,512]{3,1,2,0:T(8,128)S(1)} %copy-done.15, f32[32,32,512]{2,1,0:T(8,128)S(1)} %get-tuple-element.46, f32[31,32,512]{2,1,0:T(8,128)S(1)} %slice.163, f32[1,32,512]{2,1,0:T(8,128)S(1)} %get-tuple-element.52, f32[32,32,512]{2,1,0:T(8,128)S(1)} %get-tuple-element.45, ...), kind=kLoop, calls=%fused_computation.14 | loop fusion | flops 4194304 | bytes 16773120 | tf_op jit(solution)/shard_map/sub | solution.py:143
  154.4 2.1 %multiply_add_fusion = f32[32,32,512]{2,1,0:T(8,128)} fusion(f32[32,32,512]{2,1,0:T(8,128)S(1)} %multiply_add_fusion.1, f32[32,32,512]{2,1,0:T(8,128)S(1)} %fusion.26, f32[32,32,512]{2,1,0:T(8,128)S(1)} %copy-done.3), kind=kLoop, calls=%fused_computation.37 | loop fusion | flops 3670016 | bytes 8388608 | tf_op jit(solution)/shard_map/add | solution.py:142
  (90 shorter events, 16.0 us)
Async XLA Ops:
  0.6 44.4 %copy-start = (bf16[16,32,512]{2,1,0:T(8,128)(2,1)S(1)}, bf16[16,32,512]{2,1,0:T(8,128)(2,1)}, u32[]{:S(2)}) copy-start(bf16[16,32,512]{2,1,0:T(8,128)(2,1)} %param.20) | copy-start | bytes 1572868
  0.6 17.0 %copy-start.19 = (s32[768,1]{0,1:T(1,128)S(1)}, s32[768,1]{0,1:T(1,128)}, u32[]{:S(2)}) copy-start(s32[768,1]{0,1:T(1,128)} %param.18) | copy-start | bytes 9220
  0.7 17.4 %copy-start.18 = (s32[768]{0:T(1024)S(1)}, s32[768]{0:T(1024)}, u32[]{:S(2)}) copy-start(s32[768]{0:T(1024)} %param.19) | copy-start | bytes 9220
  0.7 18.1 %copy-start.16 = (bf16[768,2,512]{2,1,0:T(2,128)(2,1)S(1)}, bf16[768,2,512]{2,1,0:T(2,128)(2,1)}, u32[]{:S(2)}) copy-start(bf16[768,2,512]{2,1,0:T(2,128)(2,1)} %param.17) | copy-start | bytes 4718596
  1.7 18.7 %collective-permute-start = (f32[1,32,512]{2,1,0:T(8,128)S(1)}, f32[1,32,512]{2,1,0:T(8,128)S(1)}, u32[]{:S(2)}, u32[]{:S(2)}) collective-permute-start(f32[1,32,512]{2,1,0:T(8,128)S(1)} %get-tuple-element.57), channel_id=1, source_target_pairs={{4,0},{8,4},{12,8},{16,12},{20,16},{24,20},{28,24},{5,1},{9,5},{13... | collective-permute-start | bytes 196616 | tf_op jit(solution)/shard_map/ppermute | solution.py:14
  5.0 15.4 %collective-permute-start.1 = (f32[32,512]{1,0:T(8,128)S(1)}, f32[32,512]{1,0:T(8,128)S(1)}, u32[]{:S(2)}, u32[]{:S(2)}) collective-permute-start(f32[32,512]{1,0:T(8,128)S(1)} %bitcast.75), channel_id=1, source_target_pairs={{1,0},{2,1},{3,2},{5,4},{6,5},{7,6},{9,8},{10,9},{11,10},{13,12},{... | collective-permute-start | bytes 196616 | tf_op jit(solution)/shard_map/ppermute | solution.py:14
  9.7 10.7 %collective-permute-start.3 = (f32[3,32,512]{2,1,0:T(8,128)S(1)}, f32[3,32,512]{2,1,0:T(8,128)S(1)}, u32[]{:S(2)}, u32[]{:S(2)}) collective-permute-start(f32[3,32,512]{2,1,0:T(8,128)S(1)} %pad_maximum_fusion.1), channel_id=1, source_target_pairs={{0,1},{1,2},{2,3},{4,5},{5,6},{6,7},{8,9},{9,10},{10,11},{12,13},{... | collective-permute-start | bytes 589832 | tf_op jit(solution)/shard_map/ppermute | solution.py:14
  15.7 7.0 %collective-permute-start.2 = (f32[3,32,512]{2,1,0:T(8,128)S(1)}, f32[3,32,512]{2,1,0:T(8,128)S(1)}, u32[]{:S(2)}, u32[]{:S(2)}) collective-permute-start(f32[3,32,512]{2,1,0:T(8,128)S(1)} %pad_maximum_fusion), channel_id=1, source_target_pairs={{0,4},{4,8},{8,12},{12,16},{16,20},{20,24},{24,28},{1,5},{5,9},{9,... | collective-permute-start | bytes 589832 | tf_op jit(solution)/shard_map/ppermute | solution.py:14
  23.4 10.4 %all-to-all-start = ((s32[32,1,48]{2,1,0:T(1,128)}), s32[32,1,48]{2,1,0:T(1,128)S(1)}, u32[]{:S(2)}, u32[]{:S(2)}) async-start(s32[32,1,48]{2,1,0:T(1,128)} %all_to_all.14), calls=%async_computation | async-start | bytes 32768 | tf_op jit(solution)/shard_map/all_to_all | solution.py:52
  33.8 5.9 %copy-start.2 = (f32[32,32,512]{2,1,0:T(8,128)S(1)}, f32[32,32,512]{2,1,0:T(8,128)}, u32[]{:S(2)}) copy-start(f32[32,32,512]{2,1,0:T(8,128)} %param.12) | copy-start | bytes 6291460
  33.8 74.1 %all-to-all-start.1 = ((bf16[32,48,1024]{2,1,0:T(8,128)(2,1)}), bf16[32,48,1024]{2,1,0:T(8,128)(2,1)}, u32[]{:S(2)}, u32[]{:S(2)}) async-start(bf16[32,48,1024]{2,1,0:T(8,128)(2,1)} %bitcast.65), calls=%async_computation.1 | async-start | bytes 6291456 | tf_op jit(solution)/shard_map/all_to_all | solution.py:60
  43.1 1.7 %copy-start.17 = (s32[8,8]{1,0:T(8,128)S(1)}, s32[8,8]{1,0:T(8,128)}, u32[]{:S(2)}) copy-start(s32[8,8]{1,0:T(8,128)} %param.21) | copy-start | bytes 772
  53.3 1.3 copy-start.4
  53.3 2.0 %copy-start.6 = (f32[32,32,512]{2,1,0:T(8,128)}, f32[32,32,512]{2,1,0:T(8,128)S(1)}, u32[]{:S(2)}) copy-start(f32[32,32,512]{2,1,0:T(8,128)S(1)} %get-tuple-element.48) | copy-start | bytes 6291460
  53.3 2.7 %copy-start.8 = (f32[32,32,512]{2,1,0:T(8,128)}, f32[32,32,512]{2,1,0:T(8,128)S(1)}, u32[]{:S(2)}) copy-start(f32[32,32,512]{2,1,0:T(8,128)S(1)} %get-tuple-element.49) | copy-start | bytes 6291460
  107.9 21.0 %all-to-all-start.2 = ((bf16[8,32,512]{2,1,0:T(8,128)(2,1)}), bf16[8,32,512]{2,1,0:T(8,128)(2,1)S(1)}, u32[]{:S(2)}, u32[]{:S(2)}) async-start(bf16[8,32,512]{2,1,0:T(8,128)(2,1)} %broadcast_select_fusion), calls=%async_computation.2 | async-start | bytes 524288 | tf_op jit(solution)/shard_map/all_to_all | solution.py:86
  119.6 7.4 %copy-start.13 = (f32[32,32,512]{2,1,0:T(8,128)S(1)}, f32[32,32,512]{2,1,0:T(8,128)}, u32[]{:S(2)}) copy-start(f32[32,32,512]{2,1,0:T(8,128)} %fusion.14) | copy-start | bytes 6291460
  125.1 1.9 %copy-start.14 = (f32[32,32,2,512]{3,1,2,0:T(8,128)}, f32[32,32,2,512]{3,1,2,0:T(8,128)S(1)}, u32[]{:S(2)}) copy-start(f32[32,32,2,512]{3,1,2,0:T(8,128)S(1)} %fusion) | copy-start | bytes 12582916
  133.6 6.2 %collective-permute-start.7 = (f32[32,512]{1,0:T(8,128)S(1)}, f32[32,512]{1,0:T(8,128)S(1)}, u32[]{:S(2)}, u32[]{:S(2)}) collective-permute-start(f32[32,512]{1,0:T(8,128)S(1)} %bitcast.76), channel_id=1, source_target_pairs={{0,1},{1,2},{2,3},{4,5},{5,6},{6,7},{8,9},{9,10},{10,11},{12,13},{... | collective-permute-start | bytes 196616 | tf_op jit(solution)/shard_map/ppermute | solution.py:14
  136.6 5.6 %collective-permute-start.5 = (f32[1,32,512]{2,1,0:T(8,128)S(1)}, f32[1,32,512]{2,1,0:T(8,128)S(1)}, u32[]{:S(2)}, u32[]{:S(2)}) collective-permute-start(f32[1,32,512]{2,1,0:T(8,128)S(1)} %slice.162), channel_id=1, source_target_pairs={{0,4},{4,8},{8,12},{12,16},{16,20},{20,24},{24,28},{1,5},{5,9},{9,... | collective-permute-start | bytes 196616 | tf_op jit(solution)/shard_map/ppermute | solution.py:14
  139.8 7.1 %collective-permute-start.6 = (f32[32,512]{1,0:T(8,128)S(1)}, f32[32,512]{1,0:T(8,128)S(1)}, u32[]{:S(2)}, u32[]{:S(2)}) collective-permute-start(f32[32,512]{1,0:T(8,128)S(1)} %get-tuple-element.59), channel_id=1, source_target_pairs={{1,0},{2,1},{3,2},{5,4},{6,5},{7,6},{9,8},{10,9},{11,10},{13,12},{... | collective-permute-start | bytes 196616 | tf_op jit(solution)/shard_map/ppermute | solution.py:14
  142.2 4.8 %collective-permute-start.4 = (f32[1,32,512]{2,1,0:T(8,128)S(1)}, f32[1,32,512]{2,1,0:T(8,128)S(1)}, u32[]{:S(2)}, u32[]{:S(2)}) collective-permute-start(f32[1,32,512]{2,1,0:T(8,128)S(1)} %get-tuple-element.53), channel_id=1, source_target_pairs={{4,0},{8,4},{12,8},{16,12},{20,16},{24,20},{28,24},{5,1},{9,5},{13... | collective-permute-start | bytes 196616 | tf_op jit(solution)/shard_map/ppermute | solution.py:14
  145.1 1.9 %copy-start.7 = (f32[32,32,512]{2,1,0:T(8,128)S(1)}, f32[32,32,512]{2,1,0:T(8,128)}, u32[]{:S(2)}) copy-start(f32[32,32,512]{2,1,0:T(8,128)} %copy-done.6) | copy-start | bytes 6291460
  145.1 2.2 %copy-start.9 = (f32[32,32,512]{2,1,0:T(8,128)S(1)}, f32[32,32,512]{2,1,0:T(8,128)}, u32[]{:S(2)}) copy-start(f32[32,32,512]{2,1,0:T(8,128)} %copy-done.8) | copy-start | bytes 6291460
  145.5 2.6 %copy-start.3 = (f32[32,32,512]{2,1,0:T(8,128)S(1)}, f32[32,32,512]{2,1,0:T(8,128)}, u32[]{:S(2)}) copy-start(f32[32,32,512]{2,1,0:T(8,128)} %param.16) | copy-start | bytes 6291460
  145.5 3.2 %copy-start.5 = (f32[32,32,512]{2,1,0:T(8,128)S(1)}, f32[32,32,512]{2,1,0:T(8,128)}, u32[]{:S(2)}) copy-start(f32[32,32,512]{2,1,0:T(8,128)} %copy-done.4) | copy-start | bytes 6291460
  148.7 2.6 %copy-start.15 = (f32[32,32,2,512]{3,1,2,0:T(8,128)S(1)}, f32[32,32,2,512]{3,1,2,0:T(8,128)}, u32[]{:S(2)}) copy-start(f32[32,32,2,512]{3,1,2,0:T(8,128)} %copy-done.14) | copy-start | bytes 12582916
  151.0 2.5 %copy-start.10 = (f32[32,32,512]{2,1,0:T(8,128)}, f32[32,32,512]{2,1,0:T(8,128)S(1)}, u32[]{:S(2)}) copy-start(f32[32,32,512]{2,1,0:T(8,128)S(1)} %get-tuple-element.44) | copy-start | bytes 6291460
  151.0 2.7 %copy-start.11 = (f32[32,32,512]{2,1,0:T(8,128)}, f32[32,32,512]{2,1,0:T(8,128)S(1)}, u32[]{:S(2)}) copy-start(f32[32,32,512]{2,1,0:T(8,128)S(1)} %get-tuple-element.45) | copy-start | bytes 6291460
  151.0 3.4 %copy-start.12 = (f32[32,32,512]{2,1,0:T(8,128)}, f32[32,32,512]{2,1,0:T(8,128)S(1)}, u32[]{:S(2)}) copy-start(f32[32,32,512]{2,1,0:T(8,128)S(1)} %get-tuple-element.46) | copy-start | bytes 6291460
  154.4 2.1 %copy-start.1 = (bf16[16,32,512]{2,1,0:T(8,128)(2,1)S(1)}, bf16[16,32,512]{2,1,0:T(8,128)(2,1)}, u32[]{:S(2)}) copy-start(bf16[16,32,512]{2,1,0:T(8,128)(2,1)} %param.20) | copy-start | bytes 1572868

commit v19 on v15

--- a/solution.py
+++ b/solution.py
@@ -118,7 +118,6 @@
     p_by, vy_by, void_by = below_y[:, 0:1], below_y[:, 1:2], below_y[:, 2:3]
     b_bx, _ = material(void_bx)
     b_by, _ = material(void_by)
-    forcing = jnp.zeros_like(pressure).at[0].set(incident)
     z_edge = jnp.zeros((size_x, size_y, 1), jnp.float32)
 
     for step in range(steps):
@@ -138,9 +137,10 @@
         divergence = vel_x - prev_x + (vel_y - prev_y) + (vel_z - prev_z)
         if step + 1 < steps:
             divergence = lax.optimization_barrier(divergence)
-        pressure = pressure + step_ratio * stiffness * (
-            source[:, :, step, :] - divergence + forcing
-        )
+        drive = source[:, :, step, :] - divergence
+        first = pressure[0:1] + step_ratio * stiffness[0:1] * (drive[0:1] + incident[None])
+        pressure = pressure + step_ratio * stiffness * drive
+        pressure = lax.dynamic_update_slice_in_dim(pressure, first, 0, axis=0)
         if step + 1 < steps:
             above_x = from_behind(pressure[0:1], "gx", -1)
             above_y = y_plane_from_behind(pressure[:, 0], "gy", -1)

time: 155 us -> 154 us (level)
  other arithmetic: 26.1 us -> 23.6 us
  starting transfers between devices: 38.2 us -> 40.4 us
    ppermute x8, starting transfers between devices: 20.3 us -> 22.5 us  [from_behind(): return lax.ppermute(block, axis, route)]
    dynamic_update_slice x0 -> x2, other arithmetic: none -> 1.79 us  [body(): pressure = lax.dynamic_update_slice_in_dim(pressure, first, 0, axis=0)]
    ppermute x8, waiting for transfers between devices: 2.97 us -> 4.58 us  [from_behind(): return lax.ppermute(block, axis, route)]
    add x4 -> x2, other arithmetic: 6.59 us -> 4.98 us  [body(): pressure = pressure + step_ratio * stiffness * drive]
    sub x2 -> x1, other arithmetic: 4.05 us -> 2.61 us  [body(): vel_x = vel_x - step_ratio * buoyancy * (next_x - pressure)]
    sub x2 -> x1, other arithmetic: 8.61 us -> 7.35 us  [body(): vel_z = vel_z - step_ratio * buoyancy * (next_z - pressure)]
    unnamed x46 -> x52, local copies, waits for them, and re-layouts: 7.41 us -> 6.76 us
  transfers between devices with their start and end apart: 11 -> 11, of which waited for: 5 -> 3; matrix products, arithmetic and copies ran while one was open for 26% -> 27% of each run, Pallas kernels for 0% -> 0%
where the time goes in v19:
time: 154 us; the launch traced here: 152 us
  waiting for transfers between devices  52.5 us (34%)
  starting transfers between devices  40.4 us (26%)
  local copies, waits for them, and re-layouts  24.9 us (16%)
  other arithmetic  23.6 us (15%)
  matrix products  9.88 us (6%)
    all_to_all x1, waiting for transfers between devices, bubble_source(): lax.all_to_all(outgoing.reshape(devices, capacity, steps * depth), ('gx',...  47.9 us
    ppermute x8, starting transfers between devices, from_behind(): return lax.ppermute(block, axis, route)  22.5 us
    sub x1, other arithmetic, body(): vel_z = vel_z - step_ratio * buoyancy * (next_z - pressure)  7.35 us
    all_to_all x1, starting transfers between devices, incident_plane(): rows = lax.all_to_all(chosen, 'gx', split_axis=0, concat_axis=0, tiled=True)  7.06 us
    unnamed x52, local copies, waits for them, and re-layouts  6.76 us
    all_to_all x1, starting transfers between devices, bubble_source(): lax.all_to_all(out_cols.reshape(devices, capacity), ('gx', 'gy'), split_a...  5.91 us
    dot_general x1, matrix products, bubble_source(): jnp.dot(hits, incoming.reshape(slots, steps * depth), preferred_element_t...  5.48 us
    add x2, other arithmetic, body(): pressure = pressure + step_ratio * stiffness * drive  4.98 us
  transfers between devices with their start and end apart: 11, of which 3 were waited for; matrix products, arithmetic and copies ran while one was open for 27% of the time, Pallas kernels for 0%

profile of v19, /device:TPU:18, one launch (start us, length us, event | category | flops | bytes accessed | tf_op | source)
XLA Modules:
  0.0 152.5 jit_solution(13438239398424750149)
XLA Ops:
  4.0 5.9 %all-to-all-start = ((s32[32,1,48]{2,1,0:T(1,128)}), s32[32,1,48]{2,1,0:T(1,128)S(1)}, u32[]{:S(2)}, u32[]{:S(2)}) async-start(s32[32,1,48]{2,1,0:T(1,128)} %sub.118), calls=%async_computation | async-start | bytes 32768 | tf_op jit(solution)/shard_map/all_to_all | solution.py:51
  9.9 1.5 fusion.45
  11.5 2.2 %collective-permute-start = (f32[1,32,512]{2,1,0:T(8,128)}, f32[1,32,512]{2,1,0:T(8,128)S(1)}, u32[]{:S(2)}, u32[]{:S(2)}) collective-permute-start(f32[1,32,512]{2,1,0:T(8,128)} %get-tuple-element.40), channel_id=1, source_target_pairs={{4,0},{8,4},{12,8},{16,12},{20,16},{24,20},{28,24},{5,1},{9,5},{13... | collective-permute-start | bytes 196616 | tf_op jit(solution)/shard_map/ppermute | solution.py:14
  13.7 1.3 fusion.44
  15.0 2.5 %collective-permute-start.1 = (f32[32,512]{1,0:T(8,128)S(1)}, f32[32,512]{1,0:T(8,128)S(1)}, u32[]{:S(2)}, u32[]{:S(2)}) collective-permute-start(f32[32,512]{1,0:T(8,128)S(1)} %bitcast.78), channel_id=1, source_target_pairs={{1,0},{2,1},{3,2},{5,4},{6,5},{7,6},{9,8},{10,9},{11,10},{13,12},{... | collective-permute-start | bytes 196616 | tf_op jit(solution)/shard_map/ppermute | solution.py:14
  17.5 1.1 slice.116
  18.6 1.1 slice.117
  19.8 4.3 %collective-permute-start.3 = (f32[3,32,512]{2,1,0:T(8,128)S(1)}, f32[3,32,512]{2,1,0:T(8,128)S(1)}, u32[]{:S(2)}, u32[]{:S(2)}) collective-permute-start(f32[3,32,512]{2,1,0:T(8,128)S(1)} %pad_maximum_fusion.1), channel_id=1, source_target_pairs={{0,1},{1,2},{2,3},{4,5},{5,6},{6,7},{8,9},{9,10},{10,11},{12,13},{... | collective-permute-start | bytes 589832 | tf_op jit(solution)/shard_map/ppermute | solution.py:14
  24.1 1.9 %collective-permute-start.2 = (f32[3,32,512]{2,1,0:T(8,128)S(1)}, f32[3,32,512]{2,1,0:T(8,128)S(1)}, u32[]{:S(2)}, u32[]{:S(2)}) collective-permute-start(f32[3,32,512]{2,1,0:T(8,128)S(1)} %pad_maximum_fusion), channel_id=1, source_target_pairs={{0,4},{4,8},{8,12},{12,16},{16,20},{20,24},{24,28},{1,5},{5,9},{9,... | collective-permute-start | bytes 589832 | tf_op jit(solution)/shard_map/ppermute | solution.py:14
  26.5 4.0 %fusion.4 = bf16[1536,1024]{1,0:T(8,128)(2,1)} fusion(bf16[768,1024]{1,0:T(8,128)(2,1)S(1)} %bitcast.71, s32[768]{0:T(1024)S(1)} %copy-done.22), kind=kOutput, calls=%fused_computation.7 | convolution fusion | flops 2418671616 | bytes 4721664 | tf_op jit(solution)/shard_map/dot_general | solution.py:45
  31.1 4.9 %all-to-all-start.1 = ((bf16[32,48,1024]{2,1,0:T(8,128)(2,1)}), bf16[32,48,1024]{2,1,0:T(8,128)(2,1)}, u32[]{:S(2)}, u32[]{:S(2)}) async-start(bf16[32,48,1024]{2,1,0:T(8,128)(2,1)} %bitcast.68), calls=%async_computation.1 | async-start | bytes 6291456 | tf_op jit(solution)/shard_map/all_to_all | solution.py:59
  36.0 1.5 slice.119
  37.5 1.7 %slice.124 = f32[32,31,512]{2,1,0:T(8,128)} slice(f32[32,32,512]{2,1,0:T(8,128)S(1)} %copy-done.2), slice={[0:32], [1:32], [0:512]} | slice | bytes 4063232 | tf_op jit(solution)/shard_map/slice | solution.py:125
  39.2 1.9 %slice.129 = f32[32,32,511]{2,1,0:T(8,128)} slice(f32[32,32,512]{2,1,0:T(8,128)S(1)} %copy-done.2), slice={[0:32], [0:32], [1:512]} | slice | bytes 4186112 | tf_op jit(solution)/shard_map/slice | solution.py:126
  43.2 7.4 %multiply_subtract_fusion.1 = (f32[32,32,512]{2,1,0:T(8,128)S(1)}, f32[32,32,512]{2,1,0:T(8,128)S(1)}, f32[32,32,512]{2,1,0:T(8,128)S(1)}, f32[32,32,512]{2,1,0:T(8,128)}) fusion(f32[32,32,512]{2,1,0:T(8,128)} %param.13, f32[32,32,512]{2,1,0:T(8,128)S(1)} %copy-done.2, f32[32,32,511]{2,1,0:T(8,128)} %slice.129, f32[32,32,512]{2,1,0:T(8,128)} %param.14, ...), kind=kLoop, calls=%fused_computation.40 | loop fusion | flops 9961472 | bytes 25161728 | tf_op jit(solution)/shard_map/sub | solution.py:129
  50.9 1.0 copy-done.6
  53.3 3.1 %fusion.14 = f32[32,32,512]{2,1,0:T(8,128)} fusion(f32[32,32,512]{2,1,0:T(8,128)S(1)} %get-tuple-element.33, f32[31,32,512]{2,1,0:T(8,128)S(1)} %slice.147, f32[1,32,512]{2,1,0:T(8,128)S(1)} %get-tuple-element.26, f32[32,32,512]{2,1,0:T(8,128)S(1)} %get-tuple-element.32, f32[32,31,512]{2,1,0:T(8,128)S(1)} %bitcast.65, f32[32,1,512]{2,1,0:T(1,128)S(1)} %copy.32, ...), kind=kLoop, calls=%fused_computation.22 | loop fusion | flops 3670016 | bytes 14675968 | tf_op jit(solution)/shard_map/add | solution.py:137
  56.4 47.9 %all-to-all-done.1 = bf16[32,48,1024]{2,1,0:T(8,128)(2,1)} async-done(((bf16[32,48,1024]{2,1,0:T(8,128)(2,1)}), bf16[32,48,1024]{2,1,0:T(8,128)(2,1)}, u32[]{:S(2)}, u32[]{:S(2)}) %all-to-all-start.1) | async-done | bytes 3145760 | tf_op jit(solution)/shard_map/all_to_all | solution.py:59
  104.3 7.1 %all-to-all-start.2 = ((bf16[8,32,512]{2,1,0:T(8,128)(2,1)}), bf16[8,32,512]{2,1,0:T(8,128)(2,1)S(1)}, u32[]{:S(2)}, u32[]{:S(2)}) async-start(bf16[8,32,512]{2,1,0:T(8,128)(2,1)} %broadcast_select_fusion), calls=%async_computation.2 | async-start | bytes 524288 | tf_op jit(solution)/shard_map/all_to_all | solution.py:85
  111.3 4.7 %copy.29 = bf16[1536,1024]{0,1:T(8,128)(2,1)} copy(bf16[1536,1024]{1,0:T(8,128)(2,1)} %bitcast.10) | data formatting | bytes 6291456 | tf_op jit(solution)/shard_map/reshape | solution.py:70
  116.0 5.5 %fusion = f32[32,32,2,512]{3,1,2,0:T(8,128)S(1)} fusion(bf16[2,512,1536,1]{2,1,0,3:T(8,128)(2,1)} %bitcast.69, s32[1536]{0:T(1024)S(1)} %eq.62, s32[32,32]{1,0:T(8,128)S(1)} %multiply_add_fusion.2), kind=kOutput, calls=%fused_computation.1 | convolution fusion | flops 3222798336 | bytes 7350272 | tf_op jit(solution)/shard_map/dot_general | solution.py:69
  121.5 1.9 %copy-done.16 = f32[32,32,2,512]{3,1,2,0:T(8,128)} copy-done((f32[32,32,2,512]{3,1,2,0:T(8,128)}, f32[32,32,2,512]{3,1,2,0:T(8,128)S(1)}, u32[]{:S(2)}) %copy-start.16) | copy-done | bytes 4194328
  123.4 2.4 %multiply_add_fusion.1 = (f32[32,32,512]{2,1,0:T(8,128)S(1)}, f32[32,32,512]{2,1,0:T(8,128)}) fusion(f32[32,32,512]{2,1,0:T(8,128)S(1)} %copy-done.3, f32[32,32,512]{2,1,0:T(8,128)S(1)} %copy-done.4, f32[32,32,512]{2,1,0:T(8,128)S(1)} %copy-done.15, f32[32,32,2,512]{3,1,2,0:T(8,128)S(1)} %fusion), kind=kLoop, calls=%fused_computation.39 | loop fusion | flops 4194304 | bytes 12582912 | tf_op jit(solution)/shard_map/add | solution.py:142
  125.9 0.9 constant_dynamic-update-slice_fusion
  127.0 2.9 %collective-permute-start.7 = (f32[32,512]{1,0:T(8,128)S(1)}, f32[32,512]{1,0:T(8,128)S(1)}, u32[]{:S(2)}, u32[]{:S(2)}) collective-permute-start(f32[32,512]{1,0:T(8,128)S(1)} %bitcast.79), channel_id=1, source_target_pairs={{0,1},{1,2},{2,3},{4,5},{5,6},{6,7},{8,9},{9,10},{10,11},{12,13},{... | collective-permute-start | bytes 196616 | tf_op jit(solution)/shard_map/ppermute | solution.py:14
  131.1 2.2 %collective-permute-start.5 = (f32[1,32,512]{2,1,0:T(8,128)S(1)}, f32[1,32,512]{2,1,0:T(8,128)S(1)}, u32[]{:S(2)}, u32[]{:S(2)}) collective-permute-start(f32[1,32,512]{2,1,0:T(8,128)S(1)} %slice.154), channel_id=1, source_target_pairs={{0,4},{4,8},{8,12},{12,16},{16,20},{20,24},{24,28},{1,5},{5,9},{9,... | collective-permute-start | bytes 196616 | tf_op jit(solution)/shard_map/ppermute | solution.py:14
  133.3 3.6 %collective-permute-start.4 = (f32[1,32,512]{2,1,0:T(8,128)S(1)}, f32[1,32,512]{2,1,0:T(8,128)S(1)}, u32[]{:S(2)}, u32[]{:S(2)}) collective-permute-start(f32[1,32,512]{2,1,0:T(8,128)S(1)} %get-tuple-element.21), channel_id=1, source_target_pairs={{4,0},{8,4},{12,8},{16,12},{20,16},{24,20},{28,24},{5,1},{9,5},{13... | collective-permute-start | bytes 196616 | tf_op jit(solution)/shard_map/ppermute | solution.py:14
  137.0 2.9 %collective-permute-start.6 = (f32[32,512]{1,0:T(8,128)S(1)}, f32[32,512]{1,0:T(8,128)S(1)}, u32[]{:S(2)}, u32[]{:S(2)}) collective-permute-start(f32[32,512]{1,0:T(8,128)S(1)} %get-tuple-element.42), channel_id=1, source_target_pairs={{1,0},{2,1},{3,2},{5,4},{6,5},{7,6},{9,8},{10,9},{11,10},{13,12},{... | collective-permute-start | bytes 196616 | tf_op jit(solution)/shard_map/ppermute | solution.py:14
  140.0 4.0 %collective-permute-done.6 = f32[32,512]{1,0:T(8,128)S(1)} collective-permute-done((f32[32,512]{1,0:T(8,128)S(1)}, f32[32,512]{1,0:T(8,128)S(1)}, u32[]{:S(2)}, u32[]{:S(2)}) %collective-permute-start.6) | collective-permute-done | bytes 65568 | tf_op jit(solution)/shard_map/ppermute | solution.py:14
  144.1 2.6 %fusion.18 = (f32[32,32,512]{2,1,0:T(8,128)S(1)}, f32[32,32,512]{2,1,0:T(8,128)S(1)}, f32[32,32,512]{2,1,0:T(8,128)S(1)}) fusion(f32[32,32,512]{2,1,0:T(8,128)S(1)} %copy-done.11, f32[32,32,512]{2,1,0:T(8,128)S(1)} %get-tuple-element.20, f32[1,32,512]{2,1,0:T(8,128)S(1)} %collective-permute-done.4, f32[31,32,512]{2,1,0:T(8,128)S(1)} %slice.153, ...), kind=kLoop, calls=%fused_computation.29 | loop fusion | flops 8388608 | bytes 23064576 | tf_op jit(solution)/shard_map/sub | solution.py:127
  147.1 2.6 %multiply_add_fusion = (f32[32,32,512]{2,1,0:T(8,128)S(1)}, f32[32,32,512]{2,1,0:T(8,128)S(1)}) fusion(f32[32,32,512]{2,1,0:T(8,128)S(1)} %get-tuple-element.20, f32[32,32,512]{2,1,0:T(8,128)S(1)} %copy-done.5, f32[32,32,512]{2,1,0:T(8,128)S(1)} %get-tuple-element.29, f32[32,32,511]{2,1,0:T(8,128)S(1)} %bitcast.66, f32[32,32,512]{2,1,0:T(8,128)S(1)} %get-tuple-element.30, ...), kind=kLoop, calls=%fused_computation.37 | loop fusion | flops 7864320 | bytes 23064576 | tf_op jit(solution)/shard_map/add | solution.py:142
  151.2 1.3 copy-done.18
  (96 shorter events, 11.3 us)
Async XLA Ops:
  0.6 40.7 %copy-start = (bf16[16,32,512]{2,1,0:T(8,128)(2,1)S(1)}, bf16[16,32,512]{2,1,0:T(8,128)(2,1)}, u32[]{:S(2)}) copy-start(bf16[16,32,512]{2,1,0:T(8,128)(2,1)} %param.18) | copy-start | bytes 1572868
  0.6 23.4 %slice-start = ((f32[32,32,512]{2,1,0:T(8,128)}), f32[1,32,512]{2,1,0:T(8,128)S(1)}, s32[]{:S(2)}) async-start(f32[32,32,512]{2,1,0:T(8,128)} %param.14), calls=%async_computation.3 | async-start | bytes 131072 | tf_op jit(solution)/shard_map/slice | solution.py:103
  0.7 23.4 %slice-start.1 = ((f32[32,32,512]{2,1,0:T(8,128)}), f32[1,32,512]{2,1,0:T(8,128)S(1)}, s32[]{:S(2)}) async-start(f32[32,32,512]{2,1,0:T(8,128)} %param.11), calls=%async_computation.4 | async-start | bytes 131072 | tf_op jit(solution)/shard_map/slice | solution.py:103
  0.7 25.4 %copy-start.19 = (bf16[768,2,512]{2,1,0:T(2,128)(2,1)S(1)}, bf16[768,2,512]{2,1,0:T(2,128)(2,1)}, u32[]{:S(2)}) copy-start(bf16[768,2,512]{2,1,0:T(2,128)(2,1)} %param.15) | copy-start | bytes 4718596
  4.0 26.5 %all-to-all-start = ((s32[32,1,48]{2,1,0:T(1,128)}), s32[32,1,48]{2,1,0:T(1,128)S(1)}, u32[]{:S(2)}, u32[]{:S(2)}) async-start(s32[32,1,48]{2,1,0:T(1,128)} %sub.118), calls=%async_computation | async-start | bytes 32768 | tf_op jit(solution)/shard_map/all_to_all | solution.py:51
  11.5 19.1 %collective-permute-start = (f32[1,32,512]{2,1,0:T(8,128)}, f32[1,32,512]{2,1,0:T(8,128)S(1)}, u32[]{:S(2)}, u32[]{:S(2)}) collective-permute-start(f32[1,32,512]{2,1,0:T(8,128)} %get-tuple-element.40), channel_id=1, source_target_pairs={{4,0},{8,4},{12,8},{16,12},{20,16},{24,20},{28,24},{5,1},{9,5},{13... | collective-permute-start | bytes 196616 | tf_op jit(solution)/shard_map/ppermute | solution.py:14
  15.0 15.5 %collective-permute-start.1 = (f32[32,512]{1,0:T(8,128)S(1)}, f32[32,512]{1,0:T(8,128)S(1)}, u32[]{:S(2)}, u32[]{:S(2)}) collective-permute-start(f32[32,512]{1,0:T(8,128)S(1)} %bitcast.78), channel_id=1, source_target_pairs={{1,0},{2,1},{3,2},{5,4},{6,5},{7,6},{9,8},{10,9},{11,10},{13,12},{... | collective-permute-start | bytes 196616 | tf_op jit(solution)/shard_map/ppermute | solution.py:14
  19.7 6.7 %copy-start.22 = (s32[768]{0:T(1024)S(1)}, s32[768]{0:T(1024)}, u32[]{:S(2)}) copy-start(s32[768]{0:T(1024)} %copy-done.21) | copy-start | bytes 9220
  19.8 10.8 %collective-permute-start.3 = (f32[3,32,512]{2,1,0:T(8,128)S(1)}, f32[3,32,512]{2,1,0:T(8,128)S(1)}, u32[]{:S(2)}, u32[]{:S(2)}) collective-permute-start(f32[3,32,512]{2,1,0:T(8,128)S(1)} %pad_maximum_fusion.1), channel_id=1, source_target_pairs={{0,1},{1,2},{2,3},{4,5},{5,6},{6,7},{8,9},{9,10},{10,11},{12,13},{... | collective-permute-start | bytes 589832 | tf_op jit(solution)/shard_map/ppermute | solution.py:14
  24.1 7.0 %collective-permute-start.2 = (f32[3,32,512]{2,1,0:T(8,128)S(1)}, f32[3,32,512]{2,1,0:T(8,128)S(1)}, u32[]{:S(2)}, u32[]{:S(2)}) collective-permute-start(f32[3,32,512]{2,1,0:T(8,128)S(1)} %pad_maximum_fusion), channel_id=1, source_target_pairs={{0,4},{4,8},{8,12},{12,16},{16,20},{20,24},{24,28},{1,5},{5,9},{9,... | collective-permute-start | bytes 589832 | tf_op jit(solution)/shard_map/ppermute | solution.py:14
  31.1 4.9 %copy-start.2 = (f32[32,32,512]{2,1,0:T(8,128)S(1)}, f32[32,32,512]{2,1,0:T(8,128)}, u32[]{:S(2)}) copy-start(f32[32,32,512]{2,1,0:T(8,128)} %param.10) | copy-start | bytes 6291460
  31.1 73.2 %all-to-all-start.1 = ((bf16[32,48,1024]{2,1,0:T(8,128)(2,1)}), bf16[32,48,1024]{2,1,0:T(8,128)(2,1)}, u32[]{:S(2)}, u32[]{:S(2)}) async-start(bf16[32,48,1024]{2,1,0:T(8,128)(2,1)} %bitcast.68), calls=%async_computation.1 | async-start | bytes 6291456 | tf_op jit(solution)/shard_map/all_to_all | solution.py:59
  50.6 2.1 %copy-start.8 = (f32[32,32,512]{2,1,0:T(8,128)}, f32[32,32,512]{2,1,0:T(8,128)S(1)}, u32[]{:S(2)}) copy-start(f32[32,32,512]{2,1,0:T(8,128)S(1)} %get-tuple-element.32) | copy-start | bytes 6291460
  50.6 2.7 %copy-start.10 = (f32[32,32,512]{2,1,0:T(8,128)}, f32[32,32,512]{2,1,0:T(8,128)S(1)}, u32[]{:S(2)}) copy-start(f32[32,32,512]{2,1,0:T(8,128)S(1)} %get-tuple-element.33) | copy-start | bytes 6291460
  104.3 21.5 %all-to-all-start.2 = ((bf16[8,32,512]{2,1,0:T(8,128)(2,1)}), bf16[8,32,512]{2,1,0:T(8,128)(2,1)S(1)}, u32[]{:S(2)}, u32[]{:S(2)}) async-start(bf16[8,32,512]{2,1,0:T(8,128)(2,1)} %broadcast_select_fusion), calls=%async_computation.2 | async-start | bytes 524288 | tf_op jit(solution)/shard_map/all_to_all | solution.py:85
  116.0 7.5 %copy-start.3 = (f32[32,32,512]{2,1,0:T(8,128)S(1)}, f32[32,32,512]{2,1,0:T(8,128)}, u32[]{:S(2)}) copy-start(f32[32,32,512]{2,1,0:T(8,128)} %param.10) | copy-start | bytes 6291460
  116.0 7.5 %copy-start.4 = (f32[32,32,512]{2,1,0:T(8,128)S(1)}, f32[32,32,512]{2,1,0:T(8,128)}, u32[]{:S(2)}) copy-start(f32[32,32,512]{2,1,0:T(8,128)} %param.14) | copy-start | bytes 6291460
  116.0 7.5 %copy-start.15 = (f32[32,32,512]{2,1,0:T(8,128)S(1)}, f32[32,32,512]{2,1,0:T(8,128)}, u32[]{:S(2)}) copy-start(f32[32,32,512]{2,1,0:T(8,128)} %fusion.14) | copy-start | bytes 6291460
  121.5 2.0 %copy-start.16 = (f32[32,32,2,512]{3,1,2,0:T(8,128)}, f32[32,32,2,512]{3,1,2,0:T(8,128)S(1)}, u32[]{:S(2)}) copy-start(f32[32,32,2,512]{3,1,2,0:T(8,128)S(1)} %fusion) | copy-start | bytes 12582916
  127.0 10.0 %collective-permute-start.7 = (f32[32,512]{1,0:T(8,128)S(1)}, f32[32,512]{1,0:T(8,128)S(1)}, u32[]{:S(2)}, u32[]{:S(2)}) collective-permute-start(f32[32,512]{1,0:T(8,128)S(1)} %bitcast.79), channel_id=1, source_target_pairs={{0,1},{1,2},{2,3},{4,5},{5,6},{6,7},{8,9},{9,10},{10,11},{12,13},{... | collective-permute-start | bytes 196616 | tf_op jit(solution)/shard_map/ppermute | solution.py:14
  130.1 14.0 %copy-start.9 = (f32[32,32,512]{2,1,0:T(8,128)S(1)}, f32[32,32,512]{2,1,0:T(8,128)}, u32[]{:S(2)}) copy-start(f32[32,32,512]{2,1,0:T(8,128)} %copy-done.8) | copy-start | bytes 6291460
  130.1 14.0 %copy-start.11 = (f32[32,32,512]{2,1,0:T(8,128)S(1)}, f32[32,32,512]{2,1,0:T(8,128)}, u32[]{:S(2)}) copy-start(f32[32,32,512]{2,1,0:T(8,128)} %copy-done.10) | copy-start | bytes 6291460
  130.7 13.4 %copy-start.5 = (f32[32,32,512]{2,1,0:T(8,128)S(1)}, f32[32,32,512]{2,1,0:T(8,128)}, u32[]{:S(2)}) copy-start(f32[32,32,512]{2,1,0:T(8,128)} %param.14) | copy-start | bytes 6291460
  130.7 13.4 %copy-start.7 = (f32[32,32,512]{2,1,0:T(8,128)S(1)}, f32[32,32,512]{2,1,0:T(8,128)}, u32[]{:S(2)}) copy-start(f32[32,32,512]{2,1,0:T(8,128)} %copy-done.6) | copy-start | bytes 6291460
  131.1 8.8 %collective-permute-start.5 = (f32[1,32,512]{2,1,0:T(8,128)S(1)}, f32[1,32,512]{2,1,0:T(8,128)S(1)}, u32[]{:S(2)}, u32[]{:S(2)}) collective-permute-start(f32[1,32,512]{2,1,0:T(8,128)S(1)} %slice.154), channel_id=1, source_target_pairs={{0,4},{4,8},{8,12},{12,16},{16,20},{20,24},{24,28},{1,5},{5,9},{9,... | collective-permute-start | bytes 196616 | tf_op jit(solution)/shard_map/ppermute | solution.py:14
  133.3 10.8 %collective-permute-start.4 = (f32[1,32,512]{2,1,0:T(8,128)S(1)}, f32[1,32,512]{2,1,0:T(8,128)S(1)}, u32[]{:S(2)}, u32[]{:S(2)}) collective-permute-start(f32[1,32,512]{2,1,0:T(8,128)S(1)} %get-tuple-element.21), channel_id=1, source_target_pairs={{4,0},{8,4},{12,8},{16,12},{20,16},{24,20},{28,24},{5,1},{9,5},{13... | collective-permute-start | bytes 196616 | tf_op jit(solution)/shard_map/ppermute | solution.py:14
  137.0 7.1 %collective-permute-start.6 = (f32[32,512]{1,0:T(8,128)S(1)}, f32[32,512]{1,0:T(8,128)S(1)}, u32[]{:S(2)}, u32[]{:S(2)}) collective-permute-start(f32[32,512]{1,0:T(8,128)S(1)} %get-tuple-element.42), channel_id=1, source_target_pairs={{1,0},{2,1},{3,2},{5,4},{6,5},{7,6},{9,8},{10,9},{11,10},{13,12},{... | collective-permute-start | bytes 196616 | tf_op jit(solution)/shard_map/ppermute | solution.py:14
  144.1 2.9 %copy-start.17 = (f32[32,32,2,512]{3,1,2,0:T(8,128)S(1)}, f32[32,32,2,512]{3,1,2,0:T(8,128)}, u32[]{:S(2)}) copy-start(f32[32,32,2,512]{3,1,2,0:T(8,128)} %copy-done.16) | copy-start | bytes 12582916
  146.8 3.0 %copy-start.12 = (f32[32,32,512]{2,1,0:T(8,128)}, f32[32,32,512]{2,1,0:T(8,128)S(1)}, u32[]{:S(2)}) copy-start(f32[32,32,512]{2,1,0:T(8,128)S(1)} %get-tuple-element.29) | copy-start | bytes 6291460
  146.8 3.0 %copy-start.13 = (f32[32,32,512]{2,1,0:T(8,128)}, f32[32,32,512]{2,1,0:T(8,128)S(1)}, u32[]{:S(2)}) copy-start(f32[32,32,512]{2,1,0:T(8,128)S(1)} %get-tuple-element.30) | copy-start | bytes 6291460
  146.8 3.5 %copy-start.14 = (f32[32,32,512]{2,1,0:T(8,128)}, f32[32,32,512]{2,1,0:T(8,128)S(1)}, u32[]{:S(2)}) copy-start(f32[32,32,512]{2,1,0:T(8,128)S(1)} %get-tuple-element.28) | copy-start | bytes 6291460
  147.1 5.4 %copy-start.1 = (bf16[16,32,512]{2,1,0:T(8,128)(2,1)S(1)}, bf16[16,32,512]{2,1,0:T(8,128)(2,1)}, u32[]{:S(2)}) copy-start(bf16[16,32,512]{2,1,0:T(8,128)(2,1)} %param.18) | copy-start | bytes 1572868
  (4 other events, 5.3 us)

commit v20 on v19

--- a/solution.py
+++ b/solution.py
@@ -135,8 +135,6 @@
         prev_y = jnp.concatenate([lower_y, vel_y[:, :-1]], 1)
         prev_z = jnp.concatenate([z_edge, vel_z[:, :, :-1]], 2)
         divergence = vel_x - prev_x + (vel_y - prev_y) + (vel_z - prev_z)
-        if step + 1 < steps:
-            divergence = lax.optimization_barrier(divergence)
         drive = source[:, :, step, :] - divergence
         first = pressure[0:1] + step_ratio * stiffness[0:1] * (drive[0:1] + incident[None])
         pressure = pressure + step_ratio * stiffness * drive

time: 154 us -> 155 us (level)
  waiting for transfers between devices: 52.5 us -> 55 us
    sub x1 -> x2, other arithmetic: 2.61 us -> 10.3 us  [body(): vel_x = vel_x - step_ratio * buoyancy * (next_x - pressure)]
    sub x1 -> x0, other arithmetic: 7.35 us -> none  [body(): vel_z = vel_z - step_ratio * buoyancy * (next_z - pressure)]
    add x1 -> x0, other arithmetic: 3.09 us -> none  [body(): divergence = vel_x - prev_x + (vel_y - prev_y) + (vel_z - prev_z)]
    all_to_all x1, waiting for transfers between devices: 47.9 us -> 50.4 us  [bubble_source(): lax.all_to_all(outgoing.reshape(devices, capacity, steps * depth), ('gx',...]
    add x2, other arithmetic: 4.98 us -> 6.66 us  [body(): pressure = pressure + step_ratio * stiffness * drive]
    unnamed x52 -> x54, local copies, waits for them, and re-layouts: 6.76 us -> 5.71 us
where the time goes in v20:
time: 155 us; the launch traced here: 154 us
  waiting for transfers between devices  55 us (35%)
  starting transfers between devices  40.6 us (26%)
  local copies, waits for them, and re-layouts  25.1 us (16%)
  other arithmetic  22.5 us (15%)
  matrix products  9.87 us (6%)
    all_to_all x1, waiting for transfers between devices, bubble_source(): lax.all_to_all(outgoing.reshape(devices, capacity, steps * depth), ('gx',...  50.4 us
    ppermute x8, starting transfers between devices, from_behind(): return lax.ppermute(block, axis, route)  22.7 us
    sub x2, other arithmetic, body(): vel_x = vel_x - step_ratio * buoyancy * (next_x - pressure)  10.3 us
    all_to_all x1, starting transfers between devices, incident_plane(): rows = lax.all_to_all(chosen, 'gx', split_axis=0, concat_axis=0, tiled=True)  7.06 us
    add x2, other arithmetic, body(): pressure = pressure + step_ratio * stiffness * drive  6.66 us
    all_to_all x1, starting transfers between devices, bubble_source(): lax.all_to_all(out_cols.reshape(devices, capacity), ('gx', 'gy'), split_a...  5.91 us
    unnamed x54, local copies, waits for them, and re-layouts  5.71 us
    dot_general x1, matrix products, bubble_source(): jnp.dot(hits, incoming.reshape(slots, steps * depth), preferred_element_t...  5.49 us
  transfers between devices with their start and end apart: 11, of which 3 were waited for; matrix products, arithmetic and copies ran while one was open for 27% of the time, Pallas kernels for 0%

profile of v20, /device:TPU:18, one launch (start us, length us, event | category | flops | bytes accessed | tf_op | source)
XLA Modules:
  0.0 154.4 jit_solution(15252352610290641512)
XLA Ops:
  4.0 5.9 %all-to-all-start = ((s32[32,1,48]{2,1,0:T(1,128)}), s32[32,1,48]{2,1,0:T(1,128)S(1)}, u32[]{:S(2)}, u32[]{:S(2)}) async-start(s32[32,1,48]{2,1,0:T(1,128)} %sub.118), calls=%async_computation | async-start | bytes 32768 | tf_op jit(solution)/shard_map/all_to_all | solution.py:51
  9.9 1.5 fusion.45
  11.5 2.2 %collective-permute-start = (f32[1,32,512]{2,1,0:T(8,128)}, f32[1,32,512]{2,1,0:T(8,128)S(1)}, u32[]{:S(2)}, u32[]{:S(2)}) collective-permute-start(f32[1,32,512]{2,1,0:T(8,128)} %get-tuple-element.40), channel_id=1, source_target_pairs={{4,0},{8,4},{12,8},{16,12},{20,16},{24,20},{28,24},{5,1},{9,5},{13... | collective-permute-start | bytes 196616 | tf_op jit(solution)/shard_map/ppermute | solution.py:14
  13.7 1.3 fusion.44
  15.0 2.5 %collective-permute-start.1 = (f32[32,512]{1,0:T(8,128)S(1)}, f32[32,512]{1,0:T(8,128)S(1)}, u32[]{:S(2)}, u32[]{:S(2)}) collective-permute-start(f32[32,512]{1,0:T(8,128)S(1)} %bitcast.78), channel_id=1, source_target_pairs={{1,0},{2,1},{3,2},{5,4},{6,5},{7,6},{9,8},{10,9},{11,10},{13,12},{... | collective-permute-start | bytes 196616 | tf_op jit(solution)/shard_map/ppermute | solution.py:14
  17.5 1.1 slice.116
  18.6 1.1 slice.117
  19.8 4.3 %collective-permute-start.3 = (f32[3,32,512]{2,1,0:T(8,128)S(1)}, f32[3,32,512]{2,1,0:T(8,128)S(1)}, u32[]{:S(2)}, u32[]{:S(2)}) collective-permute-start(f32[3,32,512]{2,1,0:T(8,128)S(1)} %pad_maximum_fusion.1), channel_id=1, source_target_pairs={{0,1},{1,2},{2,3},{4,5},{5,6},{6,7},{8,9},{9,10},{10,11},{12,13},{... | collective-permute-start | bytes 589832 | tf_op jit(solution)/shard_map/ppermute | solution.py:14
  24.1 1.9 %collective-permute-start.2 = (f32[3,32,512]{2,1,0:T(8,128)S(1)}, f32[3,32,512]{2,1,0:T(8,128)S(1)}, u32[]{:S(2)}, u32[]{:S(2)}) collective-permute-start(f32[3,32,512]{2,1,0:T(8,128)S(1)} %pad_maximum_fusion), channel_id=1, source_target_pairs={{0,4},{4,8},{8,12},{12,16},{16,20},{20,24},{24,28},{1,5},{5,9},{9,... | collective-permute-start | bytes 589832 | tf_op jit(solution)/shard_map/ppermute | solution.py:14
  26.5 4.0 %fusion.4 = bf16[1536,1024]{1,0:T(8,128)(2,1)} fusion(bf16[768,1024]{1,0:T(8,128)(2,1)S(1)} %bitcast.71, s32[768]{0:T(1024)S(1)} %copy-done.23), kind=kOutput, calls=%fused_computation.7 | convolution fusion | flops 2418671616 | bytes 4721664 | tf_op jit(solution)/shard_map/dot_general | solution.py:45
  31.1 4.9 %all-to-all-start.1 = ((bf16[32,48,1024]{2,1,0:T(8,128)(2,1)}), bf16[32,48,1024]{2,1,0:T(8,128)(2,1)}, u32[]{:S(2)}, u32[]{:S(2)}) async-start(bf16[32,48,1024]{2,1,0:T(8,128)(2,1)} %bitcast.68), calls=%async_computation.1 | async-start | bytes 6291456 | tf_op jit(solution)/shard_map/all_to_all | solution.py:59
  36.0 1.6 %slice.119 = f32[31,32,512]{2,1,0:T(8,128)} slice(f32[32,32,512]{2,1,0:T(8,128)S(1)} %copy-done.2), slice={[1:32], [0:32], [0:512]} | slice | bytes 4063232 | tf_op jit(solution)/shard_map/slice | solution.py:124
  37.6 1.7 %slice.124 = f32[32,31,512]{2,1,0:T(8,128)} slice(f32[32,32,512]{2,1,0:T(8,128)S(1)} %copy-done.2), slice={[0:32], [1:32], [0:512]} | slice | bytes 4063232 | tf_op jit(solution)/shard_map/slice | solution.py:125
  39.3 1.9 %slice.129 = f32[32,32,511]{2,1,0:T(8,128)} slice(f32[32,32,512]{2,1,0:T(8,128)S(1)} %copy-done.2), slice={[0:32], [0:32], [1:512]} | slice | bytes 4186112 | tf_op jit(solution)/shard_map/slice | solution.py:126
  43.3 7.7 %fusion.12 = (f32[32,32,512]{2,1,0:T(8,128)S(1)}, f32[32,32,512]{2,1,0:T(8,128)}, f32[32,32,512]{2,1,0:T(8,128)}) fusion(f32[32,32,512]{2,1,0:T(8,128)} %param.11, f32[32,32,512]{2,1,0:T(8,128)S(1)} %copy-done.2, f32[1,32,512]{2,1,0:T(8,128)S(1)} %collective-permute-done, f32[31,32,512]{2,1,0:T(8,128)} %slice.119, f32[32,32,512]{2,1,0:T(8,128)} %param.14, ...), kind=kLoop, calls=%fused_computation.19 | loop fusion | flops 8388608 | bytes 23064576 | tf_op jit(solution)/shard_map/sub | solution.py:127
  51.0 1.3 copy-done.10
  52.3 1.5 slice.147
  53.8 50.4 %all-to-all-done.1 = bf16[32,48,1024]{2,1,0:T(8,128)(2,1)} async-done(((bf16[32,48,1024]{2,1,0:T(8,128)(2,1)}), bf16[32,48,1024]{2,1,0:T(8,128)(2,1)}, u32[]{:S(2)}, u32[]{:S(2)}) %all-to-all-start.1) | async-done | bytes 3145760 | tf_op jit(solution)/shard_map/all_to_all | solution.py:59
  104.3 7.1 %all-to-all-start.2 = ((bf16[8,32,512]{2,1,0:T(8,128)(2,1)}), bf16[8,32,512]{2,1,0:T(8,128)(2,1)S(1)}, u32[]{:S(2)}, u32[]{:S(2)}) async-start(bf16[8,32,512]{2,1,0:T(8,128)(2,1)} %broadcast_select_fusion), calls=%async_computation.2 | async-start | bytes 524288 | tf_op jit(solution)/shard_map/all_to_all | solution.py:85
  111.3 4.6 %copy.29 = bf16[1536,1024]{0,1:T(8,128)(2,1)} copy(bf16[1536,1024]{1,0:T(8,128)(2,1)} %bitcast.10) | data formatting | bytes 6291456 | tf_op jit(solution)/shard_map/reshape | solution.py:70
  116.0 5.5 %fusion = f32[32,32,2,512]{3,1,2,0:T(8,128)S(1)} fusion(bf16[2,512,1536,1]{2,1,0,3:T(8,128)(2,1)} %bitcast.69, s32[1536]{0:T(1024)S(1)} %eq.62, s32[32,32]{1,0:T(8,128)S(1)} %multiply_add_fusion.2), kind=kOutput, calls=%fused_computation.1 | convolution fusion | flops 3222798336 | bytes 7350272 | tf_op jit(solution)/shard_map/dot_general | solution.py:69
  121.5 2.0 %copy-done.17 = f32[32,32,2,512]{3,1,2,0:T(8,128)} copy-done((f32[32,32,2,512]{3,1,2,0:T(8,128)}, f32[32,32,2,512]{3,1,2,0:T(8,128)S(1)}, u32[]{:S(2)}) %copy-start.17) | copy-done | bytes 4194328
  123.5 4.0 %multiply_add_fusion.1 = (f32[32,32,512]{2,1,0:T(8,128)S(1)}, f32[32,32,512]{2,1,0:T(8,128)}, f32[32,32,512]{2,1,0:T(8,128)}) fusion(f32[32,32,512]{2,1,0:T(8,128)S(1)} %copy-done.3, f32[32,32,512]{2,1,0:T(8,128)S(1)} %copy-done.4, f32[32,32,512]{2,1,0:T(8,128)S(1)} %copy-done.8, f32[32,32,511]{2,1,0:T(8,128)S(1)} %bitcast.65, ...), kind=kLoop, calls=%fused_computation.39 | loop fusion | flops 7864320 | bytes 25161728 | tf_op jit(solution)/shard_map/add | solution.py:140
  127.6 0.9 constant_dynamic-update-slice_fusion
  128.7 3.1 %collective-permute-start.7 = (f32[32,512]{1,0:T(8,128)S(1)}, f32[32,512]{1,0:T(8,128)S(1)}, u32[]{:S(2)}, u32[]{:S(2)}) collective-permute-start(f32[32,512]{1,0:T(8,128)S(1)} %bitcast.79), channel_id=1, source_target_pairs={{0,1},{1,2},{2,3},{4,5},{5,6},{6,7},{8,9},{9,10},{10,11},{12,13},{... | collective-permute-start | bytes 196616 | tf_op jit(solution)/shard_map/ppermute | solution.py:14
  133.0 2.2 %collective-permute-start.5 = (f32[1,32,512]{2,1,0:T(8,128)S(1)}, f32[1,32,512]{2,1,0:T(8,128)S(1)}, u32[]{:S(2)}, u32[]{:S(2)}) collective-permute-start(f32[1,32,512]{2,1,0:T(8,128)S(1)} %slice.154), channel_id=1, source_target_pairs={{0,4},{4,8},{8,12},{12,16},{16,20},{20,24},{24,28},{1,5},{5,9},{9,... | collective-permute-start | bytes 196616 | tf_op jit(solution)/shard_map/ppermute | solution.py:14
  135.2 3.6 %collective-permute-start.4 = (f32[1,32,512]{2,1,0:T(8,128)S(1)}, f32[1,32,512]{2,1,0:T(8,128)S(1)}, u32[]{:S(2)}, u32[]{:S(2)}) collective-permute-start(f32[1,32,512]{2,1,0:T(8,128)S(1)} %get-tuple-element.21), channel_id=1, source_target_pairs={{4,0},{8,4},{12,8},{16,12},{20,16},{24,20},{28,24},{5,1},{9,5},{13... | collective-permute-start | bytes 196616 | tf_op jit(solution)/shard_map/ppermute | solution.py:14
  138.9 2.9 %collective-permute-start.6 = (f32[32,512]{1,0:T(8,128)S(1)}, f32[32,512]{1,0:T(8,128)S(1)}, u32[]{:S(2)}, u32[]{:S(2)}) collective-permute-start(f32[32,512]{1,0:T(8,128)S(1)} %get-tuple-element.42), channel_id=1, source_target_pairs={{1,0},{2,1},{3,2},{5,4},{6,5},{7,6},{9,8},{10,9},{11,10},{13,12},{... | collective-permute-start | bytes 196616 | tf_op jit(solution)/shard_map/ppermute | solution.py:14
  141.9 4.0 %collective-permute-done.6 = f32[32,512]{1,0:T(8,128)S(1)} collective-permute-done((f32[32,512]{1,0:T(8,128)S(1)}, f32[32,512]{1,0:T(8,128)S(1)}, u32[]{:S(2)}, u32[]{:S(2)}) %collective-permute-start.6) | collective-permute-done | bytes 65568 | tf_op jit(solution)/shard_map/ppermute | solution.py:14
  146.1 2.6 %fusion.18 = (f32[32,32,512]{2,1,0:T(8,128)S(1)}, f32[32,32,512]{2,1,0:T(8,128)S(1)}, f32[32,32,512]{2,1,0:T(8,128)S(1)}) fusion(f32[32,32,512]{2,1,0:T(8,128)S(1)} %copy-done.12, f32[32,32,512]{2,1,0:T(8,128)S(1)} %get-tuple-element.20, f32[1,32,512]{2,1,0:T(8,128)S(1)} %collective-permute-done.4, f32[31,32,512]{2,1,0:T(8,128)S(1)} %slice.153, ...), kind=kLoop, calls=%fused_computation.29 | loop fusion | flops 8388608 | bytes 23064576 | tf_op jit(solution)/shard_map/sub | solution.py:127
  149.0 2.6 %multiply_add_fusion = (f32[32,32,512]{2,1,0:T(8,128)S(1)}, f32[32,32,512]{2,1,0:T(8,128)S(1)}) fusion(f32[32,32,512]{2,1,0:T(8,128)S(1)} %get-tuple-element.20, f32[32,32,512]{2,1,0:T(8,128)S(1)} %copy-done.5, f32[32,32,512]{2,1,0:T(8,128)S(1)} %get-tuple-element.29, f32[32,32,511]{2,1,0:T(8,128)S(1)} %bitcast.66, f32[32,32,512]{2,1,0:T(8,128)S(1)} %get-tuple-element.30, ...), kind=kLoop, calls=%fused_computation.37 | loop fusion | flops 7864320 | bytes 23064576 | tf_op jit(solution)/shard_map/add | solution.py:140
  153.1 1.3 copy-done.19
  (97 shorter events, 9.7 us)
Async XLA Ops:
  0.6 40.8 %copy-start = (bf16[16,32,512]{2,1,0:T(8,128)(2,1)S(1)}, bf16[16,32,512]{2,1,0:T(8,128)(2,1)}, u32[]{:S(2)}) copy-start(bf16[16,32,512]{2,1,0:T(8,128)(2,1)} %param.18) | copy-start | bytes 1572868
  0.6 23.4 %slice-start = ((f32[32,32,512]{2,1,0:T(8,128)}), f32[1,32,512]{2,1,0:T(8,128)S(1)}, s32[]{:S(2)}) async-start(f32[32,32,512]{2,1,0:T(8,128)} %param.14), calls=%async_computation.3 | async-start | bytes 131072 | tf_op jit(solution)/shard_map/slice | solution.py:103
  0.7 23.4 %slice-start.1 = ((f32[32,32,512]{2,1,0:T(8,128)}), f32[1,32,512]{2,1,0:T(8,128)S(1)}, s32[]{:S(2)}) async-start(f32[32,32,512]{2,1,0:T(8,128)} %param.11), calls=%async_computation.4 | async-start | bytes 131072 | tf_op jit(solution)/shard_map/slice | solution.py:103
  0.7 25.4 %copy-start.20 = (bf16[768,2,512]{2,1,0:T(2,128)(2,1)S(1)}, bf16[768,2,512]{2,1,0:T(2,128)(2,1)}, u32[]{:S(2)}) copy-start(bf16[768,2,512]{2,1,0:T(2,128)(2,1)} %param.15) | copy-start | bytes 4718596
  4.0 26.5 %all-to-all-start = ((s32[32,1,48]{2,1,0:T(1,128)}), s32[32,1,48]{2,1,0:T(1,128)S(1)}, u32[]{:S(2)}, u32[]{:S(2)}) async-start(s32[32,1,48]{2,1,0:T(1,128)} %sub.118), calls=%async_computation | async-start | bytes 32768 | tf_op jit(solution)/shard_map/all_to_all | solution.py:51
  11.5 19.1 %collective-permute-start = (f32[1,32,512]{2,1,0:T(8,128)}, f32[1,32,512]{2,1,0:T(8,128)S(1)}, u32[]{:S(2)}, u32[]{:S(2)}) collective-permute-start(f32[1,32,512]{2,1,0:T(8,128)} %get-tuple-element.40), channel_id=1, source_target_pairs={{4,0},{8,4},{12,8},{16,12},{20,16},{24,20},{28,24},{5,1},{9,5},{13... | collective-permute-start | bytes 196616 | tf_op jit(solution)/shard_map/ppermute | solution.py:14
  15.0 15.5 %collective-permute-start.1 = (f32[32,512]{1,0:T(8,128)S(1)}, f32[32,512]{1,0:T(8,128)S(1)}, u32[]{:S(2)}, u32[]{:S(2)}) collective-permute-start(f32[32,512]{1,0:T(8,128)S(1)} %bitcast.78), channel_id=1, source_target_pairs={{1,0},{2,1},{3,2},{5,4},{6,5},{7,6},{9,8},{10,9},{11,10},{13,12},{... | collective-permute-start | bytes 196616 | tf_op jit(solution)/shard_map/ppermute | solution.py:14
  19.7 6.7 %copy-start.23 = (s32[768]{0:T(1024)S(1)}, s32[768]{0:T(1024)}, u32[]{:S(2)}) copy-start(s32[768]{0:T(1024)} %copy-done.22) | copy-start | bytes 9220
  19.8 10.7 %collective-permute-start.3 = (f32[3,32,512]{2,1,0:T(8,128)S(1)}, f32[3,32,512]{2,1,0:T(8,128)S(1)}, u32[]{:S(2)}, u32[]{:S(2)}) collective-permute-start(f32[3,32,512]{2,1,0:T(8,128)S(1)} %pad_maximum_fusion.1), channel_id=1, source_target_pairs={{0,1},{1,2},{2,3},{4,5},{5,6},{6,7},{8,9},{9,10},{10,11},{12,13},{... | collective-permute-start | bytes 589832 | tf_op jit(solution)/shard_map/ppermute | solution.py:14
  24.1 7.0 %collective-permute-start.2 = (f32[3,32,512]{2,1,0:T(8,128)S(1)}, f32[3,32,512]{2,1,0:T(8,128)S(1)}, u32[]{:S(2)}, u32[]{:S(2)}) collective-permute-start(f32[3,32,512]{2,1,0:T(8,128)S(1)} %pad_maximum_fusion), channel_id=1, source_target_pairs={{0,4},{4,8},{8,12},{12,16},{16,20},{20,24},{24,28},{1,5},{5,9},{9,... | collective-permute-start | bytes 589832 | tf_op jit(solution)/shard_map/ppermute | solution.py:14
  31.1 4.9 %copy-start.2 = (f32[32,32,512]{2,1,0:T(8,128)S(1)}, f32[32,32,512]{2,1,0:T(8,128)}, u32[]{:S(2)}) copy-start(f32[32,32,512]{2,1,0:T(8,128)} %param.10) | copy-start | bytes 6291460
  31.1 73.2 %all-to-all-start.1 = ((bf16[32,48,1024]{2,1,0:T(8,128)(2,1)}), bf16[32,48,1024]{2,1,0:T(8,128)(2,1)}, u32[]{:S(2)}, u32[]{:S(2)}) async-start(bf16[32,48,1024]{2,1,0:T(8,128)(2,1)} %bitcast.68), calls=%async_computation.1 | async-start | bytes 6291456 | tf_op jit(solution)/shard_map/all_to_all | solution.py:59
  104.3 23.3 %all-to-all-start.2 = ((bf16[8,32,512]{2,1,0:T(8,128)(2,1)}), bf16[8,32,512]{2,1,0:T(8,128)(2,1)S(1)}, u32[]{:S(2)}, u32[]{:S(2)}) async-start(bf16[8,32,512]{2,1,0:T(8,128)(2,1)} %broadcast_select_fusion), calls=%async_computation.2 | async-start | bytes 524288 | tf_op jit(solution)/shard_map/all_to_all | solution.py:85
  116.0 7.5 %copy-start.3 = (f32[32,32,512]{2,1,0:T(8,128)S(1)}, f32[32,32,512]{2,1,0:T(8,128)}, u32[]{:S(2)}) copy-start(f32[32,32,512]{2,1,0:T(8,128)} %param.10) | copy-start | bytes 6291460
  116.0 7.5 %copy-start.4 = (f32[32,32,512]{2,1,0:T(8,128)S(1)}, f32[32,32,512]{2,1,0:T(8,128)}, u32[]{:S(2)}) copy-start(f32[32,32,512]{2,1,0:T(8,128)} %param.14) | copy-start | bytes 6291460
  116.0 7.5 %copy-start.6 = (f32[32,32,512]{2,1,0:T(8,128)S(1)}, f32[32,32,512]{2,1,0:T(8,128)}, u32[]{:S(2)}) copy-start(f32[32,32,512]{2,1,0:T(8,128)} %get-tuple-element.32) | copy-start | bytes 6291460
  116.0 7.5 %copy-start.8 = (f32[32,32,512]{2,1,0:T(8,128)S(1)}, f32[32,32,512]{2,1,0:T(8,128)}, u32[]{:S(2)}) copy-start(f32[32,32,512]{2,1,0:T(8,128)} %get-tuple-element.33) | copy-start | bytes 6291460
  116.0 7.5 %copy-start.11 = (f32[32,32,512]{2,1,0:T(8,128)S(1)}, f32[32,32,512]{2,1,0:T(8,128)}, u32[]{:S(2)}) copy-start(f32[32,32,512]{2,1,0:T(8,128)} %copy-done.10) | copy-start | bytes 6291460
  116.0 7.5 %copy-start.16 = (f32[31,32,512]{2,1,0:T(8,128)S(1)}, f32[31,32,512]{2,1,0:T(8,128)}, u32[]{:S(2)}) copy-start(f32[31,32,512]{2,1,0:T(8,128)} %slice.147) | copy-start | bytes 6094852
  128.7 10.1 %collective-permute-start.7 = (f32[32,512]{1,0:T(8,128)S(1)}, f32[32,512]{1,0:T(8,128)S(1)}, u32[]{:S(2)}, u32[]{:S(2)}) collective-permute-start(f32[32,512]{1,0:T(8,128)S(1)} %bitcast.79), channel_id=1, source_target_pairs={{0,1},{1,2},{2,3},{4,5},{5,6},{6,7},{8,9},{9,10},{10,11},{12,13},{... | collective-permute-start | bytes 196616 | tf_op jit(solution)/shard_map/ppermute | solution.py:14
  132.0 14.0 %copy-start.9 = (f32[32,32,512]{2,1,0:T(8,128)S(1)}, f32[32,32,512]{2,1,0:T(8,128)}, u32[]{:S(2)}) copy-start(f32[32,32,512]{2,1,0:T(8,128)} %get-tuple-element.33) | copy-start | bytes 6291460
  132.0 14.0 %copy-start.12 = (f32[32,32,512]{2,1,0:T(8,128)S(1)}, f32[32,32,512]{2,1,0:T(8,128)}, u32[]{:S(2)}) copy-start(f32[32,32,512]{2,1,0:T(8,128)} %copy-done.10) | copy-start | bytes 6291460
  132.6 13.4 %copy-start.5 = (f32[32,32,512]{2,1,0:T(8,128)S(1)}, f32[32,32,512]{2,1,0:T(8,128)}, u32[]{:S(2)}) copy-start(f32[32,32,512]{2,1,0:T(8,128)} %param.14) | copy-start | bytes 6291460
  132.7 13.4 %copy-start.7 = (f32[32,32,512]{2,1,0:T(8,128)S(1)}, f32[32,32,512]{2,1,0:T(8,128)}, u32[]{:S(2)}) copy-start(f32[32,32,512]{2,1,0:T(8,128)} %get-tuple-element.32) | copy-start | bytes 6291460
  133.0 8.8 %collective-permute-start.5 = (f32[1,32,512]{2,1,0:T(8,128)S(1)}, f32[1,32,512]{2,1,0:T(8,128)S(1)}, u32[]{:S(2)}, u32[]{:S(2)}) collective-permute-start(f32[1,32,512]{2,1,0:T(8,128)S(1)} %slice.154), channel_id=1, source_target_pairs={{0,4},{4,8},{8,12},{12,16},{16,20},{20,24},{24,28},{1,5},{5,9},{9,... | collective-permute-start | bytes 196616 | tf_op jit(solution)/shard_map/ppermute | solution.py:14
  135.2 10.8 %collective-permute-start.4 = (f32[1,32,512]{2,1,0:T(8,128)S(1)}, f32[1,32,512]{2,1,0:T(8,128)S(1)}, u32[]{:S(2)}, u32[]{:S(2)}) collective-permute-start(f32[1,32,512]{2,1,0:T(8,128)S(1)} %get-tuple-element.21), channel_id=1, source_target_pairs={{4,0},{8,4},{12,8},{16,12},{20,16},{24,20},{28,24},{5,1},{9,5},{13... | collective-permute-start | bytes 196616 | tf_op jit(solution)/shard_map/ppermute | solution.py:14
  138.9 7.1 %collective-permute-start.6 = (f32[32,512]{1,0:T(8,128)S(1)}, f32[32,512]{1,0:T(8,128)S(1)}, u32[]{:S(2)}, u32[]{:S(2)}) collective-permute-start(f32[32,512]{1,0:T(8,128)S(1)} %get-tuple-element.42), channel_id=1, source_target_pairs={{1,0},{2,1},{3,2},{5,4},{6,5},{7,6},{9,8},{10,9},{11,10},{13,12},{... | collective-permute-start | bytes 196616 | tf_op jit(solution)/shard_map/ppermute | solution.py:14
  146.0 2.9 %copy-start.18 = (f32[32,32,2,512]{3,1,2,0:T(8,128)S(1)}, f32[32,32,2,512]{3,1,2,0:T(8,128)}, u32[]{:S(2)}) copy-start(f32[32,32,2,512]{3,1,2,0:T(8,128)} %copy-done.17) | copy-start | bytes 12582916
  148.7 3.0 %copy-start.13 = (f32[32,32,512]{2,1,0:T(8,128)}, f32[32,32,512]{2,1,0:T(8,128)S(1)}, u32[]{:S(2)}) copy-start(f32[32,32,512]{2,1,0:T(8,128)S(1)} %get-tuple-element.29) | copy-start | bytes 6291460
  148.7 3.0 %copy-start.14 = (f32[32,32,512]{2,1,0:T(8,128)}, f32[32,32,512]{2,1,0:T(8,128)S(1)}, u32[]{:S(2)}) copy-start(f32[32,32,512]{2,1,0:T(8,128)S(1)} %get-tuple-element.30) | copy-start | bytes 6291460
  148.7 3.5 %copy-start.15 = (f32[32,32,512]{2,1,0:T(8,128)}, f32[32,32,512]{2,1,0:T(8,128)S(1)}, u32[]{:S(2)}) copy-start(f32[32,32,512]{2,1,0:T(8,128)S(1)} %get-tuple-element.28) | copy-start | bytes 6291460
  149.0 5.4 %copy-start.1 = (bf16[16,32,512]{2,1,0:T(8,128)(2,1)S(1)}, bf16[16,32,512]{2,1,0:T(8,128)(2,1)}, u32[]{:S(2)}) copy-start(bf16[16,32,512]{2,1,0:T(8,128)(2,1)} %param.18) | copy-start | bytes 1572868
  (5 other events, 7.2 us)
